TPU v7x, 256 devices: a whole 4x4x8 slice. The times are simulated.
256 devices in a mesh: zslab: 8 (over y, x_lo), blk: 32 (over z, x_hi, core).
Axes of the slice: x: 4 (x_hi: 2, x_lo: 2; x = x_hi * 2 + x_lo), y: 4, z: 8, core: 2. Of those that a mesh axis runs over, the one named last changes fastest.
Arguments:
- field: bfloat16 [256, 16, 32, 128], P('blk', None, 'zslab'), may hold values from -6 to 6
- fracture_mask: int32 [256, 16, 32], P('blk', None, 'zslab'), may hold values 0 or 1
- dilation: int32 [2, 3], replicated, may hold values from 1 to 2, as said below
- conv_weight: bfloat16 [2, 3456, 128], replicated, may hold values from -0.109375 to 0.109375
- embed_weight: bfloat16 [8, 2048, 1024], P('zslab', 'blk'), may hold values from -0.046875 to 0.046875
- qkv_weight: bfloat16 [3, 1024, 1024], P(None, 'blk', 'zslab'), may hold values from -3 to 3
- out_grad: bfloat16 [1024, 1024], P('blk', 'zslab'), may hold values from -6 to 6
Outputs:
- field_grad: bfloat16 [256, 16, 32, 128], P('blk', None, 'zslab')
Inputs may be any that keep to these rules, and one draw needn't show every extreme that they name: The dilation of each of the 2 layers along x, y and z; some entry is 1 and some entry is 2.
All inputs are finite; a program needn't handle non-finite values. No bound on the sum of `fracture_mask` on one device may be relied on, other than what follows from the above.
Results may differ from a plain program's by a relative error of at most 0.04.
Values may be sent and summed in bfloat16 or wider, within the bound.
No kernel may reach another device: no remote copies, remote signals or barrier semaphores. Data moves between devices by JAX's collectives and lax.ppermute only.
A program may use at most 64 MiB of HBM per device.

v0:
```python
import jax
import jax.numpy as jnp
from jax import lax
from jax.sharding import PartitionSpec as P

HD = 128
PY = 8
PZ = 2
LAYERS = 2
DMAX = 2


def padded_2(cells, sides, width):
    for axis, dim in sides:
        count = lax.axis_size(axis)
        ends = count - 1
        head = lax.slice_in_dim(cells, 0, width, axis=dim)
        tail = lax.slice_in_dim(cells, cells.shape[dim] - width, cells.shape[dim], axis=dim)
        cells = jnp.concatenate(
            [
                lax.ppermute(tail, axis, [(i, (i + 1) % count) for i in range(ends)]),
                cells,
                lax.ppermute(head, axis, [((i + 1) % count, i) for i in range(ends)]),
            ],
            axis=dim,
        )
    return cells


def copy_for_each(shard, axis):
    peers = lax.axis_size(axis)
    return lax.all_to_all(
        jnp.broadcast_to(shard[None], (peers, *shard.shape)), axis, 0, 0, tiled=True
    )


def taken_together(shard, axis):
    return copy_for_each(shard, axis).astype(jnp.float32).sum(axis=0)


def joined_along(pieces, dim):
    shape = list(pieces.shape[1:])
    shape[dim] *= pieces.shape[0]
    return jnp.moveaxis(pieces, 0, dim).reshape(shape)


def gather_together(arrays, axis, dims):
    line = jnp.concatenate([a.reshape(-1) for a in arrays])
    lines, at, finished = (lax.all_gather(line, axis), 0, [])
    for a, dim in zip(arrays, dims):
        pieces = lines[:, at : at + a.size].reshape(-1, *a.shape)
        finished.append(joined_along(pieces, dim))
        at += a.size
    return tuple(finished)


def side_by_side(arrays, axis, dim, along):
    ends, at = ([], 0)
    for a in arrays[:-1]:
        at += a.shape[along]
        ends.append(at)
    both = jnp.concatenate(arrays, axis=along)
    return tuple(jnp.split(lax.all_gather(both, axis, axis=dim, tiled=True), ends, axis=along))


def cut_along(shard, dim, peers):
    before, after = (shard.shape[:dim], shard.shape[dim + 1 :])
    return jnp.moveaxis(shard.reshape(*before, peers, -1, *after), dim, 0)


def sum_at_owner(shard, axis, dim):
    peers = lax.axis_size(axis)
    pieces = lax.all_to_all(cut_along(shard, dim, peers), axis, 0, 0, tiled=True)
    return jnp.sum(pieces.astype(jnp.float32), axis=0)


def with_rim(volume):
    padded = padded_2(volume, (("zslab", 2), ("blk", 0)), DMAX)
    return jnp.pad(padded, ((0, 0), (DMAX, DMAX), (0, 0), (0, 0)))


def apply_offsets(padded, weight, dilate, direction, dims_out):
    x_cells, y_cells, z_cells, channels = dims_out
    summed = jnp.zeros((x_cells * y_cells * z_cells, weight.shape[-1]), jnp.float32)
    for offset_x in (-1, 0, 1):
        pieces = []
        for offset_y in (-1, 0, 1):
            for offset_z in (-1, 0, 1):
                anchor = (
                    DMAX + direction * offset_x * dilate[0],
                    DMAX + direction * offset_y * dilate[1],
                    DMAX + direction * offset_z * dilate[2],
                    jnp.int32(0),
                )
                pieces.append(
                    lax.dynamic_slice(padded, anchor, (x_cells, y_cells, z_cells, channels))
                )
        stacked = jnp.concatenate(pieces, axis=3).reshape(x_cells * y_cells * z_cells, 9 * channels)
        group_rows = weight[(offset_x + 1) * 9 * channels : (offset_x + 2) * 9 * channels]
        summed = summed + jnp.dot(stacked, group_rows, preferred_element_type=jnp.float32)
    return summed.reshape(x_cells, y_cells, z_cells, -1)


def slab_total(term):
    return taken_together(term.astype(jnp.bfloat16), "zslab").astype(jnp.float32)


def local(field, fracture_mask, dilation, conv_weight, embed_weight, qkv_weight, out_grad):
    x_cells, y_cells, z_cells, channels = field.shape
    gate_mask = fracture_mask.astype(jnp.float32)[..., None]
    hidden = field
    conv_outs = []
    for layer_num in range(LAYERS):
        conv_out = apply_offsets(
            with_rim(hidden), conv_weight[layer_num], dilation[layer_num], 1, field.shape
        )
        conv_outs.append(conv_out)
        hidden = (
            hidden.astype(jnp.float32) + gate_mask * (conv_out * jax.nn.sigmoid(conv_out))
        ).astype(jnp.bfloat16)
    slab_view = lax.all_to_all(hidden, "zslab", split_axis=0, concat_axis=2, tiled=True)
    x_local, z_total = (slab_view.shape[0], slab_view.shape[2])
    y_blocks, z_blocks = (y_cells // PY, z_total // PZ)
    patches = slab_view.reshape(x_local, y_blocks, PY, z_blocks, PZ, channels).transpose(
        1, 3, 0, 2, 4, 5
    )
    patches = patches.reshape(y_blocks * z_blocks, x_local, PY * PZ * channels)
    embed_rows, qkv_rows = gather_together((embed_weight, qkv_weight), "blk", (1, 1))
    partial_value = jnp.einsum(
        "tpf,pfd->td", patches, embed_rows, preferred_element_type=jnp.float32
    )
    tokens = slab_total(partial_value).astype(jnp.bfloat16)
    projected = jnp.einsum(
        "td,sde->ste", tokens, qkv_rows, preferred_element_type=jnp.float32
    ).astype(jnp.bfloat16)
    key_rows, value_rows = side_by_side((projected[1], projected[2]), "blk", 0, 1)
    tok_rows = tokens.shape[0]
    head_cols = projected.shape[2]
    heads_here = head_cols // HD
    inv_root = HD ** (-0.5)
    queries = projected[0].reshape(tok_rows, heads_here, HD)
    key_all = key_rows.reshape(-1, heads_here, HD)
    value_all = value_rows.reshape(-1, heads_here, HD)
    grad_out = out_grad.reshape(tok_rows, heads_here, HD)
    scores = (
        jnp.einsum("qhd,khd->hqk", queries, key_all, preferred_element_type=jnp.float32) * inv_root
    )
    top_score = jnp.max(scores, axis=2, keepdims=True)
    expo = jnp.exp(scores - top_score)
    total = jnp.sum(expo, axis=2, keepdims=True)
    probs = expo / total
    probs_b = probs.astype(jnp.bfloat16)
    attended = jnp.einsum("hqk,khd->qhd", probs_b, value_all, preferred_element_type=jnp.float32)
    row_delta = jnp.sum(grad_out.astype(jnp.float32) * attended, axis=2).T[:, :, None]
    score_grad = jnp.einsum("qhd,khd->hqk", grad_out, value_all, preferred_element_type=jnp.float32)
    dscore = (probs * (score_grad - row_delta) * inv_root).astype(jnp.bfloat16)
    grad_query = jnp.einsum("hqk,khd->qhd", dscore, key_all, preferred_element_type=jnp.float32)
    grad_query = grad_query.astype(jnp.bfloat16).reshape(tok_rows, head_cols)
    key_term = jnp.einsum("hqk,qhd->khd", dscore, queries, preferred_element_type=jnp.float32)
    value_term = jnp.einsum("hqk,qhd->khd", probs_b, grad_out, preferred_element_type=jnp.float32)
    key_value_grad = sum_at_owner(
        jnp.concatenate(
            [
                key_term.reshape(tok_rows * lax.axis_size("blk"), head_cols),
                value_term.reshape(tok_rows * lax.axis_size("blk"), head_cols),
            ],
            axis=1,
        ).astype(jnp.bfloat16),
        "blk",
        0,
    ).astype(jnp.bfloat16)
    grad_key = key_value_grad[:, :head_cols]
    grad_value = key_value_grad[:, head_cols:]
    stacked_grads = jnp.stack([grad_query, grad_key, grad_value])
    embed_rows, qkv_rows = gather_together((embed_weight, qkv_weight), "blk", (1, 1))
    partial_grad = jnp.einsum(
        "ste,sde->td", stacked_grads, qkv_rows, preferred_element_type=jnp.float32
    )
    grad_tokens = slab_total(partial_grad).astype(jnp.bfloat16)
    patch_grad = jnp.einsum(
        "td,pfd->tpf", grad_tokens, embed_rows, preferred_element_type=jnp.float32
    ).astype(jnp.bfloat16)
    grid_grad = patch_grad.reshape(y_blocks, z_blocks, x_local, PY, PZ, channels).transpose(
        2, 0, 3, 1, 4, 5
    )
    grid_grad = grid_grad.reshape(x_local, y_cells, z_total, channels)
    grid_grad = lax.all_to_all(grid_grad, "zslab", split_axis=2, concat_axis=0, tiled=True)
    for layer_num in reversed(range(LAYERS)):
        conv_out = conv_outs[layer_num]
        sigma = jax.nn.sigmoid(conv_out)
        slope_grad = (
            gate_mask * sigma * (1.0 + conv_out * (1.0 - sigma)) * grid_grad.astype(jnp.float32)
        ).astype(jnp.bfloat16)
        flipped = (
            conv_weight[layer_num]
            .reshape(27, channels, channels)
            .transpose(0, 2, 1)
            .reshape(27 * channels, channels)
        )
        backward = apply_offsets(
            with_rim(slope_grad), flipped, dilation[layer_num], -1, field.shape
        )
        grid_grad = (grid_grad.astype(jnp.float32) + backward).astype(jnp.bfloat16)
    return grid_grad


def solution(mesh):
    return jax.shard_map(
        local,
        mesh=mesh,
        in_specs=(
            P("blk", None, "zslab", None),
            P("blk", None, "zslab"),
            P(),
            P(),
            P("zslab", "blk", None),
            P(None, "blk", "zslab"),
            P("blk", "zslab"),
        ),
        out_specs=P("blk", None, "zslab", None),
        check_vma=False,
    )
```

profile of v0, /device:TPU:103, one launch (start us, length us, event | category | flops | bytes accessed | tf_op | source)
XLA Modules:
  0.0 304.1 jit_solution(652644530733755094)
XLA Ops:
  12.5 3.7 %collective-permute-start = (bf16[8,16,2,128]{3,2,1,0:T(2,128)(2,1)S(1)}, bf16[8,16,2,128]{3,2,1,0:T(2,128)(2,1)S(1)}, u32[]{:S(2)}, u32[]{:S(2)}) collective-permute-start(bf16[8,16,2,128]{3,2,1,0:T(2,128)(2,1)S(1)} %get-tuple-element.131), channel_id=1, source_target_pairs={{0,32},{32,64},{64,96},{96,128},{128,160},{160,192},{192,224},{1,3... | collective-permute-start | bytes 196616 | tf_op jit(solution)/shard_map/ppermute | solution.py:21
  18.4 4.0 %collective-permute-start.3 = (bf16[2,16,8,128]{3,2,1,0:T(8,128)(2,1)S(1)}, bf16[2,16,8,128]{3,2,1,0:T(8,128)(2,1)S(1)}, u32[]{:S(2)}, u32[]{:S(2)}) collective-permute-start(bf16[2,16,8,128]{3,2,1,0:T(8,128)(2,1)S(1)} %get-tuple-element.124), channel_id=1, source_target_pairs={{1,0},{2,1},{3,2},{4,3},{5,4},{6,5},{7,6},{8,7},{9,8},{10,9},{11,1... | collective-permute-start | bytes 196616 | tf_op jit(solution)/shard_map/ppermute | solution.py:23
  22.4 5.2 %collective-permute-start.2 = (bf16[2,16,8,128]{3,2,1,0:T(8,128)(2,1)S(1)}, bf16[2,16,8,128]{3,2,1,0:T(8,128)(2,1)S(1)}, u32[]{:S(2)}, u32[]{:S(2)}) collective-permute-start(bf16[2,16,8,128]{3,2,1,0:T(8,128)(2,1)S(1)} %get-tuple-element.123), channel_id=1, source_target_pairs={{0,1},{1,2},{2,3},{3,4},{4,5},{5,6},{6,7},{7,8},{8,9},{9,10},{10,1... | collective-permute-start | bytes 196616 | tf_op jit(solution)/shard_map/ppermute | solution.py:21
  43.2 3.3 %reshape.258 = bf16[512,1152]{1,0:T(8,128)(2,1)} reshape(bf16[8,16,4,1152]{3,2,1,0:T(4,128)(2,1)} %copy-done.17) | data formatting | bytes 2359296 | tf_op jit(solution)/shard_map/reshape | solution.py:98
  51.5 4.6 %collective-permute-start.4 = (bf16[8,16,2,128]{3,1,2,0:T(8,128)(2,1)S(1)}, bf16[8,16,2,128]{3,1,2,0:T(8,128)(2,1)S(1)}, u32[]{:S(2)}, u32[]{:S(2)}) collective-permute-start(bf16[8,16,2,128]{3,1,2,0:T(8,128)(2,1)S(1)} %get-tuple-element.129), channel_id=1, source_target_pairs={{0,32},{32,64},{64,96},{96,128},{128,160},{160,192},{192,224},{1,3... | collective-permute-start | bytes 196616 | tf_op jit(solution)/shard_map/ppermute | solution.py:21
  59.4 7.3 %collective-permute-start.6 = (bf16[2,16,8,128]{3,1,2,0:T(8,128)(2,1)S(1)}, bf16[2,16,8,128]{3,1,2,0:T(8,128)(2,1)S(1)}, u32[]{:S(2)}, u32[]{:S(2)}) collective-permute-start(bf16[2,16,8,128]{3,1,2,0:T(8,128)(2,1)S(1)} %get-tuple-element.121), channel_id=1, source_target_pairs={{0,1},{1,2},{2,3},{3,4},{4,5},{5,6},{6,7},{7,8},{8,9},{9,10},{10,1... | collective-permute-start | bytes 196616 | tf_op jit(solution)/shard_map/ppermute | solution.py:21
  88.0 10.8 %all_to_all.39 = bf16[8,16,4,128]{3,1,2,0:T(8,128)(2,1)S(1)} all-to-all(bf16[8,16,4,128]{3,1,2,0:T(8,128)(2,1)S(1)} %add_convert_fusion), channel_id=1, replica_groups=mesh['zslab'=8,'blk'=32] {'zslab'}, dimensions={0} | all-to-all | bytes 262144 | tf_op jit(solution)/shard_map/all_to_all | solution.py:121
  101.3 6.1 %reshape.281 = bf16[32,77824]{1,0:T(8,128)(2,1)} reshape(bf16[2490368]{0:T(1024)(128)(2,1)} %all-gather.3.cloned.1.call-done) | data formatting | bytes 9961472 | tf_op jit(solution)/shard_map/all_gather | solution.py:49
  107.4 4.5 %slice.205 = bf16[32,65536]{1,0:T(8,128)(2,1)} slice(bf16[32,77824]{1,0:T(8,128)(2,1)} %reshape.281), slice={[0:32], [0:65536]} | slice | bytes 8388608 | tf_op jit(solution)/shard_map/slice | solution.py:51
  111.9 5.6 %reshape.266 = bf16[2048,1024]{1,0:T(8,128)(2,1)} reshape(bf16[32,65536]{1,0:T(8,128)(2,1)} %slice.205) | data formatting | bytes 8388608 | tf_op jit(solution)/shard_map/reshape.20
  117.5 3.0 convolution_convert_fusion.3
  121.4 5.2 %all-to-all-start.1 = ((bf16[8,32,1024]{2,1,0:T(8,128)(2,1)}), bf16[8,32,1024]{2,1,0:T(8,128)(2,1)S(1)}, u32[]{:S(2)}, u32[]{:S(2)}) async-start(bf16[8,32,1024]{2,1,0:T(8,128)(2,1)} %broadcast_in_dim.4), calls=%async_computation.1 | async-start | bytes 1048576 | tf_op jit(solution)/shard_map/all_to_all | solution.py:32
  128.0 7.2 %all-to-all-done.1 = bf16[8,32,1024]{2,1,0:T(8,128)(2,1)S(1)} async-done(((bf16[8,32,1024]{2,1,0:T(8,128)(2,1)}), bf16[8,32,1024]{2,1,0:T(8,128)(2,1)S(1)}, u32[]{:S(2)}, u32[]{:S(2)}) %all-to-all-start.1) | async-done | bytes 524320 | tf_op jit(solution)/shard_map/all_to_all | solution.py:32
  135.5 39.4 %all_gather.13 = bf16[1024,256]{1,0:T(8,128)(2,1)S(1)} all-gather(bf16[32,256]{1,0:T(8,128)(2,1)S(1)} %pad_maximum_fusion.14), channel_id=1, replica_groups=mesh['zslab'=8,'blk'=32] {'blk'}, dimensions={0}, use_global_device_ids=true | all-gather | bytes 540672 | tf_op jit(solution)/shard_map/all_gather | solution.py:63
  181.6 10.1 %all-to-all-start.2 = ((bf16[32,32,256]{2,1,0:T(8,128)(2,1)}), bf16[32,32,256]{2,1,0:T(8,128)(2,1)}, u32[]{:S(2)}, u32[]{:S(2)}) async-start(bf16[32,32,256]{2,1,0:T(8,128)(2,1)} %pad_maximum_fusion), calls=%async_computation.2 | async-start | bytes 1048576 | tf_op jit(solution)/shard_map/all_to_all | solution.py:73
  191.8 14.4 %all-to-all-done.2 = bf16[32,32,256]{2,1,0:T(8,128)(2,1)} async-done(((bf16[32,32,256]{2,1,0:T(8,128)(2,1)}), bf16[32,32,256]{2,1,0:T(8,128)(2,1)}, u32[]{:S(2)}, u32[]{:S(2)}) %all-to-all-start.2) | async-done | bytes 524320 | tf_op jit(solution)/shard_map/all_to_all | solution.py:73
  207.8 11.9 %all_to_all.40 = bf16[8,32,1024]{2,1,0:T(8,128)(2,1)S(1)} all-to-all(bf16[8,32,1024]{2,1,0:T(8,128)(2,1)S(1)} %broadcast_in_dim.5), channel_id=1, replica_groups=mesh['zslab'=8,'blk'=32] {'zslab'}, dimensions={0} | all-to-all | bytes 1048576 | tf_op jit(solution)/shard_map/all_to_all | solution.py:32
  219.8 3.5 %convolution_convert_fusion = bf16[32,2048]{1,0:T(8,128)(2,1)S(1)} fusion(bf16[32,1024]{1,0:T(8,128)(2,1)S(1)} %reduce_sum.58, bf16[2048,1024]{1,0:T(8,128)(2,1)} %reshape.266), kind=kOutput, calls=%fused_computation | convolution fusion | flops 134283264 | bytes 4390912 | tf_op jit(solution)/shard_map/td,pfd->tpf/dot_general | solution.py:180
  223.4 8.1 %all_to_all.41 = bf16[1,16,32,128]{3,1,0,2:T(8,128)(2,1)S(1)} all-to-all(bf16[1,16,32,128]{3,1,0,2:T(8,128)(2,1)S(1)} %bitcast.204), channel_id=1, replica_groups=mesh['zslab'=8,'blk'=32] {'zslab'}, dimensions={2} | all-to-all | bytes 262144 | tf_op jit(solution)/shard_map/all_to_all | solution.py:187
  234.6 3.3 %collective-permute-start.8 = (bf16[8,16,2,128]{3,1,2,0:T(8,128)(2,1)S(1)}, bf16[8,16,2,128]{3,1,2,0:T(8,128)(2,1)S(1)}, u32[]{:S(2)}, u32[]{:S(2)}) collective-permute-start(bf16[8,16,2,128]{3,1,2,0:T(8,128)(2,1)S(1)} %get-tuple-element.127), channel_id=1, source_target_pairs={{0,32},{32,64},{64,96},{96,128},{128,160},{160,192},{192,224},{1,3... | collective-permute-start | bytes 196616 | tf_op jit(solution)/shard_map/ppermute | solution.py:21
  239.6 5.8 %collective-permute-start.11 = (bf16[2,16,8,128]{3,1,2,0:T(8,128)(2,1)S(1)}, bf16[2,16,8,128]{3,1,2,0:T(8,128)(2,1)S(1)}, u32[]{:S(2)}, u32[]{:S(2)}) collective-permute-start(bf16[2,16,8,128]{3,1,2,0:T(8,128)(2,1)S(1)} %get-tuple-element.120), channel_id=1, source_target_pairs={{1,0},{2,1},{3,2},{4,3},{5,4},{6,5},{7,6},{8,7},{9,8},{10,9},{11,1... | collective-permute-start | bytes 196616 | tf_op jit(solution)/shard_map/ppermute | solution.py:23
  245.5 5.5 %collective-permute-start.10 = (bf16[2,16,8,128]{3,1,2,0:T(8,128)(2,1)S(1)}, bf16[2,16,8,128]{3,1,2,0:T(8,128)(2,1)S(1)}, u32[]{:S(2)}, u32[]{:S(2)}) collective-permute-start(bf16[2,16,8,128]{3,1,2,0:T(8,128)(2,1)S(1)} %get-tuple-element.119), channel_id=1, source_target_pairs={{0,1},{1,2},{2,3},{3,4},{4,5},{5,6},{6,7},{7,8},{8,9},{9,10},{10,1... | collective-permute-start | bytes 196616 | tf_op jit(solution)/shard_map/ppermute | solution.py:21
  267.6 4.3 %collective-permute-start.12 = (bf16[8,16,2,128]{3,1,2,0:T(8,128)(2,1)S(1)}, bf16[8,16,2,128]{3,1,2,0:T(8,128)(2,1)S(1)}, u32[]{:S(2)}, u32[]{:S(2)}) collective-permute-start(bf16[8,16,2,128]{3,1,2,0:T(8,128)(2,1)S(1)} %get-tuple-element.125), channel_id=1, source_target_pairs={{0,32},{32,64},{64,96},{96,128},{128,160},{160,192},{192,224},{1,3... | collective-permute-start | bytes 196616 | tf_op jit(solution)/shard_map/ppermute | solution.py:21
  275.4 7.2 %collective-permute-start.14 = (bf16[2,16,8,128]{3,1,2,0:T(8,128)(2,1)S(1)}, bf16[2,16,8,128]{3,1,2,0:T(8,128)(2,1)S(1)}, u32[]{:S(2)}, u32[]{:S(2)}) collective-permute-start(bf16[2,16,8,128]{3,1,2,0:T(8,128)(2,1)S(1)} %get-tuple-element.117), channel_id=1, source_target_pairs={{0,1},{1,2},{2,3},{3,4},{4,5},{5,6},{6,7},{7,8},{8,9},{9,10},{10,1... | collective-permute-start | bytes 196616 | tf_op jit(solution)/shard_map/ppermute | solution.py:21
  (212 shorter events, 94.6 us)
Async XLA Ops:
  6.5 27.6 %copy-start.8 = (bf16[8,16,4,128]{3,2,1,0:T(4,128)(2,1)S(1)}, bf16[8,16,4,128]{3,2,1,0:T(4,128)(2,1)}, u32[]{:S(2)}) copy-start(bf16[8,16,4,128]{3,2,1,0:T(4,128)(2,1)} %param.7) | copy-start | bytes 393220
  6.5 21.1 %copy-start.27 = (s32[2,3]{1,0:T(2,128)S(1)}, s32[2,3]{1,0:T(2,128)}, u32[]{:S(2)}) copy-start(s32[2,3]{1,0:T(2,128)} %param.9) | copy-start | bytes 76
  6.5 27.5 %copy-start.26 = (s32[8,16,4]{1,2,0:T(4,128)S(1)}, s32[8,16,4]{1,2,0:T(4,128)}, u32[]{:S(2)}) copy-start(s32[8,16,4]{1,2,0:T(4,128)} %param.8) | copy-start | bytes 6148
  6.5 94.7 %all-gather.3.cloned.1.call-start = ((), (), s32[]{:S(2)}) async-start(), calls=%async_computation.5 | async-start | bytes 5136384 | tf_op jit(solution)/shard_map/all_gather | solution.py:49
  10.0 6.2 %collective-permute-start.1 = (bf16[8,16,2,128]{3,2,1,0:T(2,128)(2,1)S(1)}, bf16[8,16,2,128]{3,2,1,0:T(2,128)(2,1)S(1)}, u32[]{:S(2)}, u32[]{:S(2)}) collective-permute-start(bf16[8,16,2,128]{3,2,1,0:T(2,128)(2,1)S(1)} %get-tuple-element.132), channel_id=1, source_target_pairs={{32,0},{64,32},{96,64},{128,96},{160,128},{192,160},{224,192},{33,... | collective-permute-start | bytes 196616 | tf_op jit(solution)/shard_map/ppermute | solution.py:23
  12.5 5.0 %collective-permute-start = (bf16[8,16,2,128]{3,2,1,0:T(2,128)(2,1)S(1)}, bf16[8,16,2,128]{3,2,1,0:T(2,128)(2,1)S(1)}, u32[]{:S(2)}, u32[]{:S(2)}) collective-permute-start(bf16[8,16,2,128]{3,2,1,0:T(2,128)(2,1)S(1)} %get-tuple-element.131), channel_id=1, source_target_pairs={{0,32},{32,64},{64,96},{96,128},{128,160},{160,192},{192,224},{1,3... | collective-permute-start | bytes 196616 | tf_op jit(solution)/shard_map/ppermute | solution.py:21
  18.4 15.7 %collective-permute-start.3 = (bf16[2,16,8,128]{3,2,1,0:T(8,128)(2,1)S(1)}, bf16[2,16,8,128]{3,2,1,0:T(8,128)(2,1)S(1)}, u32[]{:S(2)}, u32[]{:S(2)}) collective-permute-start(bf16[2,16,8,128]{3,2,1,0:T(8,128)(2,1)S(1)} %get-tuple-element.124), channel_id=1, source_target_pairs={{1,0},{2,1},{3,2},{4,3},{5,4},{6,5},{7,6},{8,7},{9,8},{10,9},{11,1... | collective-permute-start | bytes 196616 | tf_op jit(solution)/shard_map/ppermute | solution.py:23
  22.4 11.7 %collective-permute-start.2 = (bf16[2,16,8,128]{3,2,1,0:T(8,128)(2,1)S(1)}, bf16[2,16,8,128]{3,2,1,0:T(8,128)(2,1)S(1)}, u32[]{:S(2)}, u32[]{:S(2)}) collective-permute-start(bf16[2,16,8,128]{3,2,1,0:T(8,128)(2,1)S(1)} %get-tuple-element.123), channel_id=1, source_target_pairs={{0,1},{1,2},{2,3},{3,4},{4,5},{5,6},{6,7},{7,8},{8,9},{9,10},{10,1... | collective-permute-start | bytes 196616 | tf_op jit(solution)/shard_map/ppermute | solution.py:21
  49.4 23.1 %copy-start.11 = (f32[512,128]{1,0:T(8,128)}, f32[512,128]{1,0:T(8,128)S(1)}, u32[]{:S(2)}) copy-start(f32[512,128]{1,0:T(8,128)S(1)} %convolution_add_fusion.6) | copy-start | bytes 786436
  49.6 6.5 %collective-permute-start.5 = (bf16[8,16,2,128]{3,1,2,0:T(8,128)(2,1)S(1)}, bf16[8,16,2,128]{3,1,2,0:T(8,128)(2,1)S(1)}, u32[]{:S(2)}, u32[]{:S(2)}) collective-permute-start(bf16[8,16,2,128]{3,1,2,0:T(8,128)(2,1)S(1)} %get-tuple-element.130), channel_id=1, source_target_pairs={{32,0},{64,32},{96,64},{128,96},{160,128},{192,160},{224,192},{33,... | collective-permute-start | bytes 196616 | tf_op jit(solution)/shard_map/ppermute | solution.py:23
  51.5 5.9 %collective-permute-start.4 = (bf16[8,16,2,128]{3,1,2,0:T(8,128)(2,1)S(1)}, bf16[8,16,2,128]{3,1,2,0:T(8,128)(2,1)S(1)}, u32[]{:S(2)}, u32[]{:S(2)}) collective-permute-start(bf16[8,16,2,128]{3,1,2,0:T(8,128)(2,1)S(1)} %get-tuple-element.129), channel_id=1, source_target_pairs={{0,32},{32,64},{64,96},{96,128},{128,160},{160,192},{192,224},{1,3... | collective-permute-start | bytes 196616 | tf_op jit(solution)/shard_map/ppermute | solution.py:21
  57.4 14.6 %collective-permute-start.7 = (bf16[2,16,8,128]{3,1,2,0:T(8,128)(2,1)S(1)}, bf16[2,16,8,128]{3,1,2,0:T(8,128)(2,1)S(1)}, u32[]{:S(2)}, u32[]{:S(2)}) collective-permute-start(bf16[2,16,8,128]{3,1,2,0:T(8,128)(2,1)S(1)} %get-tuple-element.122), channel_id=1, source_target_pairs={{1,0},{2,1},{3,2},{4,3},{5,4},{6,5},{7,6},{8,7},{9,8},{10,9},{11,1... | collective-permute-start | bytes 196616 | tf_op jit(solution)/shard_map/ppermute | solution.py:23
  59.4 12.7 %collective-permute-start.6 = (bf16[2,16,8,128]{3,1,2,0:T(8,128)(2,1)S(1)}, bf16[2,16,8,128]{3,1,2,0:T(8,128)(2,1)S(1)}, u32[]{:S(2)}, u32[]{:S(2)}) collective-permute-start(bf16[2,16,8,128]{3,1,2,0:T(8,128)(2,1)S(1)} %get-tuple-element.121), channel_id=1, source_target_pairs={{0,1},{1,2},{2,3},{3,4},{4,5},{5,6},{6,7},{7,8},{8,9},{9,10},{10,1... | collective-permute-start | bytes 196616 | tf_op jit(solution)/shard_map/ppermute | solution.py:21
  121.4 13.7 %all-to-all-start.1 = ((bf16[8,32,1024]{2,1,0:T(8,128)(2,1)}), bf16[8,32,1024]{2,1,0:T(8,128)(2,1)S(1)}, u32[]{:S(2)}, u32[]{:S(2)}) async-start(bf16[8,32,1024]{2,1,0:T(8,128)(2,1)} %broadcast_in_dim.4), calls=%async_computation.1 | async-start | bytes 1048576 | tf_op jit(solution)/shard_map/all_to_all | solution.py:32
  128.0 47.4 %copy-start.28 = (bf16[32,128]{1,0:T(8,128)(2,1)S(1)}, bf16[32,128]{1,0:T(8,128)(2,1)}, u32[]{:S(2)}) copy-start(bf16[32,128]{1,0:T(8,128)(2,1)} %param.13) | copy-start | bytes 24580
  181.6 24.6 %all-to-all-start.2 = ((bf16[32,32,256]{2,1,0:T(8,128)(2,1)}), bf16[32,32,256]{2,1,0:T(8,128)(2,1)}, u32[]{:S(2)}, u32[]{:S(2)}) async-start(bf16[32,32,256]{2,1,0:T(8,128)(2,1)} %pad_maximum_fusion), calls=%async_computation.2 | async-start | bytes 1048576 | tf_op jit(solution)/shard_map/all_to_all | solution.py:73
  231.7 7.2 %collective-permute-start.9 = (bf16[8,16,2,128]{3,1,2,0:T(8,128)(2,1)S(1)}, bf16[8,16,2,128]{3,1,2,0:T(8,128)(2,1)S(1)}, u32[]{:S(2)}, u32[]{:S(2)}) collective-permute-start(bf16[8,16,2,128]{3,1,2,0:T(8,128)(2,1)S(1)} %get-tuple-element.128), channel_id=1, source_target_pairs={{32,0},{64,32},{96,64},{128,96},{160,128},{192,160},{224,192},{33,... | collective-permute-start | bytes 196616 | tf_op jit(solution)/shard_map/ppermute | solution.py:23
  234.6 5.0 %collective-permute-start.8 = (bf16[8,16,2,128]{3,1,2,0:T(8,128)(2,1)S(1)}, bf16[8,16,2,128]{3,1,2,0:T(8,128)(2,1)S(1)}, u32[]{:S(2)}, u32[]{:S(2)}) collective-permute-start(bf16[8,16,2,128]{3,1,2,0:T(8,128)(2,1)S(1)} %get-tuple-element.127), channel_id=1, source_target_pairs={{0,32},{32,64},{64,96},{96,128},{128,160},{160,192},{192,224},{1,3... | collective-permute-start | bytes 196616 | tf_op jit(solution)/shard_map/ppermute | solution.py:21
  239.6 14.1 %collective-permute-start.11 = (bf16[2,16,8,128]{3,1,2,0:T(8,128)(2,1)S(1)}, bf16[2,16,8,128]{3,1,2,0:T(8,128)(2,1)S(1)}, u32[]{:S(2)}, u32[]{:S(2)}) collective-permute-start(bf16[2,16,8,128]{3,1,2,0:T(8,128)(2,1)S(1)} %get-tuple-element.120), channel_id=1, source_target_pairs={{1,0},{2,1},{3,2},{4,3},{5,4},{6,5},{7,6},{8,7},{9,8},{10,9},{11,1... | collective-permute-start | bytes 196616 | tf_op jit(solution)/shard_map/ppermute | solution.py:23
  245.5 8.2 %collective-permute-start.10 = (bf16[2,16,8,128]{3,1,2,0:T(8,128)(2,1)S(1)}, bf16[2,16,8,128]{3,1,2,0:T(8,128)(2,1)S(1)}, u32[]{:S(2)}, u32[]{:S(2)}) collective-permute-start(bf16[2,16,8,128]{3,1,2,0:T(8,128)(2,1)S(1)} %get-tuple-element.119), channel_id=1, source_target_pairs={{0,1},{1,2},{2,3},{3,4},{4,5},{5,6},{6,7},{7,8},{8,9},{9,10},{10,1... | collective-permute-start | bytes 196616 | tf_op jit(solution)/shard_map/ppermute | solution.py:21
  265.7 6.2 %collective-permute-start.13 = (bf16[8,16,2,128]{3,1,2,0:T(8,128)(2,1)S(1)}, bf16[8,16,2,128]{3,1,2,0:T(8,128)(2,1)S(1)}, u32[]{:S(2)}, u32[]{:S(2)}) collective-permute-start(bf16[8,16,2,128]{3,1,2,0:T(8,128)(2,1)S(1)} %get-tuple-element.126), channel_id=1, source_target_pairs={{32,0},{64,32},{96,64},{128,96},{160,128},{192,160},{224,192},{33,... | collective-permute-start | bytes 196616 | tf_op jit(solution)/shard_map/ppermute | solution.py:23
  267.6 5.8 %collective-permute-start.12 = (bf16[8,16,2,128]{3,1,2,0:T(8,128)(2,1)S(1)}, bf16[8,16,2,128]{3,1,2,0:T(8,128)(2,1)S(1)}, u32[]{:S(2)}, u32[]{:S(2)}) collective-permute-start(bf16[8,16,2,128]{3,1,2,0:T(8,128)(2,1)S(1)} %get-tuple-element.125), channel_id=1, source_target_pairs={{0,32},{32,64},{64,96},{96,128},{128,160},{160,192},{192,224},{1,3... | collective-permute-start | bytes 196616 | tf_op jit(solution)/shard_map/ppermute | solution.py:21
  273.4 12.0 %collective-permute-start.15 = (bf16[2,16,8,128]{3,1,2,0:T(8,128)(2,1)S(1)}, bf16[2,16,8,128]{3,1,2,0:T(8,128)(2,1)S(1)}, u32[]{:S(2)}, u32[]{:S(2)}) collective-permute-start(bf16[2,16,8,128]{3,1,2,0:T(8,128)(2,1)S(1)} %get-tuple-element.118), channel_id=1, source_target_pairs={{1,0},{2,1},{3,2},{4,3},{5,4},{6,5},{7,6},{8,7},{9,8},{10,9},{11,1... | collective-permute-start | bytes 196616 | tf_op jit(solution)/shard_map/ppermute | solution.py:23
  275.4 10.0 %collective-permute-start.14 = (bf16[2,16,8,128]{3,1,2,0:T(8,128)(2,1)S(1)}, bf16[2,16,8,128]{3,1,2,0:T(8,128)(2,1)S(1)}, u32[]{:S(2)}, u32[]{:S(2)}) collective-permute-start(bf16[2,16,8,128]{3,1,2,0:T(8,128)(2,1)S(1)} %get-tuple-element.117), channel_id=1, source_target_pairs={{0,1},{1,2},{2,3},{3,4},{4,5},{5,6},{6,7},{7,8},{8,9},{9,10},{10,1... | collective-permute-start | bytes 196616 | tf_op jit(solution)/shard_map/ppermute | solution.py:21
  (24 other events, 56.0 us)
Sparse Core Ops, SparseCore 0:
  10.1 91.0 all-gather.2
where the time goes:
time: 308 us; the launch traced here: 304 us
  starting transfers between devices  79.1 us (26%)
  local copies, waits for them, and re-layouts  73.7 us (24%)
  blocking collectives  70.1 us (23%)
  waiting for transfers between devices  28.7 us (9%)
  between operations  25.7 us (8%)
  matrix products  19.2 us (6%)
  other arithmetic  7.48 us (2%)
    ppermute x8, starting transfers between devices, padded_2(): lax.ppermute(tail, axis, [(i, (i + 1) % count) for i in range(ends)])  40.9 us
    all_gather x1, blocking collectives, side_by_side(): lax.all_gather(both, axis, axis=dim, tiled=True)  39.4 us
    ppermute x8, starting transfers between devices, padded_2(): lax.ppermute(head, axis, [((i + 1) % count, i) for i in range(ends)])  22.9 us
    unnamed x97, local copies, waits for them, and re-layouts  20.7 us
    all_to_all x1, waiting for transfers between devices, sum_at_owner(): lax.all_to_all(cut_along(shard, dim, peers), axis, 0, 0, tiled=True)  14.4 us
    reshape x12, local copies, waits for them, and re-layouts, apply_offsets(): jnp.concatenate(pieces, axis=3)  14.2 us
    all_to_all x1, blocking collectives, copy_for_each(): lax.all_to_all(jnp.broadcast_to(shard[None], (peers, *shard.shape)), axis...  11.9 us
    all_to_all x1, blocking collectives, local(): lax.all_to_all(hidden, 'zslab', split_axis=0, concat_axis=2, tiled=True)  10.8 us
  transfers between devices with their start and end apart: 19, of which 7 were waited for; matrix products, arithmetic and copies ran while one was open for 12% of the time, Pallas kernels for 0%

commit v1 on v0

--- a/solution.py
+++ b/solution.py
@@ -105,6 +105,11 @@
     return taken_together(term.astype(jnp.bfloat16), "zslab").astype(jnp.float32)
 
 
+def slab_sum(term):
+    total = lax.psum(term, "zslab")
+    return lax.reduce_precision(total, exponent_bits=8, mantissa_bits=7).astype(jnp.bfloat16)
+
+
 def local(field, fracture_mask, dilation, conv_weight, embed_weight, qkv_weight, out_grad):
     x_cells, y_cells, z_cells, channels = field.shape
     gate_mask = fracture_mask.astype(jnp.float32)[..., None]
@@ -125,15 +130,16 @@
         1, 3, 0, 2, 4, 5
     )
     patches = patches.reshape(y_blocks * z_blocks, x_local, PY * PZ * channels)
-    embed_rows, qkv_rows = gather_together((embed_weight, qkv_weight), "blk", (1, 1))
+    embed_rows = lax.all_gather(embed_weight, "blk", axis=1, tiled=True)
+    qkv_rows = lax.all_gather(qkv_weight, "blk", axis=1, tiled=True)
     partial_value = jnp.einsum(
         "tpf,pfd->td", patches, embed_rows, preferred_element_type=jnp.float32
     )
-    tokens = slab_total(partial_value).astype(jnp.bfloat16)
+    tokens = slab_sum(partial_value)
     projected = jnp.einsum(
         "td,sde->ste", tokens, qkv_rows, preferred_element_type=jnp.float32
     ).astype(jnp.bfloat16)
-    key_rows, value_rows = side_by_side((projected[1], projected[2]), "blk", 0, 1)
+    key_rows, value_rows = gather_together((projected[1], projected[2]), "blk", (0, 0))
     tok_rows = tokens.shape[0]
     head_cols = projected.shape[2]
     heads_here = head_cols // HD
@@ -158,25 +164,25 @@
     grad_query = grad_query.astype(jnp.bfloat16).reshape(tok_rows, head_cols)
     key_term = jnp.einsum("hqk,qhd->khd", dscore, queries, preferred_element_type=jnp.float32)
     value_term = jnp.einsum("hqk,qhd->khd", probs_b, grad_out, preferred_element_type=jnp.float32)
-    key_value_grad = sum_at_owner(
+    key_value_grad = lax.psum_scatter(
         jnp.concatenate(
             [
                 key_term.reshape(tok_rows * lax.axis_size("blk"), head_cols),
                 value_term.reshape(tok_rows * lax.axis_size("blk"), head_cols),
             ],
             axis=1,
-        ).astype(jnp.bfloat16),
+        ),
         "blk",
-        0,
+        scatter_dimension=0,
+        tiled=True,
     ).astype(jnp.bfloat16)
     grad_key = key_value_grad[:, :head_cols]
     grad_value = key_value_grad[:, head_cols:]
     stacked_grads = jnp.stack([grad_query, grad_key, grad_value])
-    embed_rows, qkv_rows = gather_together((embed_weight, qkv_weight), "blk", (1, 1))
     partial_grad = jnp.einsum(
         "ste,sde->td", stacked_grads, qkv_rows, preferred_element_type=jnp.float32
     )
-    grad_tokens = slab_total(partial_grad).astype(jnp.bfloat16)
+    grad_tokens = slab_sum(partial_grad)
     patch_grad = jnp.einsum(
         "td,pfd->tpf", grad_tokens, embed_rows, preferred_element_type=jnp.float32
     ).astype(jnp.bfloat16)

time: 308 us -> 526 us (1.71)
  waiting for transfers between devices: 28.7 us -> 238 us
  blocking collectives: 70.1 us -> 108 us
  starting transfers between devices: 79.1 us -> 62.4 us
  local copies, waits for them, and re-layouts: 73.7 us -> 62.1 us
    reduce_scatter x0 -> x1, waiting for transfers between devices: none -> 109 us  [local(): lax.psum_scatter(jnp.concatenate([key_term.reshape(tok_rows * lax.axis_si...]
    psum x0 -> x2, waiting for transfers between devices: none -> 107 us  [slab_sum(): total = lax.psum(term, 'zslab')]
    all_gather x1 -> x2, blocking collectives: 39.4 us -> 89.1 us  [the longest x1 46.7 us: gather_together(): lines, at, finished = (lax.all_gather(line, axis), 0, [])]
    all_to_all x2 -> x0, waiting for transfers between devices: 21.6 us -> none  [the longest x1 14.4 us: sum_at_owner(): lax.all_to_all(cut_along(shard, dim, peers), axis, 0, 0, tiled=True)]
    ppermute x8, waiting for transfers between devices: 0.02 us -> 21.5 us  [padded_2(): lax.ppermute(head, axis, [((i + 1) % count, i) for i in range(ends)])]
    all_to_all x2 -> x0, starting transfers between devices: 15.2 us -> none  [the longest x1 10.1 us: sum_at_owner(): lax.all_to_all(cut_along(shard, dim, peers), axis, 0, 0, tiled=True)]
    all_to_all x1 -> x0, blocking collectives: 11.9 us -> none  [copy_for_each(): lax.all_to_all(jnp.broadcast_to(shard[None], (peers, *shard.shape)), axis...]
    unnamed x97 -> x100, local copies, waits for them, and re-layouts: 20.7 us -> 20.5 us
  transfers between devices with their start and end apart: 19 -> 20, of which waited for: 7 -> 11; matrix products, arithmetic and copies ran while one was open for 12% -> 7% of each run, Pallas kernels for 0% -> 0%
where the time goes in v1:
time: 526 us; the launch traced here: 524 us
  waiting for transfers between devices  238 us (45%)
  blocking collectives  108 us (21%)
  starting transfers between devices  62.4 us (12%)
  local copies, waits for them, and re-layouts  62.1 us (12%)
  between operations  26.1 us (5%)
  matrix products  21.6 us (4%)
  other arithmetic  6.31 us (1%)
    reduce_scatter x1, waiting for transfers between devices, local(): lax.psum_scatter(jnp.concatenate([key_term.reshape(tok_rows * lax.axis_si...  109 us
    psum x2, waiting for transfers between devices, slab_sum(): total = lax.psum(term, 'zslab')  107 us
    all_gather x1, blocking collectives, gather_together(): lines, at, finished = (lax.all_gather(line, axis), 0, [])  46.7 us
    ppermute x8, starting transfers between devices, padded_2(): lax.ppermute(tail, axis, [(i, (i + 1) % count) for i in range(ends)])  43.2 us
    all_gather x1, blocking collectives, local(): qkv_rows = lax.all_gather(qkv_weight, 'blk', axis=1, tiled=True)  42.4 us
    ppermute x8, waiting for transfers between devices, padded_2(): lax.ppermute(head, axis, [((i + 1) % count, i) for i in range(ends)])  21.5 us
    unnamed x100, local copies, waits for them, and re-layouts  20.5 us
    ppermute x8, starting transfers between devices, padded_2(): lax.ppermute(head, axis, [((i + 1) % count, i) for i in range(ends)])  19.1 us
  transfers between devices with their start and end apart: 20, of which 11 were waited for; matrix products, arithmetic and copies ran while one was open for 7% of the time, Pallas kernels for 0%

profile of v1, /device:TPU:103, one launch (start us, length us, event | category | flops | bytes accessed | tf_op | source)
XLA Modules:
  0.0 524.3 jit_solution(2170155590760829583)
XLA Ops:
  8.4 3.5 collective-permute-start
  13.8 4.0 collective-permute-done.1
  18.7 7.3 %collective-permute-start.2 = (bf16[2,16,8,128]{3,2,1,0:T(8,128)(2,1)S(1)}, bf16[2,16,8,128]{3,2,1,0:T(8,128)(2,1)S(1)}, u32[]{:S(2)}, u32[]{:S(2)}) collective-permute-start(bf16[2,16,8,128]{3,2,1,0:T(8,128)(2,1)S(1)} %get-tuple-element.125), channel_id=1, source_target_pairs={{0,1},{1,2},{2,3},{3,4},{4,5},{5,6},{6,7},{7,8},{8,9},{9,10},{10,1... | collective-permute-start | bytes 196616 | tf_op jit(solution)/shard_map/ppermute | solution.py:21
  45.8 3.3 reshape.231
  54.2 3.4 collective-permute-start.5
  58.0 2.7 collective-permute-done.5
  60.7 8.4 %collective-permute-start.6 = (bf16[2,16,8,128]{3,1,2,0:T(8,128)(2,1)S(1)}, bf16[2,16,8,128]{3,1,2,0:T(8,128)(2,1)S(1)}, u32[]{:S(2)}, u32[]{:S(2)}) collective-permute-start(bf16[2,16,8,128]{3,1,2,0:T(8,128)(2,1)S(1)} %get-tuple-element.123), channel_id=1, source_target_pairs={{0,1},{1,2},{2,3},{3,4},{4,5},{5,6},{6,7},{7,8},{8,9},{9,10},{10,1... | collective-permute-start | bytes 196616 | tf_op jit(solution)/shard_map/ppermute | solution.py:21
  94.3 9.5 %all_to_all.24 = bf16[8,16,4,128]{3,1,2,0:T(8,128)(2,1)S(1)} all-to-all(bf16[8,16,4,128]{3,1,2,0:T(8,128)(2,1)S(1)} %add_convert_fusion), channel_id=1, replica_groups=mesh['zslab'=8,'blk'=32] {'zslab'}, dimensions={0} | all-to-all | bytes 262144 | tf_op jit(solution)/shard_map/all_to_all | solution.py:126
  104.0 3.7 fusion.2
  107.8 42.4 %all_gather.13 = bf16[3,1024,128]{2,1,0:T(8,128)(2,1)S(1)} all-gather(bf16[3,32,128]{2,1,0:T(8,128)(2,1)S(1)} %copy-done.29), channel_id=1, replica_groups=mesh['zslab'=8,'blk'=32] {'blk'}, dimensions={1}, use_global_device_ids=true | all-gather | bytes 811008 | tf_op jit(solution)/shard_map/all_gather | solution.py:134
  150.1 29.6 %all-reduce.7.cloned.1.call-done = f32[32,1024]{1,0:T(8,128)} async-done(((f32[32,1024]{1,0:T(8,128)}), f32[32,1024]{1,0:T(8,128)}) %all-reduce.7.cloned.1.call-update) | async-done | bytes 131088 | tf_op jit(solution)/shard_map/psum | solution.py:109
  181.0 46.7 %all-gather = bf16[262144]{0:T(1024)(128)(2,1)} all-gather(bf16[8192]{0:T(1024)(128)(2,1)S(1)} %pad_maximum_fusion.13), channel_id=2, replica_groups=mesh['zslab'=8,'blk'=32] {'blk'}, dimensions={0}, use_global_device_ids=true | all-gather | bytes 540672 | tf_op jit(solution)/shard_map/all_gather | solution.py:49
  236.3 108.8 %reduce-scatter.2.cloned.1.call-done = f32[32,256]{1,0:T(8,128)} async-done(((f32[1024,256]{1,0:T(8,128)}), f32[32,256]{1,0:T(8,128)}) %reduce-scatter.2.cloned.1.call-update) | async-done | bytes 32784 | tf_op jit(solution)/shard_map/reduce_scatter | solution.py:167
  346.9 77.3 %all-reduce.9.cloned.1.call-done = f32[32,1024]{1,0:T(8,128)} async-done(((f32[32,1024]{1,0:T(8,128)}), f32[32,1024]{1,0:T(8,128)}) %all-reduce.9.cloned.1.call-update) | async-done | bytes 131088 | tf_op jit(solution)/shard_map/psum | solution.py:109
  424.1 3.6 fusion.4
  427.9 8.9 %all_to_all.25 = bf16[1,16,32,128]{3,1,0,2:T(8,128)(2,1)S(1)} all-to-all(bf16[1,16,32,128]{3,1,0,2:T(8,128)(2,1)S(1)} %bitcast.196), channel_id=1, replica_groups=mesh['zslab'=8,'blk'=32] {'zslab'}, dimensions={2} | all-to-all | bytes 262144 | tf_op jit(solution)/shard_map/all_to_all | solution.py:193
  436.9 2.7 collective-permute-start.8
  439.7 2.5 collective-permute-start.9
  445.6 13.3 %collective-permute-start.10 = (bf16[2,16,8,128]{3,1,2,0:T(8,128)(2,1)S(1)}, bf16[2,16,8,128]{3,1,2,0:T(8,128)(2,1)S(1)}, u32[]{:S(2)}, u32[]{:S(2)}) collective-permute-start(bf16[2,16,8,128]{3,1,2,0:T(8,128)(2,1)S(1)} %get-tuple-element.121), channel_id=1, source_target_pairs={{0,1},{1,2},{2,3},{3,4},{4,5},{5,6},{6,7},{7,8},{8,9},{9,10},{10,1... | collective-permute-start | bytes 196616 | tf_op jit(solution)/shard_map/ppermute | solution.py:21
  463.7 4.4 collective-permute-done.11
  484.3 3.4 collective-permute-start.13
  487.7 2.5 collective-permute-done.13
  490.2 4.2 collective-permute-start.14
  499.4 4.2 collective-permute-done.15
  (214 shorter events, 97.9 us)
Async XLA Ops:
  6.5 97.5 %all-gather.3.cloned.1.call-start = ((), (), s32[]{:S(2)}) async-start(), calls=%async_computation.3 | async-start | bytes 4325376 | tf_op jit(solution)/shard_map/all_gather | solution.py:133
  7.3 172.5 %all-reduce.7.cloned.1.call-start = ((), (), s32[]{:S(2)}) async-start(), calls=%async_computation.4 | async-start | bytes 262144 | tf_op jit(solution)/shard_map/psum | solution.py:109
  8.4 5.4 %collective-permute-start = (bf16[8,16,2,128]{3,2,1,0:T(2,128)(2,1)S(1)}, bf16[8,16,2,128]{3,2,1,0:T(2,128)(2,1)S(1)}, u32[]{:S(2)}, u32[]{:S(2)}) collective-permute-start(bf16[8,16,2,128]{3,2,1,0:T(2,128)(2,1)S(1)} %get-tuple-element.133), channel_id=1, source_target_pairs={{0,32},{32,64},{64,96},{96,128},{128,160},{160,192},{192,224},{1,3... | collective-permute-start | bytes 196616 | tf_op jit(solution)/shard_map/ppermute | solution.py:21
  11.9 5.9 %collective-permute-start.1 = (bf16[8,16,2,128]{3,2,1,0:T(2,128)(2,1)S(1)}, bf16[8,16,2,128]{3,2,1,0:T(2,128)(2,1)S(1)}, u32[]{:S(2)}, u32[]{:S(2)}) collective-permute-start(bf16[8,16,2,128]{3,2,1,0:T(2,128)(2,1)S(1)} %get-tuple-element.134), channel_id=1, source_target_pairs={{32,0},{64,32},{96,64},{128,96},{160,128},{192,160},{224,192},{33,... | collective-permute-start | bytes 196616 | tf_op jit(solution)/shard_map/ppermute | solution.py:23
  18.7 17.3 %collective-permute-start.2 = (bf16[2,16,8,128]{3,2,1,0:T(8,128)(2,1)S(1)}, bf16[2,16,8,128]{3,2,1,0:T(8,128)(2,1)S(1)}, u32[]{:S(2)}, u32[]{:S(2)}) collective-permute-start(bf16[2,16,8,128]{3,2,1,0:T(8,128)(2,1)S(1)} %get-tuple-element.125), channel_id=1, source_target_pairs={{0,1},{1,2},{2,3},{3,4},{4,5},{5,6},{6,7},{7,8},{8,9},{9,10},{10,1... | collective-permute-start | bytes 196616 | tf_op jit(solution)/shard_map/ppermute | solution.py:21
  26.0 10.0 %collective-permute-start.3 = (bf16[2,16,8,128]{3,2,1,0:T(8,128)(2,1)S(1)}, bf16[2,16,8,128]{3,2,1,0:T(8,128)(2,1)S(1)}, u32[]{:S(2)}, u32[]{:S(2)}) collective-permute-start(bf16[2,16,8,128]{3,2,1,0:T(8,128)(2,1)S(1)} %get-tuple-element.126), channel_id=1, source_target_pairs={{1,0},{2,1},{3,2},{4,3},{5,4},{6,5},{7,6},{8,7},{9,8},{10,9},{11,1... | collective-permute-start | bytes 196616 | tf_op jit(solution)/shard_map/ppermute | solution.py:23
  52.1 26.7 %copy-start.11 = (f32[512,128]{1,0:T(8,128)}, f32[512,128]{1,0:T(8,128)S(1)}, u32[]{:S(2)}) copy-start(f32[512,128]{1,0:T(8,128)S(1)} %convolution_add_fusion.6) | copy-start | bytes 786436
  52.3 5.7 %collective-permute-start.4 = (bf16[8,16,2,128]{3,1,2,0:T(8,128)(2,1)S(1)}, bf16[8,16,2,128]{3,1,2,0:T(8,128)(2,1)S(1)}, u32[]{:S(2)}, u32[]{:S(2)}) collective-permute-start(bf16[8,16,2,128]{3,1,2,0:T(8,128)(2,1)S(1)} %get-tuple-element.131), channel_id=1, source_target_pairs={{0,32},{32,64},{64,96},{96,128},{128,160},{160,192},{192,224},{1,3... | collective-permute-start | bytes 196616 | tf_op jit(solution)/shard_map/ppermute | solution.py:21
  54.2 6.5 %collective-permute-start.5 = (bf16[8,16,2,128]{3,1,2,0:T(8,128)(2,1)S(1)}, bf16[8,16,2,128]{3,1,2,0:T(8,128)(2,1)S(1)}, u32[]{:S(2)}, u32[]{:S(2)}) collective-permute-start(bf16[8,16,2,128]{3,1,2,0:T(8,128)(2,1)S(1)} %get-tuple-element.132), channel_id=1, source_target_pairs={{32,0},{64,32},{96,64},{128,96},{160,128},{192,160},{224,192},{33,... | collective-permute-start | bytes 196616 | tf_op jit(solution)/shard_map/ppermute | solution.py:23
  60.7 16.5 %collective-permute-start.6 = (bf16[2,16,8,128]{3,1,2,0:T(8,128)(2,1)S(1)}, bf16[2,16,8,128]{3,1,2,0:T(8,128)(2,1)S(1)}, u32[]{:S(2)}, u32[]{:S(2)}) collective-permute-start(bf16[2,16,8,128]{3,1,2,0:T(8,128)(2,1)S(1)} %get-tuple-element.123), channel_id=1, source_target_pairs={{0,1},{1,2},{2,3},{3,4},{4,5},{5,6},{6,7},{7,8},{8,9},{9,10},{10,1... | collective-permute-start | bytes 196616 | tf_op jit(solution)/shard_map/ppermute | solution.py:21
  69.2 9.3 %collective-permute-start.7 = (bf16[2,16,8,128]{3,1,2,0:T(8,128)(2,1)S(1)}, bf16[2,16,8,128]{3,1,2,0:T(8,128)(2,1)S(1)}, u32[]{:S(2)}, u32[]{:S(2)}) collective-permute-start(bf16[2,16,8,128]{3,1,2,0:T(8,128)(2,1)S(1)} %get-tuple-element.124), channel_id=1, source_target_pairs={{1,0},{2,1},{3,2},{4,3},{5,4},{6,5},{7,6},{8,7},{9,8},{10,9},{11,1... | collective-permute-start | bytes 196616 | tf_op jit(solution)/shard_map/ppermute | solution.py:23
  104.0 3.8 copy-start.29
  107.7 237.4 %reduce-scatter.2.cloned.1.call-start = ((), (), s32[]{:S(2)}) async-start(), calls=%async_computation.5 | async-start | bytes 1081344 | tf_op jit(solution)/shard_map/reduce_scatter | solution.py:167
  180.9 49.9 %copy-start.28 = (bf16[3,32,128]{2,1,0:T(8,128)(2,1)}, bf16[3,32,128]{2,1,0:T(8,128)(2,1)S(1)}, u32[]{:S(2)}) copy-start(bf16[3,32,128]{2,1,0:T(8,128)(2,1)S(1)} %fusion.12) | copy-start | bytes 73732
  236.1 188.0 %all-reduce.9.cloned.1.call-start = ((), (), s32[]{:S(2)}) async-start(), calls=%async_computation.6 | async-start | bytes 262144 | tf_op jit(solution)/shard_map/psum | solution.py:109
  436.9 6.4 %collective-permute-start.8 = (bf16[8,16,2,128]{3,1,2,0:T(8,128)(2,1)S(1)}, bf16[8,16,2,128]{3,1,2,0:T(8,128)(2,1)S(1)}, u32[]{:S(2)}, u32[]{:S(2)}) collective-permute-start(bf16[8,16,2,128]{3,1,2,0:T(8,128)(2,1)S(1)} %get-tuple-element.129), channel_id=1, source_target_pairs={{0,32},{32,64},{64,96},{96,128},{128,160},{160,192},{192,224},{1,3... | collective-permute-start | bytes 196616 | tf_op jit(solution)/shard_map/ppermute | solution.py:21
  439.7 5.9 %collective-permute-start.9 = (bf16[8,16,2,128]{3,1,2,0:T(8,128)(2,1)S(1)}, bf16[8,16,2,128]{3,1,2,0:T(8,128)(2,1)S(1)}, u32[]{:S(2)}, u32[]{:S(2)}) collective-permute-start(bf16[8,16,2,128]{3,1,2,0:T(8,128)(2,1)S(1)} %get-tuple-element.130), channel_id=1, source_target_pairs={{32,0},{64,32},{96,64},{128,96},{160,128},{192,160},{224,192},{33,... | collective-permute-start | bytes 196616 | tf_op jit(solution)/shard_map/ppermute | solution.py:23
  445.6 18.0 %collective-permute-start.10 = (bf16[2,16,8,128]{3,1,2,0:T(8,128)(2,1)S(1)}, bf16[2,16,8,128]{3,1,2,0:T(8,128)(2,1)S(1)}, u32[]{:S(2)}, u32[]{:S(2)}) collective-permute-start(bf16[2,16,8,128]{3,1,2,0:T(8,128)(2,1)S(1)} %get-tuple-element.121), channel_id=1, source_target_pairs={{0,1},{1,2},{2,3},{3,4},{4,5},{5,6},{6,7},{7,8},{8,9},{9,10},{10,1... | collective-permute-start | bytes 196616 | tf_op jit(solution)/shard_map/ppermute | solution.py:21
  458.9 9.2 %collective-permute-start.11 = (bf16[2,16,8,128]{3,1,2,0:T(8,128)(2,1)S(1)}, bf16[2,16,8,128]{3,1,2,0:T(8,128)(2,1)S(1)}, u32[]{:S(2)}, u32[]{:S(2)}) collective-permute-start(bf16[2,16,8,128]{3,1,2,0:T(8,128)(2,1)S(1)} %get-tuple-element.122), channel_id=1, source_target_pairs={{1,0},{2,1},{3,2},{4,3},{5,4},{6,5},{7,6},{8,7},{9,8},{10,9},{11,1... | collective-permute-start | bytes 196616 | tf_op jit(solution)/shard_map/ppermute | solution.py:23
  481.5 15.1 %copy-start.7 = (bf16[1,3456,128]{2,1,0:T(8,128)(2,1)S(1)}, bf16[1,3456,128]{2,1,0:T(8,128)(2,1)}, u32[]{:S(2)}) copy-start(bf16[1,3456,128]{2,1,0:T(8,128)(2,1)} %get-tuple-element.5) | copy-start | bytes 2654212
  482.4 5.3 %collective-permute-start.12 = (bf16[8,16,2,128]{3,1,2,0:T(8,128)(2,1)S(1)}, bf16[8,16,2,128]{3,1,2,0:T(8,128)(2,1)S(1)}, u32[]{:S(2)}, u32[]{:S(2)}) collective-permute-start(bf16[8,16,2,128]{3,1,2,0:T(8,128)(2,1)S(1)} %get-tuple-element.127), channel_id=1, source_target_pairs={{0,32},{32,64},{64,96},{96,128},{128,160},{160,192},{192,224},{1,3... | collective-permute-start | bytes 196616 | tf_op jit(solution)/shard_map/ppermute | solution.py:21
  484.3 5.9 %collective-permute-start.13 = (bf16[8,16,2,128]{3,1,2,0:T(8,128)(2,1)S(1)}, bf16[8,16,2,128]{3,1,2,0:T(8,128)(2,1)S(1)}, u32[]{:S(2)}, u32[]{:S(2)}) collective-permute-start(bf16[8,16,2,128]{3,1,2,0:T(8,128)(2,1)S(1)} %get-tuple-element.128), channel_id=1, source_target_pairs={{32,0},{64,32},{96,64},{128,96},{160,128},{192,160},{224,192},{33,... | collective-permute-start | bytes 196616 | tf_op jit(solution)/shard_map/ppermute | solution.py:23
  490.2 9.2 %collective-permute-start.14 = (bf16[2,16,8,128]{3,1,2,0:T(8,128)(2,1)S(1)}, bf16[2,16,8,128]{3,1,2,0:T(8,128)(2,1)S(1)}, u32[]{:S(2)}, u32[]{:S(2)}) collective-permute-start(bf16[2,16,8,128]{3,1,2,0:T(8,128)(2,1)S(1)} %get-tuple-element.119), channel_id=1, source_target_pairs={{0,1},{1,2},{2,3},{3,4},{4,5},{5,6},{6,7},{7,8},{8,9},{9,10},{10,1... | collective-permute-start | bytes 196616 | tf_op jit(solution)/shard_map/ppermute | solution.py:21
  494.4 9.2 %collective-permute-start.15 = (bf16[2,16,8,128]{3,1,2,0:T(8,128)(2,1)S(1)}, bf16[2,16,8,128]{3,1,2,0:T(8,128)(2,1)S(1)}, u32[]{:S(2)}, u32[]{:S(2)}) collective-permute-start(bf16[2,16,8,128]{3,1,2,0:T(8,128)(2,1)S(1)} %get-tuple-element.120), channel_id=1, source_target_pairs={{1,0},{2,1},{3,2},{4,3},{5,4},{6,5},{7,6},{8,7},{9,8},{10,9},{11,1... | collective-permute-start | bytes 196616 | tf_op jit(solution)/shard_map/ppermute | solution.py:23
  (28 other events, 42.0 us)
Sparse Core Ops, SparseCore 0:
  10.1 88.2 all-gather.2
  107.8 71.9 all-reduce.6
  236.2 108.7 reduce-scatter.1
  347.6 76.5 all-reduce.8

commit v2 on v0

--- a/solution.py
+++ b/solution.py
@@ -72,6 +72,24 @@
     peers = lax.axis_size(axis)
     pieces = lax.all_to_all(cut_along(shard, dim, peers), axis, 0, 0, tiled=True)
     return jnp.sum(pieces.astype(jnp.float32), axis=0)
+
+
+def gather_weights(embed_weight, qkv_weight):
+    _, feat, width = embed_weight.shape
+    qkv_flat = qkv_weight.reshape(-1, width)
+    extra = -qkv_flat.shape[0] % 16
+    rows = jnp.concatenate(
+        [embed_weight[0], qkv_flat, jnp.zeros((extra, width), qkv_flat.dtype)], axis=0
+    )
+    gathered = lax.all_gather(rows, "blk", axis=0, tiled=True)
+    peers = lax.axis_size("blk")
+    gathered = gathered.reshape(peers, rows.shape[0], width)
+    embed_rows = gathered[:, :feat, :]
+    qkv_rows = gathered[:, feat : feat + qkv_flat.shape[0], :].reshape(peers, *qkv_weight.shape)
+    qkv_rows = jnp.moveaxis(qkv_rows, 0, 1).reshape(
+        qkv_weight.shape[0], peers * qkv_weight.shape[1], qkv_weight.shape[2]
+    )
+    return embed_rows, qkv_rows
 
 
 def with_rim(volume):
@@ -125,15 +143,20 @@
         1, 3, 0, 2, 4, 5
     )
     patches = patches.reshape(y_blocks * z_blocks, x_local, PY * PZ * channels)
-    embed_rows, qkv_rows = gather_together((embed_weight, qkv_weight), "blk", (1, 1))
+    embed_rows, qkv_rows = gather_weights(embed_weight, qkv_weight)
+    patches = patches.reshape(patches.shape[0], embed_rows.shape[0], embed_rows.shape[1])
     partial_value = jnp.einsum(
-        "tpf,pfd->td", patches, embed_rows, preferred_element_type=jnp.float32
+        "tbf,bfd->td", patches, embed_rows, preferred_element_type=jnp.float32
     )
     tokens = slab_total(partial_value).astype(jnp.bfloat16)
     projected = jnp.einsum(
         "td,sde->ste", tokens, qkv_rows, preferred_element_type=jnp.float32
     ).astype(jnp.bfloat16)
-    key_rows, value_rows = side_by_side((projected[1], projected[2]), "blk", 0, 1)
+    key_rows, value_rows = jnp.split(
+        joined_along(copy_for_each(jnp.concatenate([projected[1], projected[2]], axis=1), "blk"), 0),
+        2,
+        axis=1,
+    )
     tok_rows = tokens.shape[0]
     head_cols = projected.shape[2]
     heads_here = head_cols // HD
@@ -172,13 +195,12 @@
     grad_key = key_value_grad[:, :head_cols]
     grad_value = key_value_grad[:, head_cols:]
     stacked_grads = jnp.stack([grad_query, grad_key, grad_value])
-    embed_rows, qkv_rows = gather_together((embed_weight, qkv_weight), "blk", (1, 1))
     partial_grad = jnp.einsum(
         "ste,sde->td", stacked_grads, qkv_rows, preferred_element_type=jnp.float32
     )
     grad_tokens = slab_total(partial_grad).astype(jnp.bfloat16)
     patch_grad = jnp.einsum(
-        "td,pfd->tpf", grad_tokens, embed_rows, preferred_element_type=jnp.float32
+        "td,bfd->tbf", grad_tokens, embed_rows, preferred_element_type=jnp.float32
     ).astype(jnp.bfloat16)
     grid_grad = patch_grad.reshape(y_blocks, z_blocks, x_local, PY, PZ, channels).transpose(
         2, 0, 3, 1, 4, 5

time: 308 us -> 286 us (0.929)
  blocking collectives: 70.1 us -> 51.4 us
  waiting for transfers between devices: 28.7 us -> 43.4 us
  local copies, waits for them, and re-layouts: 73.7 us -> 64.3 us
  starting transfers between devices: 79.1 us -> 70.9 us
    all_gather x1 -> x0, blocking collectives: 39.4 us -> none  [side_by_side(): lax.all_gather(both, axis, axis=dim, tiled=True)]
    ppermute x8, waiting for transfers between devices: 0.02 us -> 24.1 us  [padded_2(): lax.ppermute(head, axis, [((i + 1) % count, i) for i in range(ends)])]
    all_to_all x1 -> x2, blocking collectives: 11.9 us -> 33.9 us  [copy_for_each(): lax.all_to_all(jnp.broadcast_to(shard[None], (peers, *shard.shape)), axis...]
    all_gather x1 -> x0, local copies, waits for them, and re-layouts: 6.11 us -> none  [gather_together(): lines, at, finished = (lax.all_gather(line, axis), 0, [])]
    another operation x2 -> x1, local copies, waits for them, and re-layouts: 5.7 us -> 0.13 us  [local(): patches.reshape(patches.shape[0], embed_rows.shape[0], embed_rows.shape[1])]
    ppermute x8, waiting for transfers between devices: 4.79 us -> 0.02 us  [padded_2(): lax.ppermute(tail, axis, [(i, (i + 1) % count) for i in range(ends)])]
    ppermute x8, starting transfers between devices: 22.9 us -> 19.3 us  [padded_2(): lax.ppermute(head, axis, [((i + 1) % count, i) for i in range(ends)])]
    slice x1, local copies, waits for them, and re-layouts: 4.51 us -> 1.3 us  [gather_weights(): gathered[:, feat:feat + qkv_flat.shape[0], :]]
  transfers between devices with their start and end apart: 19 -> 19, of which waited for: 7 -> 10; matrix products, arithmetic and copies ran while one was open for 12% -> 13% of each run, Pallas kernels for 0% -> 0%
where the time goes in v2:
time: 286 us; the launch traced here: 284 us
  starting transfers between devices  70.9 us (25%)
  local copies, waits for them, and re-layouts  64.3 us (22%)
  blocking collectives  51.4 us (18%)
  waiting for transfers between devices  43.4 us (15%)
  between operations  25.7 us (9%)
  matrix products  19.3 us (7%)
  other arithmetic  8.76 us (3%)
    ppermute x8, starting transfers between devices, padded_2(): lax.ppermute(tail, axis, [(i, (i + 1) % count) for i in range(ends)])  38.4 us
    all_to_all x2, blocking collectives, copy_for_each(): lax.all_to_all(jnp.broadcast_to(shard[None], (peers, *shard.shape)), axis...  33.9 us
    ppermute x8, waiting for transfers between devices, padded_2(): lax.ppermute(head, axis, [((i + 1) % count, i) for i in range(ends)])  24.1 us
    unnamed x90, local copies, waits for them, and re-layouts  19.8 us
    ppermute x8, starting transfers between devices, padded_2(): lax.ppermute(head, axis, [((i + 1) % count, i) for i in range(ends)])  19.3 us
    reshape x12, local copies, waits for them, and re-layouts, apply_offsets(): jnp.concatenate(pieces, axis=3)  15.8 us
    all_to_all x1, waiting for transfers between devices, sum_at_owner(): lax.all_to_all(cut_along(shard, dim, peers), axis, 0, 0, tiled=True)  13.5 us
    concatenate x13, local copies, waits for them, and re-layouts, apply_offsets(): jnp.concatenate(pieces, axis=3)  13.1 us
  transfers between devices with their start and end apart: 19, of which 10 were waited for; matrix products, arithmetic and copies ran while one was open for 13% of the time, Pallas kernels for 0%

profile of v2, /device:TPU:103, one launch (start us, length us, event | category | flops | bytes accessed | tf_op | source)
XLA Modules:
  0.0 283.8 jit_solution(709787792103026627)
XLA Ops:
  10.2 3.5 %collective-permute-start = (bf16[8,16,2,128]{3,2,1,0:T(2,128)(2,1)S(1)}, bf16[8,16,2,128]{3,2,1,0:T(2,128)(2,1)S(1)}, u32[]{:S(2)}, u32[]{:S(2)}) collective-permute-start(bf16[8,16,2,128]{3,2,1,0:T(2,128)(2,1)S(1)} %get-tuple-element.131), channel_id=1, source_target_pairs={{0,32},{32,64},{64,96},{96,128},{128,160},{160,192},{192,224},{1,3... | collective-permute-start | bytes 196616 | tf_op jit(solution)/shard_map/ppermute | solution.py:21
  15.6 4.0 %collective-permute-done.1 = bf16[8,16,2,128]{3,2,1,0:T(2,128)(2,1)S(1)} collective-permute-done((bf16[8,16,2,128]{3,2,1,0:T(2,128)(2,1)S(1)}, bf16[8,16,2,128]{3,2,1,0:T(2,128)(2,1)S(1)}, u32[]{:S(2)}, u32[]{:S(2)}) %collective-permute-start.1) | collective-permute-done | bytes 65568 | tf_op jit(solution)/shard_map/ppermute | solution.py:23
  20.5 7.3 %collective-permute-start.2 = (bf16[2,16,8,128]{3,2,1,0:T(8,128)(2,1)S(1)}, bf16[2,16,8,128]{3,2,1,0:T(8,128)(2,1)S(1)}, u32[]{:S(2)}, u32[]{:S(2)}) collective-permute-start(bf16[2,16,8,128]{3,2,1,0:T(8,128)(2,1)S(1)} %get-tuple-element.123), channel_id=1, source_target_pairs={{0,1},{1,2},{2,3},{3,4},{4,5},{5,6},{6,7},{7,8},{8,9},{9,10},{10,1... | collective-permute-start | bytes 196616 | tf_op jit(solution)/shard_map/ppermute | solution.py:21
  46.5 3.2 %reshape.244 = bf16[512,1152]{1,0:T(8,128)(2,1)} reshape(bf16[8,16,4,1152]{3,2,1,0:T(4,128)(2,1)} %copy-done.15) | data formatting | bytes 2359296 | tf_op jit(solution)/shard_map/reshape | solution.py:116
  54.8 3.4 %collective-permute-start.5 = (bf16[8,16,2,128]{3,1,2,0:T(8,128)(2,1)S(1)}, bf16[8,16,2,128]{3,1,2,0:T(8,128)(2,1)S(1)}, u32[]{:S(2)}, u32[]{:S(2)}) collective-permute-start(bf16[8,16,2,128]{3,1,2,0:T(8,128)(2,1)S(1)} %get-tuple-element.130), channel_id=1, source_target_pairs={{32,0},{64,32},{96,64},{128,96},{160,128},{192,160},{224,192},{33,... | collective-permute-start | bytes 196616 | tf_op jit(solution)/shard_map/ppermute | solution.py:23
  58.2 2.7 collective-permute-done.5
  60.9 7.6 %collective-permute-start.6 = (bf16[2,16,8,128]{3,1,2,0:T(8,128)(2,1)S(1)}, bf16[2,16,8,128]{3,1,2,0:T(8,128)(2,1)S(1)}, u32[]{:S(2)}, u32[]{:S(2)}) collective-permute-start(bf16[2,16,8,128]{3,1,2,0:T(8,128)(2,1)S(1)} %get-tuple-element.121), channel_id=1, source_target_pairs={{0,1},{1,2},{2,3},{3,4},{4,5},{5,6},{6,7},{7,8},{8,9},{9,10},{10,1... | collective-permute-start | bytes 196616 | tf_op jit(solution)/shard_map/ppermute | solution.py:21
  93.8 9.4 %all_to_all.44 = bf16[8,16,4,128]{3,1,2,0:T(8,128)(2,1)S(1)} all-to-all(bf16[8,16,4,128]{3,1,2,0:T(8,128)(2,1)S(1)} %add_convert_fusion), channel_id=1, replica_groups=mesh['zslab'=8,'blk'=32] {'zslab'}, dimensions={0} | all-to-all | bytes 262144 | tf_op jit(solution)/shard_map/all_to_all | solution.py:139
  103.4 3.0 %fusion.17 = bf16[32,1024]{1,0:T(8,128)(2,1)S(1)} fusion(bf16[32,80,1024]{2,1,0:T(8,128)(2,1)} %bitcast.208, bf16[32,32,64]{2,1,0:T(8,128)(2,1)S(1)} %reshape_reshape.3), kind=kOutput, calls=%fused_computation.30 | convolution fusion | flops 134250496 | bytes 4390912 | tf_op jit(solution)/shard_map/tbf,bfd->td/dot_general | solution.py:148
  107.4 5.0 %all-to-all-start.1 = ((bf16[8,32,1024]{2,1,0:T(8,128)(2,1)}), bf16[8,32,1024]{2,1,0:T(8,128)(2,1)}, u32[]{:S(2)}, u32[]{:S(2)}) async-start(bf16[8,32,1024]{2,1,0:T(8,128)(2,1)} %broadcast_in_dim.9), calls=%async_computation.1 | async-start | bytes 1048576 | tf_op jit(solution)/shard_map/all_to_all | solution.py:32
  116.4 5.8 %all-to-all-done.1 = bf16[8,32,1024]{2,1,0:T(8,128)(2,1)} async-done(((bf16[8,32,1024]{2,1,0:T(8,128)(2,1)}), bf16[8,32,1024]{2,1,0:T(8,128)(2,1)}, u32[]{:S(2)}, u32[]{:S(2)}) %all-to-all-start.1) | async-done | bytes 524320 | tf_op jit(solution)/shard_map/all_to_all | solution.py:32
  123.7 22.2 %all_to_all.45 = bf16[32,32,256]{2,1,0:T(8,128)(2,1)S(1)} all-to-all(bf16[32,32,256]{2,1,0:T(8,128)(2,1)S(1)} %broadcast_in_dim.10), channel_id=1, replica_groups=mesh['zslab'=8,'blk'=32] {'blk'}, dimensions={0} | all-to-all | bytes 1048576 | tf_op jit(solution)/shard_map/all_to_all | solution.py:32
  151.0 8.2 %all-to-all-start.3 = ((bf16[32,32,256]{2,1,0:T(8,128)(2,1)}), bf16[32,32,256]{2,1,0:T(8,128)(2,1)}, u32[]{:S(2)}, u32[]{:S(2)}) async-start(bf16[32,32,256]{2,1,0:T(8,128)(2,1)} %pad_maximum_fusion), calls=%async_computation.3 | async-start | bytes 1048576 | tf_op jit(solution)/shard_map/all_to_all | solution.py:73
  160.3 13.5 %all-to-all-done.3 = bf16[32,32,256]{2,1,0:T(8,128)(2,1)} async-done(((bf16[32,32,256]{2,1,0:T(8,128)(2,1)}), bf16[32,32,256]{2,1,0:T(8,128)(2,1)}, u32[]{:S(2)}, u32[]{:S(2)}) %all-to-all-start.3) | async-done | bytes 524320 | tf_op jit(solution)/shard_map/all_to_all | solution.py:73
  175.3 11.7 %all_to_all.46 = bf16[8,32,1024]{2,1,0:T(8,128)(2,1)S(1)} all-to-all(bf16[8,32,1024]{2,1,0:T(8,128)(2,1)S(1)} %broadcast_in_dim.11), channel_id=1, replica_groups=mesh['zslab'=8,'blk'=32] {'zslab'}, dimensions={0} | all-to-all | bytes 1048576 | tf_op jit(solution)/shard_map/all_to_all | solution.py:32
  187.1 4.2 %fusion.4 = bf16[32,32,64]{2,0,1:T(8,128)(2,1)S(1)} fusion(bf16[32,80,1024]{2,1,0:T(8,128)(2,1)} %bitcast.210, bf16[32,1024]{1,0:T(8,128)(2,1)S(1)} %reduce_sum.58), kind=kOutput, calls=%fused_computation.8 | convolution fusion | flops 134283264 | bytes 4390912 | tf_op jit(solution)/shard_map/td,bfd->tbf/dot_general | solution.py:202
  191.7 8.1 %all_to_all.47 = bf16[1,16,32,128]{3,1,0,2:T(8,128)(2,1)S(1)} all-to-all(bf16[1,16,32,128]{3,1,0,2:T(8,128)(2,1)S(1)} %bitcast.206), channel_id=1, replica_groups=mesh['zslab'=8,'blk'=32] {'zslab'}, dimensions={2} | all-to-all | bytes 262144 | tf_op jit(solution)/shard_map/all_to_all | solution.py:209
  199.9 2.7 collective-permute-start.8
  202.7 2.5 collective-permute-start.9
  208.7 9.1 %collective-permute-start.10 = (bf16[2,16,8,128]{3,1,2,0:T(8,128)(2,1)S(1)}, bf16[2,16,8,128]{3,1,2,0:T(8,128)(2,1)S(1)}, u32[]{:S(2)}, u32[]{:S(2)}) collective-permute-start(bf16[2,16,8,128]{3,1,2,0:T(8,128)(2,1)S(1)} %get-tuple-element.119), channel_id=1, source_target_pairs={{0,1},{1,2},{2,3},{3,4},{4,5},{5,6},{6,7},{7,8},{8,9},{9,10},{10,1... | collective-permute-start | bytes 196616 | tf_op jit(solution)/shard_map/ppermute | solution.py:21
  222.8 4.2 %collective-permute-done.11 = bf16[2,16,8,128]{3,1,2,0:T(8,128)(2,1)S(1)} collective-permute-done((bf16[2,16,8,128]{3,1,2,0:T(8,128)(2,1)S(1)}, bf16[2,16,8,128]{3,1,2,0:T(8,128)(2,1)S(1)}, u32[]{:S(2)}, u32[]{:S(2)}) %collective-permute-start.11) | collective-permute-done | bytes 65568 | tf_op jit(solution)/shard_map/ppermute | solution.py:23
  242.7 3.4 %collective-permute-start.13 = (bf16[8,16,2,128]{3,1,2,0:T(8,128)(2,1)S(1)}, bf16[8,16,2,128]{3,1,2,0:T(8,128)(2,1)S(1)}, u32[]{:S(2)}, u32[]{:S(2)}) collective-permute-start(bf16[8,16,2,128]{3,1,2,0:T(8,128)(2,1)S(1)} %get-tuple-element.126), channel_id=1, source_target_pairs={{32,0},{64,32},{96,64},{128,96},{160,128},{192,160},{224,192},{33,... | collective-permute-start | bytes 196616 | tf_op jit(solution)/shard_map/ppermute | solution.py:23
  248.6 4.2 %collective-permute-start.14 = (bf16[2,16,8,128]{3,1,2,0:T(8,128)(2,1)S(1)}, bf16[2,16,8,128]{3,1,2,0:T(8,128)(2,1)S(1)}, u32[]{:S(2)}, u32[]{:S(2)}) collective-permute-start(bf16[2,16,8,128]{3,1,2,0:T(8,128)(2,1)S(1)} %get-tuple-element.117), channel_id=1, source_target_pairs={{0,1},{1,2},{2,3},{3,4},{4,5},{5,6},{6,7},{7,8},{8,9},{9,10},{10,1... | collective-permute-start | bytes 196616 | tf_op jit(solution)/shard_map/ppermute | solution.py:21
  256.8 5.2 %collective-permute-done.15 = bf16[2,16,8,128]{3,1,2,0:T(8,128)(2,1)S(1)} collective-permute-done((bf16[2,16,8,128]{3,1,2,0:T(8,128)(2,1)S(1)}, bf16[2,16,8,128]{3,1,2,0:T(8,128)(2,1)S(1)}, u32[]{:S(2)}, u32[]{:S(2)}) %collective-permute-start.15) | collective-permute-done | bytes 65568 | tf_op jit(solution)/shard_map/ppermute | solution.py:23
  (209 shorter events, 103.9 us)
Async XLA Ops:
  6.5 30.9 %copy-start.10 = (bf16[8,16,4,128]{3,2,1,0:T(4,128)(2,1)S(1)}, bf16[8,16,4,128]{3,2,1,0:T(4,128)(2,1)}, u32[]{:S(2)}) copy-start(bf16[8,16,4,128]{3,2,1,0:T(4,128)(2,1)} %param.7) | copy-start | bytes 393220
  6.5 23.2 %copy-start.25 = (s32[2,3]{1,0:T(2,128)S(1)}, s32[2,3]{1,0:T(2,128)}, u32[]{:S(2)}) copy-start(s32[2,3]{1,0:T(2,128)} %param.9) | copy-start | bytes 76
  6.5 29.5 %copy-start.24 = (s32[8,16,4]{1,2,0:T(4,128)S(1)}, s32[8,16,4]{1,2,0:T(4,128)}, u32[]{:S(2)}) copy-start(s32[8,16,4]{1,2,0:T(4,128)} %param.8) | copy-start | bytes 6148
  6.5 96.9 %all-gather.2.cloned.1.call-start = ((), (), s32[]{:S(2)}) async-start(), calls=%async_computation.6 | async-start | bytes 5406720 | tf_op jit(solution)/shard_map/all_gather | solution.py:84
  10.2 5.4 %collective-permute-start = (bf16[8,16,2,128]{3,2,1,0:T(2,128)(2,1)S(1)}, bf16[8,16,2,128]{3,2,1,0:T(2,128)(2,1)S(1)}, u32[]{:S(2)}, u32[]{:S(2)}) collective-permute-start(bf16[8,16,2,128]{3,2,1,0:T(2,128)(2,1)S(1)} %get-tuple-element.131), channel_id=1, source_target_pairs={{0,32},{32,64},{64,96},{96,128},{128,160},{160,192},{192,224},{1,3... | collective-permute-start | bytes 196616 | tf_op jit(solution)/shard_map/ppermute | solution.py:21
  13.7 5.9 %collective-permute-start.1 = (bf16[8,16,2,128]{3,2,1,0:T(2,128)(2,1)S(1)}, bf16[8,16,2,128]{3,2,1,0:T(2,128)(2,1)S(1)}, u32[]{:S(2)}, u32[]{:S(2)}) collective-permute-start(bf16[8,16,2,128]{3,2,1,0:T(2,128)(2,1)S(1)} %get-tuple-element.132), channel_id=1, source_target_pairs={{32,0},{64,32},{96,64},{128,96},{160,128},{192,160},{224,192},{33,... | collective-permute-start | bytes 196616 | tf_op jit(solution)/shard_map/ppermute | solution.py:23
  20.5 15.6 %collective-permute-start.2 = (bf16[2,16,8,128]{3,2,1,0:T(8,128)(2,1)S(1)}, bf16[2,16,8,128]{3,2,1,0:T(8,128)(2,1)S(1)}, u32[]{:S(2)}, u32[]{:S(2)}) collective-permute-start(bf16[2,16,8,128]{3,2,1,0:T(8,128)(2,1)S(1)} %get-tuple-element.123), channel_id=1, source_target_pairs={{0,1},{1,2},{2,3},{3,4},{4,5},{5,6},{6,7},{7,8},{8,9},{9,10},{10,1... | collective-permute-start | bytes 196616 | tf_op jit(solution)/shard_map/ppermute | solution.py:21
  27.8 9.6 %collective-permute-start.3 = (bf16[2,16,8,128]{3,2,1,0:T(8,128)(2,1)S(1)}, bf16[2,16,8,128]{3,2,1,0:T(8,128)(2,1)S(1)}, u32[]{:S(2)}, u32[]{:S(2)}) collective-permute-start(bf16[2,16,8,128]{3,2,1,0:T(8,128)(2,1)S(1)} %get-tuple-element.124), channel_id=1, source_target_pairs={{1,0},{2,1},{3,2},{4,3},{5,4},{6,5},{7,6},{8,7},{9,8},{10,9},{11,1... | collective-permute-start | bytes 196616 | tf_op jit(solution)/shard_map/ppermute | solution.py:23
  52.9 5.3 %collective-permute-start.4 = (bf16[8,16,2,128]{3,1,2,0:T(8,128)(2,1)S(1)}, bf16[8,16,2,128]{3,1,2,0:T(8,128)(2,1)S(1)}, u32[]{:S(2)}, u32[]{:S(2)}) collective-permute-start(bf16[8,16,2,128]{3,1,2,0:T(8,128)(2,1)S(1)} %get-tuple-element.129), channel_id=1, source_target_pairs={{0,32},{32,64},{64,96},{96,128},{128,160},{160,192},{192,224},{1,3... | collective-permute-start | bytes 196616 | tf_op jit(solution)/shard_map/ppermute | solution.py:21
  54.8 6.0 %collective-permute-start.5 = (bf16[8,16,2,128]{3,1,2,0:T(8,128)(2,1)S(1)}, bf16[8,16,2,128]{3,1,2,0:T(8,128)(2,1)S(1)}, u32[]{:S(2)}, u32[]{:S(2)}) collective-permute-start(bf16[8,16,2,128]{3,1,2,0:T(8,128)(2,1)S(1)} %get-tuple-element.130), channel_id=1, source_target_pairs={{32,0},{64,32},{96,64},{128,96},{160,128},{192,160},{224,192},{33,... | collective-permute-start | bytes 196616 | tf_op jit(solution)/shard_map/ppermute | solution.py:23
  60.9 15.2 %collective-permute-start.6 = (bf16[2,16,8,128]{3,1,2,0:T(8,128)(2,1)S(1)}, bf16[2,16,8,128]{3,1,2,0:T(8,128)(2,1)S(1)}, u32[]{:S(2)}, u32[]{:S(2)}) collective-permute-start(bf16[2,16,8,128]{3,1,2,0:T(8,128)(2,1)S(1)} %get-tuple-element.121), channel_id=1, source_target_pairs={{0,1},{1,2},{2,3},{3,4},{4,5},{5,6},{6,7},{7,8},{8,9},{9,10},{10,1... | collective-permute-start | bytes 196616 | tf_op jit(solution)/shard_map/ppermute | solution.py:21
  68.5 9.4 %collective-permute-start.7 = (bf16[2,16,8,128]{3,1,2,0:T(8,128)(2,1)S(1)}, bf16[2,16,8,128]{3,1,2,0:T(8,128)(2,1)S(1)}, u32[]{:S(2)}, u32[]{:S(2)}) collective-permute-start(bf16[2,16,8,128]{3,1,2,0:T(8,128)(2,1)S(1)} %get-tuple-element.122), channel_id=1, source_target_pairs={{1,0},{2,1},{3,2},{4,3},{5,4},{6,5},{7,6},{8,7},{9,8},{10,9},{11,1... | collective-permute-start | bytes 196616 | tf_op jit(solution)/shard_map/ppermute | solution.py:23
  107.4 14.8 %all-to-all-start.1 = ((bf16[8,32,1024]{2,1,0:T(8,128)(2,1)}), bf16[8,32,1024]{2,1,0:T(8,128)(2,1)}, u32[]{:S(2)}, u32[]{:S(2)}) async-start(bf16[8,32,1024]{2,1,0:T(8,128)(2,1)} %broadcast_in_dim.9), calls=%async_computation.1 | async-start | bytes 1048576 | tf_op jit(solution)/shard_map/all_to_all | solution.py:32
  123.6 22.8 %copy-start.26 = (bf16[32,128]{1,0:T(8,128)(2,1)S(1)}, bf16[32,128]{1,0:T(8,128)(2,1)}, u32[]{:S(2)}) copy-start(bf16[32,128]{1,0:T(8,128)(2,1)} %param.13) | copy-start | bytes 24580
  151.0 22.8 %all-to-all-start.3 = ((bf16[32,32,256]{2,1,0:T(8,128)(2,1)}), bf16[32,32,256]{2,1,0:T(8,128)(2,1)}, u32[]{:S(2)}, u32[]{:S(2)}) async-start(bf16[32,32,256]{2,1,0:T(8,128)(2,1)} %pad_maximum_fusion), calls=%async_computation.3 | async-start | bytes 1048576 | tf_op jit(solution)/shard_map/all_to_all | solution.py:73
  199.9 6.3 %collective-permute-start.8 = (bf16[8,16,2,128]{3,1,2,0:T(8,128)(2,1)S(1)}, bf16[8,16,2,128]{3,1,2,0:T(8,128)(2,1)S(1)}, u32[]{:S(2)}, u32[]{:S(2)}) collective-permute-start(bf16[8,16,2,128]{3,1,2,0:T(8,128)(2,1)S(1)} %get-tuple-element.127), channel_id=1, source_target_pairs={{0,32},{32,64},{64,96},{96,128},{128,160},{160,192},{192,224},{1,3... | collective-permute-start | bytes 196616 | tf_op jit(solution)/shard_map/ppermute | solution.py:21
  202.7 6.0 %collective-permute-start.9 = (bf16[8,16,2,128]{3,1,2,0:T(8,128)(2,1)S(1)}, bf16[8,16,2,128]{3,1,2,0:T(8,128)(2,1)S(1)}, u32[]{:S(2)}, u32[]{:S(2)}) collective-permute-start(bf16[8,16,2,128]{3,1,2,0:T(8,128)(2,1)S(1)} %get-tuple-element.128), channel_id=1, source_target_pairs={{32,0},{64,32},{96,64},{128,96},{160,128},{192,160},{224,192},{33,... | collective-permute-start | bytes 196616 | tf_op jit(solution)/shard_map/ppermute | solution.py:23
  208.7 14.1 %collective-permute-start.10 = (bf16[2,16,8,128]{3,1,2,0:T(8,128)(2,1)S(1)}, bf16[2,16,8,128]{3,1,2,0:T(8,128)(2,1)S(1)}, u32[]{:S(2)}, u32[]{:S(2)}) collective-permute-start(bf16[2,16,8,128]{3,1,2,0:T(8,128)(2,1)S(1)} %get-tuple-element.119), channel_id=1, source_target_pairs={{0,1},{1,2},{2,3},{3,4},{4,5},{5,6},{6,7},{7,8},{8,9},{9,10},{10,1... | collective-permute-start | bytes 196616 | tf_op jit(solution)/shard_map/ppermute | solution.py:21
  217.9 9.2 %collective-permute-start.11 = (bf16[2,16,8,128]{3,1,2,0:T(8,128)(2,1)S(1)}, bf16[2,16,8,128]{3,1,2,0:T(8,128)(2,1)S(1)}, u32[]{:S(2)}, u32[]{:S(2)}) collective-permute-start(bf16[2,16,8,128]{3,1,2,0:T(8,128)(2,1)S(1)} %get-tuple-element.120), channel_id=1, source_target_pairs={{1,0},{2,1},{3,2},{4,3},{5,4},{6,5},{7,6},{8,7},{9,8},{10,9},{11,1... | collective-permute-start | bytes 196616 | tf_op jit(solution)/shard_map/ppermute | solution.py:23
  240.4 14.3 %copy-start.9 = (bf16[1,3456,128]{2,1,0:T(8,128)(2,1)S(1)}, bf16[1,3456,128]{2,1,0:T(8,128)(2,1)}, u32[]{:S(2)}) copy-start(bf16[1,3456,128]{2,1,0:T(8,128)(2,1)} %get-tuple-element.5) | copy-start | bytes 2654212
  240.6 5.4 %collective-permute-start.12 = (bf16[8,16,2,128]{3,1,2,0:T(8,128)(2,1)S(1)}, bf16[8,16,2,128]{3,1,2,0:T(8,128)(2,1)S(1)}, u32[]{:S(2)}, u32[]{:S(2)}) collective-permute-start(bf16[8,16,2,128]{3,1,2,0:T(8,128)(2,1)S(1)} %get-tuple-element.125), channel_id=1, source_target_pairs={{0,32},{32,64},{64,96},{96,128},{128,160},{160,192},{192,224},{1,3... | collective-permute-start | bytes 196616 | tf_op jit(solution)/shard_map/ppermute | solution.py:21
  242.7 5.9 %collective-permute-start.13 = (bf16[8,16,2,128]{3,1,2,0:T(8,128)(2,1)S(1)}, bf16[8,16,2,128]{3,1,2,0:T(8,128)(2,1)S(1)}, u32[]{:S(2)}, u32[]{:S(2)}) collective-permute-start(bf16[8,16,2,128]{3,1,2,0:T(8,128)(2,1)S(1)} %get-tuple-element.126), channel_id=1, source_target_pairs={{32,0},{64,32},{96,64},{128,96},{160,128},{192,160},{224,192},{33,... | collective-permute-start | bytes 196616 | tf_op jit(solution)/shard_map/ppermute | solution.py:23
  248.6 8.2 %collective-permute-start.14 = (bf16[2,16,8,128]{3,1,2,0:T(8,128)(2,1)S(1)}, bf16[2,16,8,128]{3,1,2,0:T(8,128)(2,1)S(1)}, u32[]{:S(2)}, u32[]{:S(2)}) collective-permute-start(bf16[2,16,8,128]{3,1,2,0:T(8,128)(2,1)S(1)} %get-tuple-element.117), channel_id=1, source_target_pairs={{0,1},{1,2},{2,3},{3,4},{4,5},{5,6},{6,7},{7,8},{8,9},{9,10},{10,1... | collective-permute-start | bytes 196616 | tf_op jit(solution)/shard_map/ppermute | solution.py:21
  252.8 9.2 %collective-permute-start.15 = (bf16[2,16,8,128]{3,1,2,0:T(8,128)(2,1)S(1)}, bf16[2,16,8,128]{3,1,2,0:T(8,128)(2,1)S(1)}, u32[]{:S(2)}, u32[]{:S(2)}) collective-permute-start(bf16[2,16,8,128]{3,1,2,0:T(8,128)(2,1)S(1)} %get-tuple-element.118), channel_id=1, source_target_pairs={{1,0},{2,1},{3,2},{4,3},{5,4},{6,5},{7,6},{8,7},{9,8},{10,9},{11,1... | collective-permute-start | bytes 196616 | tf_op jit(solution)/shard_map/ppermute | solution.py:23
  (22 other events, 30.3 us)
Sparse Core Ops, SparseCore 0:
  10.1 92.0 all-gather.1

commit v3 on v2

--- a/solution.py
+++ b/solution.py
@@ -93,30 +93,46 @@
 
 
 def with_rim(volume):
-    padded = padded_2(volume, (("zslab", 2), ("blk", 0)), DMAX)
-    return jnp.pad(padded, ((0, 0), (DMAX, DMAX), (0, 0), (0, 0)))
+    return padded_2(volume, (("zslab", 1), ("blk", 0)), DMAX)
+
+
+def picked(cells, dim, step, rate, size):
+    near = lax.slice_in_dim(cells, DMAX + step, DMAX + step + size, axis=dim)
+    if step == 0:
+        return near
+    far = lax.slice_in_dim(cells, DMAX + 2 * step, DMAX + 2 * step + size, axis=dim)
+    return jnp.where(rate == 1, near, far)
+
+
+def shifted_y(values, step, rate):
+    def by(amount):
+        cells = values.shape[2]
+        zeros = jnp.zeros_like(values[:, :, : abs(amount)])
+        if amount > 0:
+            return jnp.concatenate([values[:, :, amount:], zeros], axis=2)
+        return jnp.concatenate([zeros, values[:, :, : cells + amount]], axis=2)
+
+    if step == 0:
+        return values
+    return jnp.where(rate == 1, by(step), by(2 * step))
 
 
 def apply_offsets(padded, weight, dilate, direction, dims_out):
-    x_cells, y_cells, z_cells, channels = dims_out
-    summed = jnp.zeros((x_cells * y_cells * z_cells, weight.shape[-1]), jnp.float32)
+    x_cells, z_cells, y_cells, channels = dims_out
+    windows = []
     for offset_x in (-1, 0, 1):
-        pieces = []
-        for offset_y in (-1, 0, 1):
-            for offset_z in (-1, 0, 1):
-                anchor = (
-                    DMAX + direction * offset_x * dilate[0],
-                    DMAX + direction * offset_y * dilate[1],
-                    DMAX + direction * offset_z * dilate[2],
-                    jnp.int32(0),
-                )
-                pieces.append(
-                    lax.dynamic_slice(padded, anchor, (x_cells, y_cells, z_cells, channels))
-                )
-        stacked = jnp.concatenate(pieces, axis=3).reshape(x_cells * y_cells * z_cells, 9 * channels)
-        group_rows = weight[(offset_x + 1) * 9 * channels : (offset_x + 2) * 9 * channels]
-        summed = summed + jnp.dot(stacked, group_rows, preferred_element_type=jnp.float32)
-    return summed.reshape(x_cells, y_cells, z_cells, -1)
+        along_x = picked(padded, 0, direction * offset_x, dilate[0], x_cells)
+        for offset_z in (-1, 0, 1):
+            windows.append(picked(along_x, 1, direction * offset_z, dilate[2], z_cells))
+    stacked = jnp.concatenate(windows, axis=3).reshape(x_cells * z_cells * y_cells, 9 * channels)
+    taps = weight.reshape(3, 3, 3, channels, -1)
+    summed = None
+    for offset_y in (-1, 0, 1):
+        rows = taps[:, offset_y + 1].reshape(9 * channels, -1)
+        part = jnp.dot(stacked, rows, preferred_element_type=jnp.float32)
+        part = shifted_y(part.reshape(x_cells, z_cells, y_cells, -1), direction * offset_y, dilate[1])
+        summed = part if summed is None else summed + part
+    return summed
 
 
 def slab_total(term):
@@ -124,7 +140,9 @@
 
 
 def local(field, fracture_mask, dilation, conv_weight, embed_weight, qkv_weight, out_grad):
-    x_cells, y_cells, z_cells, channels = field.shape
+    field = field.transpose(0, 2, 1, 3)
+    fracture_mask = fracture_mask.transpose(0, 2, 1)
+    x_cells, z_cells, y_cells, channels = field.shape
     gate_mask = fracture_mask.astype(jnp.float32)[..., None]
     hidden = field
     conv_outs = []
@@ -136,11 +154,11 @@
         hidden = (
             hidden.astype(jnp.float32) + gate_mask * (conv_out * jax.nn.sigmoid(conv_out))
         ).astype(jnp.bfloat16)
-    slab_view = lax.all_to_all(hidden, "zslab", split_axis=0, concat_axis=2, tiled=True)
-    x_local, z_total = (slab_view.shape[0], slab_view.shape[2])
+    slab_view = lax.all_to_all(hidden, "zslab", split_axis=0, concat_axis=1, tiled=True)
+    x_local, z_total = (slab_view.shape[0], slab_view.shape[1])
     y_blocks, z_blocks = (y_cells // PY, z_total // PZ)
-    patches = slab_view.reshape(x_local, y_blocks, PY, z_blocks, PZ, channels).transpose(
-        1, 3, 0, 2, 4, 5
+    patches = slab_view.reshape(x_local, z_blocks, PZ, y_blocks, PY, channels).transpose(
+        3, 1, 0, 4, 2, 5
     )
     patches = patches.reshape(y_blocks * z_blocks, x_local, PY * PZ * channels)
     embed_rows, qkv_rows = gather_weights(embed_weight, qkv_weight)
@@ -203,10 +221,10 @@
         "td,bfd->tbf", grad_tokens, embed_rows, preferred_element_type=jnp.float32
     ).astype(jnp.bfloat16)
     grid_grad = patch_grad.reshape(y_blocks, z_blocks, x_local, PY, PZ, channels).transpose(
-        2, 0, 3, 1, 4, 5
-    )
-    grid_grad = grid_grad.reshape(x_local, y_cells, z_total, channels)
-    grid_grad = lax.all_to_all(grid_grad, "zslab", split_axis=2, concat_axis=0, tiled=True)
+        2, 1, 4, 0, 3, 5
+    )
+    grid_grad = grid_grad.reshape(x_local, z_total, y_cells, channels)
+    grid_grad = lax.all_to_all(grid_grad, "zslab", split_axis=1, concat_axis=0, tiled=True)
     for layer_num in reversed(range(LAYERS)):
         conv_out = conv_outs[layer_num]
         sigma = jax.nn.sigmoid(conv_out)
@@ -223,7 +241,7 @@
             with_rim(slope_grad), flipped, dilation[layer_num], -1, field.shape
         )
         grid_grad = (grid_grad.astype(jnp.float32) + backward).astype(jnp.bfloat16)
-    return grid_grad
+    return grid_grad.transpose(0, 2, 1, 3)
 
 
 def solution(mesh):

time: 286 us -> 256 us (0.90)
  local copies, waits for them, and re-layouts: 64.3 us -> 16.2 us
  waiting for transfers between devices: 43.4 us -> 67.3 us
  between operations: 25.7 us -> 18.1 us
    all_gather x1, waiting for transfers between devices: 0.02 us -> 28 us  [gather_weights(): gathered = lax.all_gather(rows, 'blk', axis=0, tiled=True)]
    unnamed x90 -> x25, local copies, waits for them, and re-layouts: 19.8 us -> 3.03 us
    reshape x12 -> x1, local copies, waits for them, and re-layouts: 15.8 us -> 0.1 us  [local(): slab_view.reshape(x_local, z_blocks, PZ, y_blocks, PY, channels)]
    concatenate x13 -> x0, local copies, waits for them, and re-layouts: 13.1 us -> none  [apply_offsets(): jnp.concatenate(pieces, axis=3)]
    ppermute x8, waiting for transfers between devices: 24.1 us -> 17.8 us  [padded_2(): lax.ppermute(head, axis, [((i + 1) % count, i) for i in range(ends)])]
    ppermute x8, starting transfers between devices: 19.3 us -> 24.5 us  [padded_2(): lax.ppermute(head, axis, [((i + 1) % count, i) for i in range(ends)])]
    ppermute x8, starting transfers between devices: 38.4 us -> 34 us  [padded_2(): lax.ppermute(tail, axis, [(i, (i + 1) % count) for i in range(ends)])]
    slice x9 -> x13, local copies, waits for them, and re-layouts: 5.46 us -> 1.14 us  [the longest x1 0.66 us: apply_offsets(): dilate[1]]
  transfers between devices with their start and end apart: 19 -> 19, of which waited for: 10 -> 12; matrix products, arithmetic and copies ran while one was open for 13% -> 6% of each run, Pallas kernels for 0% -> 0%
where the time goes in v3:
time: 256 us; the launch traced here: 252 us
  starting transfers between devices  71.9 us (28%)
  waiting for transfers between devices  67.3 us (26%)
  blocking collectives  53.7 us (21%)
  between operations  18.1 us (7%)
  matrix products  17.4 us (7%)
  local copies, waits for them, and re-layouts  16.2 us (6%)
  other arithmetic  6.95 us (3%)
    all_to_all x2, blocking collectives, copy_for_each(): lax.all_to_all(jnp.broadcast_to(shard[None], (peers, *shard.shape)), axis...  35.3 us
    ppermute x8, starting transfers between devices, padded_2(): lax.ppermute(tail, axis, [(i, (i + 1) % count) for i in range(ends)])  34 us
    all_gather x1, waiting for transfers between devices, gather_weights(): gathered = lax.all_gather(rows, 'blk', axis=0, tiled=True)  28 us
    ppermute x8, starting transfers between devices, padded_2(): lax.ppermute(head, axis, [((i + 1) % count, i) for i in range(ends)])  24.5 us
    ppermute x8, waiting for transfers between devices, padded_2(): lax.ppermute(head, axis, [((i + 1) % count, i) for i in range(ends)])  17.8 us
    all_to_all x1, waiting for transfers between devices, sum_at_owner(): lax.all_to_all(cut_along(shard, dim, peers), axis, 0, 0, tiled=True)  14.4 us
    all_to_all x1, blocking collectives, local(): lax.all_to_all(hidden, 'zslab', split_axis=0, concat_axis=1, tiled=True)  10.3 us
    all_to_all x1, starting transfers between devices, sum_at_owner(): lax.all_to_all(cut_along(shard, dim, peers), axis, 0, 0, tiled=True)  8.21 us
  transfers between devices with their start and end apart: 19, of which 12 were waited for; matrix products, arithmetic and copies ran while one was open for 6% of the time, Pallas kernels for 0%

profile of v3, /device:TPU:103, one launch (start us, length us, event | category | flops | bytes accessed | tf_op | source)
XLA Modules:
  0.0 251.5 jit_solution(991089287344288184)
XLA Ops:
  10.0 3.5 %collective-permute-start = (bf16[8,2,16,128]{3,2,1,0:T(8,128)(2,1)S(1)}, bf16[8,2,16,128]{3,2,1,0:T(8,128)(2,1)S(1)}, u32[]{:S(2)}, u32[]{:S(2)}) collective-permute-start(bf16[8,2,16,128]{3,2,1,0:T(8,128)(2,1)S(1)} %get-tuple-element.41), channel_id=1, source_target_pairs={{0,32},{32,64},{64,96},{96,128},{128,160},{160,192},{192,224},{1,3... | collective-permute-start | bytes 196616 | tf_op jit(solution)/shard_map/ppermute | solution.py:21
  19.5 7.3 %collective-permute-start.2 = (bf16[2,8,16,128]{3,2,1,0:T(8,128)(2,1)S(1)}, bf16[2,8,16,128]{3,2,1,0:T(8,128)(2,1)S(1)}, u32[]{:S(2)}, u32[]{:S(2)}) collective-permute-start(bf16[2,8,16,128]{3,2,1,0:T(8,128)(2,1)S(1)} %get-tuple-element.34), channel_id=1, source_target_pairs={{0,1},{1,2},{2,3},{3,4},{4,5},{5,6},{6,7},{7,8},{8,9},{9,10},{10,1... | collective-permute-start | bytes 196616 | tf_op jit(solution)/shard_map/ppermute | solution.py:21
  31.2 4.8 %collective-permute-done.3 = bf16[2,8,16,128]{3,2,1,0:T(8,128)(2,1)S(1)} collective-permute-done((bf16[2,8,16,128]{3,2,1,0:T(8,128)(2,1)S(1)}, bf16[2,8,16,128]{3,2,1,0:T(8,128)(2,1)S(1)}, u32[]{:S(2)}, u32[]{:S(2)}) %collective-permute-start.3) | collective-permute-done | bytes 65568 | tf_op jit(solution)/shard_map/ppermute | solution.py:23
  41.5 3.4 %collective-permute-start.5 = (bf16[8,2,16,128]{3,2,1,0:T(8,128)(2,1)S(1)}, bf16[8,2,16,128]{3,2,1,0:T(8,128)(2,1)S(1)}, u32[]{:S(2)}, u32[]{:S(2)}) collective-permute-start(bf16[8,2,16,128]{3,2,1,0:T(8,128)(2,1)S(1)} %get-tuple-element.40), channel_id=1, source_target_pairs={{32,0},{64,32},{96,64},{128,96},{160,128},{192,160},{224,192},{33,... | collective-permute-start | bytes 196616 | tf_op jit(solution)/shard_map/ppermute | solution.py:23
  45.0 2.7 %collective-permute-done.5 = bf16[8,2,16,128]{3,2,1,0:T(8,128)(2,1)S(1)} collective-permute-done((bf16[8,2,16,128]{3,2,1,0:T(8,128)(2,1)S(1)}, bf16[8,2,16,128]{3,2,1,0:T(8,128)(2,1)S(1)}, u32[]{:S(2)}, u32[]{:S(2)}) %collective-permute-start.5) | collective-permute-done | bytes 65568 | tf_op jit(solution)/shard_map/ppermute | solution.py:23
  47.7 3.9 %collective-permute-start.6 = (bf16[2,8,16,128]{3,2,1,0:T(8,128)(2,1)S(1)}, bf16[2,8,16,128]{3,2,1,0:T(8,128)(2,1)S(1)}, u32[]{:S(2)}, u32[]{:S(2)}) collective-permute-start(bf16[2,8,16,128]{3,2,1,0:T(8,128)(2,1)S(1)} %get-tuple-element.30), channel_id=1, source_target_pairs={{0,1},{1,2},{2,3},{3,4},{4,5},{5,6},{6,7},{7,8},{8,9},{9,10},{10,1... | collective-permute-start | bytes 196616 | tf_op jit(solution)/shard_map/ppermute | solution.py:21
  55.5 5.3 %collective-permute-done.7 = bf16[2,8,16,128]{3,2,1,0:T(8,128)(2,1)S(1)} collective-permute-done((bf16[2,8,16,128]{3,2,1,0:T(8,128)(2,1)S(1)}, bf16[2,8,16,128]{3,2,1,0:T(8,128)(2,1)S(1)}, u32[]{:S(2)}, u32[]{:S(2)}) %collective-permute-start.7) | collective-permute-done | bytes 65568 | tf_op jit(solution)/shard_map/ppermute | solution.py:23
  63.7 10.3 %all_to_all.38 = bf16[8,4,16,128]{3,2,1,0:T(8,128)(2,1)S(1)} all-to-all(bf16[8,4,16,128]{3,2,1,0:T(8,128)(2,1)S(1)} %get-tuple-element.55), channel_id=1, replica_groups=mesh['zslab'=8,'blk'=32] {'zslab'}, dimensions={0} | all-to-all | bytes 262144 | tf_op jit(solution)/shard_map/all_to_all | solution.py:157
  74.2 28.0 %all-gather.2.cloned.1.call-done = bf16[2560,1024]{1,0:T(8,128)(2,1)} async-done(((bf16[80,1024]{1,0:T(8,128)(2,1)}), bf16[2560,1024]{1,0:T(8,128)(2,1)}) %all-gather.2.cloned.1.call-update) | async-done | bytes 5242896 | tf_op jit(solution)/shard_map/all_gather | solution.py:84
  102.2 3.0 %fusion.26 = bf16[32,1024]{1,0:T(8,128)(2,1)S(1)} fusion(bf16[32,80,1024]{2,1,0:T(8,128)(2,1)} %bitcast.261, bf16[32,32,64]{2,1,0:T(8,128)(2,1)S(1)} %reshape_reshape.9), kind=kOutput, calls=%fused_computation.31 | convolution fusion | flops 134250496 | bytes 4390912 | tf_op jit(solution)/shard_map/tbf,bfd->td/dot_general | solution.py:166
  106.1 5.2 %all-to-all-start.1 = ((bf16[8,32,1024]{2,1,0:T(8,128)(2,1)}), bf16[8,32,1024]{2,1,0:T(8,128)(2,1)S(1)}, u32[]{:S(2)}, u32[]{:S(2)}) async-start(bf16[8,32,1024]{2,1,0:T(8,128)(2,1)} %broadcast_in_dim.9), calls=%async_computation.1 | async-start | bytes 1048576 | tf_op jit(solution)/shard_map/all_to_all | solution.py:32
  115.3 4.6 %all-to-all-done.1 = bf16[8,32,1024]{2,1,0:T(8,128)(2,1)S(1)} async-done(((bf16[8,32,1024]{2,1,0:T(8,128)(2,1)}), bf16[8,32,1024]{2,1,0:T(8,128)(2,1)S(1)}, u32[]{:S(2)}, u32[]{:S(2)}) %all-to-all-start.1) | async-done | bytes 524320 | tf_op jit(solution)/shard_map/all_to_all | solution.py:32
  120.3 23.4 %all_to_all.39 = bf16[32,32,256]{2,1,0:T(8,128)(2,1)S(1)} all-to-all(bf16[32,32,256]{2,1,0:T(8,128)(2,1)S(1)} %broadcast_in_dim.10), channel_id=1, replica_groups=mesh['zslab'=8,'blk'=32] {'blk'}, dimensions={0} | all-to-all | bytes 1048576 | tf_op jit(solution)/shard_map/all_to_all | solution.py:32
  148.8 8.2 %all-to-all-start.3 = ((bf16[32,32,256]{2,1,0:T(8,128)(2,1)}), bf16[32,32,256]{2,1,0:T(8,128)(2,1)}, u32[]{:S(2)}, u32[]{:S(2)}) async-start(bf16[32,32,256]{2,1,0:T(8,128)(2,1)} %pad_maximum_fusion), calls=%async_computation.3 | async-start | bytes 1048576 | tf_op jit(solution)/shard_map/all_to_all | solution.py:73
  157.2 14.4 %all-to-all-done.3 = bf16[32,32,256]{2,1,0:T(8,128)(2,1)} async-done(((bf16[32,32,256]{2,1,0:T(8,128)(2,1)}), bf16[32,32,256]{2,1,0:T(8,128)(2,1)}, u32[]{:S(2)}, u32[]{:S(2)}) %all-to-all-start.3) | async-done | bytes 524320 | tf_op jit(solution)/shard_map/all_to_all | solution.py:73
  173.2 11.9 %all_to_all.40 = bf16[8,32,1024]{2,1,0:T(8,128)(2,1)S(1)} all-to-all(bf16[8,32,1024]{2,1,0:T(8,128)(2,1)S(1)} %broadcast_in_dim.11), channel_id=1, replica_groups=mesh['zslab'=8,'blk'=32] {'zslab'}, dimensions={0} | all-to-all | bytes 1048576 | tf_op jit(solution)/shard_map/all_to_all | solution.py:32
  185.2 4.2 %fusion.4 = bf16[32,32,64]{2,0,1:T(8,128)(2,1)S(1)} fusion(bf16[32,80,1024]{2,1,0:T(8,128)(2,1)} %bitcast.263, bf16[32,1024]{1,0:T(8,128)(2,1)S(1)} %reduce_sum.58), kind=kOutput, calls=%fused_computation.4 | convolution fusion | flops 134283264 | bytes 4390912 | tf_op jit(solution)/shard_map/td,bfd->tbf/dot_general | solution.py:220
  189.7 8.1 %all_to_all.41 = bf16[1,32,16,128]{3,2,0,1:T(8,128)(2,1)S(1)} all-to-all(bf16[1,32,16,128]{3,2,0,1:T(8,128)(2,1)S(1)} %bitcast.248), channel_id=1, replica_groups=mesh['zslab'=8,'blk'=32] {'zslab'}, dimensions={1} | all-to-all | bytes 262144 | tf_op jit(solution)/shard_map/all_to_all | solution.py:227
  198.0 2.7 %collective-permute-start.8 = (bf16[8,2,16,128]{3,2,1,0:T(8,128)(2,1)S(1)}, bf16[8,2,16,128]{3,2,1,0:T(8,128)(2,1)S(1)}, u32[]{:S(2)}, u32[]{:S(2)}) collective-permute-start(bf16[8,2,16,128]{3,2,1,0:T(8,128)(2,1)S(1)} %get-tuple-element.37), channel_id=1, source_target_pairs={{0,32},{32,64},{64,96},{96,128},{128,160},{160,192},{192,224},{1,3... | collective-permute-start | bytes 196616 | tf_op jit(solution)/shard_map/ppermute | solution.py:21
  206.7 5.8 %collective-permute-start.10 = (bf16[2,8,16,128]{3,2,1,0:T(8,128)(2,1)S(1)}, bf16[2,8,16,128]{3,2,1,0:T(8,128)(2,1)S(1)}, u32[]{:S(2)}, u32[]{:S(2)}) collective-permute-start(bf16[2,8,16,128]{3,2,1,0:T(8,128)(2,1)S(1)} %get-tuple-element.26), channel_id=1, source_target_pairs={{1,0},{2,1},{3,2},{4,3},{5,4},{6,5},{7,6},{8,7},{9,8},{10,9},{11,1... | collective-permute-start | bytes 196616 | tf_op jit(solution)/shard_map/ppermute | solution.py:23
  212.5 5.4 %collective-permute-start.11 = (bf16[2,8,16,128]{3,2,1,0:T(8,128)(2,1)S(1)}, bf16[2,8,16,128]{3,2,1,0:T(8,128)(2,1)S(1)}, u32[]{:S(2)}, u32[]{:S(2)}) collective-permute-start(bf16[2,8,16,128]{3,2,1,0:T(8,128)(2,1)S(1)} %get-tuple-element.25), channel_id=1, source_target_pairs={{0,1},{1,2},{2,3},{3,4},{4,5},{5,6},{6,7},{7,8},{8,9},{9,10},{10,1... | collective-permute-start | bytes 196616 | tf_op jit(solution)/shard_map/ppermute | solution.py:21
  223.7 3.4 %collective-permute-start.13 = (bf16[8,2,16,128]{3,2,1,0:T(8,128)(2,1)S(1)}, bf16[8,2,16,128]{3,2,1,0:T(8,128)(2,1)S(1)}, u32[]{:S(2)}, u32[]{:S(2)}) collective-permute-start(bf16[8,2,16,128]{3,2,1,0:T(8,128)(2,1)S(1)} %get-tuple-element.36), channel_id=1, source_target_pairs={{32,0},{64,32},{96,64},{128,96},{160,128},{192,160},{224,192},{33,... | collective-permute-start | bytes 196616 | tf_op jit(solution)/shard_map/ppermute | solution.py:23
  229.6 3.6 %collective-permute-start.14 = (bf16[2,8,16,128]{3,2,1,0:T(8,128)(2,1)S(1)}, bf16[2,8,16,128]{3,2,1,0:T(8,128)(2,1)S(1)}, u32[]{:S(2)}, u32[]{:S(2)}) collective-permute-start(bf16[2,8,16,128]{3,2,1,0:T(8,128)(2,1)S(1)} %get-tuple-element.22), channel_id=1, source_target_pairs={{1,0},{2,1},{3,2},{4,3},{5,4},{6,5},{7,6},{8,7},{9,8},{10,9},{11,1... | collective-permute-start | bytes 196616 | tf_op jit(solution)/shard_map/ppermute | solution.py:23
  233.2 7.4 %collective-permute-start.15 = (bf16[2,8,16,128]{3,2,1,0:T(8,128)(2,1)S(1)}, bf16[2,8,16,128]{3,2,1,0:T(8,128)(2,1)S(1)}, u32[]{:S(2)}, u32[]{:S(2)}) collective-permute-start(bf16[2,8,16,128]{3,2,1,0:T(8,128)(2,1)S(1)} %get-tuple-element.21), channel_id=1, source_target_pairs={{0,1},{1,2},{2,3},{3,4},{4,5},{5,6},{6,7},{7,8},{8,9},{9,10},{10,1... | collective-permute-start | bytes 196616 | tf_op jit(solution)/shard_map/ppermute | solution.py:21
  (152 shorter events, 52.9 us)
Async XLA Ops:
  6.5 95.7 %all-gather.2.cloned.1.call-start = ((), (), s32[]{:S(2)}) async-start(), calls=%async_computation.6 | async-start | bytes 5406720 | tf_op jit(solution)/shard_map/all_gather | solution.py:84
  10.0 7.7 %collective-permute-start = (bf16[8,2,16,128]{3,2,1,0:T(8,128)(2,1)S(1)}, bf16[8,2,16,128]{3,2,1,0:T(8,128)(2,1)S(1)}, u32[]{:S(2)}, u32[]{:S(2)}) collective-permute-start(bf16[8,2,16,128]{3,2,1,0:T(8,128)(2,1)S(1)} %get-tuple-element.41), channel_id=1, source_target_pairs={{0,32},{32,64},{64,96},{96,128},{128,160},{160,192},{192,224},{1,3... | collective-permute-start | bytes 196616 | tf_op jit(solution)/shard_map/ppermute | solution.py:21
  13.5 5.9 %collective-permute-start.1 = (bf16[8,2,16,128]{3,2,1,0:T(8,128)(2,1)S(1)}, bf16[8,2,16,128]{3,2,1,0:T(8,128)(2,1)S(1)}, u32[]{:S(2)}, u32[]{:S(2)}) collective-permute-start(bf16[8,2,16,128]{3,2,1,0:T(8,128)(2,1)S(1)} %get-tuple-element.42), channel_id=1, source_target_pairs={{32,0},{64,32},{96,64},{128,96},{160,128},{192,160},{224,192},{33,... | collective-permute-start | bytes 196616 | tf_op jit(solution)/shard_map/ppermute | solution.py:23
  17.0 11.7 %copy-start.3 = (s32[2,3]{1,0:T(2,128)S(1)}, s32[2,3]{1,0:T(2,128)}, u32[]{:S(2)}) copy-start(s32[2,3]{1,0:T(2,128)} %param.9) | copy-start | bytes 76
  19.5 11.8 %collective-permute-start.2 = (bf16[2,8,16,128]{3,2,1,0:T(8,128)(2,1)S(1)}, bf16[2,8,16,128]{3,2,1,0:T(8,128)(2,1)S(1)}, u32[]{:S(2)}, u32[]{:S(2)}) collective-permute-start(bf16[2,8,16,128]{3,2,1,0:T(8,128)(2,1)S(1)} %get-tuple-element.34), channel_id=1, source_target_pairs={{0,1},{1,2},{2,3},{3,4},{4,5},{5,6},{6,7},{7,8},{8,9},{9,10},{10,1... | collective-permute-start | bytes 196616 | tf_op jit(solution)/shard_map/ppermute | solution.py:21
  26.8 9.3 %collective-permute-start.3 = (bf16[2,8,16,128]{3,2,1,0:T(8,128)(2,1)S(1)}, bf16[2,8,16,128]{3,2,1,0:T(8,128)(2,1)S(1)}, u32[]{:S(2)}, u32[]{:S(2)}) collective-permute-start(bf16[2,8,16,128]{3,2,1,0:T(8,128)(2,1)S(1)} %get-tuple-element.33), channel_id=1, source_target_pairs={{1,0},{2,1},{3,2},{4,3},{5,4},{6,5},{7,6},{8,7},{9,8},{10,9},{11,1... | collective-permute-start | bytes 196616 | tf_op jit(solution)/shard_map/ppermute | solution.py:23
  36.1 0.9 copy-start
  39.6 5.4 %collective-permute-start.4 = (bf16[8,2,16,128]{3,2,1,0:T(8,128)(2,1)S(1)}, bf16[8,2,16,128]{3,2,1,0:T(8,128)(2,1)S(1)}, u32[]{:S(2)}, u32[]{:S(2)}) collective-permute-start(bf16[8,2,16,128]{3,2,1,0:T(8,128)(2,1)S(1)} %get-tuple-element.39), channel_id=1, source_target_pairs={{0,32},{32,64},{64,96},{96,128},{128,160},{160,192},{192,224},{1,3... | collective-permute-start | bytes 196616 | tf_op jit(solution)/shard_map/ppermute | solution.py:21
  41.5 6.2 %collective-permute-start.5 = (bf16[8,2,16,128]{3,2,1,0:T(8,128)(2,1)S(1)}, bf16[8,2,16,128]{3,2,1,0:T(8,128)(2,1)S(1)}, u32[]{:S(2)}, u32[]{:S(2)}) collective-permute-start(bf16[8,2,16,128]{3,2,1,0:T(8,128)(2,1)S(1)} %get-tuple-element.40), channel_id=1, source_target_pairs={{32,0},{64,32},{96,64},{128,96},{160,128},{192,160},{224,192},{33,... | collective-permute-start | bytes 196616 | tf_op jit(solution)/shard_map/ppermute | solution.py:23
  47.7 7.8 %collective-permute-start.6 = (bf16[2,8,16,128]{3,2,1,0:T(8,128)(2,1)S(1)}, bf16[2,8,16,128]{3,2,1,0:T(8,128)(2,1)S(1)}, u32[]{:S(2)}, u32[]{:S(2)}) collective-permute-start(bf16[2,8,16,128]{3,2,1,0:T(8,128)(2,1)S(1)} %get-tuple-element.30), channel_id=1, source_target_pairs={{0,1},{1,2},{2,3},{3,4},{4,5},{5,6},{6,7},{7,8},{8,9},{9,10},{10,1... | collective-permute-start | bytes 196616 | tf_op jit(solution)/shard_map/ppermute | solution.py:21
  51.6 9.2 %collective-permute-start.7 = (bf16[2,8,16,128]{3,2,1,0:T(8,128)(2,1)S(1)}, bf16[2,8,16,128]{3,2,1,0:T(8,128)(2,1)S(1)}, u32[]{:S(2)}, u32[]{:S(2)}) collective-permute-start(bf16[2,8,16,128]{3,2,1,0:T(8,128)(2,1)S(1)} %get-tuple-element.29), channel_id=1, source_target_pairs={{1,0},{2,1},{3,2},{4,3},{5,4},{6,5},{7,6},{8,7},{9,8},{10,9},{11,1... | collective-permute-start | bytes 196616 | tf_op jit(solution)/shard_map/ppermute | solution.py:23
  106.1 13.8 %all-to-all-start.1 = ((bf16[8,32,1024]{2,1,0:T(8,128)(2,1)}), bf16[8,32,1024]{2,1,0:T(8,128)(2,1)S(1)}, u32[]{:S(2)}, u32[]{:S(2)}) async-start(bf16[8,32,1024]{2,1,0:T(8,128)(2,1)} %broadcast_in_dim.9), calls=%async_computation.1 | async-start | bytes 1048576 | tf_op jit(solution)/shard_map/all_to_all | solution.py:32
  120.2 24.0 %copy-start.4 = (bf16[32,128]{1,0:T(8,128)(2,1)S(1)}, bf16[32,128]{1,0:T(8,128)(2,1)}, u32[]{:S(2)}) copy-start(bf16[32,128]{1,0:T(8,128)(2,1)} %param.13) | copy-start | bytes 24580
  148.8 22.8 %all-to-all-start.3 = ((bf16[32,32,256]{2,1,0:T(8,128)(2,1)}), bf16[32,32,256]{2,1,0:T(8,128)(2,1)}, u32[]{:S(2)}, u32[]{:S(2)}) async-start(bf16[32,32,256]{2,1,0:T(8,128)(2,1)} %pad_maximum_fusion), calls=%async_computation.3 | async-start | bytes 1048576 | tf_op jit(solution)/shard_map/all_to_all | solution.py:73
  189.4 8.4 %copy-start.1 = (f32[8,4,16,128]{3,2,1,0:T(8,128)S(1)}, f32[8,4,16,128]{3,2,1,0:T(8,128)}, u32[]{:S(2)}) copy-start(f32[8,4,16,128]{3,2,1,0:T(8,128)} %get-tuple-element.56) | copy-start | bytes 786436
  198.0 6.6 %collective-permute-start.8 = (bf16[8,2,16,128]{3,2,1,0:T(8,128)(2,1)S(1)}, bf16[8,2,16,128]{3,2,1,0:T(8,128)(2,1)S(1)}, u32[]{:S(2)}, u32[]{:S(2)}) collective-permute-start(bf16[8,2,16,128]{3,2,1,0:T(8,128)(2,1)S(1)} %get-tuple-element.37), channel_id=1, source_target_pairs={{0,32},{32,64},{64,96},{96,128},{128,160},{160,192},{192,224},{1,3... | collective-permute-start | bytes 196616 | tf_op jit(solution)/shard_map/ppermute | solution.py:21
  200.8 5.9 %collective-permute-start.9 = (bf16[8,2,16,128]{3,2,1,0:T(8,128)(2,1)S(1)}, bf16[8,2,16,128]{3,2,1,0:T(8,128)(2,1)S(1)}, u32[]{:S(2)}, u32[]{:S(2)}) collective-permute-start(bf16[8,2,16,128]{3,2,1,0:T(8,128)(2,1)S(1)} %get-tuple-element.38), channel_id=1, source_target_pairs={{32,0},{64,32},{96,64},{128,96},{160,128},{192,160},{224,192},{33,... | collective-permute-start | bytes 196616 | tf_op jit(solution)/shard_map/ppermute | solution.py:23
  206.7 11.3 %collective-permute-start.10 = (bf16[2,8,16,128]{3,2,1,0:T(8,128)(2,1)S(1)}, bf16[2,8,16,128]{3,2,1,0:T(8,128)(2,1)S(1)}, u32[]{:S(2)}, u32[]{:S(2)}) collective-permute-start(bf16[2,8,16,128]{3,2,1,0:T(8,128)(2,1)S(1)} %get-tuple-element.26), channel_id=1, source_target_pairs={{1,0},{2,1},{3,2},{4,3},{5,4},{6,5},{7,6},{8,7},{9,8},{10,9},{11,1... | collective-permute-start | bytes 196616 | tf_op jit(solution)/shard_map/ppermute | solution.py:23
  212.5 6.6 %collective-permute-start.11 = (bf16[2,8,16,128]{3,2,1,0:T(8,128)(2,1)S(1)}, bf16[2,8,16,128]{3,2,1,0:T(8,128)(2,1)S(1)}, u32[]{:S(2)}, u32[]{:S(2)}) collective-permute-start(bf16[2,8,16,128]{3,2,1,0:T(8,128)(2,1)S(1)} %get-tuple-element.25), channel_id=1, source_target_pairs={{0,1},{1,2},{2,3},{3,4},{4,5},{5,6},{6,7},{7,8},{8,9},{9,10},{10,1... | collective-permute-start | bytes 196616 | tf_op jit(solution)/shard_map/ppermute | solution.py:21
  220.2 1.0 copy-start.5
  221.7 6.6 %collective-permute-start.12 = (bf16[8,2,16,128]{3,2,1,0:T(8,128)(2,1)S(1)}, bf16[8,2,16,128]{3,2,1,0:T(8,128)(2,1)S(1)}, u32[]{:S(2)}, u32[]{:S(2)}) collective-permute-start(bf16[8,2,16,128]{3,2,1,0:T(8,128)(2,1)S(1)} %get-tuple-element.35), channel_id=1, source_target_pairs={{0,32},{32,64},{64,96},{96,128},{128,160},{160,192},{192,224},{1,3... | collective-permute-start | bytes 196616 | tf_op jit(solution)/shard_map/ppermute | solution.py:21
  223.7 5.9 %collective-permute-start.13 = (bf16[8,2,16,128]{3,2,1,0:T(8,128)(2,1)S(1)}, bf16[8,2,16,128]{3,2,1,0:T(8,128)(2,1)S(1)}, u32[]{:S(2)}, u32[]{:S(2)}) collective-permute-start(bf16[8,2,16,128]{3,2,1,0:T(8,128)(2,1)S(1)} %get-tuple-element.36), channel_id=1, source_target_pairs={{32,0},{64,32},{96,64},{128,96},{160,128},{192,160},{224,192},{33,... | collective-permute-start | bytes 196616 | tf_op jit(solution)/shard_map/ppermute | solution.py:23
  229.6 11.1 %collective-permute-start.14 = (bf16[2,8,16,128]{3,2,1,0:T(8,128)(2,1)S(1)}, bf16[2,8,16,128]{3,2,1,0:T(8,128)(2,1)S(1)}, u32[]{:S(2)}, u32[]{:S(2)}) collective-permute-start(bf16[2,8,16,128]{3,2,1,0:T(8,128)(2,1)S(1)} %get-tuple-element.22), channel_id=1, source_target_pairs={{1,0},{2,1},{3,2},{4,3},{5,4},{6,5},{7,6},{8,7},{9,8},{10,9},{11,1... | collective-permute-start | bytes 196616 | tf_op jit(solution)/shard_map/ppermute | solution.py:23
  233.2 8.7 %collective-permute-start.15 = (bf16[2,8,16,128]{3,2,1,0:T(8,128)(2,1)S(1)}, bf16[2,8,16,128]{3,2,1,0:T(8,128)(2,1)S(1)}, u32[]{:S(2)}, u32[]{:S(2)}) collective-permute-start(bf16[2,8,16,128]{3,2,1,0:T(8,128)(2,1)S(1)} %get-tuple-element.21), channel_id=1, source_target_pairs={{0,1},{1,2},{2,3},{3,4},{4,5},{5,6},{6,7},{7,8},{8,9},{9,10},{10,1... | collective-permute-start | bytes 196616 | tf_op jit(solution)/shard_map/ppermute | solution.py:21
  (1 other events, 0.7 us)
Sparse Core Ops, SparseCore 0:
  10.1 92.0 all-gather.1

commit v4 on v3

--- a/solution.py
+++ b/solution.py
@@ -74,6 +74,21 @@
     return jnp.sum(pieces.astype(jnp.float32), axis=0)
 
 
+def gathered_by_doubling(block, axis):
+    peers = lax.axis_size(axis)
+    here = lax.axis_index(axis)
+    held = block[None]
+    distance = peers // 2
+    while distance >= 1:
+        got = lax.ppermute(held, axis, [(i, i ^ distance) for i in range(peers)])
+        upper = (here & distance) != 0
+        lower_half = jnp.where(upper, got, held)
+        upper_half = jnp.where(upper, held, got)
+        held = jnp.stack([lower_half, upper_half], axis=1).reshape(-1, *block.shape)
+        distance //= 2
+    return held.reshape(peers * block.shape[0], *block.shape[1:])
+
+
 def gather_weights(embed_weight, qkv_weight):
     _, feat, width = embed_weight.shape
     qkv_flat = qkv_weight.reshape(-1, width)
@@ -81,9 +96,8 @@
     rows = jnp.concatenate(
         [embed_weight[0], qkv_flat, jnp.zeros((extra, width), qkv_flat.dtype)], axis=0
     )
-    gathered = lax.all_gather(rows, "blk", axis=0, tiled=True)
     peers = lax.axis_size("blk")
-    gathered = gathered.reshape(peers, rows.shape[0], width)
+    gathered = gathered_by_doubling(rows, "blk").reshape(peers, rows.shape[0], width)
     embed_rows = gathered[:, :feat, :]
     qkv_rows = gathered[:, feat : feat + qkv_flat.shape[0], :].reshape(peers, *qkv_weight.shape)
     qkv_rows = jnp.moveaxis(qkv_rows, 0, 1).reshape(

time: 256 us -> 281 us (1.098)
  waiting for transfers between devices: 67.3 us -> 92.6 us
  between operations: 18.1 us -> 5.09 us
  starting transfers between devices: 71.9 us -> 82.7 us
  local copies, waits for them, and re-layouts: 16.2 us -> 25.4 us
  blocking collectives: 53.7 us -> 46 us
  other arithmetic: 6.95 us -> 11 us
    ppermute x0 -> x5, waiting for transfers between devices: none -> 30.4 us  [gathered_by_doubling(): got = lax.ppermute(held, axis, [(i, i ^ distance) for i in range(peers)])]
    all_gather x1 -> x0, waiting for transfers between devices: 28 us -> none  [gather_weights(): gathered = lax.all_gather(rows, 'blk', axis=0, tiled=True)]
    ppermute x8, waiting for transfers between devices: 17.8 us -> 37.2 us  [padded_2(): lax.ppermute(head, axis, [((i + 1) % count, i) for i in range(ends)])]
    all_to_all x1 -> x0, blocking collectives: 10.3 us -> none  [local(): lax.all_to_all(hidden, 'zslab', split_axis=0, concat_axis=1, tiled=True)]
    all_to_all x0 -> x1, starting transfers between devices: none -> 6.19 us  [local(): lax.all_to_all(hidden, 'zslab', split_axis=0, concat_axis=1, tiled=True)]
    another operation x0 -> x9, other arithmetic: none -> 6.13 us  [gathered_by_doubling(): held = jnp.stack([lower_half, upper_half], axis=1).reshape(-1, *block.shape)]
    ppermute x0 -> x5, starting transfers between devices: none -> 5.07 us  [gathered_by_doubling(): got = lax.ppermute(held, axis, [(i, i ^ distance) for i in range(peers)])]
    all_to_all x0 -> x1, waiting for transfers between devices: none -> 4.66 us  [local(): lax.all_to_all(hidden, 'zslab', split_axis=0, concat_axis=1, tiled=True)]
  transfers between devices with their start and end apart: 19 -> 24, of which waited for: 12 -> 9; matrix products, arithmetic and copies ran while one was open for 6% -> 7% of each run, Pallas kernels for 0% -> 0%
where the time goes in v4:
time: 281 us; the launch traced here: 278 us
  waiting for transfers between devices  92.6 us (33%)
  starting transfers between devices  82.7 us (29%)
  blocking collectives  46 us (16%)
  local copies, waits for them, and re-layouts  25.4 us (9%)
  matrix products  15.2 us (5%)
  other arithmetic  11 us (4%)
  between operations  5.09 us (2%)
    ppermute x8, starting transfers between devices, padded_2(): lax.ppermute(tail, axis, [(i, (i + 1) % count) for i in range(ends)])  37.9 us
    all_to_all x2, blocking collectives, copy_for_each(): lax.all_to_all(jnp.broadcast_to(shard[None], (peers, *shard.shape)), axis...  37.8 us
    ppermute x8, waiting for transfers between devices, padded_2(): lax.ppermute(head, axis, [((i + 1) % count, i) for i in range(ends)])  37.2 us
    ppermute x5, waiting for transfers between devices, gathered_by_doubling(): got = lax.ppermute(held, axis, [(i, i ^ distance) for i in range(peers)])  30.4 us
    ppermute x8, starting transfers between devices, padded_2(): lax.ppermute(head, axis, [((i + 1) % count, i) for i in range(ends)])  20.8 us
    all_to_all x1, waiting for transfers between devices, sum_at_owner(): lax.all_to_all(cut_along(shard, dim, peers), axis, 0, 0, tiled=True)  14.4 us
    all_to_all x1, blocking collectives, local(): lax.all_to_all(grid_grad, 'zslab', split_axis=1, concat_axis=0, tiled=True)  8.21 us
    all_to_all x1, starting transfers between devices, sum_at_owner(): lax.all_to_all(cut_along(shard, dim, peers), axis, 0, 0, tiled=True)  8.16 us
  transfers between devices with their start and end apart: 24, of which 9 were waited for; matrix products, arithmetic and copies ran while one was open for 7% of the time, Pallas kernels for 0%

profile of v4, /device:TPU:103, one launch (start us, length us, event | category | flops | bytes accessed | tf_op | source)
XLA Modules:
  0.0 278.1 jit_solution(2908178260441349400)
XLA Ops:
  3.4 3.7 %collective-permute-start.5 = (bf16[8,2,16,128]{3,2,1,0:T(8,128)(2,1)S(1)}, bf16[8,2,16,128]{3,2,1,0:T(8,128)(2,1)S(1)}, u32[]{:S(2)}, u32[]{:S(2)}) collective-permute-start(bf16[8,2,16,128]{3,2,1,0:T(8,128)(2,1)S(1)} %get-tuple-element.51), channel_id=1, source_target_pairs={{0,32},{32,64},{64,96},{96,128},{128,160},{160,192},{192,224},{1,3... | collective-permute-start | bytes 196616 | tf_op jit(solution)/shard_map/ppermute | solution.py:21
  9.7 4.2 %collective-permute-start = (bf16[1,80,1024]{2,1,0:T(8,128)(2,1)}, bf16[1,80,1024]{2,1,0:T(8,128)(2,1)}, u32[]{:S(2)}, u32[]{:S(2)}) collective-permute-start(bf16[1,80,1024]{2,1,0:T(8,128)(2,1)} %maximum_bitcast_fusion.1), channel_id=1, source_target_pairs={{0,16},{1,17},{2,18},{3,19},{4,20},{5,21},{6,22},{7,23},{8,24},{9,... | collective-permute-start | bytes 491528 | tf_op jit(solution)/shard_map/ppermute | solution.py:83
  16.4 3.4 %collective-permute-start.8 = (bf16[2,8,16,128]{3,2,1,0:T(8,128)(2,1)S(1)}, bf16[2,8,16,128]{3,2,1,0:T(8,128)(2,1)S(1)}, u32[]{:S(2)}, u32[]{:S(2)}) collective-permute-start(bf16[2,8,16,128]{3,2,1,0:T(8,128)(2,1)S(1)} %get-tuple-element.43), channel_id=1, source_target_pairs={{1,0},{2,1},{3,2},{4,3},{5,4},{6,5},{7,6},{8,7},{9,8},{10,9},{11,1... | collective-permute-start | bytes 196616 | tf_op jit(solution)/shard_map/ppermute | solution.py:23
  19.9 5.8 %collective-permute-start.7 = (bf16[2,8,16,128]{3,2,1,0:T(8,128)(2,1)S(1)}, bf16[2,8,16,128]{3,2,1,0:T(8,128)(2,1)S(1)}, u32[]{:S(2)}, u32[]{:S(2)}) collective-permute-start(bf16[2,8,16,128]{3,2,1,0:T(8,128)(2,1)S(1)} %get-tuple-element.44), channel_id=1, source_target_pairs={{0,1},{1,2},{2,3},{3,4},{4,5},{5,6},{6,7},{7,8},{8,9},{9,10},{10,1... | collective-permute-start | bytes 196616 | tf_op jit(solution)/shard_map/ppermute | solution.py:21
  30.7 16.7 %collective-permute-done.1 = bf16[2,80,1024]{2,1,0:T(8,128)(2,1)S(1)} collective-permute-done((bf16[2,80,1024]{2,1,0:T(8,128)(2,1)S(1)}, bf16[2,80,1024]{2,1,0:T(8,128)(2,1)S(1)}, u32[]{:S(2)}, u32[]{:S(2)}) %collective-permute-start.1) | collective-permute-done | bytes 327712 | tf_op jit(solution)/shard_map/ppermute | solution.py:83
  49.8 13.7 %collective-permute-done.2 = bf16[4,80,1024]{2,1,0:T(8,128)(2,1)S(1)} collective-permute-done((bf16[4,80,1024]{2,1,0:T(8,128)(2,1)S(1)}, bf16[4,80,1024]{2,1,0:T(8,128)(2,1)S(1)}, u32[]{:S(2)}, u32[]{:S(2)}) %collective-permute-start.2) | collective-permute-done | bytes 655392 | tf_op jit(solution)/shard_map/ppermute | solution.py:83
  68.1 4.3 %collective-permute-start.9 = (bf16[8,2,16,128]{3,2,1,0:T(8,128)(2,1)S(1)}, bf16[8,2,16,128]{3,2,1,0:T(8,128)(2,1)S(1)}, u32[]{:S(2)}, u32[]{:S(2)}) collective-permute-start(bf16[8,2,16,128]{3,2,1,0:T(8,128)(2,1)S(1)} %get-tuple-element.49), channel_id=1, source_target_pairs={{0,32},{32,64},{64,96},{96,128},{128,160},{160,192},{192,224},{1,3... | collective-permute-start | bytes 196616 | tf_op jit(solution)/shard_map/ppermute | solution.py:21
  72.4 22.8 %collective-permute-done.10 = bf16[8,2,16,128]{3,2,1,0:T(8,128)(2,1)S(1)} collective-permute-done((bf16[8,2,16,128]{3,2,1,0:T(8,128)(2,1)S(1)}, bf16[8,2,16,128]{3,2,1,0:T(8,128)(2,1)S(1)}, u32[]{:S(2)}, u32[]{:S(2)}) %collective-permute-start.10) | collective-permute-done | bytes 65568 | tf_op jit(solution)/shard_map/ppermute | solution.py:23
  95.3 4.4 %collective-permute-start.12 = (bf16[2,8,16,128]{3,2,1,0:T(8,128)(2,1)S(1)}, bf16[2,8,16,128]{3,2,1,0:T(8,128)(2,1)S(1)}, u32[]{:S(2)}, u32[]{:S(2)}) collective-permute-start(bf16[2,8,16,128]{3,2,1,0:T(8,128)(2,1)S(1)} %get-tuple-element.39), channel_id=1, source_target_pairs={{1,0},{2,1},{3,2},{4,3},{5,4},{6,5},{7,6},{8,7},{9,8},{10,9},{11,1... | collective-permute-start | bytes 196616 | tf_op jit(solution)/shard_map/ppermute | solution.py:23
  99.6 4.8 %collective-permute-start.11 = (bf16[2,8,16,128]{3,2,1,0:T(8,128)(2,1)S(1)}, bf16[2,8,16,128]{3,2,1,0:T(8,128)(2,1)S(1)}, u32[]{:S(2)}, u32[]{:S(2)}) collective-permute-start(bf16[2,8,16,128]{3,2,1,0:T(8,128)(2,1)S(1)} %get-tuple-element.40), channel_id=1, source_target_pairs={{0,1},{1,2},{2,3},{3,4},{4,5},{5,6},{6,7},{7,8},{8,9},{9,10},{10,1... | collective-permute-start | bytes 196616 | tf_op jit(solution)/shard_map/ppermute | solution.py:21
  114.6 6.2 %all-to-all-start = ((bf16[8,4,16,128]{3,2,1,0:T(8,128)(2,1)}), bf16[8,4,16,128]{3,2,1,0:T(8,128)(2,1)}, u32[]{:S(2)}, u32[]{:S(2)}) async-start(bf16[8,4,16,128]{3,2,1,0:T(8,128)(2,1)} %get-tuple-element.65), calls=%async_computation | async-start | bytes 262144 | tf_op jit(solution)/shard_map/all_to_all | solution.py:171
  120.8 4.7 %all-to-all-done = bf16[8,4,16,128]{3,2,1,0:T(8,128)(2,1)} async-done(((bf16[8,4,16,128]{3,2,1,0:T(8,128)(2,1)}), bf16[8,4,16,128]{3,2,1,0:T(8,128)(2,1)}, u32[]{:S(2)}, u32[]{:S(2)}) %all-to-all-start) | async-done | bytes 131104 | tf_op jit(solution)/shard_map/all_to_all | solution.py:171
  136.4 4.6 %all-to-all-start.1 = ((bf16[8,32,1024]{2,1,0:T(8,128)(2,1)}), bf16[8,32,1024]{2,1,0:T(8,128)(2,1)S(1)}, u32[]{:S(2)}, u32[]{:S(2)}) async-start(bf16[8,32,1024]{2,1,0:T(8,128)(2,1)} %broadcast_in_dim.12), calls=%async_computation.1 | async-start | bytes 1048576 | tf_op jit(solution)/shard_map/all_to_all | solution.py:32
  142.9 5.6 %all-to-all-done.1 = bf16[8,32,1024]{2,1,0:T(8,128)(2,1)S(1)} async-done(((bf16[8,32,1024]{2,1,0:T(8,128)(2,1)}), bf16[8,32,1024]{2,1,0:T(8,128)(2,1)S(1)}, u32[]{:S(2)}, u32[]{:S(2)}) %all-to-all-start.1) | async-done | bytes 524320 | tf_op jit(solution)/shard_map/all_to_all | solution.py:32
  148.9 26.1 %all_to_all.38 = bf16[32,32,256]{2,1,0:T(8,128)(2,1)S(1)} all-to-all(bf16[32,32,256]{2,1,0:T(8,128)(2,1)S(1)} %broadcast_in_dim.13), channel_id=1, replica_groups=mesh['zslab'=8,'blk'=32] {'blk'}, dimensions={0} | all-to-all | bytes 1048576 | tf_op jit(solution)/shard_map/all_to_all | solution.py:32
  177.8 8.2 %all-to-all-start.3 = ((bf16[32,32,256]{2,1,0:T(8,128)(2,1)}), bf16[32,32,256]{2,1,0:T(8,128)(2,1)S(1)}, u32[]{:S(2)}, u32[]{:S(2)}) async-start(bf16[32,32,256]{2,1,0:T(8,128)(2,1)} %pad_maximum_fusion.4), calls=%async_computation.3 | async-start | bytes 1048576 | tf_op jit(solution)/shard_map/all_to_all | solution.py:73
  186.1 14.4 %all-to-all-done.3 = bf16[32,32,256]{2,1,0:T(8,128)(2,1)S(1)} async-done(((bf16[32,32,256]{2,1,0:T(8,128)(2,1)}), bf16[32,32,256]{2,1,0:T(8,128)(2,1)S(1)}, u32[]{:S(2)}, u32[]{:S(2)}) %all-to-all-start.3) | async-done | bytes 524320 | tf_op jit(solution)/shard_map/all_to_all | solution.py:73
  201.0 11.7 %all_to_all.39 = bf16[8,32,1024]{2,1,0:T(8,128)(2,1)S(1)} all-to-all(bf16[8,32,1024]{2,1,0:T(8,128)(2,1)S(1)} %broadcast_in_dim.14), channel_id=1, replica_groups=mesh['zslab'=8,'blk'=32] {'zslab'}, dimensions={0} | all-to-all | bytes 1048576 | tf_op jit(solution)/shard_map/all_to_all | solution.py:32
  212.8 4.2 %fusion.4 = bf16[32,32,64]{2,0,1:T(8,128)(2,1)S(1)} fusion(bf16[32,80,1024]{2,1,0:T(8,128)(2,1)} %bitcast.263, bf16[32,1024]{1,0:T(8,128)(2,1)S(1)} %reduce_sum.58), kind=kOutput, calls=%fused_computation.11 | convolution fusion | flops 134283264 | bytes 4390912 | tf_op jit(solution)/shard_map/td,bfd->tbf/dot_general | solution.py:234
  217.3 8.2 %all_to_all.40 = bf16[1,32,16,128]{3,2,0,1:T(8,128)(2,1)S(1)} all-to-all(bf16[1,32,16,128]{3,2,0,1:T(8,128)(2,1)S(1)} %bitcast.295), channel_id=1, replica_groups=mesh['zslab'=8,'blk'=32] {'zslab'}, dimensions={1} | all-to-all | bytes 262144 | tf_op jit(solution)/shard_map/all_to_all | solution.py:241
  233.7 8.8 %collective-permute-start.16 = (bf16[2,8,16,128]{3,2,1,0:T(8,128)(2,1)S(1)}, bf16[2,8,16,128]{3,2,1,0:T(8,128)(2,1)S(1)}, u32[]{:S(2)}, u32[]{:S(2)}) collective-permute-start(bf16[2,8,16,128]{3,2,1,0:T(8,128)(2,1)S(1)} %get-tuple-element.35), channel_id=1, source_target_pairs={{0,1},{1,2},{2,3},{3,4},{4,5},{5,6},{6,7},{7,8},{8,9},{9,10},{10,1... | collective-permute-start | bytes 196616 | tf_op jit(solution)/shard_map/ppermute | solution.py:21
  244.5 7.2 %collective-permute-done.15 = bf16[2,8,16,128]{3,2,1,0:T(8,128)(2,1)S(1)} collective-permute-done((bf16[2,8,16,128]{3,2,1,0:T(8,128)(2,1)S(1)}, bf16[2,8,16,128]{3,2,1,0:T(8,128)(2,1)S(1)}, u32[]{:S(2)}, u32[]{:S(2)}) %collective-permute-start.15) | collective-permute-done | bytes 65568 | tf_op jit(solution)/shard_map/ppermute | solution.py:23
  257.0 4.3 %collective-permute-start.17 = (bf16[8,2,16,128]{3,2,1,0:T(8,128)(2,1)S(1)}, bf16[8,2,16,128]{3,2,1,0:T(8,128)(2,1)S(1)}, u32[]{:S(2)}, u32[]{:S(2)}) collective-permute-start(bf16[8,2,16,128]{3,2,1,0:T(8,128)(2,1)S(1)} %get-tuple-element.45), channel_id=1, source_target_pairs={{0,32},{32,64},{64,96},{96,128},{128,160},{160,192},{192,224},{1,3... | collective-permute-start | bytes 196616 | tf_op jit(solution)/shard_map/ppermute | solution.py:21
  267.6 7.2 %collective-permute-done.19 = bf16[2,8,16,128]{3,2,1,0:T(8,128)(2,1)S(1)} collective-permute-done((bf16[2,8,16,128]{3,2,1,0:T(8,128)(2,1)S(1)}, bf16[2,8,16,128]{3,2,1,0:T(8,128)(2,1)S(1)}, u32[]{:S(2)}, u32[]{:S(2)}) %collective-permute-start.19) | collective-permute-done | bytes 65568 | tf_op jit(solution)/shard_map/ppermute | solution.py:23
  (217 shorter events, 68.0 us)
Async XLA Ops:
  0.9 15.5 %collective-permute-start.6 = (bf16[8,2,16,128]{3,2,1,0:T(8,128)(2,1)S(1)}, bf16[8,2,16,128]{3,2,1,0:T(8,128)(2,1)S(1)}, u32[]{:S(2)}, u32[]{:S(2)}) collective-permute-start(bf16[8,2,16,128]{3,2,1,0:T(8,128)(2,1)S(1)} %get-tuple-element.52), channel_id=1, source_target_pairs={{32,0},{64,32},{96,64},{128,96},{160,128},{192,160},{224,192},{33,... | collective-permute-start | bytes 196616 | tf_op jit(solution)/shard_map/ppermute | solution.py:23
  3.4 13.0 %collective-permute-start.5 = (bf16[8,2,16,128]{3,2,1,0:T(8,128)(2,1)S(1)}, bf16[8,2,16,128]{3,2,1,0:T(8,128)(2,1)S(1)}, u32[]{:S(2)}, u32[]{:S(2)}) collective-permute-start(bf16[8,2,16,128]{3,2,1,0:T(8,128)(2,1)S(1)} %get-tuple-element.51), channel_id=1, source_target_pairs={{0,32},{32,64},{64,96},{96,128},{128,160},{160,192},{192,224},{1,3... | collective-permute-start | bytes 196616 | tf_op jit(solution)/shard_map/ppermute | solution.py:21
  9.7 19.7 %collective-permute-start = (bf16[1,80,1024]{2,1,0:T(8,128)(2,1)}, bf16[1,80,1024]{2,1,0:T(8,128)(2,1)}, u32[]{:S(2)}, u32[]{:S(2)}) collective-permute-start(bf16[1,80,1024]{2,1,0:T(8,128)(2,1)} %maximum_bitcast_fusion.1), channel_id=1, source_target_pairs={{0,16},{1,17},{2,18},{3,19},{4,20},{5,21},{6,22},{7,23},{8,24},{9,... | collective-permute-start | bytes 491528 | tf_op jit(solution)/shard_map/ppermute | solution.py:83
  16.4 11.8 %collective-permute-start.8 = (bf16[2,8,16,128]{3,2,1,0:T(8,128)(2,1)S(1)}, bf16[2,8,16,128]{3,2,1,0:T(8,128)(2,1)S(1)}, u32[]{:S(2)}, u32[]{:S(2)}) collective-permute-start(bf16[2,8,16,128]{3,2,1,0:T(8,128)(2,1)S(1)} %get-tuple-element.43), channel_id=1, source_target_pairs={{1,0},{2,1},{3,2},{4,3},{5,4},{6,5},{7,6},{8,7},{9,8},{10,9},{11,1... | collective-permute-start | bytes 196616 | tf_op jit(solution)/shard_map/ppermute | solution.py:23
  19.9 8.4 %collective-permute-start.7 = (bf16[2,8,16,128]{3,2,1,0:T(8,128)(2,1)S(1)}, bf16[2,8,16,128]{3,2,1,0:T(8,128)(2,1)S(1)}, u32[]{:S(2)}, u32[]{:S(2)}) collective-permute-start(bf16[2,8,16,128]{3,2,1,0:T(8,128)(2,1)S(1)} %get-tuple-element.44), channel_id=1, source_target_pairs={{0,1},{1,2},{2,3},{3,4},{4,5},{5,6},{6,7},{7,8},{8,9},{9,10},{10,1... | collective-permute-start | bytes 196616 | tf_op jit(solution)/shard_map/ppermute | solution.py:21
  30.5 16.9 %collective-permute-start.1 = (bf16[2,80,1024]{2,1,0:T(8,128)(2,1)S(1)}, bf16[2,80,1024]{2,1,0:T(8,128)(2,1)S(1)}, u32[]{:S(2)}, u32[]{:S(2)}) collective-permute-start(bf16[2,80,1024]{2,1,0:T(8,128)(2,1)S(1)} %maximum_bitcast_fusion), channel_id=1, source_target_pairs={{0,8},{1,9},{2,10},{3,11},{4,12},{5,13},{6,14},{7,15},{8,0},{9,1},... | collective-permute-start | bytes 983048 | tf_op jit(solution)/shard_map/ppermute | solution.py:83
  47.5 16.0 %collective-permute-start.2 = (bf16[4,80,1024]{2,1,0:T(8,128)(2,1)S(1)}, bf16[4,80,1024]{2,1,0:T(8,128)(2,1)S(1)}, u32[]{:S(2)}, u32[]{:S(2)}) collective-permute-start(bf16[4,80,1024]{2,1,0:T(8,128)(2,1)S(1)} %bitcast.274), channel_id=1, source_target_pairs={{0,4},{1,5},{2,6},{3,7},{4,0},{5,1},{6,2},{7,3},{8,12},{9,13},{10,... | collective-permute-start | bytes 1966088 | tf_op jit(solution)/shard_map/ppermute | solution.py:83
  65.0 42.5 %collective-permute-start.3 = (bf16[8,80,1024]{2,1,0:T(8,128)(2,1)}, bf16[8,80,1024]{2,1,0:T(8,128)(2,1)}, u32[]{:S(2)}, u32[]{:S(2)}) collective-permute-start(bf16[8,80,1024]{2,1,0:T(8,128)(2,1)} %bitcast.11), channel_id=1, source_target_pairs={{0,2},{1,3},{2,0},{3,1},{4,6},{5,7},{6,4},{7,5},{8,10},{9,11},{10,... | collective-permute-start | bytes 3932168 | tf_op jit(solution)/shard_map/ppermute | solution.py:83
  66.2 29.0 %collective-permute-start.10 = (bf16[8,2,16,128]{3,2,1,0:T(8,128)(2,1)S(1)}, bf16[8,2,16,128]{3,2,1,0:T(8,128)(2,1)S(1)}, u32[]{:S(2)}, u32[]{:S(2)}) collective-permute-start(bf16[8,2,16,128]{3,2,1,0:T(8,128)(2,1)S(1)} %get-tuple-element.50), channel_id=1, source_target_pairs={{32,0},{64,32},{96,64},{128,96},{160,128},{192,160},{224,192},{33,... | collective-permute-start | bytes 196616 | tf_op jit(solution)/shard_map/ppermute | solution.py:23
  68.1 27.1 %collective-permute-start.9 = (bf16[8,2,16,128]{3,2,1,0:T(8,128)(2,1)S(1)}, bf16[8,2,16,128]{3,2,1,0:T(8,128)(2,1)S(1)}, u32[]{:S(2)}, u32[]{:S(2)}) collective-permute-start(bf16[8,2,16,128]{3,2,1,0:T(8,128)(2,1)S(1)} %get-tuple-element.49), channel_id=1, source_target_pairs={{0,32},{32,64},{64,96},{96,128},{128,160},{160,192},{192,224},{1,3... | collective-permute-start | bytes 196616 | tf_op jit(solution)/shard_map/ppermute | solution.py:21
  95.3 12.1 %collective-permute-start.12 = (bf16[2,8,16,128]{3,2,1,0:T(8,128)(2,1)S(1)}, bf16[2,8,16,128]{3,2,1,0:T(8,128)(2,1)S(1)}, u32[]{:S(2)}, u32[]{:S(2)}) collective-permute-start(bf16[2,8,16,128]{3,2,1,0:T(8,128)(2,1)S(1)} %get-tuple-element.39), channel_id=1, source_target_pairs={{1,0},{2,1},{3,2},{4,3},{5,4},{6,5},{7,6},{8,7},{9,8},{10,9},{11,1... | collective-permute-start | bytes 196616 | tf_op jit(solution)/shard_map/ppermute | solution.py:23
  99.6 7.7 %collective-permute-start.11 = (bf16[2,8,16,128]{3,2,1,0:T(8,128)(2,1)S(1)}, bf16[2,8,16,128]{3,2,1,0:T(8,128)(2,1)S(1)}, u32[]{:S(2)}, u32[]{:S(2)}) collective-permute-start(bf16[2,8,16,128]{3,2,1,0:T(8,128)(2,1)S(1)} %get-tuple-element.40), channel_id=1, source_target_pairs={{0,1},{1,2},{2,3},{3,4},{4,5},{5,6},{6,7},{7,8},{8,9},{9,10},{10,1... | collective-permute-start | bytes 196616 | tf_op jit(solution)/shard_map/ppermute | solution.py:21
  110.0 18.9 %collective-permute-start.4 = (bf16[16,80,1024]{2,1,0:T(8,128)(2,1)S(1)}, bf16[16,80,1024]{2,1,0:T(8,128)(2,1)}, u32[]{:S(2)}, u32[]{:S(2)}) collective-permute-start(bf16[16,80,1024]{2,1,0:T(8,128)(2,1)S(1)} %bitcast.256), channel_id=1, source_target_pairs={{0,1},{1,0},{2,3},{3,2},{4,5},{5,4},{6,7},{7,6},{8,9},{9,8},{10,11... | collective-permute-start | bytes 7864328 | tf_op jit(solution)/shard_map/ppermute | solution.py:83
  114.6 10.9 %all-to-all-start = ((bf16[8,4,16,128]{3,2,1,0:T(8,128)(2,1)}), bf16[8,4,16,128]{3,2,1,0:T(8,128)(2,1)}, u32[]{:S(2)}, u32[]{:S(2)}) async-start(bf16[8,4,16,128]{3,2,1,0:T(8,128)(2,1)} %get-tuple-element.65), calls=%async_computation | async-start | bytes 262144 | tf_op jit(solution)/shard_map/all_to_all | solution.py:171
  136.4 12.1 %all-to-all-start.1 = ((bf16[8,32,1024]{2,1,0:T(8,128)(2,1)}), bf16[8,32,1024]{2,1,0:T(8,128)(2,1)S(1)}, u32[]{:S(2)}, u32[]{:S(2)}) async-start(bf16[8,32,1024]{2,1,0:T(8,128)(2,1)} %broadcast_in_dim.12), calls=%async_computation.1 | async-start | bytes 1048576 | tf_op jit(solution)/shard_map/all_to_all | solution.py:32
  177.8 22.7 %all-to-all-start.3 = ((bf16[32,32,256]{2,1,0:T(8,128)(2,1)}), bf16[32,32,256]{2,1,0:T(8,128)(2,1)S(1)}, u32[]{:S(2)}, u32[]{:S(2)}) async-start(bf16[32,32,256]{2,1,0:T(8,128)(2,1)} %pad_maximum_fusion.4), calls=%async_computation.3 | async-start | bytes 1048576 | tf_op jit(solution)/shard_map/all_to_all | solution.py:73
  225.7 7.5 %collective-permute-start.14 = (bf16[8,2,16,128]{3,2,1,0:T(8,128)(2,1)S(1)}, bf16[8,2,16,128]{3,2,1,0:T(8,128)(2,1)S(1)}, u32[]{:S(2)}, u32[]{:S(2)}) collective-permute-start(bf16[8,2,16,128]{3,2,1,0:T(8,128)(2,1)S(1)} %get-tuple-element.48), channel_id=1, source_target_pairs={{32,0},{64,32},{96,64},{128,96},{160,128},{192,160},{224,192},{33,... | collective-permute-start | bytes 196616 | tf_op jit(solution)/shard_map/ppermute | solution.py:23
  228.6 5.0 %collective-permute-start.13 = (bf16[8,2,16,128]{3,2,1,0:T(8,128)(2,1)S(1)}, bf16[8,2,16,128]{3,2,1,0:T(8,128)(2,1)S(1)}, u32[]{:S(2)}, u32[]{:S(2)}) collective-permute-start(bf16[8,2,16,128]{3,2,1,0:T(8,128)(2,1)S(1)} %get-tuple-element.47), channel_id=1, source_target_pairs={{0,32},{32,64},{64,96},{96,128},{128,160},{160,192},{192,224},{1,3... | collective-permute-start | bytes 196616 | tf_op jit(solution)/shard_map/ppermute | solution.py:21
  233.7 10.8 %collective-permute-start.16 = (bf16[2,8,16,128]{3,2,1,0:T(8,128)(2,1)S(1)}, bf16[2,8,16,128]{3,2,1,0:T(8,128)(2,1)S(1)}, u32[]{:S(2)}, u32[]{:S(2)}) collective-permute-start(bf16[2,8,16,128]{3,2,1,0:T(8,128)(2,1)S(1)} %get-tuple-element.35), channel_id=1, source_target_pairs={{0,1},{1,2},{2,3},{3,4},{4,5},{5,6},{6,7},{7,8},{8,9},{9,10},{10,1... | collective-permute-start | bytes 196616 | tf_op jit(solution)/shard_map/ppermute | solution.py:21
  242.5 9.2 %collective-permute-start.15 = (bf16[2,8,16,128]{3,2,1,0:T(8,128)(2,1)S(1)}, bf16[2,8,16,128]{3,2,1,0:T(8,128)(2,1)S(1)}, u32[]{:S(2)}, u32[]{:S(2)}) collective-permute-start(bf16[2,8,16,128]{3,2,1,0:T(8,128)(2,1)S(1)} %get-tuple-element.36), channel_id=1, source_target_pairs={{1,0},{2,1},{3,2},{4,3},{5,4},{6,5},{7,6},{8,7},{9,8},{10,9},{11,1... | collective-permute-start | bytes 196616 | tf_op jit(solution)/shard_map/ppermute | solution.py:23
  255.1 7.5 %collective-permute-start.18 = (bf16[8,2,16,128]{3,2,1,0:T(8,128)(2,1)S(1)}, bf16[8,2,16,128]{3,2,1,0:T(8,128)(2,1)S(1)}, u32[]{:S(2)}, u32[]{:S(2)}) collective-permute-start(bf16[8,2,16,128]{3,2,1,0:T(8,128)(2,1)S(1)} %get-tuple-element.46), channel_id=1, source_target_pairs={{32,0},{64,32},{96,64},{128,96},{160,128},{192,160},{224,192},{33,... | collective-permute-start | bytes 196616 | tf_op jit(solution)/shard_map/ppermute | solution.py:23
  257.0 5.6 %collective-permute-start.17 = (bf16[8,2,16,128]{3,2,1,0:T(8,128)(2,1)S(1)}, bf16[8,2,16,128]{3,2,1,0:T(8,128)(2,1)S(1)}, u32[]{:S(2)}, u32[]{:S(2)}) collective-permute-start(bf16[8,2,16,128]{3,2,1,0:T(8,128)(2,1)S(1)} %get-tuple-element.45), channel_id=1, source_target_pairs={{0,32},{32,64},{64,96},{96,128},{128,160},{160,192},{192,224},{1,3... | collective-permute-start | bytes 196616 | tf_op jit(solution)/shard_map/ppermute | solution.py:21
  262.6 5.0 %collective-permute-start.20 = (bf16[2,8,16,128]{3,2,1,0:T(8,128)(2,1)S(1)}, bf16[2,8,16,128]{3,2,1,0:T(8,128)(2,1)S(1)}, u32[]{:S(2)}, u32[]{:S(2)}) collective-permute-start(bf16[2,8,16,128]{3,2,1,0:T(8,128)(2,1)S(1)} %get-tuple-element.31), channel_id=1, source_target_pairs={{0,1},{1,2},{2,3},{3,4},{4,5},{5,6},{6,7},{7,8},{8,9},{9,10},{10,1... | collective-permute-start | bytes 196616 | tf_op jit(solution)/shard_map/ppermute | solution.py:21
  265.6 9.2 %collective-permute-start.19 = (bf16[2,8,16,128]{3,2,1,0:T(8,128)(2,1)S(1)}, bf16[2,8,16,128]{3,2,1,0:T(8,128)(2,1)S(1)}, u32[]{:S(2)}, u32[]{:S(2)}) collective-permute-start(bf16[2,8,16,128]{3,2,1,0:T(8,128)(2,1)S(1)} %get-tuple-element.32), channel_id=1, source_target_pairs={{1,0},{2,1},{3,2},{4,3},{5,4},{6,5},{7,6},{8,7},{9,8},{10,9},{11,1... | collective-permute-start | bytes 196616 | tf_op jit(solution)/shard_map/ppermute | solution.py:23
  (28 other events, 250.1 us)

commit v5 on v3

--- a/solution.py
+++ b/solution.py
@@ -75,20 +75,11 @@
 
 
 def gather_weights(embed_weight, qkv_weight):
-    _, feat, width = embed_weight.shape
-    qkv_flat = qkv_weight.reshape(-1, width)
-    extra = -qkv_flat.shape[0] % 16
-    rows = jnp.concatenate(
-        [embed_weight[0], qkv_flat, jnp.zeros((extra, width), qkv_flat.dtype)], axis=0
-    )
-    gathered = lax.all_gather(rows, "blk", axis=0, tiled=True)
     peers = lax.axis_size("blk")
-    gathered = gathered.reshape(peers, rows.shape[0], width)
-    embed_rows = gathered[:, :feat, :]
-    qkv_rows = gathered[:, feat : feat + qkv_flat.shape[0], :].reshape(peers, *qkv_weight.shape)
-    qkv_rows = jnp.moveaxis(qkv_rows, 0, 1).reshape(
-        qkv_weight.shape[0], peers * qkv_weight.shape[1], qkv_weight.shape[2]
-    )
+    embed_rows = lax.all_gather(embed_weight[0], "blk", axis=0, tiled=True)
+    embed_rows = embed_rows.reshape(peers, embed_weight.shape[1], embed_weight.shape[2])
+    qkv_rows = jnp.moveaxis(copy_for_each(qkv_weight, "blk").reshape(peers, *qkv_weight.shape), 0, 1)
+    qkv_rows = qkv_rows.reshape(qkv_weight.shape[0], -1, qkv_weight.shape[2])
     return embed_rows, qkv_rows
 
 
@@ -163,6 +154,7 @@
     patches = patches.reshape(y_blocks * z_blocks, x_local, PY * PZ * channels)
     embed_rows, qkv_rows = gather_weights(embed_weight, qkv_weight)
     patches = patches.reshape(patches.shape[0], embed_rows.shape[0], embed_rows.shape[1])
+    patches, qkv_rows = lax.optimization_barrier((patches, qkv_rows))
     partial_value = jnp.einsum(
         "tbf,bfd->td", patches, embed_rows, preferred_element_type=jnp.float32
     )

time: 256 us -> 260 us (1.016)
  blocking collectives: 53.7 us -> 66.3 us
  waiting for transfers between devices: 67.3 us -> 63.1 us
  local copies, waits for them, and re-layouts: 16.2 us -> 12.4 us
    all_gather x1, waiting for transfers between devices: 28 us -> 1.99 us  [gather_weights(): embed_rows = lax.all_gather(embed_weight[0], 'blk', axis=0, tiled=True)]
    all_to_all x1, waiting for transfers between devices: 4.64 us -> 26.5 us  [copy_for_each(): lax.all_to_all(jnp.broadcast_to(shard[None], (peers, *shard.shape)), axis...]
    all_to_all x2 -> x3, blocking collectives: 35.3 us -> 48 us  [copy_for_each(): lax.all_to_all(jnp.broadcast_to(shard[None], (peers, *shard.shape)), axis...]
  transfers between devices with their start and end apart: 19 -> 19, of which waited for: 12 -> 11; matrix products, arithmetic and copies ran while one was open for 6% -> 5% of each run, Pallas kernels for 0% -> 0%
where the time goes in v5:
time: 260 us; the launch traced here: 257 us
  starting transfers between devices  74.1 us (28%)
  blocking collectives  66.3 us (26%)
  waiting for transfers between devices  63.1 us (24%)
  between operations  17.9 us (7%)
  matrix products  17.5 us (7%)
  local copies, waits for them, and re-layouts  12.4 us (5%)
  other arithmetic  5.28 us (2%)
    all_to_all x3, blocking collectives, copy_for_each(): lax.all_to_all(jnp.broadcast_to(shard[None], (peers, *shard.shape)), axis...  48 us
    ppermute x8, starting transfers between devices, padded_2(): lax.ppermute(tail, axis, [(i, (i + 1) % count) for i in range(ends)])  34 us
    all_to_all x1, waiting for transfers between devices, copy_for_each(): lax.all_to_all(jnp.broadcast_to(shard[None], (peers, *shard.shape)), axis...  26.5 us
    ppermute x8, starting transfers between devices, padded_2(): lax.ppermute(head, axis, [((i + 1) % count, i) for i in range(ends)])  24.5 us
    ppermute x8, waiting for transfers between devices, padded_2(): lax.ppermute(head, axis, [((i + 1) % count, i) for i in range(ends)])  17.8 us
    all_to_all x1, waiting for transfers between devices, sum_at_owner(): lax.all_to_all(cut_along(shard, dim, peers), axis, 0, 0, tiled=True)  14.4 us
    all_to_all x1, blocking collectives, local(): lax.all_to_all(hidden, 'zslab', split_axis=0, concat_axis=1, tiled=True)  10.1 us
    all_to_all x1, starting transfers between devices, sum_at_owner(): lax.all_to_all(cut_along(shard, dim, peers), axis, 0, 0, tiled=True)  8.22 us
  transfers between devices with their start and end apart: 19, of which 11 were waited for; matrix products, arithmetic and copies ran while one was open for 5% of the time, Pallas kernels for 0%

profile of v5, /device:TPU:103, one launch (start us, length us, event | category | flops | bytes accessed | tf_op | source)
XLA Modules:
  0.0 256.6 jit_solution(9001227448499288795)
XLA Ops:
  7.5 3.5 %collective-permute-start = (bf16[8,2,16,128]{3,2,1,0:T(8,128)(2,1)S(1)}, bf16[8,2,16,128]{3,2,1,0:T(8,128)(2,1)S(1)}, u32[]{:S(2)}, u32[]{:S(2)}) collective-permute-start(bf16[8,2,16,128]{3,2,1,0:T(8,128)(2,1)S(1)} %get-tuple-element.45), channel_id=1, source_target_pairs={{0,32},{32,64},{64,96},{96,128},{128,160},{160,192},{192,224},{1,3... | collective-permute-start | bytes 196616 | tf_op jit(solution)/shard_map/ppermute | solution.py:21
  16.9 7.3 %collective-permute-start.2 = (bf16[2,8,16,128]{3,2,1,0:T(8,128)(2,1)S(1)}, bf16[2,8,16,128]{3,2,1,0:T(8,128)(2,1)S(1)}, u32[]{:S(2)}, u32[]{:S(2)}) collective-permute-start(bf16[2,8,16,128]{3,2,1,0:T(8,128)(2,1)S(1)} %get-tuple-element.38), channel_id=1, source_target_pairs={{0,1},{1,2},{2,3},{3,4},{4,5},{5,6},{6,7},{7,8},{8,9},{9,10},{10,1... | collective-permute-start | bytes 196616 | tf_op jit(solution)/shard_map/ppermute | solution.py:21
  28.6 4.8 %collective-permute-done.3 = bf16[2,8,16,128]{3,2,1,0:T(8,128)(2,1)S(1)} collective-permute-done((bf16[2,8,16,128]{3,2,1,0:T(8,128)(2,1)S(1)}, bf16[2,8,16,128]{3,2,1,0:T(8,128)(2,1)S(1)}, u32[]{:S(2)}, u32[]{:S(2)}) %collective-permute-start.3) | collective-permute-done | bytes 65568 | tf_op jit(solution)/shard_map/ppermute | solution.py:23
  38.8 3.4 %collective-permute-start.5 = (bf16[8,2,16,128]{3,2,1,0:T(8,128)(2,1)S(1)}, bf16[8,2,16,128]{3,2,1,0:T(8,128)(2,1)S(1)}, u32[]{:S(2)}, u32[]{:S(2)}) collective-permute-start(bf16[8,2,16,128]{3,2,1,0:T(8,128)(2,1)S(1)} %get-tuple-element.44), channel_id=1, source_target_pairs={{32,0},{64,32},{96,64},{128,96},{160,128},{192,160},{224,192},{33,... | collective-permute-start | bytes 196616 | tf_op jit(solution)/shard_map/ppermute | solution.py:23
  42.2 2.8 %collective-permute-done.5 = bf16[8,2,16,128]{3,2,1,0:T(8,128)(2,1)S(1)} collective-permute-done((bf16[8,2,16,128]{3,2,1,0:T(8,128)(2,1)S(1)}, bf16[8,2,16,128]{3,2,1,0:T(8,128)(2,1)S(1)}, u32[]{:S(2)}, u32[]{:S(2)}) %collective-permute-start.5) | collective-permute-done | bytes 65568 | tf_op jit(solution)/shard_map/ppermute | solution.py:23
  45.0 3.9 %collective-permute-start.6 = (bf16[2,8,16,128]{3,2,1,0:T(8,128)(2,1)S(1)}, bf16[2,8,16,128]{3,2,1,0:T(8,128)(2,1)S(1)}, u32[]{:S(2)}, u32[]{:S(2)}) collective-permute-start(bf16[2,8,16,128]{3,2,1,0:T(8,128)(2,1)S(1)} %get-tuple-element.34), channel_id=1, source_target_pairs={{0,1},{1,2},{2,3},{3,4},{4,5},{5,6},{6,7},{7,8},{8,9},{9,10},{10,1... | collective-permute-start | bytes 196616 | tf_op jit(solution)/shard_map/ppermute | solution.py:21
  52.8 5.3 %collective-permute-done.7 = bf16[2,8,16,128]{3,2,1,0:T(8,128)(2,1)S(1)} collective-permute-done((bf16[2,8,16,128]{3,2,1,0:T(8,128)(2,1)S(1)}, bf16[2,8,16,128]{3,2,1,0:T(8,128)(2,1)S(1)}, u32[]{:S(2)}, u32[]{:S(2)}) %collective-permute-start.7) | collective-permute-done | bytes 65568 | tf_op jit(solution)/shard_map/ppermute | solution.py:23
  61.0 10.1 %all_to_all.43 = bf16[8,4,16,128]{3,2,1,0:T(8,128)(2,1)S(1)} all-to-all(bf16[8,4,16,128]{3,2,1,0:T(8,128)(2,1)S(1)} %get-tuple-element.59), channel_id=1, replica_groups=mesh['zslab'=8,'blk'=32] {'zslab'}, dimensions={0} | all-to-all | bytes 262144 | tf_op jit(solution)/shard_map/all_to_all | solution.py:148
  72.1 7.4 %all-to-all-start.1 = ((bf16[32,3,32,128]{3,2,1,0:T(8,128)(2,1)}), bf16[32,3,32,128]{3,2,1,0:T(8,128)(2,1)S(1)}, u32[]{:S(2)}, u32[]{:S(2)}) async-start(bf16[32,3,32,128]{3,2,1,0:T(8,128)(2,1)} %broadcast_in_dim.8), calls=%async_computation.1 | async-start | bytes 1572864 | tf_op jit(solution)/shard_map/all_to_all | solution.py:32
  80.5 26.5 %all-to-all-done.1 = bf16[32,3,32,128]{3,2,1,0:T(8,128)(2,1)S(1)} async-done(((bf16[32,3,32,128]{3,2,1,0:T(8,128)(2,1)}), bf16[32,3,32,128]{3,2,1,0:T(8,128)(2,1)S(1)}, u32[]{:S(2)}, u32[]{:S(2)}) %all-to-all-start.1) | async-done | bytes 786464 | tf_op jit(solution)/shard_map/all_to_all | solution.py:32
  109.1 3.1 %fusion.16 = bf16[32,1024]{1,0:T(8,128)(2,1)S(1)} fusion(bf16[32,64,1024]{2,1,0:T(8,128)(2,1)} %bitcast.217, bf16[32,32,64]{2,1,0:T(8,128)(2,1)} %reshape_reshape.9), kind=kOutput, calls=%fused_computation.27 | convolution fusion | flops 134250496 | bytes 4390912 | tf_op jit(solution)/shard_map/tbf,bfd->td/dot_general | solution.py:158
  112.3 12.2 %all_to_all.44 = bf16[8,32,1024]{2,1,0:T(8,128)(2,1)S(1)} all-to-all(bf16[8,32,1024]{2,1,0:T(8,128)(2,1)S(1)} %broadcast_in_dim.9), channel_id=1, replica_groups=mesh['zslab'=8,'blk'=32] {'zslab'}, dimensions={0} | all-to-all | bytes 1048576 | tf_op jit(solution)/shard_map/all_to_all | solution.py:32
  124.9 23.9 %all_to_all.45 = bf16[32,32,256]{2,1,0:T(8,128)(2,1)S(1)} all-to-all(bf16[32,32,256]{2,1,0:T(8,128)(2,1)S(1)} %broadcast_in_dim.10), channel_id=1, replica_groups=mesh['zslab'=8,'blk'=32] {'blk'}, dimensions={0} | all-to-all | bytes 1048576 | tf_op jit(solution)/shard_map/all_to_all | solution.py:32
  153.9 8.2 %all-to-all-start.4 = ((bf16[32,32,256]{2,1,0:T(8,128)(2,1)}), bf16[32,32,256]{2,1,0:T(8,128)(2,1)}, u32[]{:S(2)}, u32[]{:S(2)}) async-start(bf16[32,32,256]{2,1,0:T(8,128)(2,1)} %pad_maximum_fusion), calls=%async_computation.4 | async-start | bytes 1048576 | tf_op jit(solution)/shard_map/all_to_all | solution.py:73
  162.2 14.4 %all-to-all-done.4 = bf16[32,32,256]{2,1,0:T(8,128)(2,1)} async-done(((bf16[32,32,256]{2,1,0:T(8,128)(2,1)}), bf16[32,32,256]{2,1,0:T(8,128)(2,1)}, u32[]{:S(2)}, u32[]{:S(2)}) %all-to-all-start.4) | async-done | bytes 524320 | tf_op jit(solution)/shard_map/all_to_all | solution.py:73
  178.2 11.9 %all_to_all.46 = bf16[8,32,1024]{2,1,0:T(8,128)(2,1)S(1)} all-to-all(bf16[8,32,1024]{2,1,0:T(8,128)(2,1)S(1)} %broadcast_in_dim.11), channel_id=1, replica_groups=mesh['zslab'=8,'blk'=32] {'zslab'}, dimensions={0} | all-to-all | bytes 1048576 | tf_op jit(solution)/shard_map/all_to_all | solution.py:32
  190.2 4.2 %convolution_convert_fusion = bf16[32,32,64]{2,0,1:T(8,128)(2,1)S(1)} fusion(bf16[32,64,1024]{2,1,0:T(8,128)(2,1)} %bitcast.218, bf16[32,1024]{1,0:T(8,128)(2,1)S(1)} %reduce_sum.58), kind=kOutput, calls=%fused_computation | convolution fusion | flops 134283264 | bytes 4390912 | tf_op jit(solution)/shard_map/td,bfd->tbf/dot_general | solution.py:212
  194.8 8.1 %all_to_all.47 = bf16[1,32,16,128]{3,2,0,1:T(8,128)(2,1)S(1)} all-to-all(bf16[1,32,16,128]{3,2,0,1:T(8,128)(2,1)S(1)} %bitcast.251), channel_id=1, replica_groups=mesh['zslab'=8,'blk'=32] {'zslab'}, dimensions={1} | all-to-all | bytes 262144 | tf_op jit(solution)/shard_map/all_to_all | solution.py:219
  203.0 2.7 %collective-permute-start.8 = (bf16[8,2,16,128]{3,2,1,0:T(8,128)(2,1)S(1)}, bf16[8,2,16,128]{3,2,1,0:T(8,128)(2,1)S(1)}, u32[]{:S(2)}, u32[]{:S(2)}) collective-permute-start(bf16[8,2,16,128]{3,2,1,0:T(8,128)(2,1)S(1)} %get-tuple-element.41), channel_id=1, source_target_pairs={{0,32},{32,64},{64,96},{96,128},{128,160},{160,192},{192,224},{1,3... | collective-permute-start | bytes 196616 | tf_op jit(solution)/shard_map/ppermute | solution.py:21
  211.7 5.8 %collective-permute-start.10 = (bf16[2,8,16,128]{3,2,1,0:T(8,128)(2,1)S(1)}, bf16[2,8,16,128]{3,2,1,0:T(8,128)(2,1)S(1)}, u32[]{:S(2)}, u32[]{:S(2)}) collective-permute-start(bf16[2,8,16,128]{3,2,1,0:T(8,128)(2,1)S(1)} %get-tuple-element.30), channel_id=1, source_target_pairs={{1,0},{2,1},{3,2},{4,3},{5,4},{6,5},{7,6},{8,7},{9,8},{10,9},{11,1... | collective-permute-start | bytes 196616 | tf_op jit(solution)/shard_map/ppermute | solution.py:23
  217.6 5.4 %collective-permute-start.11 = (bf16[2,8,16,128]{3,2,1,0:T(8,128)(2,1)S(1)}, bf16[2,8,16,128]{3,2,1,0:T(8,128)(2,1)S(1)}, u32[]{:S(2)}, u32[]{:S(2)}) collective-permute-start(bf16[2,8,16,128]{3,2,1,0:T(8,128)(2,1)S(1)} %get-tuple-element.29), channel_id=1, source_target_pairs={{0,1},{1,2},{2,3},{3,4},{4,5},{5,6},{6,7},{7,8},{8,9},{9,10},{10,1... | collective-permute-start | bytes 196616 | tf_op jit(solution)/shard_map/ppermute | solution.py:21
  228.7 3.4 %collective-permute-start.13 = (bf16[8,2,16,128]{3,2,1,0:T(8,128)(2,1)S(1)}, bf16[8,2,16,128]{3,2,1,0:T(8,128)(2,1)S(1)}, u32[]{:S(2)}, u32[]{:S(2)}) collective-permute-start(bf16[8,2,16,128]{3,2,1,0:T(8,128)(2,1)S(1)} %get-tuple-element.40), channel_id=1, source_target_pairs={{32,0},{64,32},{96,64},{128,96},{160,128},{192,160},{224,192},{33,... | collective-permute-start | bytes 196616 | tf_op jit(solution)/shard_map/ppermute | solution.py:23
  234.6 3.6 %collective-permute-start.14 = (bf16[2,8,16,128]{3,2,1,0:T(8,128)(2,1)S(1)}, bf16[2,8,16,128]{3,2,1,0:T(8,128)(2,1)S(1)}, u32[]{:S(2)}, u32[]{:S(2)}) collective-permute-start(bf16[2,8,16,128]{3,2,1,0:T(8,128)(2,1)S(1)} %get-tuple-element.26), channel_id=1, source_target_pairs={{1,0},{2,1},{3,2},{4,3},{5,4},{6,5},{7,6},{8,7},{9,8},{10,9},{11,1... | collective-permute-start | bytes 196616 | tf_op jit(solution)/shard_map/ppermute | solution.py:23
  238.2 7.3 %collective-permute-start.15 = (bf16[2,8,16,128]{3,2,1,0:T(8,128)(2,1)S(1)}, bf16[2,8,16,128]{3,2,1,0:T(8,128)(2,1)S(1)}, u32[]{:S(2)}, u32[]{:S(2)}) collective-permute-start(bf16[2,8,16,128]{3,2,1,0:T(8,128)(2,1)S(1)} %get-tuple-element.25), channel_id=1, source_target_pairs={{0,1},{1,2},{2,3},{3,4},{4,5},{5,6},{6,7},{7,8},{8,9},{9,10},{10,1... | collective-permute-start | bytes 196616 | tf_op jit(solution)/shard_map/ppermute | solution.py:21
  (150 shorter events, 49.2 us)
Async XLA Ops:
  6.5 102.5 %all-gather.3.cloned.1.call-start = ((), (), s32[]{:S(2)}) async-start(), calls=%async_computation.7 | async-start | bytes 4325376 | tf_op jit(solution)/shard_map/all_gather | solution.py:79
  7.5 7.7 %collective-permute-start = (bf16[8,2,16,128]{3,2,1,0:T(8,128)(2,1)S(1)}, bf16[8,2,16,128]{3,2,1,0:T(8,128)(2,1)S(1)}, u32[]{:S(2)}, u32[]{:S(2)}) collective-permute-start(bf16[8,2,16,128]{3,2,1,0:T(8,128)(2,1)S(1)} %get-tuple-element.45), channel_id=1, source_target_pairs={{0,32},{32,64},{64,96},{96,128},{128,160},{160,192},{192,224},{1,3... | collective-permute-start | bytes 196616 | tf_op jit(solution)/shard_map/ppermute | solution.py:21
  11.0 5.9 %collective-permute-start.1 = (bf16[8,2,16,128]{3,2,1,0:T(8,128)(2,1)S(1)}, bf16[8,2,16,128]{3,2,1,0:T(8,128)(2,1)S(1)}, u32[]{:S(2)}, u32[]{:S(2)}) collective-permute-start(bf16[8,2,16,128]{3,2,1,0:T(8,128)(2,1)S(1)} %get-tuple-element.46), channel_id=1, source_target_pairs={{32,0},{64,32},{96,64},{128,96},{160,128},{192,160},{224,192},{33,... | collective-permute-start | bytes 196616 | tf_op jit(solution)/shard_map/ppermute | solution.py:23
  14.5 11.6 %copy-start.4 = (s32[2,3]{1,0:T(2,128)S(1)}, s32[2,3]{1,0:T(2,128)}, u32[]{:S(2)}) copy-start(s32[2,3]{1,0:T(2,128)} %param.9) | copy-start | bytes 76
  16.9 11.7 %collective-permute-start.2 = (bf16[2,8,16,128]{3,2,1,0:T(8,128)(2,1)S(1)}, bf16[2,8,16,128]{3,2,1,0:T(8,128)(2,1)S(1)}, u32[]{:S(2)}, u32[]{:S(2)}) collective-permute-start(bf16[2,8,16,128]{3,2,1,0:T(8,128)(2,1)S(1)} %get-tuple-element.38), channel_id=1, source_target_pairs={{0,1},{1,2},{2,3},{3,4},{4,5},{5,6},{6,7},{7,8},{8,9},{9,10},{10,1... | collective-permute-start | bytes 196616 | tf_op jit(solution)/shard_map/ppermute | solution.py:21
  24.2 9.2 %collective-permute-start.3 = (bf16[2,8,16,128]{3,2,1,0:T(8,128)(2,1)S(1)}, bf16[2,8,16,128]{3,2,1,0:T(8,128)(2,1)S(1)}, u32[]{:S(2)}, u32[]{:S(2)}) collective-permute-start(bf16[2,8,16,128]{3,2,1,0:T(8,128)(2,1)S(1)} %get-tuple-element.37), channel_id=1, source_target_pairs={{1,0},{2,1},{3,2},{4,3},{5,4},{6,5},{7,6},{8,7},{9,8},{10,9},{11,1... | collective-permute-start | bytes 196616 | tf_op jit(solution)/shard_map/ppermute | solution.py:23
  36.9 5.3 %collective-permute-start.4 = (bf16[8,2,16,128]{3,2,1,0:T(8,128)(2,1)S(1)}, bf16[8,2,16,128]{3,2,1,0:T(8,128)(2,1)S(1)}, u32[]{:S(2)}, u32[]{:S(2)}) collective-permute-start(bf16[8,2,16,128]{3,2,1,0:T(8,128)(2,1)S(1)} %get-tuple-element.43), channel_id=1, source_target_pairs={{0,32},{32,64},{64,96},{96,128},{128,160},{160,192},{192,224},{1,3... | collective-permute-start | bytes 196616 | tf_op jit(solution)/shard_map/ppermute | solution.py:21
  38.8 6.2 %collective-permute-start.5 = (bf16[8,2,16,128]{3,2,1,0:T(8,128)(2,1)S(1)}, bf16[8,2,16,128]{3,2,1,0:T(8,128)(2,1)S(1)}, u32[]{:S(2)}, u32[]{:S(2)}) collective-permute-start(bf16[8,2,16,128]{3,2,1,0:T(8,128)(2,1)S(1)} %get-tuple-element.44), channel_id=1, source_target_pairs={{32,0},{64,32},{96,64},{128,96},{160,128},{192,160},{224,192},{33,... | collective-permute-start | bytes 196616 | tf_op jit(solution)/shard_map/ppermute | solution.py:23
  45.0 7.8 %collective-permute-start.6 = (bf16[2,8,16,128]{3,2,1,0:T(8,128)(2,1)S(1)}, bf16[2,8,16,128]{3,2,1,0:T(8,128)(2,1)S(1)}, u32[]{:S(2)}, u32[]{:S(2)}) collective-permute-start(bf16[2,8,16,128]{3,2,1,0:T(8,128)(2,1)S(1)} %get-tuple-element.34), channel_id=1, source_target_pairs={{0,1},{1,2},{2,3},{3,4},{4,5},{5,6},{6,7},{7,8},{8,9},{9,10},{10,1... | collective-permute-start | bytes 196616 | tf_op jit(solution)/shard_map/ppermute | solution.py:21
  48.9 9.2 %collective-permute-start.7 = (bf16[2,8,16,128]{3,2,1,0:T(8,128)(2,1)S(1)}, bf16[2,8,16,128]{3,2,1,0:T(8,128)(2,1)S(1)}, u32[]{:S(2)}, u32[]{:S(2)}) collective-permute-start(bf16[2,8,16,128]{3,2,1,0:T(8,128)(2,1)S(1)} %get-tuple-element.33), channel_id=1, source_target_pairs={{1,0},{2,1},{3,2},{4,3},{5,4},{6,5},{7,6},{8,7},{9,8},{10,9},{11,1... | collective-permute-start | bytes 196616 | tf_op jit(solution)/shard_map/ppermute | solution.py:23
  59.7 11.4 %copy-start.2 = (bf16[3,32,128]{2,1,0:T(8,128)(2,1)S(1)}, bf16[3,32,128]{2,1,0:T(8,128)(2,1)}, u32[]{:S(2)}) copy-start(bf16[3,32,128]{2,1,0:T(8,128)(2,1)} %param.12) | copy-start | bytes 73732
  72.1 34.9 %all-to-all-start.1 = ((bf16[32,3,32,128]{3,2,1,0:T(8,128)(2,1)}), bf16[32,3,32,128]{3,2,1,0:T(8,128)(2,1)S(1)}, u32[]{:S(2)}, u32[]{:S(2)}) async-start(bf16[32,3,32,128]{3,2,1,0:T(8,128)(2,1)} %broadcast_in_dim.8), calls=%async_computation.1 | async-start | bytes 1572864 | tf_op jit(solution)/shard_map/all_to_all | solution.py:32
  124.8 24.5 %copy-start.5 = (bf16[32,128]{1,0:T(8,128)(2,1)S(1)}, bf16[32,128]{1,0:T(8,128)(2,1)}, u32[]{:S(2)}) copy-start(bf16[32,128]{1,0:T(8,128)(2,1)} %param.13) | copy-start | bytes 24580
  153.9 22.8 %all-to-all-start.4 = ((bf16[32,32,256]{2,1,0:T(8,128)(2,1)}), bf16[32,32,256]{2,1,0:T(8,128)(2,1)}, u32[]{:S(2)}, u32[]{:S(2)}) async-start(bf16[32,32,256]{2,1,0:T(8,128)(2,1)} %pad_maximum_fusion), calls=%async_computation.4 | async-start | bytes 1048576 | tf_op jit(solution)/shard_map/all_to_all | solution.py:73
  194.4 8.4 %copy-start.1 = (f32[8,4,16,128]{3,2,1,0:T(8,128)S(1)}, f32[8,4,16,128]{3,2,1,0:T(8,128)}, u32[]{:S(2)}) copy-start(f32[8,4,16,128]{3,2,1,0:T(8,128)} %get-tuple-element.60) | copy-start | bytes 786436
  203.0 6.6 %collective-permute-start.8 = (bf16[8,2,16,128]{3,2,1,0:T(8,128)(2,1)S(1)}, bf16[8,2,16,128]{3,2,1,0:T(8,128)(2,1)S(1)}, u32[]{:S(2)}, u32[]{:S(2)}) collective-permute-start(bf16[8,2,16,128]{3,2,1,0:T(8,128)(2,1)S(1)} %get-tuple-element.41), channel_id=1, source_target_pairs={{0,32},{32,64},{64,96},{96,128},{128,160},{160,192},{192,224},{1,3... | collective-permute-start | bytes 196616 | tf_op jit(solution)/shard_map/ppermute | solution.py:21
  205.8 5.9 %collective-permute-start.9 = (bf16[8,2,16,128]{3,2,1,0:T(8,128)(2,1)S(1)}, bf16[8,2,16,128]{3,2,1,0:T(8,128)(2,1)S(1)}, u32[]{:S(2)}, u32[]{:S(2)}) collective-permute-start(bf16[8,2,16,128]{3,2,1,0:T(8,128)(2,1)S(1)} %get-tuple-element.42), channel_id=1, source_target_pairs={{32,0},{64,32},{96,64},{128,96},{160,128},{192,160},{224,192},{33,... | collective-permute-start | bytes 196616 | tf_op jit(solution)/shard_map/ppermute | solution.py:23
  211.7 11.3 %collective-permute-start.10 = (bf16[2,8,16,128]{3,2,1,0:T(8,128)(2,1)S(1)}, bf16[2,8,16,128]{3,2,1,0:T(8,128)(2,1)S(1)}, u32[]{:S(2)}, u32[]{:S(2)}) collective-permute-start(bf16[2,8,16,128]{3,2,1,0:T(8,128)(2,1)S(1)} %get-tuple-element.30), channel_id=1, source_target_pairs={{1,0},{2,1},{3,2},{4,3},{5,4},{6,5},{7,6},{8,7},{9,8},{10,9},{11,1... | collective-permute-start | bytes 196616 | tf_op jit(solution)/shard_map/ppermute | solution.py:23
  217.6 6.6 %collective-permute-start.11 = (bf16[2,8,16,128]{3,2,1,0:T(8,128)(2,1)S(1)}, bf16[2,8,16,128]{3,2,1,0:T(8,128)(2,1)S(1)}, u32[]{:S(2)}, u32[]{:S(2)}) collective-permute-start(bf16[2,8,16,128]{3,2,1,0:T(8,128)(2,1)S(1)} %get-tuple-element.29), channel_id=1, source_target_pairs={{0,1},{1,2},{2,3},{3,4},{4,5},{5,6},{6,7},{7,8},{8,9},{9,10},{10,1... | collective-permute-start | bytes 196616 | tf_op jit(solution)/shard_map/ppermute | solution.py:21
  225.2 1.0 copy-start.6
  226.8 6.6 %collective-permute-start.12 = (bf16[8,2,16,128]{3,2,1,0:T(8,128)(2,1)S(1)}, bf16[8,2,16,128]{3,2,1,0:T(8,128)(2,1)S(1)}, u32[]{:S(2)}, u32[]{:S(2)}) collective-permute-start(bf16[8,2,16,128]{3,2,1,0:T(8,128)(2,1)S(1)} %get-tuple-element.39), channel_id=1, source_target_pairs={{0,32},{32,64},{64,96},{96,128},{128,160},{160,192},{192,224},{1,3... | collective-permute-start | bytes 196616 | tf_op jit(solution)/shard_map/ppermute | solution.py:21
  228.7 5.9 %collective-permute-start.13 = (bf16[8,2,16,128]{3,2,1,0:T(8,128)(2,1)S(1)}, bf16[8,2,16,128]{3,2,1,0:T(8,128)(2,1)S(1)}, u32[]{:S(2)}, u32[]{:S(2)}) collective-permute-start(bf16[8,2,16,128]{3,2,1,0:T(8,128)(2,1)S(1)} %get-tuple-element.40), channel_id=1, source_target_pairs={{32,0},{64,32},{96,64},{128,96},{160,128},{192,160},{224,192},{33,... | collective-permute-start | bytes 196616 | tf_op jit(solution)/shard_map/ppermute | solution.py:23
  234.6 11.0 %collective-permute-start.14 = (bf16[2,8,16,128]{3,2,1,0:T(8,128)(2,1)S(1)}, bf16[2,8,16,128]{3,2,1,0:T(8,128)(2,1)S(1)}, u32[]{:S(2)}, u32[]{:S(2)}) collective-permute-start(bf16[2,8,16,128]{3,2,1,0:T(8,128)(2,1)S(1)} %get-tuple-element.26), channel_id=1, source_target_pairs={{1,0},{2,1},{3,2},{4,3},{5,4},{6,5},{7,6},{8,7},{9,8},{10,9},{11,1... | collective-permute-start | bytes 196616 | tf_op jit(solution)/shard_map/ppermute | solution.py:23
  238.2 8.7 %collective-permute-start.15 = (bf16[2,8,16,128]{3,2,1,0:T(8,128)(2,1)S(1)}, bf16[2,8,16,128]{3,2,1,0:T(8,128)(2,1)S(1)}, u32[]{:S(2)}, u32[]{:S(2)}) collective-permute-start(bf16[2,8,16,128]{3,2,1,0:T(8,128)(2,1)S(1)} %get-tuple-element.25), channel_id=1, source_target_pairs={{0,1},{1,2},{2,3},{3,4},{4,5},{5,6},{6,7},{7,8},{8,9},{9,10},{10,1... | collective-permute-start | bytes 196616 | tf_op jit(solution)/shard_map/ppermute | solution.py:21
  (2 other events, 1.6 us)
Sparse Core Ops, SparseCore 0:
  13.0 95.9 all-gather.2

commit v6 on v3

--- a/solution.py
+++ b/solution.py
@@ -81,8 +81,14 @@
     rows = jnp.concatenate(
         [embed_weight[0], qkv_flat, jnp.zeros((extra, width), qkv_flat.dtype)], axis=0
     )
-    gathered = lax.all_gather(rows, "blk", axis=0, tiled=True)
     peers = lax.axis_size("blk")
+    groups = [list(range(core, peers, 2)) for core in (0, 1)]
+    own = lax.all_gather(rows, "blk", axis=0, tiled=True, axis_index_groups=groups)
+    other = lax.ppermute(own, "blk", [(i, i ^ 1) for i in range(peers)])
+    odd = (lax.axis_index("blk") & 1) != 0
+    own = own.reshape(peers // 2, rows.shape[0], width)
+    other = other.reshape(peers // 2, rows.shape[0], width)
+    gathered = jnp.stack([jnp.where(odd, other, own), jnp.where(odd, own, other)], axis=1)
     gathered = gathered.reshape(peers, rows.shape[0], width)
     embed_rows = gathered[:, :feat, :]
     qkv_rows = gathered[:, feat : feat + qkv_flat.shape[0], :].reshape(peers, *qkv_weight.shape)

time: 256 us -> 279 us (1.090)
  waiting for transfers between devices: 67.3 us -> 86.1 us
  starting transfers between devices: 71.9 us -> 81.6 us
  blocking collectives: 53.7 us -> 44.6 us
  other arithmetic: 6.95 us -> 11 us
  local copies, waits for them, and re-layouts: 16.2 us -> 19.7 us
    all_gather x1, waiting for transfers between devices: 28 us -> 47 us  [gather_weights(): lax.all_gather(rows, 'blk', axis=0, tiled=True, axis_index_groups=groups)]
    all_to_all x1 -> x0, blocking collectives: 10.3 us -> none  [local(): lax.all_to_all(hidden, 'zslab', split_axis=0, concat_axis=1, tiled=True)]
    ppermute x8, starting transfers between devices: 34 us -> 41.3 us  [padded_2(): lax.ppermute(tail, axis, [(i, (i + 1) % count) for i in range(ends)])]
    ppermute x8, starting transfers between devices: 24.5 us -> 18.1 us  [padded_2(): lax.ppermute(head, axis, [((i + 1) % count, i) for i in range(ends)])]
    all_to_all x0 -> x1, starting transfers between devices: none -> 5.19 us  [local(): lax.all_to_all(hidden, 'zslab', split_axis=0, concat_axis=1, tiled=True)]
    all_to_all x0 -> x1, waiting for transfers between devices: none -> 4.84 us  [local(): lax.all_to_all(hidden, 'zslab', split_axis=0, concat_axis=1, tiled=True)]
    ppermute x0 -> x1, starting transfers between devices: none -> 4.63 us  [gather_weights(): other = lax.ppermute(own, 'blk', [(i, i ^ 1) for i in range(peers)])]
    ppermute x8, waiting for transfers between devices: 17.8 us -> 14.4 us  [padded_2(): lax.ppermute(head, axis, [((i + 1) % count, i) for i in range(ends)])]
  transfers between devices with their start and end apart: 19 -> 21, of which waited for: 12 -> 8; matrix products, arithmetic and copies ran while one was open for 6% -> 7% of each run, Pallas kernels for 0% -> 0%
where the time goes in v6:
time: 279 us; the launch traced here: 276 us
  waiting for transfers between devices  86.1 us (31%)
  starting transfers between devices  81.6 us (29%)
  blocking collectives  44.6 us (16%)
  local copies, waits for them, and re-layouts  19.7 us (7%)
  between operations  18.1 us (6%)
  matrix products  15.3 us (5%)
  other arithmetic  11 us (4%)
    all_gather x1, waiting for transfers between devices, gather_weights(): lax.all_gather(rows, 'blk', axis=0, tiled=True, axis_index_groups=groups)  47 us
    ppermute x8, starting transfers between devices, padded_2(): lax.ppermute(tail, axis, [(i, (i + 1) % count) for i in range(ends)])  41.3 us
    all_to_all x2, blocking collectives, copy_for_each(): lax.all_to_all(jnp.broadcast_to(shard[None], (peers, *shard.shape)), axis...  36.5 us
    ppermute x8, starting transfers between devices, padded_2(): lax.ppermute(head, axis, [((i + 1) % count, i) for i in range(ends)])  18.1 us
    all_to_all x1, waiting for transfers between devices, sum_at_owner(): lax.all_to_all(cut_along(shard, dim, peers), axis, 0, 0, tiled=True)  14.4 us
    ppermute x8, waiting for transfers between devices, padded_2(): lax.ppermute(head, axis, [((i + 1) % count, i) for i in range(ends)])  14.4 us
    all_to_all x1, starting transfers between devices, sum_at_owner(): lax.all_to_all(cut_along(shard, dim, peers), axis, 0, 0, tiled=True)  8.23 us
    all_to_all x1, blocking collectives, local(): lax.all_to_all(grid_grad, 'zslab', split_axis=1, concat_axis=0, tiled=True)  8.09 us
  transfers between devices with their start and end apart: 21, of which 8 were waited for; matrix products, arithmetic and copies ran while one was open for 7% of the time, Pallas kernels for 0%

profile of v6, /device:TPU:103, one launch (start us, length us, event | category | flops | bytes accessed | tf_op | source)
XLA Modules:
  0.0 276.5 jit_solution(17716939208877578658)
XLA Ops:
  9.9 3.7 %collective-permute-start.1 = (bf16[8,2,16,128]{3,2,1,0:T(8,128)(2,1)S(1)}, bf16[8,2,16,128]{3,2,1,0:T(8,128)(2,1)S(1)}, u32[]{:S(2)}, u32[]{:S(2)}) collective-permute-start(bf16[8,2,16,128]{3,2,1,0:T(8,128)(2,1)S(1)} %get-tuple-element.43), channel_id=1, source_target_pairs={{0,32},{32,64},{64,96},{96,128},{128,160},{160,192},{192,224},{1,3... | collective-permute-start | bytes 196616 | tf_op jit(solution)/shard_map/ppermute | solution.py:21
  18.6 3.1 %collective-permute-start.4 = (bf16[2,8,16,128]{3,2,1,0:T(8,128)(2,1)S(1)}, bf16[2,8,16,128]{3,2,1,0:T(8,128)(2,1)S(1)}, u32[]{:S(2)}, u32[]{:S(2)}) collective-permute-start(bf16[2,8,16,128]{3,2,1,0:T(8,128)(2,1)S(1)} %get-tuple-element.35), channel_id=1, source_target_pairs={{1,0},{2,1},{3,2},{4,3},{5,4},{6,5},{7,6},{8,7},{9,8},{10,9},{11,1... | collective-permute-start | bytes 196616 | tf_op jit(solution)/shard_map/ppermute | solution.py:23
  21.7 6.0 %collective-permute-start.3 = (bf16[2,8,16,128]{3,2,1,0:T(8,128)(2,1)S(1)}, bf16[2,8,16,128]{3,2,1,0:T(8,128)(2,1)S(1)}, u32[]{:S(2)}, u32[]{:S(2)}) collective-permute-start(bf16[2,8,16,128]{3,2,1,0:T(8,128)(2,1)S(1)} %get-tuple-element.36), channel_id=1, source_target_pairs={{0,1},{1,2},{2,3},{3,4},{4,5},{5,6},{6,7},{7,8},{8,9},{9,10},{10,1... | collective-permute-start | bytes 196616 | tf_op jit(solution)/shard_map/ppermute | solution.py:21
  35.7 4.3 %collective-permute-start.5 = (bf16[8,2,16,128]{3,2,1,0:T(8,128)(2,1)S(1)}, bf16[8,2,16,128]{3,2,1,0:T(8,128)(2,1)S(1)}, u32[]{:S(2)}, u32[]{:S(2)}) collective-permute-start(bf16[8,2,16,128]{3,2,1,0:T(8,128)(2,1)S(1)} %get-tuple-element.41), channel_id=1, source_target_pairs={{0,32},{32,64},{64,96},{96,128},{128,160},{160,192},{192,224},{1,3... | collective-permute-start | bytes 196616 | tf_op jit(solution)/shard_map/ppermute | solution.py:21
  43.4 7.6 %collective-permute-start.7 = (bf16[2,8,16,128]{3,2,1,0:T(8,128)(2,1)S(1)}, bf16[2,8,16,128]{3,2,1,0:T(8,128)(2,1)S(1)}, u32[]{:S(2)}, u32[]{:S(2)}) collective-permute-start(bf16[2,8,16,128]{3,2,1,0:T(8,128)(2,1)S(1)} %get-tuple-element.32), channel_id=1, source_target_pairs={{0,1},{1,2},{2,3},{3,4},{4,5},{5,6},{6,7},{7,8},{8,9},{9,10},{10,1... | collective-permute-start | bytes 196616 | tf_op jit(solution)/shard_map/ppermute | solution.py:21
  54.8 47.0 %all-gather.2.cloned.1.call-done = bf16[1280,1024]{1,0:T(8,128)(2,1)} async-done(((bf16[80,1024]{1,0:T(8,128)(2,1)}), bf16[1280,1024]{1,0:T(8,128)(2,1)}) %all-gather.2.cloned.1.call-update) | async-done | bytes 2621456 | tf_op jit(solution)/shard_map/all_gather | solution.py:86
  101.8 4.6 %collective-permute-start = (bf16[1280,1024]{1,0:T(8,128)(2,1)}, bf16[1280,1024]{1,0:T(8,128)(2,1)}, u32[]{:S(2)}, u32[]{:S(2)}) collective-permute-start(bf16[1280,1024]{1,0:T(8,128)(2,1)} %all-gather.2.cloned.1.call-done), channel_id=1, source_target_pairs={{0,1},{1,0},{2,3},{3,2},{4,5},{5,4},{6,7},{7,6},{8,9},{9,8},{10,11... | collective-permute-start | bytes 7864328 | tf_op jit(solution)/shard_map/ppermute | solution.py:87
  110.3 5.2 %all-to-all-start = ((bf16[8,4,16,128]{3,2,1,0:T(8,128)(2,1)}), bf16[8,4,16,128]{3,2,1,0:T(8,128)(2,1)S(1)}, u32[]{:S(2)}, u32[]{:S(2)}) async-start(bf16[8,4,16,128]{3,2,1,0:T(8,128)(2,1)} %get-tuple-element.57), calls=%async_computation | async-start | bytes 262144 | tf_op jit(solution)/shard_map/all_to_all | solution.py:163
  115.5 4.8 %all-to-all-done = bf16[8,4,16,128]{3,2,1,0:T(8,128)(2,1)S(1)} async-done(((bf16[8,4,16,128]{3,2,1,0:T(8,128)(2,1)}), bf16[8,4,16,128]{3,2,1,0:T(8,128)(2,1)S(1)}, u32[]{:S(2)}, u32[]{:S(2)}) %all-to-all-start) | async-done | bytes 131104 | tf_op jit(solution)/shard_map/all_to_all | solution.py:163
  127.1 4.2 %all-to-all-start.1 = ((bf16[8,32,1024]{2,1,0:T(8,128)(2,1)}), bf16[8,32,1024]{2,1,0:T(8,128)(2,1)S(1)}, u32[]{:S(2)}, u32[]{:S(2)}) async-start(bf16[8,32,1024]{2,1,0:T(8,128)(2,1)} %broadcast_in_dim.9), calls=%async_computation.1 | async-start | bytes 1048576 | tf_op jit(solution)/shard_map/all_to_all | solution.py:32
  135.3 3.6 %all-to-all-done.1 = bf16[8,32,1024]{2,1,0:T(8,128)(2,1)S(1)} async-done(((bf16[8,32,1024]{2,1,0:T(8,128)(2,1)}), bf16[8,32,1024]{2,1,0:T(8,128)(2,1)S(1)}, u32[]{:S(2)}, u32[]{:S(2)}) %all-to-all-start.1) | async-done | bytes 524320 | tf_op jit(solution)/shard_map/all_to_all | solution.py:32
  139.3 24.5 %all_to_all.38 = bf16[32,32,256]{2,1,0:T(8,128)(2,1)S(1)} all-to-all(bf16[32,32,256]{2,1,0:T(8,128)(2,1)S(1)} %broadcast_in_dim.10), channel_id=1, replica_groups=mesh['zslab'=8,'blk'=32] {'blk'}, dimensions={0} | all-to-all | bytes 1048576 | tf_op jit(solution)/shard_map/all_to_all | solution.py:32
  168.9 8.2 %all-to-all-start.3 = ((bf16[32,32,256]{2,1,0:T(8,128)(2,1)}), bf16[32,32,256]{2,1,0:T(8,128)(2,1)}, u32[]{:S(2)}, u32[]{:S(2)}) async-start(bf16[32,32,256]{2,1,0:T(8,128)(2,1)} %pad_maximum_fusion.1), calls=%async_computation.3 | async-start | bytes 1048576 | tf_op jit(solution)/shard_map/all_to_all | solution.py:73
  177.3 14.4 %all-to-all-done.3 = bf16[32,32,256]{2,1,0:T(8,128)(2,1)} async-done(((bf16[32,32,256]{2,1,0:T(8,128)(2,1)}), bf16[32,32,256]{2,1,0:T(8,128)(2,1)}, u32[]{:S(2)}, u32[]{:S(2)}) %all-to-all-start.3) | async-done | bytes 524320 | tf_op jit(solution)/shard_map/all_to_all | solution.py:73
  193.3 12.0 %all_to_all.39 = bf16[8,32,1024]{2,1,0:T(8,128)(2,1)S(1)} all-to-all(bf16[8,32,1024]{2,1,0:T(8,128)(2,1)S(1)} %broadcast_in_dim.11), channel_id=1, replica_groups=mesh['zslab'=8,'blk'=32] {'zslab'}, dimensions={0} | all-to-all | bytes 1048576 | tf_op jit(solution)/shard_map/all_to_all | solution.py:32
  205.3 4.2 %fusion.4 = bf16[32,32,64]{2,0,1:T(8,128)(2,1)S(1)} fusion(bf16[32,80,1024]{2,1,0:T(8,128)(2,1)} %bitcast.229, bf16[32,1024]{1,0:T(8,128)(2,1)S(1)} %reduce_sum.58), kind=kOutput, calls=%fused_computation.7 | convolution fusion | flops 134283264 | bytes 4390912 | tf_op jit(solution)/shard_map/td,bfd->tbf/dot_general | solution.py:226
  209.8 8.1 %all_to_all.40 = bf16[1,32,16,128]{3,2,0,1:T(8,128)(2,1)S(1)} all-to-all(bf16[1,32,16,128]{3,2,0,1:T(8,128)(2,1)S(1)} %bitcast.259), channel_id=1, replica_groups=mesh['zslab'=8,'blk'=32] {'zslab'}, dimensions={1} | all-to-all | bytes 262144 | tf_op jit(solution)/shard_map/all_to_all | solution.py:233
  218.1 2.9 %collective-permute-start.10 = (bf16[8,2,16,128]{3,2,1,0:T(8,128)(2,1)S(1)}, bf16[8,2,16,128]{3,2,1,0:T(8,128)(2,1)S(1)}, u32[]{:S(2)}, u32[]{:S(2)}) collective-permute-start(bf16[8,2,16,128]{3,2,1,0:T(8,128)(2,1)S(1)} %get-tuple-element.40), channel_id=1, source_target_pairs={{32,0},{64,32},{96,64},{128,96},{160,128},{192,160},{224,192},{33,... | collective-permute-start | bytes 196616 | tf_op jit(solution)/shard_map/ppermute | solution.py:23
  221.0 3.3 %collective-permute-start.9 = (bf16[8,2,16,128]{3,2,1,0:T(8,128)(2,1)S(1)}, bf16[8,2,16,128]{3,2,1,0:T(8,128)(2,1)S(1)}, u32[]{:S(2)}, u32[]{:S(2)}) collective-permute-start(bf16[8,2,16,128]{3,2,1,0:T(8,128)(2,1)S(1)} %get-tuple-element.39), channel_id=1, source_target_pairs={{0,32},{32,64},{64,96},{96,128},{128,160},{160,192},{192,224},{1,3... | collective-permute-start | bytes 196616 | tf_op jit(solution)/shard_map/ppermute | solution.py:21
  226.1 9.2 %collective-permute-start.12 = (bf16[2,8,16,128]{3,2,1,0:T(8,128)(2,1)S(1)}, bf16[2,8,16,128]{3,2,1,0:T(8,128)(2,1)S(1)}, u32[]{:S(2)}, u32[]{:S(2)}) collective-permute-start(bf16[2,8,16,128]{3,2,1,0:T(8,128)(2,1)S(1)} %get-tuple-element.27), channel_id=1, source_target_pairs={{0,1},{1,2},{2,3},{3,4},{4,5},{5,6},{6,7},{7,8},{8,9},{9,10},{10,1... | collective-permute-start | bytes 196616 | tf_op jit(solution)/shard_map/ppermute | solution.py:21
  237.3 7.2 %collective-permute-done.11 = bf16[2,8,16,128]{3,2,1,0:T(8,128)(2,1)S(1)} collective-permute-done((bf16[2,8,16,128]{3,2,1,0:T(8,128)(2,1)S(1)}, bf16[2,8,16,128]{3,2,1,0:T(8,128)(2,1)S(1)}, u32[]{:S(2)}, u32[]{:S(2)}) %collective-permute-start.11) | collective-permute-done | bytes 65568 | tf_op jit(solution)/shard_map/ppermute | solution.py:23
  249.0 4.3 %collective-permute-start.13 = (bf16[8,2,16,128]{3,2,1,0:T(8,128)(2,1)S(1)}, bf16[8,2,16,128]{3,2,1,0:T(8,128)(2,1)S(1)}, u32[]{:S(2)}, u32[]{:S(2)}) collective-permute-start(bf16[8,2,16,128]{3,2,1,0:T(8,128)(2,1)S(1)} %get-tuple-element.37), channel_id=1, source_target_pairs={{0,32},{32,64},{64,96},{96,128},{128,160},{160,192},{192,224},{1,3... | collective-permute-start | bytes 196616 | tf_op jit(solution)/shard_map/ppermute | solution.py:21
  254.6 3.0 %collective-permute-start.16 = (bf16[2,8,16,128]{3,2,1,0:T(8,128)(2,1)S(1)}, bf16[2,8,16,128]{3,2,1,0:T(8,128)(2,1)S(1)}, u32[]{:S(2)}, u32[]{:S(2)}) collective-permute-start(bf16[2,8,16,128]{3,2,1,0:T(8,128)(2,1)S(1)} %get-tuple-element.23), channel_id=1, source_target_pairs={{0,1},{1,2},{2,3},{3,4},{4,5},{5,6},{6,7},{7,8},{8,9},{9,10},{10,1... | collective-permute-start | bytes 196616 | tf_op jit(solution)/shard_map/ppermute | solution.py:21
  259.6 7.2 %collective-permute-done.15 = bf16[2,8,16,128]{3,2,1,0:T(8,128)(2,1)S(1)} collective-permute-done((bf16[2,8,16,128]{3,2,1,0:T(8,128)(2,1)S(1)}, bf16[2,8,16,128]{3,2,1,0:T(8,128)(2,1)S(1)}, u32[]{:S(2)}, u32[]{:S(2)}) %collective-permute-start.15) | collective-permute-done | bytes 65568 | tf_op jit(solution)/shard_map/ppermute | solution.py:23
  (167 shorter events, 55.8 us)
Async XLA Ops:
  6.5 95.2 %all-gather.2.cloned.1.call-start = ((), (), s32[]{:S(2)}) async-start(), calls=%async_computation.6 | async-start | bytes 2785280 | tf_op jit(solution)/shard_map/all_gather | solution.py:86
  7.5 11.0 %collective-permute-start.2 = (bf16[8,2,16,128]{3,2,1,0:T(8,128)(2,1)S(1)}, bf16[8,2,16,128]{3,2,1,0:T(8,128)(2,1)S(1)}, u32[]{:S(2)}, u32[]{:S(2)}) collective-permute-start(bf16[8,2,16,128]{3,2,1,0:T(8,128)(2,1)S(1)} %get-tuple-element.44), channel_id=1, source_target_pairs={{32,0},{64,32},{96,64},{128,96},{160,128},{192,160},{224,192},{33,... | collective-permute-start | bytes 196616 | tf_op jit(solution)/shard_map/ppermute | solution.py:23
  9.9 8.6 %collective-permute-start.1 = (bf16[8,2,16,128]{3,2,1,0:T(8,128)(2,1)S(1)}, bf16[8,2,16,128]{3,2,1,0:T(8,128)(2,1)S(1)}, u32[]{:S(2)}, u32[]{:S(2)}) collective-permute-start(bf16[8,2,16,128]{3,2,1,0:T(8,128)(2,1)S(1)} %get-tuple-element.43), channel_id=1, source_target_pairs={{0,32},{32,64},{64,96},{96,128},{128,160},{160,192},{192,224},{1,3... | collective-permute-start | bytes 196616 | tf_op jit(solution)/shard_map/ppermute | solution.py:21
  17.8 9.9 %copy-start.8 = (s32[2,3]{1,0:T(2,128)S(1)}, s32[2,3]{1,0:T(2,128)}, u32[]{:S(2)}) copy-start(s32[2,3]{1,0:T(2,128)} %param.9) | copy-start | bytes 76
  18.6 11.7 %collective-permute-start.4 = (bf16[2,8,16,128]{3,2,1,0:T(8,128)(2,1)S(1)}, bf16[2,8,16,128]{3,2,1,0:T(8,128)(2,1)S(1)}, u32[]{:S(2)}, u32[]{:S(2)}) collective-permute-start(bf16[2,8,16,128]{3,2,1,0:T(8,128)(2,1)S(1)} %get-tuple-element.35), channel_id=1, source_target_pairs={{1,0},{2,1},{3,2},{4,3},{5,4},{6,5},{7,6},{8,7},{9,8},{10,9},{11,1... | collective-permute-start | bytes 196616 | tf_op jit(solution)/shard_map/ppermute | solution.py:23
  21.7 8.6 %collective-permute-start.3 = (bf16[2,8,16,128]{3,2,1,0:T(8,128)(2,1)S(1)}, bf16[2,8,16,128]{3,2,1,0:T(8,128)(2,1)S(1)}, u32[]{:S(2)}, u32[]{:S(2)}) collective-permute-start(bf16[2,8,16,128]{3,2,1,0:T(8,128)(2,1)S(1)} %get-tuple-element.36), channel_id=1, source_target_pairs={{0,1},{1,2},{2,3},{3,4},{4,5},{5,6},{6,7},{7,8},{8,9},{9,10},{10,1... | collective-permute-start | bytes 196616 | tf_op jit(solution)/shard_map/ppermute | solution.py:21
  33.8 6.2 %collective-permute-start.6 = (bf16[8,2,16,128]{3,2,1,0:T(8,128)(2,1)S(1)}, bf16[8,2,16,128]{3,2,1,0:T(8,128)(2,1)S(1)}, u32[]{:S(2)}, u32[]{:S(2)}) collective-permute-start(bf16[8,2,16,128]{3,2,1,0:T(8,128)(2,1)S(1)} %get-tuple-element.42), channel_id=1, source_target_pairs={{32,0},{64,32},{96,64},{128,96},{160,128},{192,160},{224,192},{33,... | collective-permute-start | bytes 196616 | tf_op jit(solution)/shard_map/ppermute | solution.py:23
  35.7 5.7 %collective-permute-start.5 = (bf16[8,2,16,128]{3,2,1,0:T(8,128)(2,1)S(1)}, bf16[8,2,16,128]{3,2,1,0:T(8,128)(2,1)S(1)}, u32[]{:S(2)}, u32[]{:S(2)}) collective-permute-start(bf16[8,2,16,128]{3,2,1,0:T(8,128)(2,1)S(1)} %get-tuple-element.41), channel_id=1, source_target_pairs={{0,32},{32,64},{64,96},{96,128},{128,160},{160,192},{192,224},{1,3... | collective-permute-start | bytes 196616 | tf_op jit(solution)/shard_map/ppermute | solution.py:21
  41.5 12.4 %collective-permute-start.8 = (bf16[2,8,16,128]{3,2,1,0:T(8,128)(2,1)S(1)}, bf16[2,8,16,128]{3,2,1,0:T(8,128)(2,1)S(1)}, u32[]{:S(2)}, u32[]{:S(2)}) collective-permute-start(bf16[2,8,16,128]{3,2,1,0:T(8,128)(2,1)S(1)} %get-tuple-element.31), channel_id=1, source_target_pairs={{1,0},{2,1},{3,2},{4,3},{5,4},{6,5},{7,6},{8,7},{9,8},{10,9},{11,1... | collective-permute-start | bytes 196616 | tf_op jit(solution)/shard_map/ppermute | solution.py:23
  43.4 10.4 %collective-permute-start.7 = (bf16[2,8,16,128]{3,2,1,0:T(8,128)(2,1)S(1)}, bf16[2,8,16,128]{3,2,1,0:T(8,128)(2,1)S(1)}, u32[]{:S(2)}, u32[]{:S(2)}) collective-permute-start(bf16[2,8,16,128]{3,2,1,0:T(8,128)(2,1)S(1)} %get-tuple-element.32), channel_id=1, source_target_pairs={{0,1},{1,2},{2,3},{3,4},{4,5},{5,6},{6,7},{7,8},{8,9},{9,10},{10,1... | collective-permute-start | bytes 196616 | tf_op jit(solution)/shard_map/ppermute | solution.py:21
  101.8 18.8 %collective-permute-start = (bf16[1280,1024]{1,0:T(8,128)(2,1)}, bf16[1280,1024]{1,0:T(8,128)(2,1)}, u32[]{:S(2)}, u32[]{:S(2)}) collective-permute-start(bf16[1280,1024]{1,0:T(8,128)(2,1)} %all-gather.2.cloned.1.call-done), channel_id=1, source_target_pairs={{0,1},{1,0},{2,3},{3,2},{4,5},{5,4},{6,7},{7,6},{8,9},{9,8},{10,11... | collective-permute-start | bytes 7864328 | tf_op jit(solution)/shard_map/ppermute | solution.py:87
  110.3 10.0 %all-to-all-start = ((bf16[8,4,16,128]{3,2,1,0:T(8,128)(2,1)}), bf16[8,4,16,128]{3,2,1,0:T(8,128)(2,1)S(1)}, u32[]{:S(2)}, u32[]{:S(2)}) async-start(bf16[8,4,16,128]{3,2,1,0:T(8,128)(2,1)} %get-tuple-element.57), calls=%async_computation | async-start | bytes 262144 | tf_op jit(solution)/shard_map/all_to_all | solution.py:163
  127.1 11.7 %all-to-all-start.1 = ((bf16[8,32,1024]{2,1,0:T(8,128)(2,1)}), bf16[8,32,1024]{2,1,0:T(8,128)(2,1)S(1)}, u32[]{:S(2)}, u32[]{:S(2)}) async-start(bf16[8,32,1024]{2,1,0:T(8,128)(2,1)} %broadcast_in_dim.9), calls=%async_computation.1 | async-start | bytes 1048576 | tf_op jit(solution)/shard_map/all_to_all | solution.py:32
  139.2 25.1 %copy-start.9 = (bf16[32,128]{1,0:T(8,128)(2,1)S(1)}, bf16[32,128]{1,0:T(8,128)(2,1)}, u32[]{:S(2)}) copy-start(bf16[32,128]{1,0:T(8,128)(2,1)} %param.13) | copy-start | bytes 24580
  168.9 22.8 %all-to-all-start.3 = ((bf16[32,32,256]{2,1,0:T(8,128)(2,1)}), bf16[32,32,256]{2,1,0:T(8,128)(2,1)}, u32[]{:S(2)}, u32[]{:S(2)}) async-start(bf16[32,32,256]{2,1,0:T(8,128)(2,1)} %pad_maximum_fusion.1), calls=%async_computation.3 | async-start | bytes 1048576 | tf_op jit(solution)/shard_map/all_to_all | solution.py:73
  209.5 8.4 %copy-start.6 = (f32[8,4,16,128]{3,2,1,0:T(8,128)S(1)}, f32[8,4,16,128]{3,2,1,0:T(8,128)}, u32[]{:S(2)}) copy-start(f32[8,4,16,128]{3,2,1,0:T(8,128)} %get-tuple-element.58) | copy-start | bytes 786436
  218.1 7.5 %collective-permute-start.10 = (bf16[8,2,16,128]{3,2,1,0:T(8,128)(2,1)S(1)}, bf16[8,2,16,128]{3,2,1,0:T(8,128)(2,1)S(1)}, u32[]{:S(2)}, u32[]{:S(2)}) collective-permute-start(bf16[8,2,16,128]{3,2,1,0:T(8,128)(2,1)S(1)} %get-tuple-element.40), channel_id=1, source_target_pairs={{32,0},{64,32},{96,64},{128,96},{160,128},{192,160},{224,192},{33,... | collective-permute-start | bytes 196616 | tf_op jit(solution)/shard_map/ppermute | solution.py:23
  221.0 5.0 %collective-permute-start.9 = (bf16[8,2,16,128]{3,2,1,0:T(8,128)(2,1)S(1)}, bf16[8,2,16,128]{3,2,1,0:T(8,128)(2,1)S(1)}, u32[]{:S(2)}, u32[]{:S(2)}) collective-permute-start(bf16[8,2,16,128]{3,2,1,0:T(8,128)(2,1)S(1)} %get-tuple-element.39), channel_id=1, source_target_pairs={{0,32},{32,64},{64,96},{96,128},{128,160},{160,192},{192,224},{1,3... | collective-permute-start | bytes 196616 | tf_op jit(solution)/shard_map/ppermute | solution.py:21
  226.1 11.2 %collective-permute-start.12 = (bf16[2,8,16,128]{3,2,1,0:T(8,128)(2,1)S(1)}, bf16[2,8,16,128]{3,2,1,0:T(8,128)(2,1)S(1)}, u32[]{:S(2)}, u32[]{:S(2)}) collective-permute-start(bf16[2,8,16,128]{3,2,1,0:T(8,128)(2,1)S(1)} %get-tuple-element.27), channel_id=1, source_target_pairs={{0,1},{1,2},{2,3},{3,4},{4,5},{5,6},{6,7},{7,8},{8,9},{9,10},{10,1... | collective-permute-start | bytes 196616 | tf_op jit(solution)/shard_map/ppermute | solution.py:21
  235.2 9.2 %collective-permute-start.11 = (bf16[2,8,16,128]{3,2,1,0:T(8,128)(2,1)S(1)}, bf16[2,8,16,128]{3,2,1,0:T(8,128)(2,1)S(1)}, u32[]{:S(2)}, u32[]{:S(2)}) collective-permute-start(bf16[2,8,16,128]{3,2,1,0:T(8,128)(2,1)S(1)} %get-tuple-element.28), channel_id=1, source_target_pairs={{1,0},{2,1},{3,2},{4,3},{5,4},{6,5},{7,6},{8,7},{9,8},{10,9},{11,1... | collective-permute-start | bytes 196616 | tf_op jit(solution)/shard_map/ppermute | solution.py:23
  247.1 7.5 %collective-permute-start.14 = (bf16[8,2,16,128]{3,2,1,0:T(8,128)(2,1)S(1)}, bf16[8,2,16,128]{3,2,1,0:T(8,128)(2,1)S(1)}, u32[]{:S(2)}, u32[]{:S(2)}) collective-permute-start(bf16[8,2,16,128]{3,2,1,0:T(8,128)(2,1)S(1)} %get-tuple-element.38), channel_id=1, source_target_pairs={{32,0},{64,32},{96,64},{128,96},{160,128},{192,160},{224,192},{33,... | collective-permute-start | bytes 196616 | tf_op jit(solution)/shard_map/ppermute | solution.py:23
  249.0 5.6 %collective-permute-start.13 = (bf16[8,2,16,128]{3,2,1,0:T(8,128)(2,1)S(1)}, bf16[8,2,16,128]{3,2,1,0:T(8,128)(2,1)S(1)}, u32[]{:S(2)}, u32[]{:S(2)}) collective-permute-start(bf16[8,2,16,128]{3,2,1,0:T(8,128)(2,1)S(1)} %get-tuple-element.37), channel_id=1, source_target_pairs={{0,32},{32,64},{64,96},{96,128},{128,160},{160,192},{192,224},{1,3... | collective-permute-start | bytes 196616 | tf_op jit(solution)/shard_map/ppermute | solution.py:21
  254.6 5.0 %collective-permute-start.16 = (bf16[2,8,16,128]{3,2,1,0:T(8,128)(2,1)S(1)}, bf16[2,8,16,128]{3,2,1,0:T(8,128)(2,1)S(1)}, u32[]{:S(2)}, u32[]{:S(2)}) collective-permute-start(bf16[2,8,16,128]{3,2,1,0:T(8,128)(2,1)S(1)} %get-tuple-element.23), channel_id=1, source_target_pairs={{0,1},{1,2},{2,3},{3,4},{4,5},{5,6},{6,7},{7,8},{8,9},{9,10},{10,1... | collective-permute-start | bytes 196616 | tf_op jit(solution)/shard_map/ppermute | solution.py:21
  257.6 9.2 %collective-permute-start.15 = (bf16[2,8,16,128]{3,2,1,0:T(8,128)(2,1)S(1)}, bf16[2,8,16,128]{3,2,1,0:T(8,128)(2,1)S(1)}, u32[]{:S(2)}, u32[]{:S(2)}) collective-permute-start(bf16[2,8,16,128]{3,2,1,0:T(8,128)(2,1)S(1)} %get-tuple-element.24), channel_id=1, source_target_pairs={{1,0},{2,1},{3,2},{4,3},{5,4},{6,5},{7,6},{8,7},{9,8},{10,9},{11,1... | collective-permute-start | bytes 196616 | tf_op jit(solution)/shard_map/ppermute | solution.py:23
  (8 other events, 12.7 us)
Sparse Core Ops, SparseCore 0:
  16.4 85.3 all-gather.1

commit v7 on v3

--- a/solution.py
+++ b/solution.py
@@ -81,8 +81,11 @@
     rows = jnp.concatenate(
         [embed_weight[0], qkv_flat, jnp.zeros((extra, width), qkv_flat.dtype)], axis=0
     )
-    gathered = lax.all_gather(rows, "blk", axis=0, tiled=True)
     peers = lax.axis_size("blk")
+    near = [list(range(start, start + 4)) for start in range(0, peers, 4)]
+    far = [list(range(start, peers, 4)) for start in range(4)]
+    gathered = lax.all_gather(rows, "blk", axis=0, tiled=True, axis_index_groups=near)
+    gathered = lax.all_gather(gathered, "blk", axis=0, tiled=True, axis_index_groups=far)
     gathered = gathered.reshape(peers, rows.shape[0], width)
     embed_rows = gathered[:, :feat, :]
     qkv_rows = gathered[:, feat : feat + qkv_flat.shape[0], :].reshape(peers, *qkv_weight.shape)

time: 256 us -> 239 us (0.934)
  waiting for transfers between devices: 67.3 us -> 43.7 us
  blocking collectives: 53.7 us -> 64.7 us
    all_gather x1, waiting for transfers between devices: 28 us -> 0.75 us  [gather_weights(): lax.all_gather(gathered, 'blk', axis=0, tiled=True, axis_index_groups=far)]
    all_gather x0 -> x1, blocking collectives: none -> 9.96 us  [gather_weights(): lax.all_gather(rows, 'blk', axis=0, tiled=True, axis_index_groups=near)]
    ppermute x8, waiting for transfers between devices: 17.8 us -> 22 us  [padded_2(): lax.ppermute(head, axis, [((i + 1) % count, i) for i in range(ends)])]
where the time goes in v7:
time: 239 us; the launch traced here: 235 us
  starting transfers between devices  70.5 us (29%)
  blocking collectives  64.7 us (27%)
  waiting for transfers between devices  43.7 us (18%)
  between operations  18.1 us (8%)
  matrix products  17.4 us (7%)
  local copies, waits for them, and re-layouts  13.9 us (6%)
  other arithmetic  6.38 us (3%)
    all_to_all x2, blocking collectives, copy_for_each(): lax.all_to_all(jnp.broadcast_to(shard[None], (peers, *shard.shape)), axis...  37.2 us
    ppermute x8, starting transfers between devices, padded_2(): lax.ppermute(tail, axis, [(i, (i + 1) % count) for i in range(ends)])  32.6 us
    ppermute x8, starting transfers between devices, padded_2(): lax.ppermute(head, axis, [((i + 1) % count, i) for i in range(ends)])  24.5 us
    ppermute x8, waiting for transfers between devices, padded_2(): lax.ppermute(head, axis, [((i + 1) % count, i) for i in range(ends)])  22 us
    all_to_all x1, waiting for transfers between devices, sum_at_owner(): lax.all_to_all(cut_along(shard, dim, peers), axis, 0, 0, tiled=True)  14.4 us
    all_gather x1, blocking collectives, gather_weights(): lax.all_gather(rows, 'blk', axis=0, tiled=True, axis_index_groups=near)  9.96 us
    all_to_all x1, blocking collectives, local(): lax.all_to_all(hidden, 'zslab', split_axis=0, concat_axis=1, tiled=True)  9.42 us
    all_to_all x1, starting transfers between devices, sum_at_owner(): lax.all_to_all(cut_along(shard, dim, peers), axis, 0, 0, tiled=True)  8.22 us
  transfers between devices with their start and end apart: 19, of which 12 were waited for; matrix products, arithmetic and copies ran while one was open for 6% of the time, Pallas kernels for 0%

profile of v7, /device:TPU:103, one launch (start us, length us, event | category | flops | bytes accessed | tf_op | source)
XLA Modules:
  0.0 234.7 jit_solution(655205904712775235)
XLA Ops:
  8.6 10.0 %all_gather.6 = bf16[320,1024]{1,0:T(8,128)(2,1)} all-gather(bf16[80,1024]{1,0:T(8,128)(2,1)S(1)} %maximum_maximum_fusion.4), channel_id=1, replica_groups={{0,1,2,3},{4,5,6,7},{8,9,10,11},{12,13,14,15},{16,17,18,19},{20,21,22,2..., dimensions={0}, use_global_device_ids=true | all-gather | bytes 819200 | tf_op jit(solution)/shard_map/all_gather | solution.py:87
  18.6 3.5 %collective-permute-start = (bf16[8,2,16,128]{3,2,1,0:T(8,128)(2,1)S(1)}, bf16[8,2,16,128]{3,2,1,0:T(8,128)(2,1)S(1)}, u32[]{:S(2)}, u32[]{:S(2)}) collective-permute-start(bf16[8,2,16,128]{3,2,1,0:T(8,128)(2,1)S(1)} %get-tuple-element.41), channel_id=1, source_target_pairs={{0,32},{32,64},{64,96},{96,128},{128,160},{160,192},{192,224},{1,3... | collective-permute-start | bytes 196616 | tf_op jit(solution)/shard_map/ppermute | solution.py:21
  24.9 3.1 %collective-permute-done.1 = bf16[8,2,16,128]{3,2,1,0:T(8,128)(2,1)S(1)} collective-permute-done((bf16[8,2,16,128]{3,2,1,0:T(8,128)(2,1)S(1)}, bf16[8,2,16,128]{3,2,1,0:T(8,128)(2,1)S(1)}, u32[]{:S(2)}, u32[]{:S(2)}) %collective-permute-start.1) | collective-permute-done | bytes 65568 | tf_op jit(solution)/shard_map/ppermute | solution.py:23
  28.0 7.2 %collective-permute-start.2 = (bf16[2,8,16,128]{3,2,1,0:T(8,128)(2,1)S(1)}, bf16[2,8,16,128]{3,2,1,0:T(8,128)(2,1)S(1)}, u32[]{:S(2)}, u32[]{:S(2)}) collective-permute-start(bf16[2,8,16,128]{3,2,1,0:T(8,128)(2,1)S(1)} %get-tuple-element.34), channel_id=1, source_target_pairs={{0,1},{1,2},{2,3},{3,4},{4,5},{5,6},{6,7},{7,8},{8,9},{9,10},{10,1... | collective-permute-start | bytes 196616 | tf_op jit(solution)/shard_map/ppermute | solution.py:21
  39.7 6.1 %collective-permute-done.3 = bf16[2,8,16,128]{3,2,1,0:T(8,128)(2,1)S(1)} collective-permute-done((bf16[2,8,16,128]{3,2,1,0:T(8,128)(2,1)S(1)}, bf16[2,8,16,128]{3,2,1,0:T(8,128)(2,1)S(1)}, u32[]{:S(2)}, u32[]{:S(2)}) %collective-permute-start.3) | collective-permute-done | bytes 65568 | tf_op jit(solution)/shard_map/ppermute | solution.py:23
  51.2 3.4 %collective-permute-start.5 = (bf16[8,2,16,128]{3,2,1,0:T(8,128)(2,1)S(1)}, bf16[8,2,16,128]{3,2,1,0:T(8,128)(2,1)S(1)}, u32[]{:S(2)}, u32[]{:S(2)}) collective-permute-start(bf16[8,2,16,128]{3,2,1,0:T(8,128)(2,1)S(1)} %get-tuple-element.40), channel_id=1, source_target_pairs={{32,0},{64,32},{96,64},{128,96},{160,128},{192,160},{224,192},{33,... | collective-permute-start | bytes 196616 | tf_op jit(solution)/shard_map/ppermute | solution.py:23
  54.7 2.9 %collective-permute-done.5 = bf16[8,2,16,128]{3,2,1,0:T(8,128)(2,1)S(1)} collective-permute-done((bf16[8,2,16,128]{3,2,1,0:T(8,128)(2,1)S(1)}, bf16[8,2,16,128]{3,2,1,0:T(8,128)(2,1)S(1)}, u32[]{:S(2)}, u32[]{:S(2)}) %collective-permute-start.5) | collective-permute-done | bytes 65568 | tf_op jit(solution)/shard_map/ppermute | solution.py:23
  64.2 6.6 %collective-permute-done.7 = bf16[2,8,16,128]{3,2,1,0:T(8,128)(2,1)S(1)} collective-permute-done((bf16[2,8,16,128]{3,2,1,0:T(8,128)(2,1)S(1)}, bf16[2,8,16,128]{3,2,1,0:T(8,128)(2,1)S(1)}, u32[]{:S(2)}, u32[]{:S(2)}) %collective-permute-start.7) | collective-permute-done | bytes 65568 | tf_op jit(solution)/shard_map/ppermute | solution.py:23
  73.7 9.4 %all_to_all.38 = bf16[8,4,16,128]{3,2,1,0:T(8,128)(2,1)S(1)} all-to-all(bf16[8,4,16,128]{3,2,1,0:T(8,128)(2,1)S(1)} %get-tuple-element.55), channel_id=1, replica_groups=mesh['zslab'=8,'blk'=32] {'zslab'}, dimensions={0} | all-to-all | bytes 262144 | tf_op jit(solution)/shard_map/all_to_all | solution.py:160
  84.1 3.0 %fusion.26 = bf16[32,1024]{1,0:T(8,128)(2,1)S(1)} fusion(bf16[32,80,1024]{2,1,0:T(8,128)(2,1)} %bitcast.261, bf16[32,32,64]{2,1,0:T(8,128)(2,1)S(1)} %reshape_reshape.9), kind=kOutput, calls=%fused_computation.31 | convolution fusion | flops 134250496 | bytes 4390912 | tf_op jit(solution)/shard_map/tbf,bfd->td/dot_general | solution.py:169
  88.0 5.2 %all-to-all-start.1 = ((bf16[8,32,1024]{2,1,0:T(8,128)(2,1)}), bf16[8,32,1024]{2,1,0:T(8,128)(2,1)S(1)}, u32[]{:S(2)}, u32[]{:S(2)}) async-start(bf16[8,32,1024]{2,1,0:T(8,128)(2,1)} %broadcast_in_dim.9), calls=%async_computation.1 | async-start | bytes 1048576 | tf_op jit(solution)/shard_map/all_to_all | solution.py:32
  97.1 4.0 %all-to-all-done.1 = bf16[8,32,1024]{2,1,0:T(8,128)(2,1)S(1)} async-done(((bf16[8,32,1024]{2,1,0:T(8,128)(2,1)}), bf16[8,32,1024]{2,1,0:T(8,128)(2,1)S(1)}, u32[]{:S(2)}, u32[]{:S(2)}) %all-to-all-start.1) | async-done | bytes 524320 | tf_op jit(solution)/shard_map/all_to_all | solution.py:32
  101.6 25.2 %all_to_all.39 = bf16[32,32,256]{2,1,0:T(8,128)(2,1)S(1)} all-to-all(bf16[32,32,256]{2,1,0:T(8,128)(2,1)S(1)} %broadcast_in_dim.10), channel_id=1, replica_groups=mesh['zslab'=8,'blk'=32] {'blk'}, dimensions={0} | all-to-all | bytes 1048576 | tf_op jit(solution)/shard_map/all_to_all | solution.py:32
  131.9 8.2 %all-to-all-start.3 = ((bf16[32,32,256]{2,1,0:T(8,128)(2,1)}), bf16[32,32,256]{2,1,0:T(8,128)(2,1)}, u32[]{:S(2)}, u32[]{:S(2)}) async-start(bf16[32,32,256]{2,1,0:T(8,128)(2,1)} %pad_maximum_fusion), calls=%async_computation.3 | async-start | bytes 1048576 | tf_op jit(solution)/shard_map/all_to_all | solution.py:73
  140.3 14.4 %all-to-all-done.3 = bf16[32,32,256]{2,1,0:T(8,128)(2,1)} async-done(((bf16[32,32,256]{2,1,0:T(8,128)(2,1)}), bf16[32,32,256]{2,1,0:T(8,128)(2,1)}, u32[]{:S(2)}, u32[]{:S(2)}) %all-to-all-start.3) | async-done | bytes 524320 | tf_op jit(solution)/shard_map/all_to_all | solution.py:73
  156.3 11.9 %all_to_all.40 = bf16[8,32,1024]{2,1,0:T(8,128)(2,1)S(1)} all-to-all(bf16[8,32,1024]{2,1,0:T(8,128)(2,1)S(1)} %broadcast_in_dim.11), channel_id=1, replica_groups=mesh['zslab'=8,'blk'=32] {'zslab'}, dimensions={0} | all-to-all | bytes 1048576 | tf_op jit(solution)/shard_map/all_to_all | solution.py:32
  168.3 4.2 %fusion.4 = bf16[32,32,64]{2,0,1:T(8,128)(2,1)S(1)} fusion(bf16[32,80,1024]{2,1,0:T(8,128)(2,1)} %bitcast.263, bf16[32,1024]{1,0:T(8,128)(2,1)S(1)} %reduce_sum.58), kind=kOutput, calls=%fused_computation.4 | convolution fusion | flops 134283264 | bytes 4390912 | tf_op jit(solution)/shard_map/td,bfd->tbf/dot_general | solution.py:223
  172.8 8.1 %all_to_all.41 = bf16[1,32,16,128]{3,2,0,1:T(8,128)(2,1)S(1)} all-to-all(bf16[1,32,16,128]{3,2,0,1:T(8,128)(2,1)S(1)} %bitcast.248), channel_id=1, replica_groups=mesh['zslab'=8,'blk'=32] {'zslab'}, dimensions={1} | all-to-all | bytes 262144 | tf_op jit(solution)/shard_map/all_to_all | solution.py:230
  181.1 2.7 %collective-permute-start.8 = (bf16[8,2,16,128]{3,2,1,0:T(8,128)(2,1)S(1)}, bf16[8,2,16,128]{3,2,1,0:T(8,128)(2,1)S(1)}, u32[]{:S(2)}, u32[]{:S(2)}) collective-permute-start(bf16[8,2,16,128]{3,2,1,0:T(8,128)(2,1)S(1)} %get-tuple-element.37), channel_id=1, source_target_pairs={{0,32},{32,64},{64,96},{96,128},{128,160},{160,192},{192,224},{1,3... | collective-permute-start | bytes 196616 | tf_op jit(solution)/shard_map/ppermute | solution.py:21
  189.8 5.8 %collective-permute-start.10 = (bf16[2,8,16,128]{3,2,1,0:T(8,128)(2,1)S(1)}, bf16[2,8,16,128]{3,2,1,0:T(8,128)(2,1)S(1)}, u32[]{:S(2)}, u32[]{:S(2)}) collective-permute-start(bf16[2,8,16,128]{3,2,1,0:T(8,128)(2,1)S(1)} %get-tuple-element.26), channel_id=1, source_target_pairs={{1,0},{2,1},{3,2},{4,3},{5,4},{6,5},{7,6},{8,7},{9,8},{10,9},{11,1... | collective-permute-start | bytes 196616 | tf_op jit(solution)/shard_map/ppermute | solution.py:23
  195.7 5.4 %collective-permute-start.11 = (bf16[2,8,16,128]{3,2,1,0:T(8,128)(2,1)S(1)}, bf16[2,8,16,128]{3,2,1,0:T(8,128)(2,1)S(1)}, u32[]{:S(2)}, u32[]{:S(2)}) collective-permute-start(bf16[2,8,16,128]{3,2,1,0:T(8,128)(2,1)S(1)} %get-tuple-element.25), channel_id=1, source_target_pairs={{0,1},{1,2},{2,3},{3,4},{4,5},{5,6},{6,7},{7,8},{8,9},{9,10},{10,1... | collective-permute-start | bytes 196616 | tf_op jit(solution)/shard_map/ppermute | solution.py:21
  206.8 3.4 %collective-permute-start.13 = (bf16[8,2,16,128]{3,2,1,0:T(8,128)(2,1)S(1)}, bf16[8,2,16,128]{3,2,1,0:T(8,128)(2,1)S(1)}, u32[]{:S(2)}, u32[]{:S(2)}) collective-permute-start(bf16[8,2,16,128]{3,2,1,0:T(8,128)(2,1)S(1)} %get-tuple-element.36), channel_id=1, source_target_pairs={{32,0},{64,32},{96,64},{128,96},{160,128},{192,160},{224,192},{33,... | collective-permute-start | bytes 196616 | tf_op jit(solution)/shard_map/ppermute | solution.py:23
  212.7 3.6 %collective-permute-start.14 = (bf16[2,8,16,128]{3,2,1,0:T(8,128)(2,1)S(1)}, bf16[2,8,16,128]{3,2,1,0:T(8,128)(2,1)S(1)}, u32[]{:S(2)}, u32[]{:S(2)}) collective-permute-start(bf16[2,8,16,128]{3,2,1,0:T(8,128)(2,1)S(1)} %get-tuple-element.22), channel_id=1, source_target_pairs={{1,0},{2,1},{3,2},{4,3},{5,4},{6,5},{7,6},{8,7},{9,8},{10,9},{11,1... | collective-permute-start | bytes 196616 | tf_op jit(solution)/shard_map/ppermute | solution.py:23
  216.3 7.3 %collective-permute-start.15 = (bf16[2,8,16,128]{3,2,1,0:T(8,128)(2,1)S(1)}, bf16[2,8,16,128]{3,2,1,0:T(8,128)(2,1)S(1)}, u32[]{:S(2)}, u32[]{:S(2)}) collective-permute-start(bf16[2,8,16,128]{3,2,1,0:T(8,128)(2,1)S(1)} %get-tuple-element.21), channel_id=1, source_target_pairs={{0,1},{1,2},{2,3},{3,4},{4,5},{5,6},{6,7},{7,8},{8,9},{9,10},{10,1... | collective-permute-start | bytes 196616 | tf_op jit(solution)/shard_map/ppermute | solution.py:21
  (157 shorter events, 51.6 us)
Async XLA Ops:
  6.5 12.0 %copy-start.1 = (bf16[8,16,4,128]{3,2,1,0:T(4,128)(2,1)S(1)}, bf16[8,16,4,128]{3,2,1,0:T(4,128)(2,1)}, u32[]{:S(2)}) copy-start(bf16[8,16,4,128]{3,2,1,0:T(4,128)(2,1)} %param.7) | copy-start | bytes 393220
  6.5 77.6 %all-gather.2.cloned.1.call-start = ((), (), s32[]{:S(2)}) async-start(), calls=%async_computation.6 | async-start | bytes 5898240 | tf_op jit(solution)/shard_map/all_gather | solution.py:88
  7.4 16.7 %copy-start = (bf16[2,3456,128]{2,1,0:T(8,128)(2,1)S(1)}, bf16[2,3456,128]{2,1,0:T(8,128)(2,1)}, u32[]{:S(2)}) copy-start(bf16[2,3456,128]{2,1,0:T(8,128)(2,1)} %param.10) | copy-start | bytes 5308420
  18.6 6.3 %collective-permute-start = (bf16[8,2,16,128]{3,2,1,0:T(8,128)(2,1)S(1)}, bf16[8,2,16,128]{3,2,1,0:T(8,128)(2,1)S(1)}, u32[]{:S(2)}, u32[]{:S(2)}) collective-permute-start(bf16[8,2,16,128]{3,2,1,0:T(8,128)(2,1)S(1)} %get-tuple-element.41), channel_id=1, source_target_pairs={{0,32},{32,64},{64,96},{96,128},{128,160},{160,192},{192,224},{1,3... | collective-permute-start | bytes 196616 | tf_op jit(solution)/shard_map/ppermute | solution.py:21
  22.1 5.9 %collective-permute-start.1 = (bf16[8,2,16,128]{3,2,1,0:T(8,128)(2,1)S(1)}, bf16[8,2,16,128]{3,2,1,0:T(8,128)(2,1)S(1)}, u32[]{:S(2)}, u32[]{:S(2)}) collective-permute-start(bf16[8,2,16,128]{3,2,1,0:T(8,128)(2,1)S(1)} %get-tuple-element.42), channel_id=1, source_target_pairs={{32,0},{64,32},{96,64},{128,96},{160,128},{192,160},{224,192},{33,... | collective-permute-start | bytes 196616 | tf_op jit(solution)/shard_map/ppermute | solution.py:23
  24.2 13.0 %copy-start.5 = (s32[2,3]{1,0:T(2,128)S(1)}, s32[2,3]{1,0:T(2,128)}, u32[]{:S(2)}) copy-start(s32[2,3]{1,0:T(2,128)} %param.9) | copy-start | bytes 76
  28.0 11.7 %collective-permute-start.2 = (bf16[2,8,16,128]{3,2,1,0:T(8,128)(2,1)S(1)}, bf16[2,8,16,128]{3,2,1,0:T(8,128)(2,1)S(1)}, u32[]{:S(2)}, u32[]{:S(2)}) collective-permute-start(bf16[2,8,16,128]{3,2,1,0:T(8,128)(2,1)S(1)} %get-tuple-element.34), channel_id=1, source_target_pairs={{0,1},{1,2},{2,3},{3,4},{4,5},{5,6},{6,7},{7,8},{8,9},{9,10},{10,1... | collective-permute-start | bytes 196616 | tf_op jit(solution)/shard_map/ppermute | solution.py:21
  35.2 10.6 %collective-permute-start.3 = (bf16[2,8,16,128]{3,2,1,0:T(8,128)(2,1)S(1)}, bf16[2,8,16,128]{3,2,1,0:T(8,128)(2,1)S(1)}, u32[]{:S(2)}, u32[]{:S(2)}) collective-permute-start(bf16[2,8,16,128]{3,2,1,0:T(8,128)(2,1)S(1)} %get-tuple-element.33), channel_id=1, source_target_pairs={{1,0},{2,1},{3,2},{4,3},{5,4},{6,5},{7,6},{8,7},{9,8},{10,9},{11,1... | collective-permute-start | bytes 196616 | tf_op jit(solution)/shard_map/ppermute | solution.py:23
  49.3 5.4 %collective-permute-start.4 = (bf16[8,2,16,128]{3,2,1,0:T(8,128)(2,1)S(1)}, bf16[8,2,16,128]{3,2,1,0:T(8,128)(2,1)S(1)}, u32[]{:S(2)}, u32[]{:S(2)}) collective-permute-start(bf16[8,2,16,128]{3,2,1,0:T(8,128)(2,1)S(1)} %get-tuple-element.39), channel_id=1, source_target_pairs={{0,32},{32,64},{64,96},{96,128},{128,160},{160,192},{192,224},{1,3... | collective-permute-start | bytes 196616 | tf_op jit(solution)/shard_map/ppermute | solution.py:21
  51.2 6.4 %collective-permute-start.5 = (bf16[8,2,16,128]{3,2,1,0:T(8,128)(2,1)S(1)}, bf16[8,2,16,128]{3,2,1,0:T(8,128)(2,1)S(1)}, u32[]{:S(2)}, u32[]{:S(2)}) collective-permute-start(bf16[8,2,16,128]{3,2,1,0:T(8,128)(2,1)S(1)} %get-tuple-element.40), channel_id=1, source_target_pairs={{32,0},{64,32},{96,64},{128,96},{160,128},{192,160},{224,192},{33,... | collective-permute-start | bytes 196616 | tf_op jit(solution)/shard_map/ppermute | solution.py:23
  57.7 6.5 %collective-permute-start.6 = (bf16[2,8,16,128]{3,2,1,0:T(8,128)(2,1)S(1)}, bf16[2,8,16,128]{3,2,1,0:T(8,128)(2,1)S(1)}, u32[]{:S(2)}, u32[]{:S(2)}) collective-permute-start(bf16[2,8,16,128]{3,2,1,0:T(8,128)(2,1)S(1)} %get-tuple-element.30), channel_id=1, source_target_pairs={{0,1},{1,2},{2,3},{3,4},{4,5},{5,6},{6,7},{7,8},{8,9},{9,10},{10,1... | collective-permute-start | bytes 196616 | tf_op jit(solution)/shard_map/ppermute | solution.py:21
  60.3 10.6 %collective-permute-start.7 = (bf16[2,8,16,128]{3,2,1,0:T(8,128)(2,1)S(1)}, bf16[2,8,16,128]{3,2,1,0:T(8,128)(2,1)S(1)}, u32[]{:S(2)}, u32[]{:S(2)}) collective-permute-start(bf16[2,8,16,128]{3,2,1,0:T(8,128)(2,1)S(1)} %get-tuple-element.29), channel_id=1, source_target_pairs={{1,0},{2,1},{3,2},{4,3},{5,4},{6,5},{7,6},{8,7},{9,8},{10,9},{11,1... | collective-permute-start | bytes 196616 | tf_op jit(solution)/shard_map/ppermute | solution.py:23
  88.0 13.2 %all-to-all-start.1 = ((bf16[8,32,1024]{2,1,0:T(8,128)(2,1)}), bf16[8,32,1024]{2,1,0:T(8,128)(2,1)S(1)}, u32[]{:S(2)}, u32[]{:S(2)}) async-start(bf16[8,32,1024]{2,1,0:T(8,128)(2,1)} %broadcast_in_dim.9), calls=%async_computation.1 | async-start | bytes 1048576 | tf_op jit(solution)/shard_map/all_to_all | solution.py:32
  101.5 25.8 %copy-start.6 = (bf16[32,128]{1,0:T(8,128)(2,1)S(1)}, bf16[32,128]{1,0:T(8,128)(2,1)}, u32[]{:S(2)}) copy-start(bf16[32,128]{1,0:T(8,128)(2,1)} %param.13) | copy-start | bytes 24580
  131.9 22.8 %all-to-all-start.3 = ((bf16[32,32,256]{2,1,0:T(8,128)(2,1)}), bf16[32,32,256]{2,1,0:T(8,128)(2,1)}, u32[]{:S(2)}, u32[]{:S(2)}) async-start(bf16[32,32,256]{2,1,0:T(8,128)(2,1)} %pad_maximum_fusion), calls=%async_computation.3 | async-start | bytes 1048576 | tf_op jit(solution)/shard_map/all_to_all | solution.py:73
  172.5 8.4 %copy-start.3 = (f32[8,4,16,128]{3,2,1,0:T(8,128)S(1)}, f32[8,4,16,128]{3,2,1,0:T(8,128)}, u32[]{:S(2)}) copy-start(f32[8,4,16,128]{3,2,1,0:T(8,128)} %get-tuple-element.56) | copy-start | bytes 786436
  181.1 6.6 %collective-permute-start.8 = (bf16[8,2,16,128]{3,2,1,0:T(8,128)(2,1)S(1)}, bf16[8,2,16,128]{3,2,1,0:T(8,128)(2,1)S(1)}, u32[]{:S(2)}, u32[]{:S(2)}) collective-permute-start(bf16[8,2,16,128]{3,2,1,0:T(8,128)(2,1)S(1)} %get-tuple-element.37), channel_id=1, source_target_pairs={{0,32},{32,64},{64,96},{96,128},{128,160},{160,192},{192,224},{1,3... | collective-permute-start | bytes 196616 | tf_op jit(solution)/shard_map/ppermute | solution.py:21
  183.9 5.9 %collective-permute-start.9 = (bf16[8,2,16,128]{3,2,1,0:T(8,128)(2,1)S(1)}, bf16[8,2,16,128]{3,2,1,0:T(8,128)(2,1)S(1)}, u32[]{:S(2)}, u32[]{:S(2)}) collective-permute-start(bf16[8,2,16,128]{3,2,1,0:T(8,128)(2,1)S(1)} %get-tuple-element.38), channel_id=1, source_target_pairs={{32,0},{64,32},{96,64},{128,96},{160,128},{192,160},{224,192},{33,... | collective-permute-start | bytes 196616 | tf_op jit(solution)/shard_map/ppermute | solution.py:23
  189.8 11.3 %collective-permute-start.10 = (bf16[2,8,16,128]{3,2,1,0:T(8,128)(2,1)S(1)}, bf16[2,8,16,128]{3,2,1,0:T(8,128)(2,1)S(1)}, u32[]{:S(2)}, u32[]{:S(2)}) collective-permute-start(bf16[2,8,16,128]{3,2,1,0:T(8,128)(2,1)S(1)} %get-tuple-element.26), channel_id=1, source_target_pairs={{1,0},{2,1},{3,2},{4,3},{5,4},{6,5},{7,6},{8,7},{9,8},{10,9},{11,1... | collective-permute-start | bytes 196616 | tf_op jit(solution)/shard_map/ppermute | solution.py:23
  195.7 6.6 %collective-permute-start.11 = (bf16[2,8,16,128]{3,2,1,0:T(8,128)(2,1)S(1)}, bf16[2,8,16,128]{3,2,1,0:T(8,128)(2,1)S(1)}, u32[]{:S(2)}, u32[]{:S(2)}) collective-permute-start(bf16[2,8,16,128]{3,2,1,0:T(8,128)(2,1)S(1)} %get-tuple-element.25), channel_id=1, source_target_pairs={{0,1},{1,2},{2,3},{3,4},{4,5},{5,6},{6,7},{7,8},{8,9},{9,10},{10,1... | collective-permute-start | bytes 196616 | tf_op jit(solution)/shard_map/ppermute | solution.py:21
  204.9 6.6 %collective-permute-start.12 = (bf16[8,2,16,128]{3,2,1,0:T(8,128)(2,1)S(1)}, bf16[8,2,16,128]{3,2,1,0:T(8,128)(2,1)S(1)}, u32[]{:S(2)}, u32[]{:S(2)}) collective-permute-start(bf16[8,2,16,128]{3,2,1,0:T(8,128)(2,1)S(1)} %get-tuple-element.35), channel_id=1, source_target_pairs={{0,32},{32,64},{64,96},{96,128},{128,160},{160,192},{192,224},{1,3... | collective-permute-start | bytes 196616 | tf_op jit(solution)/shard_map/ppermute | solution.py:21
  206.8 5.9 %collective-permute-start.13 = (bf16[8,2,16,128]{3,2,1,0:T(8,128)(2,1)S(1)}, bf16[8,2,16,128]{3,2,1,0:T(8,128)(2,1)S(1)}, u32[]{:S(2)}, u32[]{:S(2)}) collective-permute-start(bf16[8,2,16,128]{3,2,1,0:T(8,128)(2,1)S(1)} %get-tuple-element.36), channel_id=1, source_target_pairs={{32,0},{64,32},{96,64},{128,96},{160,128},{192,160},{224,192},{33,... | collective-permute-start | bytes 196616 | tf_op jit(solution)/shard_map/ppermute | solution.py:23
  212.7 11.1 %collective-permute-start.14 = (bf16[2,8,16,128]{3,2,1,0:T(8,128)(2,1)S(1)}, bf16[2,8,16,128]{3,2,1,0:T(8,128)(2,1)S(1)}, u32[]{:S(2)}, u32[]{:S(2)}) collective-permute-start(bf16[2,8,16,128]{3,2,1,0:T(8,128)(2,1)S(1)} %get-tuple-element.22), channel_id=1, source_target_pairs={{1,0},{2,1},{3,2},{4,3},{5,4},{6,5},{7,6},{8,7},{9,8},{10,9},{11,1... | collective-permute-start | bytes 196616 | tf_op jit(solution)/shard_map/ppermute | solution.py:23
  216.3 8.7 %collective-permute-start.15 = (bf16[2,8,16,128]{3,2,1,0:T(8,128)(2,1)S(1)}, bf16[2,8,16,128]{3,2,1,0:T(8,128)(2,1)S(1)}, u32[]{:S(2)}, u32[]{:S(2)}) collective-permute-start(bf16[2,8,16,128]{3,2,1,0:T(8,128)(2,1)S(1)} %get-tuple-element.21), channel_id=1, source_target_pairs={{0,1},{1,2},{2,3},{3,4},{4,5},{5,6},{6,7},{7,8},{8,9},{9,10},{10,1... | collective-permute-start | bytes 196616 | tf_op jit(solution)/shard_map/ppermute | solution.py:21
  (3 other events, 2.6 us)
Sparse Core Ops, SparseCore 0:
  18.7 65.3 all-gather.1

commit v8 on v7

--- a/solution.py
+++ b/solution.py
@@ -85,7 +85,16 @@
     near = [list(range(start, start + 4)) for start in range(0, peers, 4)]
     far = [list(range(start, peers, 4)) for start in range(4)]
     gathered = lax.all_gather(rows, "blk", axis=0, tiled=True, axis_index_groups=near)
-    gathered = lax.all_gather(gathered, "blk", axis=0, tiled=True, axis_index_groups=far)
+    half = gathered.shape[0] // 2
+    odd = (lax.axis_index("blk") & 1) != 0
+    mine = jnp.where(odd, gathered[half:], gathered[:half])
+    own = lax.all_gather(mine, "blk", axis=0, tiled=True, axis_index_groups=far)
+    other = lax.ppermute(own, "blk", [(i, i ^ 1) for i in range(peers)])
+    own = own.reshape(len(far[0]), half, width)
+    other = other.reshape(len(far[0]), half, width)
+    gathered = jnp.concatenate(
+        [jnp.where(odd, other, own), jnp.where(odd, own, other)], axis=1
+    )
     gathered = gathered.reshape(peers, rows.shape[0], width)
     embed_rows = gathered[:, :feat, :]
     qkv_rows = gathered[:, feat : feat + qkv_flat.shape[0], :].reshape(peers, *qkv_weight.shape)

time: 239 us -> 242 us (1.013)
  waiting for transfers between devices: 43.7 us -> 35.4 us
  local copies, waits for them, and re-layouts: 13.9 us -> 19.7 us
  starting transfers between devices: 70.5 us -> 75.8 us
  other arithmetic: 6.38 us -> 11.2 us
    ppermute x8, starting transfers between devices: 32.6 us -> 42.4 us  [padded_2(): lax.ppermute(tail, axis, [(i, (i + 1) % count) for i in range(ends)])]
    ppermute x8, waiting for transfers between devices: 22 us -> 14.5 us  [padded_2(): lax.ppermute(head, axis, [((i + 1) % count, i) for i in range(ends)])]
    ppermute x8, starting transfers between devices: 24.5 us -> 17.1 us  [padded_2(): lax.ppermute(head, axis, [((i + 1) % count, i) for i in range(ends)])]
    ppermute x0 -> x1, starting transfers between devices: none -> 3.82 us  [gather_weights(): other = lax.ppermute(own, 'blk', [(i, i ^ 1) for i in range(peers)])]
    select_n x0 -> x2, other arithmetic: none -> 3.64 us  [the longest x1 2.88 us: gather_weights(): jnp.where(odd, other, own)]
    unnamed x29 -> x35, local copies, waits for them, and re-layouts: 2.14 us -> 5.62 us
  transfers between devices with their start and end apart: 19 -> 20, of which waited for: 12 -> 8; matrix products, arithmetic and copies ran while one was open for 6% -> 8% of each run, Pallas kernels for 0% -> 0%
where the time goes in v8:
time: 242 us; the launch traced here: 240 us
  starting transfers between devices  75.8 us (31%)
  blocking collectives  64.1 us (26%)
  waiting for transfers between devices  35.4 us (15%)
  local copies, waits for them, and re-layouts  19.7 us (8%)
  between operations  18.1 us (7%)
  matrix products  15.2 us (6%)
  other arithmetic  11.2 us (5%)
    ppermute x8, starting transfers between devices, padded_2(): lax.ppermute(tail, axis, [(i, (i + 1) % count) for i in range(ends)])  42.4 us
    all_to_all x2, blocking collectives, copy_for_each(): lax.all_to_all(jnp.broadcast_to(shard[None], (peers, *shard.shape)), axis...  36.9 us
    ppermute x8, starting transfers between devices, padded_2(): lax.ppermute(head, axis, [((i + 1) % count, i) for i in range(ends)])  17.1 us
    ppermute x8, waiting for transfers between devices, padded_2(): lax.ppermute(head, axis, [((i + 1) % count, i) for i in range(ends)])  14.5 us
    all_to_all x1, waiting for transfers between devices, sum_at_owner(): lax.all_to_all(cut_along(shard, dim, peers), axis, 0, 0, tiled=True)  14.4 us
    all_to_all x1, blocking collectives, local(): lax.all_to_all(hidden, 'zslab', split_axis=0, concat_axis=1, tiled=True)  9.62 us
    all_gather x1, blocking collectives, gather_weights(): lax.all_gather(rows, 'blk', axis=0, tiled=True, axis_index_groups=near)  9.51 us
    all_to_all x1, starting transfers between devices, sum_at_owner(): lax.all_to_all(cut_along(shard, dim, peers), axis, 0, 0, tiled=True)  8.22 us
  transfers between devices with their start and end apart: 20, of which 8 were waited for; matrix products, arithmetic and copies ran while one was open for 8% of the time, Pallas kernels for 0%

profile of v8, /device:TPU:103, one launch (start us, length us, event | category | flops | bytes accessed | tf_op | source)
XLA Modules:
  0.0 239.6 jit_solution(16621210580653872315)
XLA Ops:
  7.5 2.5 %collective-permute-start.2 = (bf16[8,2,16,128]{3,2,1,0:T(8,128)(2,1)S(1)}, bf16[8,2,16,128]{3,2,1,0:T(8,128)(2,1)S(1)}, u32[]{:S(2)}, u32[]{:S(2)}) collective-permute-start(bf16[8,2,16,128]{3,2,1,0:T(8,128)(2,1)S(1)} %get-tuple-element.44), channel_id=1, source_target_pairs={{32,0},{64,32},{96,64},{128,96},{160,128},{192,160},{224,192},{33,... | collective-permute-start | bytes 196616 | tf_op jit(solution)/shard_map/ppermute | solution.py:23
  9.9 3.7 %collective-permute-start.1 = (bf16[8,2,16,128]{3,2,1,0:T(8,128)(2,1)S(1)}, bf16[8,2,16,128]{3,2,1,0:T(8,128)(2,1)S(1)}, u32[]{:S(2)}, u32[]{:S(2)}) collective-permute-start(bf16[8,2,16,128]{3,2,1,0:T(8,128)(2,1)S(1)} %get-tuple-element.43), channel_id=1, source_target_pairs={{0,32},{32,64},{64,96},{96,128},{128,160},{160,192},{192,224},{1,3... | collective-permute-start | bytes 196616 | tf_op jit(solution)/shard_map/ppermute | solution.py:21
  15.6 9.5 %all_gather.6 = bf16[320,1024]{1,0:T(8,128)(2,1)S(1)} all-gather(bf16[80,1024]{1,0:T(8,128)(2,1)S(1)} %maximum_maximum_fusion.4), channel_id=1, replica_groups={{0,1,2,3},{4,5,6,7},{8,9,10,11},{12,13,14,15},{16,17,18,19},{20,21,22,2..., dimensions={0}, use_global_device_ids=true | all-gather | bytes 819200 | tf_op jit(solution)/shard_map/all_gather | solution.py:87
  30.2 7.1 %collective-permute-start.3 = (bf16[2,8,16,128]{3,2,1,0:T(8,128)(2,1)S(1)}, bf16[2,8,16,128]{3,2,1,0:T(8,128)(2,1)S(1)}, u32[]{:S(2)}, u32[]{:S(2)}) collective-permute-start(bf16[2,8,16,128]{3,2,1,0:T(8,128)(2,1)S(1)} %get-tuple-element.36), channel_id=1, source_target_pairs={{0,1},{1,2},{2,3},{3,4},{4,5},{5,6},{6,7},{7,8},{8,9},{9,10},{10,1... | collective-permute-start | bytes 196616 | tf_op jit(solution)/shard_map/ppermute | solution.py:21
  45.3 4.3 %collective-permute-start.5 = (bf16[8,2,16,128]{3,2,1,0:T(8,128)(2,1)S(1)}, bf16[8,2,16,128]{3,2,1,0:T(8,128)(2,1)S(1)}, u32[]{:S(2)}, u32[]{:S(2)}) collective-permute-start(bf16[8,2,16,128]{3,2,1,0:T(8,128)(2,1)S(1)} %get-tuple-element.41), channel_id=1, source_target_pairs={{0,32},{32,64},{64,96},{96,128},{128,160},{160,192},{192,224},{1,3... | collective-permute-start | bytes 196616 | tf_op jit(solution)/shard_map/ppermute | solution.py:21
  53.1 7.7 %collective-permute-start.7 = (bf16[2,8,16,128]{3,2,1,0:T(8,128)(2,1)S(1)}, bf16[2,8,16,128]{3,2,1,0:T(8,128)(2,1)S(1)}, u32[]{:S(2)}, u32[]{:S(2)}) collective-permute-start(bf16[2,8,16,128]{3,2,1,0:T(8,128)(2,1)S(1)} %get-tuple-element.32), channel_id=1, source_target_pairs={{0,1},{1,2},{2,3},{3,4},{4,5},{5,6},{6,7},{7,8},{8,9},{9,10},{10,1... | collective-permute-start | bytes 196616 | tf_op jit(solution)/shard_map/ppermute | solution.py:21
  65.7 3.8 %collective-permute-start = (bf16[1280,1024]{1,0:T(8,128)(2,1)}, bf16[1280,1024]{1,0:T(8,128)(2,1)}, u32[]{:S(2)}, u32[]{:S(2)}) collective-permute-start(bf16[1280,1024]{1,0:T(8,128)(2,1)} %all-gather.2.cloned.1.call-done), channel_id=1, source_target_pairs={{0,1},{1,0},{2,3},{3,2},{4,5},{5,4},{6,7},{7,6},{8,9},{9,8},{10,11... | collective-permute-start | bytes 7864328 | tf_op jit(solution)/shard_map/ppermute | solution.py:92
  73.4 9.6 %all_to_all.38 = bf16[8,4,16,128]{3,2,1,0:T(8,128)(2,1)S(1)} all-to-all(bf16[8,4,16,128]{3,2,1,0:T(8,128)(2,1)S(1)} %get-tuple-element.57), channel_id=1, replica_groups=mesh['zslab'=8,'blk'=32] {'zslab'}, dimensions={0} | all-to-all | bytes 262144 | tf_op jit(solution)/shard_map/all_to_all | solution.py:169
  83.3 2.9 %broadcast_select_fusion.1 = (bf16[1280,1024]{1,0:T(8,128)(2,1)S(1)}, bf16[1280,1024]{1,0:T(8,128)(2,1)S(1)}) fusion(bf16[1280,1024]{1,0:T(8,128)(2,1)} %collective-permute-done, bf16[1280,1024]{1,0:T(8,128)(2,1)} %all-gather.2.cloned.1.call-done, pred[]{:T(512)S(6)} %ne.3), kind=kLoop, calls=%fused_computation.6 | loop fusion | flops 2621440 | bytes 10485761 | tf_op jit(solution)/shard_map/jit(_where)/select_n | solution.py:96
  89.9 4.2 %all-to-all-start.1 = ((bf16[8,32,1024]{2,1,0:T(8,128)(2,1)}), bf16[8,32,1024]{2,1,0:T(8,128)(2,1)S(1)}, u32[]{:S(2)}, u32[]{:S(2)}) async-start(bf16[8,32,1024]{2,1,0:T(8,128)(2,1)} %broadcast_in_dim.9), calls=%async_computation.1 | async-start | bytes 1048576 | tf_op jit(solution)/shard_map/all_to_all | solution.py:32
  98.0 3.6 %all-to-all-done.1 = bf16[8,32,1024]{2,1,0:T(8,128)(2,1)S(1)} async-done(((bf16[8,32,1024]{2,1,0:T(8,128)(2,1)}), bf16[8,32,1024]{2,1,0:T(8,128)(2,1)S(1)}, u32[]{:S(2)}, u32[]{:S(2)}) %all-to-all-start.1) | async-done | bytes 524320 | tf_op jit(solution)/shard_map/all_to_all | solution.py:32
  102.0 25.0 %all_to_all.39 = bf16[32,32,256]{2,1,0:T(8,128)(2,1)S(1)} all-to-all(bf16[32,32,256]{2,1,0:T(8,128)(2,1)S(1)} %broadcast_in_dim.10), channel_id=1, replica_groups=mesh['zslab'=8,'blk'=32] {'blk'}, dimensions={0} | all-to-all | bytes 1048576 | tf_op jit(solution)/shard_map/all_to_all | solution.py:32
  132.1 8.2 %all-to-all-start.3 = ((bf16[32,32,256]{2,1,0:T(8,128)(2,1)}), bf16[32,32,256]{2,1,0:T(8,128)(2,1)}, u32[]{:S(2)}, u32[]{:S(2)}) async-start(bf16[32,32,256]{2,1,0:T(8,128)(2,1)} %pad_maximum_fusion.1), calls=%async_computation.3 | async-start | bytes 1048576 | tf_op jit(solution)/shard_map/all_to_all | solution.py:73
  140.5 14.4 %all-to-all-done.3 = bf16[32,32,256]{2,1,0:T(8,128)(2,1)} async-done(((bf16[32,32,256]{2,1,0:T(8,128)(2,1)}), bf16[32,32,256]{2,1,0:T(8,128)(2,1)}, u32[]{:S(2)}, u32[]{:S(2)}) %all-to-all-start.3) | async-done | bytes 524320 | tf_op jit(solution)/shard_map/all_to_all | solution.py:73
  156.4 12.0 %all_to_all.40 = bf16[8,32,1024]{2,1,0:T(8,128)(2,1)S(1)} all-to-all(bf16[8,32,1024]{2,1,0:T(8,128)(2,1)S(1)} %broadcast_in_dim.11), channel_id=1, replica_groups=mesh['zslab'=8,'blk'=32] {'zslab'}, dimensions={0} | all-to-all | bytes 1048576 | tf_op jit(solution)/shard_map/all_to_all | solution.py:32
  168.5 4.2 %fusion.4 = bf16[32,32,64]{2,0,1:T(8,128)(2,1)S(1)} fusion(bf16[32,80,1024]{2,1,0:T(8,128)(2,1)} %bitcast.225, bf16[32,1024]{1,0:T(8,128)(2,1)S(1)} %reduce_sum.58), kind=kOutput, calls=%fused_computation.7 | convolution fusion | flops 134283264 | bytes 4390912 | tf_op jit(solution)/shard_map/td,bfd->tbf/dot_general | solution.py:232
  173.0 8.1 %all_to_all.41 = bf16[1,32,16,128]{3,2,0,1:T(8,128)(2,1)S(1)} all-to-all(bf16[1,32,16,128]{3,2,0,1:T(8,128)(2,1)S(1)} %bitcast.255), channel_id=1, replica_groups=mesh['zslab'=8,'blk'=32] {'zslab'}, dimensions={1} | all-to-all | bytes 262144 | tf_op jit(solution)/shard_map/all_to_all | solution.py:239
  181.3 2.9 %collective-permute-start.10 = (bf16[8,2,16,128]{3,2,1,0:T(8,128)(2,1)S(1)}, bf16[8,2,16,128]{3,2,1,0:T(8,128)(2,1)S(1)}, u32[]{:S(2)}, u32[]{:S(2)}) collective-permute-start(bf16[8,2,16,128]{3,2,1,0:T(8,128)(2,1)S(1)} %get-tuple-element.40), channel_id=1, source_target_pairs={{32,0},{64,32},{96,64},{128,96},{160,128},{192,160},{224,192},{33,... | collective-permute-start | bytes 196616 | tf_op jit(solution)/shard_map/ppermute | solution.py:23
  184.2 3.3 %collective-permute-start.9 = (bf16[8,2,16,128]{3,2,1,0:T(8,128)(2,1)S(1)}, bf16[8,2,16,128]{3,2,1,0:T(8,128)(2,1)S(1)}, u32[]{:S(2)}, u32[]{:S(2)}) collective-permute-start(bf16[8,2,16,128]{3,2,1,0:T(8,128)(2,1)S(1)} %get-tuple-element.39), channel_id=1, source_target_pairs={{0,32},{32,64},{64,96},{96,128},{128,160},{160,192},{192,224},{1,3... | collective-permute-start | bytes 196616 | tf_op jit(solution)/shard_map/ppermute | solution.py:21
  189.2 9.2 %collective-permute-start.12 = (bf16[2,8,16,128]{3,2,1,0:T(8,128)(2,1)S(1)}, bf16[2,8,16,128]{3,2,1,0:T(8,128)(2,1)S(1)}, u32[]{:S(2)}, u32[]{:S(2)}) collective-permute-start(bf16[2,8,16,128]{3,2,1,0:T(8,128)(2,1)S(1)} %get-tuple-element.27), channel_id=1, source_target_pairs={{0,1},{1,2},{2,3},{3,4},{4,5},{5,6},{6,7},{7,8},{8,9},{9,10},{10,1... | collective-permute-start | bytes 196616 | tf_op jit(solution)/shard_map/ppermute | solution.py:21
  200.4 7.2 %collective-permute-done.11 = bf16[2,8,16,128]{3,2,1,0:T(8,128)(2,1)S(1)} collective-permute-done((bf16[2,8,16,128]{3,2,1,0:T(8,128)(2,1)S(1)}, bf16[2,8,16,128]{3,2,1,0:T(8,128)(2,1)S(1)}, u32[]{:S(2)}, u32[]{:S(2)}) %collective-permute-start.11) | collective-permute-done | bytes 65568 | tf_op jit(solution)/shard_map/ppermute | solution.py:23
  212.2 4.3 %collective-permute-start.13 = (bf16[8,2,16,128]{3,2,1,0:T(8,128)(2,1)S(1)}, bf16[8,2,16,128]{3,2,1,0:T(8,128)(2,1)S(1)}, u32[]{:S(2)}, u32[]{:S(2)}) collective-permute-start(bf16[8,2,16,128]{3,2,1,0:T(8,128)(2,1)S(1)} %get-tuple-element.37), channel_id=1, source_target_pairs={{0,32},{32,64},{64,96},{96,128},{128,160},{160,192},{192,224},{1,3... | collective-permute-start | bytes 196616 | tf_op jit(solution)/shard_map/ppermute | solution.py:21
  217.8 3.0 %collective-permute-start.16 = (bf16[2,8,16,128]{3,2,1,0:T(8,128)(2,1)S(1)}, bf16[2,8,16,128]{3,2,1,0:T(8,128)(2,1)S(1)}, u32[]{:S(2)}, u32[]{:S(2)}) collective-permute-start(bf16[2,8,16,128]{3,2,1,0:T(8,128)(2,1)S(1)} %get-tuple-element.23), channel_id=1, source_target_pairs={{0,1},{1,2},{2,3},{3,4},{4,5},{5,6},{6,7},{7,8},{8,9},{9,10},{10,1... | collective-permute-start | bytes 196616 | tf_op jit(solution)/shard_map/ppermute | solution.py:21
  222.8 7.2 %collective-permute-done.15 = bf16[2,8,16,128]{3,2,1,0:T(8,128)(2,1)S(1)} collective-permute-done((bf16[2,8,16,128]{3,2,1,0:T(8,128)(2,1)S(1)}, bf16[2,8,16,128]{3,2,1,0:T(8,128)(2,1)S(1)}, u32[]{:S(2)}, u32[]{:S(2)}) %collective-permute-start.15) | collective-permute-done | bytes 65568 | tf_op jit(solution)/shard_map/ppermute | solution.py:23
  (168 shorter events, 53.9 us)
Async XLA Ops:
  6.5 59.2 %all-gather.2.cloned.1.call-start = ((), (), s32[]{:S(2)}) async-start(), calls=%async_computation.6 | async-start | bytes 2949120 | tf_op jit(solution)/shard_map/all_gather | solution.py:91
  7.5 20.7 %collective-permute-start.2 = (bf16[8,2,16,128]{3,2,1,0:T(8,128)(2,1)S(1)}, bf16[8,2,16,128]{3,2,1,0:T(8,128)(2,1)S(1)}, u32[]{:S(2)}, u32[]{:S(2)}) collective-permute-start(bf16[8,2,16,128]{3,2,1,0:T(8,128)(2,1)S(1)} %get-tuple-element.44), channel_id=1, source_target_pairs={{32,0},{64,32},{96,64},{128,96},{160,128},{192,160},{224,192},{33,... | collective-permute-start | bytes 196616 | tf_op jit(solution)/shard_map/ppermute | solution.py:23
  9.9 18.2 %collective-permute-start.1 = (bf16[8,2,16,128]{3,2,1,0:T(8,128)(2,1)S(1)}, bf16[8,2,16,128]{3,2,1,0:T(8,128)(2,1)S(1)}, u32[]{:S(2)}, u32[]{:S(2)}) collective-permute-start(bf16[8,2,16,128]{3,2,1,0:T(8,128)(2,1)S(1)} %get-tuple-element.43), channel_id=1, source_target_pairs={{0,32},{32,64},{64,96},{96,128},{128,160},{160,192},{192,224},{1,3... | collective-permute-start | bytes 196616 | tf_op jit(solution)/shard_map/ppermute | solution.py:21
  27.4 9.9 %copy-start.8 = (s32[2,3]{1,0:T(2,128)S(1)}, s32[2,3]{1,0:T(2,128)}, u32[]{:S(2)}) copy-start(s32[2,3]{1,0:T(2,128)} %param.9) | copy-start | bytes 76
  28.2 11.7 %collective-permute-start.4 = (bf16[2,8,16,128]{3,2,1,0:T(8,128)(2,1)S(1)}, bf16[2,8,16,128]{3,2,1,0:T(8,128)(2,1)S(1)}, u32[]{:S(2)}, u32[]{:S(2)}) collective-permute-start(bf16[2,8,16,128]{3,2,1,0:T(8,128)(2,1)S(1)} %get-tuple-element.35), channel_id=1, source_target_pairs={{1,0},{2,1},{3,2},{4,3},{5,4},{6,5},{7,6},{8,7},{9,8},{10,9},{11,1... | collective-permute-start | bytes 196616 | tf_op jit(solution)/shard_map/ppermute | solution.py:23
  30.2 9.6 %collective-permute-start.3 = (bf16[2,8,16,128]{3,2,1,0:T(8,128)(2,1)S(1)}, bf16[2,8,16,128]{3,2,1,0:T(8,128)(2,1)S(1)}, u32[]{:S(2)}, u32[]{:S(2)}) collective-permute-start(bf16[2,8,16,128]{3,2,1,0:T(8,128)(2,1)S(1)} %get-tuple-element.36), channel_id=1, source_target_pairs={{0,1},{1,2},{2,3},{3,4},{4,5},{5,6},{6,7},{7,8},{8,9},{9,10},{10,1... | collective-permute-start | bytes 196616 | tf_op jit(solution)/shard_map/ppermute | solution.py:21
  43.4 6.3 %collective-permute-start.6 = (bf16[8,2,16,128]{3,2,1,0:T(8,128)(2,1)S(1)}, bf16[8,2,16,128]{3,2,1,0:T(8,128)(2,1)S(1)}, u32[]{:S(2)}, u32[]{:S(2)}) collective-permute-start(bf16[8,2,16,128]{3,2,1,0:T(8,128)(2,1)S(1)} %get-tuple-element.42), channel_id=1, source_target_pairs={{32,0},{64,32},{96,64},{128,96},{160,128},{192,160},{224,192},{33,... | collective-permute-start | bytes 196616 | tf_op jit(solution)/shard_map/ppermute | solution.py:23
  45.3 5.8 %collective-permute-start.5 = (bf16[8,2,16,128]{3,2,1,0:T(8,128)(2,1)S(1)}, bf16[8,2,16,128]{3,2,1,0:T(8,128)(2,1)S(1)}, u32[]{:S(2)}, u32[]{:S(2)}) collective-permute-start(bf16[8,2,16,128]{3,2,1,0:T(8,128)(2,1)S(1)} %get-tuple-element.41), channel_id=1, source_target_pairs={{0,32},{32,64},{64,96},{96,128},{128,160},{160,192},{192,224},{1,3... | collective-permute-start | bytes 196616 | tf_op jit(solution)/shard_map/ppermute | solution.py:21
  51.1 12.6 %collective-permute-start.8 = (bf16[2,8,16,128]{3,2,1,0:T(8,128)(2,1)S(1)}, bf16[2,8,16,128]{3,2,1,0:T(8,128)(2,1)S(1)}, u32[]{:S(2)}, u32[]{:S(2)}) collective-permute-start(bf16[2,8,16,128]{3,2,1,0:T(8,128)(2,1)S(1)} %get-tuple-element.31), channel_id=1, source_target_pairs={{1,0},{2,1},{3,2},{4,3},{5,4},{6,5},{7,6},{8,7},{9,8},{10,9},{11,1... | collective-permute-start | bytes 196616 | tf_op jit(solution)/shard_map/ppermute | solution.py:23
  53.1 10.6 %collective-permute-start.7 = (bf16[2,8,16,128]{3,2,1,0:T(8,128)(2,1)S(1)}, bf16[2,8,16,128]{3,2,1,0:T(8,128)(2,1)S(1)}, u32[]{:S(2)}, u32[]{:S(2)}) collective-permute-start(bf16[2,8,16,128]{3,2,1,0:T(8,128)(2,1)S(1)} %get-tuple-element.32), channel_id=1, source_target_pairs={{0,1},{1,2},{2,3},{3,4},{4,5},{5,6},{6,7},{7,8},{8,9},{9,10},{10,1... | collective-permute-start | bytes 196616 | tf_op jit(solution)/shard_map/ppermute | solution.py:21
  65.7 4.1 %copy-start.1 = (bf16[10,8,16,128]{3,2,1,0:T(8,128)(2,1)S(1)}, bf16[10,8,16,128]{3,2,1,0:T(8,128)(2,1)}, u32[]{:S(2)}) copy-start(bf16[10,8,16,128]{3,2,1,0:T(8,128)(2,1)} %get-tuple-element.29) | copy-start | bytes 983044
  65.7 17.5 %collective-permute-start = (bf16[1280,1024]{1,0:T(8,128)(2,1)}, bf16[1280,1024]{1,0:T(8,128)(2,1)}, u32[]{:S(2)}, u32[]{:S(2)}) collective-permute-start(bf16[1280,1024]{1,0:T(8,128)(2,1)} %all-gather.2.cloned.1.call-done), channel_id=1, source_target_pairs={{0,1},{1,0},{2,3},{3,2},{4,5},{5,4},{6,7},{7,6},{8,9},{9,8},{10,11... | collective-permute-start | bytes 7864328 | tf_op jit(solution)/shard_map/ppermute | solution.py:92
  89.9 11.7 %all-to-all-start.1 = ((bf16[8,32,1024]{2,1,0:T(8,128)(2,1)}), bf16[8,32,1024]{2,1,0:T(8,128)(2,1)S(1)}, u32[]{:S(2)}, u32[]{:S(2)}) async-start(bf16[8,32,1024]{2,1,0:T(8,128)(2,1)} %broadcast_in_dim.9), calls=%async_computation.1 | async-start | bytes 1048576 | tf_op jit(solution)/shard_map/all_to_all | solution.py:32
  101.9 25.6 %copy-start.9 = (bf16[32,128]{1,0:T(8,128)(2,1)S(1)}, bf16[32,128]{1,0:T(8,128)(2,1)}, u32[]{:S(2)}) copy-start(bf16[32,128]{1,0:T(8,128)(2,1)} %param.13) | copy-start | bytes 24580
  132.1 22.8 %all-to-all-start.3 = ((bf16[32,32,256]{2,1,0:T(8,128)(2,1)}), bf16[32,32,256]{2,1,0:T(8,128)(2,1)}, u32[]{:S(2)}, u32[]{:S(2)}) async-start(bf16[32,32,256]{2,1,0:T(8,128)(2,1)} %pad_maximum_fusion.1), calls=%async_computation.3 | async-start | bytes 1048576 | tf_op jit(solution)/shard_map/all_to_all | solution.py:73
  172.7 8.4 %copy-start.6 = (f32[8,4,16,128]{3,2,1,0:T(8,128)S(1)}, f32[8,4,16,128]{3,2,1,0:T(8,128)}, u32[]{:S(2)}) copy-start(f32[8,4,16,128]{3,2,1,0:T(8,128)} %get-tuple-element.58) | copy-start | bytes 786436
  181.3 7.5 %collective-permute-start.10 = (bf16[8,2,16,128]{3,2,1,0:T(8,128)(2,1)S(1)}, bf16[8,2,16,128]{3,2,1,0:T(8,128)(2,1)S(1)}, u32[]{:S(2)}, u32[]{:S(2)}) collective-permute-start(bf16[8,2,16,128]{3,2,1,0:T(8,128)(2,1)S(1)} %get-tuple-element.40), channel_id=1, source_target_pairs={{32,0},{64,32},{96,64},{128,96},{160,128},{192,160},{224,192},{33,... | collective-permute-start | bytes 196616 | tf_op jit(solution)/shard_map/ppermute | solution.py:23
  184.2 5.0 %collective-permute-start.9 = (bf16[8,2,16,128]{3,2,1,0:T(8,128)(2,1)S(1)}, bf16[8,2,16,128]{3,2,1,0:T(8,128)(2,1)S(1)}, u32[]{:S(2)}, u32[]{:S(2)}) collective-permute-start(bf16[8,2,16,128]{3,2,1,0:T(8,128)(2,1)S(1)} %get-tuple-element.39), channel_id=1, source_target_pairs={{0,32},{32,64},{64,96},{96,128},{128,160},{160,192},{192,224},{1,3... | collective-permute-start | bytes 196616 | tf_op jit(solution)/shard_map/ppermute | solution.py:21
  189.2 11.2 %collective-permute-start.12 = (bf16[2,8,16,128]{3,2,1,0:T(8,128)(2,1)S(1)}, bf16[2,8,16,128]{3,2,1,0:T(8,128)(2,1)S(1)}, u32[]{:S(2)}, u32[]{:S(2)}) collective-permute-start(bf16[2,8,16,128]{3,2,1,0:T(8,128)(2,1)S(1)} %get-tuple-element.27), channel_id=1, source_target_pairs={{0,1},{1,2},{2,3},{3,4},{4,5},{5,6},{6,7},{7,8},{8,9},{9,10},{10,1... | collective-permute-start | bytes 196616 | tf_op jit(solution)/shard_map/ppermute | solution.py:21
  198.4 9.2 %collective-permute-start.11 = (bf16[2,8,16,128]{3,2,1,0:T(8,128)(2,1)S(1)}, bf16[2,8,16,128]{3,2,1,0:T(8,128)(2,1)S(1)}, u32[]{:S(2)}, u32[]{:S(2)}) collective-permute-start(bf16[2,8,16,128]{3,2,1,0:T(8,128)(2,1)S(1)} %get-tuple-element.28), channel_id=1, source_target_pairs={{1,0},{2,1},{3,2},{4,3},{5,4},{6,5},{7,6},{8,7},{9,8},{10,9},{11,1... | collective-permute-start | bytes 196616 | tf_op jit(solution)/shard_map/ppermute | solution.py:23
  210.2 7.5 %collective-permute-start.14 = (bf16[8,2,16,128]{3,2,1,0:T(8,128)(2,1)S(1)}, bf16[8,2,16,128]{3,2,1,0:T(8,128)(2,1)S(1)}, u32[]{:S(2)}, u32[]{:S(2)}) collective-permute-start(bf16[8,2,16,128]{3,2,1,0:T(8,128)(2,1)S(1)} %get-tuple-element.38), channel_id=1, source_target_pairs={{32,0},{64,32},{96,64},{128,96},{160,128},{192,160},{224,192},{33,... | collective-permute-start | bytes 196616 | tf_op jit(solution)/shard_map/ppermute | solution.py:23
  212.2 5.6 %collective-permute-start.13 = (bf16[8,2,16,128]{3,2,1,0:T(8,128)(2,1)S(1)}, bf16[8,2,16,128]{3,2,1,0:T(8,128)(2,1)S(1)}, u32[]{:S(2)}, u32[]{:S(2)}) collective-permute-start(bf16[8,2,16,128]{3,2,1,0:T(8,128)(2,1)S(1)} %get-tuple-element.37), channel_id=1, source_target_pairs={{0,32},{32,64},{64,96},{96,128},{128,160},{160,192},{192,224},{1,3... | collective-permute-start | bytes 196616 | tf_op jit(solution)/shard_map/ppermute | solution.py:21
  217.8 5.0 %collective-permute-start.16 = (bf16[2,8,16,128]{3,2,1,0:T(8,128)(2,1)S(1)}, bf16[2,8,16,128]{3,2,1,0:T(8,128)(2,1)S(1)}, u32[]{:S(2)}, u32[]{:S(2)}) collective-permute-start(bf16[2,8,16,128]{3,2,1,0:T(8,128)(2,1)S(1)} %get-tuple-element.23), channel_id=1, source_target_pairs={{0,1},{1,2},{2,3},{3,4},{4,5},{5,6},{6,7},{7,8},{8,9},{9,10},{10,1... | collective-permute-start | bytes 196616 | tf_op jit(solution)/shard_map/ppermute | solution.py:21
  220.8 9.2 %collective-permute-start.15 = (bf16[2,8,16,128]{3,2,1,0:T(8,128)(2,1)S(1)}, bf16[2,8,16,128]{3,2,1,0:T(8,128)(2,1)S(1)}, u32[]{:S(2)}, u32[]{:S(2)}) collective-permute-start(bf16[2,8,16,128]{3,2,1,0:T(8,128)(2,1)S(1)} %get-tuple-element.24), channel_id=1, source_target_pairs={{1,0},{2,1},{3,2},{4,3},{5,4},{6,5},{7,6},{8,7},{9,8},{10,9},{11,1... | collective-permute-start | bytes 196616 | tf_op jit(solution)/shard_map/ppermute | solution.py:23
  (7 other events, 7.8 us)
Sparse Core Ops, SparseCore 0:
  26.0 39.7 all-gather.1

commit v9 on v3

--- a/solution.py
+++ b/solution.py
@@ -74,6 +74,14 @@
     return jnp.sum(pieces.astype(jnp.float32), axis=0)
 
 
+def gathered_in_stages(rows, axis):
+    peers = lax.axis_size(axis)
+    near = [list(range(start, start + 4)) for start in range(0, peers, 4)]
+    far = [list(range(start, peers, 4)) for start in range(4)]
+    rows = lax.all_gather(rows, axis, axis=0, tiled=True, axis_index_groups=near)
+    return lax.all_gather(rows, axis, axis=0, tiled=True, axis_index_groups=far)
+
+
 def gather_weights(embed_weight, qkv_weight):
     _, feat, width = embed_weight.shape
     qkv_flat = qkv_weight.reshape(-1, width)
@@ -81,8 +89,8 @@
     rows = jnp.concatenate(
         [embed_weight[0], qkv_flat, jnp.zeros((extra, width), qkv_flat.dtype)], axis=0
     )
-    gathered = lax.all_gather(rows, "blk", axis=0, tiled=True)
     peers = lax.axis_size("blk")
+    gathered = gathered_in_stages(rows, "blk")
     gathered = gathered.reshape(peers, rows.shape[0], width)
     embed_rows = gathered[:, :feat, :]
     qkv_rows = gathered[:, feat : feat + qkv_flat.shape[0], :].reshape(peers, *qkv_weight.shape)
@@ -171,9 +179,7 @@
         "td,sde->ste", tokens, qkv_rows, preferred_element_type=jnp.float32
     ).astype(jnp.bfloat16)
     key_rows, value_rows = jnp.split(
-        joined_along(copy_for_each(jnp.concatenate([projected[1], projected[2]], axis=1), "blk"), 0),
-        2,
-        axis=1,
+        gathered_in_stages(jnp.concatenate([projected[1], projected[2]], axis=1), "blk"), 2, axis=1
     )
     tok_rows = tokens.shape[0]
     head_cols = projected.shape[2]

time: 256 us -> 248 us (0.969)
  waiting for transfers between devices: 67.3 us -> 43.7 us
  blocking collectives: 53.7 us -> 67.8 us
  starting transfers between devices: 71.9 us -> 77 us
    all_gather x0 -> x3, blocking collectives: none -> 38.4 us  [the longest x1 19.7 us: gathered_in_stages(): return lax.all_gather(rows, axis, axis=0, tiled=True, axis_index_groups=far)]
    all_gather x1, waiting for transfers between devices: 28 us -> 0.75 us  [gathered_in_stages(): return lax.all_gather(rows, axis, axis=0, tiled=True, axis_index_groups=far)]
    all_to_all x2 -> x1, blocking collectives: 35.3 us -> 11.9 us  [copy_for_each(): lax.all_to_all(jnp.broadcast_to(shard[None], (peers, *shard.shape)), axis...]
    all_to_all x1, starting transfers between devices: 8.21 us -> 14.7 us  [sum_at_owner(): lax.all_to_all(cut_along(shard, dim, peers), axis, 0, 0, tiled=True)]
    ppermute x8, waiting for transfers between devices: 17.8 us -> 22 us  [padded_2(): lax.ppermute(head, axis, [((i + 1) % count, i) for i in range(ends)])]
where the time goes in v9:
time: 248 us; the launch traced here: 244 us
  starting transfers between devices  77 us (31%)
  blocking collectives  67.8 us (27%)
  waiting for transfers between devices  43.7 us (18%)
  between operations  18.1 us (7%)
  matrix products  17.4 us (7%)
  local copies, waits for them, and re-layouts  13.9 us (6%)
  other arithmetic  6.38 us (3%)
    ppermute x8, starting transfers between devices, padded_2(): lax.ppermute(tail, axis, [(i, (i + 1) % count) for i in range(ends)])  32.6 us
    ppermute x8, starting transfers between devices, padded_2(): lax.ppermute(head, axis, [((i + 1) % count, i) for i in range(ends)])  24.5 us
    ppermute x8, waiting for transfers between devices, padded_2(): lax.ppermute(head, axis, [((i + 1) % count, i) for i in range(ends)])  22 us
    all_gather x1, blocking collectives, gathered_in_stages(): return lax.all_gather(rows, axis, axis=0, tiled=True, axis_index_groups=far)  19.7 us
    all_gather x2, blocking collectives, gathered_in_stages(): lax.all_gather(rows, axis, axis=0, tiled=True, axis_index_groups=near)  18.7 us
    all_to_all x1, starting transfers between devices, sum_at_owner(): lax.all_to_all(cut_along(shard, dim, peers), axis, 0, 0, tiled=True)  14.7 us
    all_to_all x1, waiting for transfers between devices, sum_at_owner(): lax.all_to_all(cut_along(shard, dim, peers), axis, 0, 0, tiled=True)  14.4 us
    all_to_all x1, blocking collectives, copy_for_each(): lax.all_to_all(jnp.broadcast_to(shard[None], (peers, *shard.shape)), axis...  11.9 us
  transfers between devices with their start and end apart: 19, of which 12 were waited for; matrix products, arithmetic and copies ran while one was open for 6% of the time, Pallas kernels for 0%

profile of v9, /device:TPU:103, one launch (start us, length us, event | category | flops | bytes accessed | tf_op | source)
XLA Modules:
  0.0 244.3 jit_solution(5096923692221740320)
XLA Ops:
  8.6 10.0 %all_gather.12 = bf16[320,1024]{1,0:T(8,128)(2,1)} all-gather(bf16[80,1024]{1,0:T(8,128)(2,1)S(1)} %maximum_maximum_fusion.4), channel_id=1, replica_groups={{0,1,2,3},{4,5,6,7},{8,9,10,11},{12,13,14,15},{16,17,18,19},{20,21,22,2..., dimensions={0}, use_global_device_ids=true | all-gather | bytes 819200 | tf_op jit(solution)/shard_map/all_gather | solution.py:81
  18.6 3.5 %collective-permute-start = (bf16[8,2,16,128]{3,2,1,0:T(8,128)(2,1)S(1)}, bf16[8,2,16,128]{3,2,1,0:T(8,128)(2,1)S(1)}, u32[]{:S(2)}, u32[]{:S(2)}) collective-permute-start(bf16[8,2,16,128]{3,2,1,0:T(8,128)(2,1)S(1)} %get-tuple-element.41), channel_id=1, source_target_pairs={{0,32},{32,64},{64,96},{96,128},{128,160},{160,192},{192,224},{1,3... | collective-permute-start | bytes 196616 | tf_op jit(solution)/shard_map/ppermute | solution.py:21
  24.9 3.1 %collective-permute-done.1 = bf16[8,2,16,128]{3,2,1,0:T(8,128)(2,1)S(1)} collective-permute-done((bf16[8,2,16,128]{3,2,1,0:T(8,128)(2,1)S(1)}, bf16[8,2,16,128]{3,2,1,0:T(8,128)(2,1)S(1)}, u32[]{:S(2)}, u32[]{:S(2)}) %collective-permute-start.1) | collective-permute-done | bytes 65568 | tf_op jit(solution)/shard_map/ppermute | solution.py:23
  28.0 7.2 %collective-permute-start.2 = (bf16[2,8,16,128]{3,2,1,0:T(8,128)(2,1)S(1)}, bf16[2,8,16,128]{3,2,1,0:T(8,128)(2,1)S(1)}, u32[]{:S(2)}, u32[]{:S(2)}) collective-permute-start(bf16[2,8,16,128]{3,2,1,0:T(8,128)(2,1)S(1)} %get-tuple-element.34), channel_id=1, source_target_pairs={{0,1},{1,2},{2,3},{3,4},{4,5},{5,6},{6,7},{7,8},{8,9},{9,10},{10,1... | collective-permute-start | bytes 196616 | tf_op jit(solution)/shard_map/ppermute | solution.py:21
  39.7 6.1 %collective-permute-done.3 = bf16[2,8,16,128]{3,2,1,0:T(8,128)(2,1)S(1)} collective-permute-done((bf16[2,8,16,128]{3,2,1,0:T(8,128)(2,1)S(1)}, bf16[2,8,16,128]{3,2,1,0:T(8,128)(2,1)S(1)}, u32[]{:S(2)}, u32[]{:S(2)}) %collective-permute-start.3) | collective-permute-done | bytes 65568 | tf_op jit(solution)/shard_map/ppermute | solution.py:23
  51.2 3.4 %collective-permute-start.5 = (bf16[8,2,16,128]{3,2,1,0:T(8,128)(2,1)S(1)}, bf16[8,2,16,128]{3,2,1,0:T(8,128)(2,1)S(1)}, u32[]{:S(2)}, u32[]{:S(2)}) collective-permute-start(bf16[8,2,16,128]{3,2,1,0:T(8,128)(2,1)S(1)} %get-tuple-element.40), channel_id=1, source_target_pairs={{32,0},{64,32},{96,64},{128,96},{160,128},{192,160},{224,192},{33,... | collective-permute-start | bytes 196616 | tf_op jit(solution)/shard_map/ppermute | solution.py:23
  54.7 2.9 %collective-permute-done.5 = bf16[8,2,16,128]{3,2,1,0:T(8,128)(2,1)S(1)} collective-permute-done((bf16[8,2,16,128]{3,2,1,0:T(8,128)(2,1)S(1)}, bf16[8,2,16,128]{3,2,1,0:T(8,128)(2,1)S(1)}, u32[]{:S(2)}, u32[]{:S(2)}) %collective-permute-start.5) | collective-permute-done | bytes 65568 | tf_op jit(solution)/shard_map/ppermute | solution.py:23
  64.2 6.6 %collective-permute-done.7 = bf16[2,8,16,128]{3,2,1,0:T(8,128)(2,1)S(1)} collective-permute-done((bf16[2,8,16,128]{3,2,1,0:T(8,128)(2,1)S(1)}, bf16[2,8,16,128]{3,2,1,0:T(8,128)(2,1)S(1)}, u32[]{:S(2)}, u32[]{:S(2)}) %collective-permute-start.7) | collective-permute-done | bytes 65568 | tf_op jit(solution)/shard_map/ppermute | solution.py:23
  73.7 9.4 %all_to_all.33 = bf16[8,4,16,128]{3,2,1,0:T(8,128)(2,1)S(1)} all-to-all(bf16[8,4,16,128]{3,2,1,0:T(8,128)(2,1)S(1)} %get-tuple-element.55), channel_id=1, replica_groups=mesh['zslab'=8,'blk'=32] {'zslab'}, dimensions={0} | all-to-all | bytes 262144 | tf_op jit(solution)/shard_map/all_to_all | solution.py:165
  84.1 3.0 %fusion.26 = bf16[32,1024]{1,0:T(8,128)(2,1)S(1)} fusion(bf16[32,80,1024]{2,1,0:T(8,128)(2,1)} %bitcast.256, bf16[32,32,64]{2,1,0:T(8,128)(2,1)S(1)} %reshape_reshape.9), kind=kOutput, calls=%fused_computation.31 | convolution fusion | flops 134250496 | bytes 4390912 | tf_op jit(solution)/shard_map/tbf,bfd->td/dot_general | solution.py:174
  88.0 5.2 %all-to-all-start.1 = ((bf16[8,32,1024]{2,1,0:T(8,128)(2,1)}), bf16[8,32,1024]{2,1,0:T(8,128)(2,1)S(1)}, u32[]{:S(2)}, u32[]{:S(2)}) async-start(bf16[8,32,1024]{2,1,0:T(8,128)(2,1)} %broadcast_in_dim.7), calls=%async_computation.1 | async-start | bytes 1048576 | tf_op jit(solution)/shard_map/all_to_all | solution.py:32
  97.1 4.0 %all-to-all-done.1 = bf16[8,32,1024]{2,1,0:T(8,128)(2,1)S(1)} async-done(((bf16[8,32,1024]{2,1,0:T(8,128)(2,1)}), bf16[8,32,1024]{2,1,0:T(8,128)(2,1)S(1)}, u32[]{:S(2)}, u32[]{:S(2)}) %all-to-all-start.1) | async-done | bytes 524320 | tf_op jit(solution)/shard_map/all_to_all | solution.py:32
  101.5 8.7 %all_gather.14 = bf16[128,256]{1,0:T(8,128)(2,1)S(1)} all-gather(bf16[32,256]{1,0:T(8,128)(2,1)S(1)} %pad_maximum_fusion.25), channel_id=1, replica_groups={{0,1,2,3},{4,5,6,7},{8,9,10,11},{12,13,14,15},{16,17,18,19},{20,21,22,2..., dimensions={0}, use_global_device_ids=true | all-gather | bytes 81920 | tf_op jit(solution)/shard_map/all_gather | solution.py:81
  110.3 19.7 %all_gather.15 = bf16[1024,256]{1,0:T(8,128)(2,1)S(1)} all-gather(bf16[128,256]{1,0:T(8,128)(2,1)S(1)} %all_gather.14), channel_id=1, replica_groups={{0,4,8,12,16,20,24,28},{1,5,9,13,17,21,25,29},{2,6,10,14,18,22,26,30},{..., dimensions={0}, use_global_device_ids=true | all-gather | bytes 589824 | tf_op jit(solution)/shard_map/all_gather | solution.py:82
  135.1 14.7 %all-to-all-start.2 = ((bf16[32,32,256]{2,1,0:T(8,128)(2,1)}), bf16[32,32,256]{2,1,0:T(8,128)(2,1)}, u32[]{:S(2)}, u32[]{:S(2)}) async-start(bf16[32,32,256]{2,1,0:T(8,128)(2,1)} %pad_maximum_fusion), calls=%async_computation.2 | async-start | bytes 1048576 | tf_op jit(solution)/shard_map/all_to_all | solution.py:73
  149.9 14.4 %all-to-all-done.2 = bf16[32,32,256]{2,1,0:T(8,128)(2,1)} async-done(((bf16[32,32,256]{2,1,0:T(8,128)(2,1)}), bf16[32,32,256]{2,1,0:T(8,128)(2,1)}, u32[]{:S(2)}, u32[]{:S(2)}) %all-to-all-start.2) | async-done | bytes 524320 | tf_op jit(solution)/shard_map/all_to_all | solution.py:73
  165.9 11.9 %all_to_all.34 = bf16[8,32,1024]{2,1,0:T(8,128)(2,1)S(1)} all-to-all(bf16[8,32,1024]{2,1,0:T(8,128)(2,1)S(1)} %broadcast_in_dim.8), channel_id=1, replica_groups=mesh['zslab'=8,'blk'=32] {'zslab'}, dimensions={0} | all-to-all | bytes 1048576 | tf_op jit(solution)/shard_map/all_to_all | solution.py:32
  177.9 4.2 %fusion.4 = bf16[32,32,64]{2,0,1:T(8,128)(2,1)S(1)} fusion(bf16[32,80,1024]{2,1,0:T(8,128)(2,1)} %bitcast.258, bf16[32,1024]{1,0:T(8,128)(2,1)S(1)} %reduce_sum.58), kind=kOutput, calls=%fused_computation.4 | convolution fusion | flops 134283264 | bytes 4390912 | tf_op jit(solution)/shard_map/td,bfd->tbf/dot_general | solution.py:226
  182.5 8.1 %all_to_all.35 = bf16[1,32,16,128]{3,2,0,1:T(8,128)(2,1)S(1)} all-to-all(bf16[1,32,16,128]{3,2,0,1:T(8,128)(2,1)S(1)} %bitcast.243), channel_id=1, replica_groups=mesh['zslab'=8,'blk'=32] {'zslab'}, dimensions={1} | all-to-all | bytes 262144 | tf_op jit(solution)/shard_map/all_to_all | solution.py:233
  199.5 5.8 %collective-permute-start.10 = (bf16[2,8,16,128]{3,2,1,0:T(8,128)(2,1)S(1)}, bf16[2,8,16,128]{3,2,1,0:T(8,128)(2,1)S(1)}, u32[]{:S(2)}, u32[]{:S(2)}) collective-permute-start(bf16[2,8,16,128]{3,2,1,0:T(8,128)(2,1)S(1)} %get-tuple-element.26), channel_id=1, source_target_pairs={{1,0},{2,1},{3,2},{4,3},{5,4},{6,5},{7,6},{8,7},{9,8},{10,9},{11,1... | collective-permute-start | bytes 196616 | tf_op jit(solution)/shard_map/ppermute | solution.py:23
  205.3 5.4 %collective-permute-start.11 = (bf16[2,8,16,128]{3,2,1,0:T(8,128)(2,1)S(1)}, bf16[2,8,16,128]{3,2,1,0:T(8,128)(2,1)S(1)}, u32[]{:S(2)}, u32[]{:S(2)}) collective-permute-start(bf16[2,8,16,128]{3,2,1,0:T(8,128)(2,1)S(1)} %get-tuple-element.25), channel_id=1, source_target_pairs={{0,1},{1,2},{2,3},{3,4},{4,5},{5,6},{6,7},{7,8},{8,9},{9,10},{10,1... | collective-permute-start | bytes 196616 | tf_op jit(solution)/shard_map/ppermute | solution.py:21
  216.4 3.4 %collective-permute-start.13 = (bf16[8,2,16,128]{3,2,1,0:T(8,128)(2,1)S(1)}, bf16[8,2,16,128]{3,2,1,0:T(8,128)(2,1)S(1)}, u32[]{:S(2)}, u32[]{:S(2)}) collective-permute-start(bf16[8,2,16,128]{3,2,1,0:T(8,128)(2,1)S(1)} %get-tuple-element.36), channel_id=1, source_target_pairs={{32,0},{64,32},{96,64},{128,96},{160,128},{192,160},{224,192},{33,... | collective-permute-start | bytes 196616 | tf_op jit(solution)/shard_map/ppermute | solution.py:23
  222.3 3.6 %collective-permute-start.14 = (bf16[2,8,16,128]{3,2,1,0:T(8,128)(2,1)S(1)}, bf16[2,8,16,128]{3,2,1,0:T(8,128)(2,1)S(1)}, u32[]{:S(2)}, u32[]{:S(2)}) collective-permute-start(bf16[2,8,16,128]{3,2,1,0:T(8,128)(2,1)S(1)} %get-tuple-element.22), channel_id=1, source_target_pairs={{1,0},{2,1},{3,2},{4,3},{5,4},{6,5},{7,6},{8,7},{9,8},{10,9},{11,1... | collective-permute-start | bytes 196616 | tf_op jit(solution)/shard_map/ppermute | solution.py:23
  226.0 7.3 %collective-permute-start.15 = (bf16[2,8,16,128]{3,2,1,0:T(8,128)(2,1)S(1)}, bf16[2,8,16,128]{3,2,1,0:T(8,128)(2,1)S(1)}, u32[]{:S(2)}, u32[]{:S(2)}) collective-permute-start(bf16[2,8,16,128]{3,2,1,0:T(8,128)(2,1)S(1)} %get-tuple-element.21), channel_id=1, source_target_pairs={{0,1},{1,2},{2,3},{3,4},{4,5},{5,6},{6,7},{7,8},{8,9},{9,10},{10,1... | collective-permute-start | bytes 196616 | tf_op jit(solution)/shard_map/ppermute | solution.py:21
  (157 shorter events, 54.3 us)
Async XLA Ops:
  6.5 12.0 %copy-start.1 = (bf16[8,16,4,128]{3,2,1,0:T(4,128)(2,1)S(1)}, bf16[8,16,4,128]{3,2,1,0:T(4,128)(2,1)}, u32[]{:S(2)}) copy-start(bf16[8,16,4,128]{3,2,1,0:T(4,128)(2,1)} %param.7) | copy-start | bytes 393220
  6.5 77.6 %all-gather.2.cloned.1.call-start = ((), (), s32[]{:S(2)}) async-start(), calls=%async_computation.5 | async-start | bytes 5898240 | tf_op jit(solution)/shard_map/all_gather | solution.py:82
  7.4 16.7 %copy-start = (bf16[2,3456,128]{2,1,0:T(8,128)(2,1)S(1)}, bf16[2,3456,128]{2,1,0:T(8,128)(2,1)}, u32[]{:S(2)}) copy-start(bf16[2,3456,128]{2,1,0:T(8,128)(2,1)} %param.10) | copy-start | bytes 5308420
  18.6 6.3 %collective-permute-start = (bf16[8,2,16,128]{3,2,1,0:T(8,128)(2,1)S(1)}, bf16[8,2,16,128]{3,2,1,0:T(8,128)(2,1)S(1)}, u32[]{:S(2)}, u32[]{:S(2)}) collective-permute-start(bf16[8,2,16,128]{3,2,1,0:T(8,128)(2,1)S(1)} %get-tuple-element.41), channel_id=1, source_target_pairs={{0,32},{32,64},{64,96},{96,128},{128,160},{160,192},{192,224},{1,3... | collective-permute-start | bytes 196616 | tf_op jit(solution)/shard_map/ppermute | solution.py:21
  22.1 5.9 %collective-permute-start.1 = (bf16[8,2,16,128]{3,2,1,0:T(8,128)(2,1)S(1)}, bf16[8,2,16,128]{3,2,1,0:T(8,128)(2,1)S(1)}, u32[]{:S(2)}, u32[]{:S(2)}) collective-permute-start(bf16[8,2,16,128]{3,2,1,0:T(8,128)(2,1)S(1)} %get-tuple-element.42), channel_id=1, source_target_pairs={{32,0},{64,32},{96,64},{128,96},{160,128},{192,160},{224,192},{33,... | collective-permute-start | bytes 196616 | tf_op jit(solution)/shard_map/ppermute | solution.py:23
  24.2 13.0 %copy-start.5 = (s32[2,3]{1,0:T(2,128)S(1)}, s32[2,3]{1,0:T(2,128)}, u32[]{:S(2)}) copy-start(s32[2,3]{1,0:T(2,128)} %param.9) | copy-start | bytes 76
  28.0 11.7 %collective-permute-start.2 = (bf16[2,8,16,128]{3,2,1,0:T(8,128)(2,1)S(1)}, bf16[2,8,16,128]{3,2,1,0:T(8,128)(2,1)S(1)}, u32[]{:S(2)}, u32[]{:S(2)}) collective-permute-start(bf16[2,8,16,128]{3,2,1,0:T(8,128)(2,1)S(1)} %get-tuple-element.34), channel_id=1, source_target_pairs={{0,1},{1,2},{2,3},{3,4},{4,5},{5,6},{6,7},{7,8},{8,9},{9,10},{10,1... | collective-permute-start | bytes 196616 | tf_op jit(solution)/shard_map/ppermute | solution.py:21
  35.2 10.6 %collective-permute-start.3 = (bf16[2,8,16,128]{3,2,1,0:T(8,128)(2,1)S(1)}, bf16[2,8,16,128]{3,2,1,0:T(8,128)(2,1)S(1)}, u32[]{:S(2)}, u32[]{:S(2)}) collective-permute-start(bf16[2,8,16,128]{3,2,1,0:T(8,128)(2,1)S(1)} %get-tuple-element.33), channel_id=1, source_target_pairs={{1,0},{2,1},{3,2},{4,3},{5,4},{6,5},{7,6},{8,7},{9,8},{10,9},{11,1... | collective-permute-start | bytes 196616 | tf_op jit(solution)/shard_map/ppermute | solution.py:23
  49.3 5.4 %collective-permute-start.4 = (bf16[8,2,16,128]{3,2,1,0:T(8,128)(2,1)S(1)}, bf16[8,2,16,128]{3,2,1,0:T(8,128)(2,1)S(1)}, u32[]{:S(2)}, u32[]{:S(2)}) collective-permute-start(bf16[8,2,16,128]{3,2,1,0:T(8,128)(2,1)S(1)} %get-tuple-element.39), channel_id=1, source_target_pairs={{0,32},{32,64},{64,96},{96,128},{128,160},{160,192},{192,224},{1,3... | collective-permute-start | bytes 196616 | tf_op jit(solution)/shard_map/ppermute | solution.py:21
  51.2 6.4 %collective-permute-start.5 = (bf16[8,2,16,128]{3,2,1,0:T(8,128)(2,1)S(1)}, bf16[8,2,16,128]{3,2,1,0:T(8,128)(2,1)S(1)}, u32[]{:S(2)}, u32[]{:S(2)}) collective-permute-start(bf16[8,2,16,128]{3,2,1,0:T(8,128)(2,1)S(1)} %get-tuple-element.40), channel_id=1, source_target_pairs={{32,0},{64,32},{96,64},{128,96},{160,128},{192,160},{224,192},{33,... | collective-permute-start | bytes 196616 | tf_op jit(solution)/shard_map/ppermute | solution.py:23
  57.7 6.5 %collective-permute-start.6 = (bf16[2,8,16,128]{3,2,1,0:T(8,128)(2,1)S(1)}, bf16[2,8,16,128]{3,2,1,0:T(8,128)(2,1)S(1)}, u32[]{:S(2)}, u32[]{:S(2)}) collective-permute-start(bf16[2,8,16,128]{3,2,1,0:T(8,128)(2,1)S(1)} %get-tuple-element.30), channel_id=1, source_target_pairs={{0,1},{1,2},{2,3},{3,4},{4,5},{5,6},{6,7},{7,8},{8,9},{9,10},{10,1... | collective-permute-start | bytes 196616 | tf_op jit(solution)/shard_map/ppermute | solution.py:21
  60.3 10.6 %collective-permute-start.7 = (bf16[2,8,16,128]{3,2,1,0:T(8,128)(2,1)S(1)}, bf16[2,8,16,128]{3,2,1,0:T(8,128)(2,1)S(1)}, u32[]{:S(2)}, u32[]{:S(2)}) collective-permute-start(bf16[2,8,16,128]{3,2,1,0:T(8,128)(2,1)S(1)} %get-tuple-element.29), channel_id=1, source_target_pairs={{1,0},{2,1},{3,2},{4,3},{5,4},{6,5},{7,6},{8,7},{9,8},{10,9},{11,1... | collective-permute-start | bytes 196616 | tf_op jit(solution)/shard_map/ppermute | solution.py:23
  88.0 13.2 %all-to-all-start.1 = ((bf16[8,32,1024]{2,1,0:T(8,128)(2,1)}), bf16[8,32,1024]{2,1,0:T(8,128)(2,1)S(1)}, u32[]{:S(2)}, u32[]{:S(2)}) async-start(bf16[8,32,1024]{2,1,0:T(8,128)(2,1)} %broadcast_in_dim.7), calls=%async_computation.1 | async-start | bytes 1048576 | tf_op jit(solution)/shard_map/all_to_all | solution.py:32
  101.3 29.2 %copy-start.6 = (bf16[32,128]{1,0:T(8,128)(2,1)S(1)}, bf16[32,128]{1,0:T(8,128)(2,1)}, u32[]{:S(2)}) copy-start(bf16[32,128]{1,0:T(8,128)(2,1)} %param.13) | copy-start | bytes 24580
  135.1 29.3 %all-to-all-start.2 = ((bf16[32,32,256]{2,1,0:T(8,128)(2,1)}), bf16[32,32,256]{2,1,0:T(8,128)(2,1)}, u32[]{:S(2)}, u32[]{:S(2)}) async-start(bf16[32,32,256]{2,1,0:T(8,128)(2,1)} %pad_maximum_fusion), calls=%async_computation.2 | async-start | bytes 1048576 | tf_op jit(solution)/shard_map/all_to_all | solution.py:73
  182.2 8.4 %copy-start.3 = (f32[8,4,16,128]{3,2,1,0:T(8,128)S(1)}, f32[8,4,16,128]{3,2,1,0:T(8,128)}, u32[]{:S(2)}) copy-start(f32[8,4,16,128]{3,2,1,0:T(8,128)} %get-tuple-element.56) | copy-start | bytes 786436
  190.8 6.6 %collective-permute-start.8 = (bf16[8,2,16,128]{3,2,1,0:T(8,128)(2,1)S(1)}, bf16[8,2,16,128]{3,2,1,0:T(8,128)(2,1)S(1)}, u32[]{:S(2)}, u32[]{:S(2)}) collective-permute-start(bf16[8,2,16,128]{3,2,1,0:T(8,128)(2,1)S(1)} %get-tuple-element.37), channel_id=1, source_target_pairs={{0,32},{32,64},{64,96},{96,128},{128,160},{160,192},{192,224},{1,3... | collective-permute-start | bytes 196616 | tf_op jit(solution)/shard_map/ppermute | solution.py:21
  193.5 5.9 %collective-permute-start.9 = (bf16[8,2,16,128]{3,2,1,0:T(8,128)(2,1)S(1)}, bf16[8,2,16,128]{3,2,1,0:T(8,128)(2,1)S(1)}, u32[]{:S(2)}, u32[]{:S(2)}) collective-permute-start(bf16[8,2,16,128]{3,2,1,0:T(8,128)(2,1)S(1)} %get-tuple-element.38), channel_id=1, source_target_pairs={{32,0},{64,32},{96,64},{128,96},{160,128},{192,160},{224,192},{33,... | collective-permute-start | bytes 196616 | tf_op jit(solution)/shard_map/ppermute | solution.py:23
  199.5 11.3 %collective-permute-start.10 = (bf16[2,8,16,128]{3,2,1,0:T(8,128)(2,1)S(1)}, bf16[2,8,16,128]{3,2,1,0:T(8,128)(2,1)S(1)}, u32[]{:S(2)}, u32[]{:S(2)}) collective-permute-start(bf16[2,8,16,128]{3,2,1,0:T(8,128)(2,1)S(1)} %get-tuple-element.26), channel_id=1, source_target_pairs={{1,0},{2,1},{3,2},{4,3},{5,4},{6,5},{7,6},{8,7},{9,8},{10,9},{11,1... | collective-permute-start | bytes 196616 | tf_op jit(solution)/shard_map/ppermute | solution.py:23
  205.3 6.6 %collective-permute-start.11 = (bf16[2,8,16,128]{3,2,1,0:T(8,128)(2,1)S(1)}, bf16[2,8,16,128]{3,2,1,0:T(8,128)(2,1)S(1)}, u32[]{:S(2)}, u32[]{:S(2)}) collective-permute-start(bf16[2,8,16,128]{3,2,1,0:T(8,128)(2,1)S(1)} %get-tuple-element.25), channel_id=1, source_target_pairs={{0,1},{1,2},{2,3},{3,4},{4,5},{5,6},{6,7},{7,8},{8,9},{9,10},{10,1... | collective-permute-start | bytes 196616 | tf_op jit(solution)/shard_map/ppermute | solution.py:21
  214.5 6.6 %collective-permute-start.12 = (bf16[8,2,16,128]{3,2,1,0:T(8,128)(2,1)S(1)}, bf16[8,2,16,128]{3,2,1,0:T(8,128)(2,1)S(1)}, u32[]{:S(2)}, u32[]{:S(2)}) collective-permute-start(bf16[8,2,16,128]{3,2,1,0:T(8,128)(2,1)S(1)} %get-tuple-element.35), channel_id=1, source_target_pairs={{0,32},{32,64},{64,96},{96,128},{128,160},{160,192},{192,224},{1,3... | collective-permute-start | bytes 196616 | tf_op jit(solution)/shard_map/ppermute | solution.py:21
  216.4 5.9 %collective-permute-start.13 = (bf16[8,2,16,128]{3,2,1,0:T(8,128)(2,1)S(1)}, bf16[8,2,16,128]{3,2,1,0:T(8,128)(2,1)S(1)}, u32[]{:S(2)}, u32[]{:S(2)}) collective-permute-start(bf16[8,2,16,128]{3,2,1,0:T(8,128)(2,1)S(1)} %get-tuple-element.36), channel_id=1, source_target_pairs={{32,0},{64,32},{96,64},{128,96},{160,128},{192,160},{224,192},{33,... | collective-permute-start | bytes 196616 | tf_op jit(solution)/shard_map/ppermute | solution.py:23
  222.3 11.1 %collective-permute-start.14 = (bf16[2,8,16,128]{3,2,1,0:T(8,128)(2,1)S(1)}, bf16[2,8,16,128]{3,2,1,0:T(8,128)(2,1)S(1)}, u32[]{:S(2)}, u32[]{:S(2)}) collective-permute-start(bf16[2,8,16,128]{3,2,1,0:T(8,128)(2,1)S(1)} %get-tuple-element.22), channel_id=1, source_target_pairs={{1,0},{2,1},{3,2},{4,3},{5,4},{6,5},{7,6},{8,7},{9,8},{10,9},{11,1... | collective-permute-start | bytes 196616 | tf_op jit(solution)/shard_map/ppermute | solution.py:23
  226.0 8.7 %collective-permute-start.15 = (bf16[2,8,16,128]{3,2,1,0:T(8,128)(2,1)S(1)}, bf16[2,8,16,128]{3,2,1,0:T(8,128)(2,1)S(1)}, u32[]{:S(2)}, u32[]{:S(2)}) collective-permute-start(bf16[2,8,16,128]{3,2,1,0:T(8,128)(2,1)S(1)} %get-tuple-element.21), channel_id=1, source_target_pairs={{0,1},{1,2},{2,3},{3,4},{4,5},{5,6},{6,7},{7,8},{8,9},{9,10},{10,1... | collective-permute-start | bytes 196616 | tf_op jit(solution)/shard_map/ppermute | solution.py:21
  (3 other events, 2.6 us)
Sparse Core Ops, SparseCore 0:
  18.7 65.3 all-gather.1

commit v10 on v7

--- a/solution.py
+++ b/solution.py
@@ -227,22 +227,35 @@
         2, 1, 4, 0, 3, 5
     )
     grid_grad = grid_grad.reshape(x_local, z_total, y_cells, channels)
-    grid_grad = lax.all_to_all(grid_grad, "zslab", split_axis=1, concat_axis=0, tiled=True)
+    slabs = lax.axis_size("zslab")
+    grid_grad = jnp.pad(grid_grad, ((0, 0), (DMAX, DMAX), (0, 0), (0, 0)))
+    grid_grad = jnp.stack(
+        [grid_grad[:, k * z_cells : (k + 1) * z_cells + 2 * DMAX] for k in range(slabs)]
+    )
+    wide_grad = lax.all_to_all(grid_grad, "zslab", split_axis=0, concat_axis=1, tiled=True)
+    wide_grad = wide_grad.reshape(x_cells, z_cells + 2 * DMAX, y_cells, channels)
+    grid_grad = wide_grad[:, DMAX : DMAX + z_cells]
     for layer_num in reversed(range(LAYERS)):
         conv_out = conv_outs[layer_num]
         sigma = jax.nn.sigmoid(conv_out)
-        slope_grad = (
-            gate_mask * sigma * (1.0 + conv_out * (1.0 - sigma)) * grid_grad.astype(jnp.float32)
-        ).astype(jnp.bfloat16)
+        if layer_num == LAYERS - 1:
+            slope = padded_2(
+                gate_mask * sigma * (1.0 + conv_out * (1.0 - sigma)), (("zslab", 1),), DMAX
+            )
+            slope_grad = (slope * wide_grad.astype(jnp.float32)).astype(jnp.bfloat16)
+            padded = padded_2(slope_grad, (("blk", 0),), DMAX)
+        else:
+            slope_grad = (
+                gate_mask * sigma * (1.0 + conv_out * (1.0 - sigma)) * grid_grad.astype(jnp.float32)
+            ).astype(jnp.bfloat16)
+            padded = with_rim(slope_grad)
         flipped = (
             conv_weight[layer_num]
             .reshape(27, channels, channels)
             .transpose(0, 2, 1)
             .reshape(27 * channels, channels)
         )
-        backward = apply_offsets(
-            with_rim(slope_grad), flipped, dilation[layer_num], -1, field.shape
-        )
+        backward = apply_offsets(padded, flipped, dilation[layer_num], -1, field.shape)
         grid_grad = (grid_grad.astype(jnp.float32) + backward).astype(jnp.bfloat16)
     return grid_grad.transpose(0, 2, 1, 3)
 

time: 239 us -> 242 us (1.013)
  blocking collectives: 64.7 us -> 56.5 us
  local copies, waits for them, and re-layouts: 13.9 us -> 18.8 us
  starting transfers between devices: 70.5 us -> 74.8 us
    all_to_all x1 -> x0, blocking collectives: 8.11 us -> none  [local(): lax.all_to_all(grid_grad, 'zslab', split_axis=1, concat_axis=0, tiled=True)]
    unnamed x29 -> x36, local copies, waits for them, and re-layouts: 2.14 us -> 6.42 us
    all_to_all x0 -> x1, starting transfers between devices: none -> 4.1 us  [local(): lax.all_to_all(grid_grad, 'zslab', split_axis=0, concat_axis=1, tiled=True)]
  transfers between devices with their start and end apart: 19 -> 20, of which waited for: 12 -> 12; matrix products, arithmetic and copies ran while one was open for 6% -> 6% of each run, Pallas kernels for 0% -> 0%
where the time goes in v10:
time: 242 us; the launch traced here: 238 us
  starting transfers between devices  74.8 us (31%)
  blocking collectives  56.5 us (23%)
  waiting for transfers between devices  45.3 us (19%)
  local copies, waits for them, and re-layouts  18.8 us (8%)
  between operations  18 us (7%)
  matrix products  17.5 us (7%)
  other arithmetic  7.17 us (3%)
    all_to_all x2, blocking collectives, copy_for_each(): lax.all_to_all(jnp.broadcast_to(shard[None], (peers, *shard.shape)), axis...  37.2 us
    ppermute x8, starting transfers between devices, padded_2(): lax.ppermute(tail, axis, [(i, (i + 1) % count) for i in range(ends)])  34 us
    ppermute x8, waiting for transfers between devices, padded_2(): lax.ppermute(head, axis, [((i + 1) % count, i) for i in range(ends)])  23.8 us
    ppermute x8, starting transfers between devices, padded_2(): lax.ppermute(head, axis, [((i + 1) % count, i) for i in range(ends)])  23.3 us
    all_to_all x1, waiting for transfers between devices, sum_at_owner(): lax.all_to_all(cut_along(shard, dim, peers), axis, 0, 0, tiled=True)  14.4 us
    all_gather x1, blocking collectives, gather_weights(): lax.all_gather(rows, 'blk', axis=0, tiled=True, axis_index_groups=near)  9.96 us
    all_to_all x1, blocking collectives, local(): lax.all_to_all(hidden, 'zslab', split_axis=0, concat_axis=1, tiled=True)  9.42 us
    all_to_all x1, starting transfers between devices, sum_at_owner(): lax.all_to_all(cut_along(shard, dim, peers), axis, 0, 0, tiled=True)  8.21 us
  transfers between devices with their start and end apart: 20, of which 12 were waited for; matrix products, arithmetic and copies ran while one was open for 6% of the time, Pallas kernels for 0%

profile of v10, /device:TPU:103, one launch (start us, length us, event | category | flops | bytes accessed | tf_op | source)
XLA Modules:
  0.0 238.2 jit_solution(14635419716332051972)
XLA Ops:
  8.6 10.0 %all_gather.6 = bf16[320,1024]{1,0:T(8,128)(2,1)} all-gather(bf16[80,1024]{1,0:T(8,128)(2,1)S(1)} %maximum_maximum_fusion.3), channel_id=1, replica_groups={{0,1,2,3},{4,5,6,7},{8,9,10,11},{12,13,14,15},{16,17,18,19},{20,21,22,2..., dimensions={0}, use_global_device_ids=true | all-gather | bytes 819200 | tf_op jit(solution)/shard_map/all_gather | solution.py:87
  18.6 3.5 %collective-permute-start = (bf16[8,2,16,128]{3,2,1,0:T(8,128)(2,1)S(1)}, bf16[8,2,16,128]{3,2,1,0:T(8,128)(2,1)S(1)}, u32[]{:S(2)}, u32[]{:S(2)}) collective-permute-start(bf16[8,2,16,128]{3,2,1,0:T(8,128)(2,1)S(1)} %get-tuple-element.43), channel_id=1, source_target_pairs={{0,32},{32,64},{64,96},{96,128},{128,160},{160,192},{192,224},{1,3... | collective-permute-start | bytes 196616 | tf_op jit(solution)/shard_map/ppermute | solution.py:21
  24.9 3.1 %collective-permute-done.1 = bf16[8,2,16,128]{3,2,1,0:T(8,128)(2,1)S(1)} collective-permute-done((bf16[8,2,16,128]{3,2,1,0:T(8,128)(2,1)S(1)}, bf16[8,2,16,128]{3,2,1,0:T(8,128)(2,1)S(1)}, u32[]{:S(2)}, u32[]{:S(2)}) %collective-permute-start.1) | collective-permute-done | bytes 65568 | tf_op jit(solution)/shard_map/ppermute | solution.py:23
  28.0 7.2 %collective-permute-start.2 = (bf16[2,8,16,128]{3,2,1,0:T(8,128)(2,1)S(1)}, bf16[2,8,16,128]{3,2,1,0:T(8,128)(2,1)S(1)}, u32[]{:S(2)}, u32[]{:S(2)}) collective-permute-start(bf16[2,8,16,128]{3,2,1,0:T(8,128)(2,1)S(1)} %get-tuple-element.38), channel_id=1, source_target_pairs={{0,1},{1,2},{2,3},{3,4},{4,5},{5,6},{6,7},{7,8},{8,9},{9,10},{10,1... | collective-permute-start | bytes 196616 | tf_op jit(solution)/shard_map/ppermute | solution.py:21
  39.7 6.1 %collective-permute-done.3 = bf16[2,8,16,128]{3,2,1,0:T(8,128)(2,1)S(1)} collective-permute-done((bf16[2,8,16,128]{3,2,1,0:T(8,128)(2,1)S(1)}, bf16[2,8,16,128]{3,2,1,0:T(8,128)(2,1)S(1)}, u32[]{:S(2)}, u32[]{:S(2)}) %collective-permute-start.3) | collective-permute-done | bytes 65568 | tf_op jit(solution)/shard_map/ppermute | solution.py:23
  51.2 3.4 %collective-permute-start.5 = (bf16[8,2,16,128]{3,2,1,0:T(8,128)(2,1)S(1)}, bf16[8,2,16,128]{3,2,1,0:T(8,128)(2,1)S(1)}, u32[]{:S(2)}, u32[]{:S(2)}) collective-permute-start(bf16[8,2,16,128]{3,2,1,0:T(8,128)(2,1)S(1)} %get-tuple-element.42), channel_id=1, source_target_pairs={{32,0},{64,32},{96,64},{128,96},{160,128},{192,160},{224,192},{33,... | collective-permute-start | bytes 196616 | tf_op jit(solution)/shard_map/ppermute | solution.py:23
  54.7 2.9 %collective-permute-done.5 = bf16[8,2,16,128]{3,2,1,0:T(8,128)(2,1)S(1)} collective-permute-done((bf16[8,2,16,128]{3,2,1,0:T(8,128)(2,1)S(1)}, bf16[8,2,16,128]{3,2,1,0:T(8,128)(2,1)S(1)}, u32[]{:S(2)}, u32[]{:S(2)}) %collective-permute-start.5) | collective-permute-done | bytes 65568 | tf_op jit(solution)/shard_map/ppermute | solution.py:23
  64.2 6.7 %collective-permute-done.7 = bf16[2,8,16,128]{3,2,1,0:T(8,128)(2,1)S(1)} collective-permute-done((bf16[2,8,16,128]{3,2,1,0:T(8,128)(2,1)S(1)}, bf16[2,8,16,128]{3,2,1,0:T(8,128)(2,1)S(1)}, u32[]{:S(2)}, u32[]{:S(2)}) %collective-permute-start.7) | collective-permute-done | bytes 65568 | tf_op jit(solution)/shard_map/ppermute | solution.py:23
  73.8 9.4 %all_to_all.38 = bf16[8,4,16,128]{3,2,1,0:T(8,128)(2,1)S(1)} all-to-all(bf16[8,4,16,128]{3,2,1,0:T(8,128)(2,1)S(1)} %get-tuple-element.19), channel_id=1, replica_groups=mesh['zslab'=8,'blk'=32] {'zslab'}, dimensions={0} | all-to-all | bytes 262144 | tf_op jit(solution)/shard_map/all_to_all | solution.py:160
  84.1 3.0 %fusion.26 = bf16[32,1024]{1,0:T(8,128)(2,1)S(1)} fusion(bf16[32,80,1024]{2,1,0:T(8,128)(2,1)} %bitcast.297, bf16[32,32,64]{2,1,0:T(8,128)(2,1)S(1)} %reshape_reshape.9), kind=kOutput, calls=%fused_computation.31 | convolution fusion | flops 134250496 | bytes 4390912 | tf_op jit(solution)/shard_map/tbf,bfd->td/dot_general | solution.py:169
  88.0 5.2 %all-to-all-start.1 = ((bf16[8,32,1024]{2,1,0:T(8,128)(2,1)}), bf16[8,32,1024]{2,1,0:T(8,128)(2,1)S(1)}, u32[]{:S(2)}, u32[]{:S(2)}) async-start(bf16[8,32,1024]{2,1,0:T(8,128)(2,1)} %broadcast_in_dim.9), calls=%async_computation.1 | async-start | bytes 1048576 | tf_op jit(solution)/shard_map/all_to_all | solution.py:32
  97.1 4.0 %all-to-all-done.1 = bf16[8,32,1024]{2,1,0:T(8,128)(2,1)S(1)} async-done(((bf16[8,32,1024]{2,1,0:T(8,128)(2,1)}), bf16[8,32,1024]{2,1,0:T(8,128)(2,1)S(1)}, u32[]{:S(2)}, u32[]{:S(2)}) %all-to-all-start.1) | async-done | bytes 524320 | tf_op jit(solution)/shard_map/all_to_all | solution.py:32
  101.6 25.2 %all_to_all.39 = bf16[32,32,256]{2,1,0:T(8,128)(2,1)S(1)} all-to-all(bf16[32,32,256]{2,1,0:T(8,128)(2,1)S(1)} %broadcast_in_dim.10), channel_id=1, replica_groups=mesh['zslab'=8,'blk'=32] {'blk'}, dimensions={0} | all-to-all | bytes 1048576 | tf_op jit(solution)/shard_map/all_to_all | solution.py:32
  131.9 8.2 %all-to-all-start.3 = ((bf16[32,32,256]{2,1,0:T(8,128)(2,1)}), bf16[32,32,256]{2,1,0:T(8,128)(2,1)}, u32[]{:S(2)}, u32[]{:S(2)}) async-start(bf16[32,32,256]{2,1,0:T(8,128)(2,1)} %pad_maximum_fusion), calls=%async_computation.3 | async-start | bytes 1048576 | tf_op jit(solution)/shard_map/all_to_all | solution.py:73
  140.3 14.4 %all-to-all-done.3 = bf16[32,32,256]{2,1,0:T(8,128)(2,1)} async-done(((bf16[32,32,256]{2,1,0:T(8,128)(2,1)}), bf16[32,32,256]{2,1,0:T(8,128)(2,1)}, u32[]{:S(2)}, u32[]{:S(2)}) %all-to-all-start.3) | async-done | bytes 524320 | tf_op jit(solution)/shard_map/all_to_all | solution.py:73
  156.3 11.9 %all_to_all.40 = bf16[8,32,1024]{2,1,0:T(8,128)(2,1)S(1)} all-to-all(bf16[8,32,1024]{2,1,0:T(8,128)(2,1)S(1)} %broadcast_in_dim.11), channel_id=1, replica_groups=mesh['zslab'=8,'blk'=32] {'zslab'}, dimensions={0} | all-to-all | bytes 1048576 | tf_op jit(solution)/shard_map/all_to_all | solution.py:32
  168.3 4.2 %fusion.4 = bf16[32,32,64]{2,0,1:T(8,128)(2,1)S(1)} fusion(bf16[32,80,1024]{2,1,0:T(8,128)(2,1)} %bitcast.299, bf16[32,1024]{1,0:T(8,128)(2,1)S(1)} %reduce_sum.58), kind=kOutput, calls=%fused_computation.4 | convolution fusion | flops 134283264 | bytes 4390912 | tf_op jit(solution)/shard_map/td,bfd->tbf/dot_general | solution.py:223
  177.7 4.1 %all-to-all-start.5 = ((bf16[8,1,8,16,128]{4,3,2,1,0:T(8,128)(2,1)}), bf16[8,1,8,16,128]{4,3,2,1,0:T(8,128)(2,1)S(1)}, u32[]{:S(2)}, u32[]{:S(2)}) async-start(bf16[8,1,8,16,128]{4,3,2,1,0:T(8,128)(2,1)} %constant_dynamic-update-slice_fusion.2), calls=%async_computation.5 | async-start | bytes 524288 | tf_op jit(solution)/shard_map/all_to_all | solution.py:235
  181.8 3.1 %collective-permute-start.8 = (f32[8,2,16,128]{3,2,1,0:T(8,128)S(1)}, f32[8,2,16,128]{3,2,1,0:T(8,128)}, u32[]{:S(2)}, u32[]{:S(2)}) collective-permute-start(f32[8,2,16,128]{3,2,1,0:T(8,128)S(1)} %get-tuple-element.29), channel_id=1, source_target_pairs={{0,32},{32,64},{64,96},{96,128},{128,160},{160,192},{192,224},{1,3... | collective-permute-start | bytes 393224 | tf_op jit(solution)/shard_map/ppermute | solution.py:21
  189.1 3.2 %collective-permute-done.9 = f32[8,2,16,128]{3,2,1,0:T(8,128)} collective-permute-done((f32[8,2,16,128]{3,2,1,0:T(8,128)S(1)}, f32[8,2,16,128]{3,2,1,0:T(8,128)}, u32[]{:S(2)}, u32[]{:S(2)}) %collective-permute-start.9) | collective-permute-done | bytes 131104 | tf_op jit(solution)/shard_map/ppermute | solution.py:23
  193.4 4.6 %collective-permute-start.10 = (bf16[2,8,16,128]{3,2,1,0:T(8,128)(2,1)S(1)}, bf16[2,8,16,128]{3,2,1,0:T(8,128)(2,1)S(1)}, u32[]{:S(2)}, u32[]{:S(2)}) collective-permute-start(bf16[2,8,16,128]{3,2,1,0:T(8,128)(2,1)S(1)} %get-tuple-element.28), channel_id=1, source_target_pairs={{1,0},{2,1},{3,2},{4,3},{5,4},{6,5},{7,6},{8,7},{9,8},{10,9},{11,1... | collective-permute-start | bytes 196616 | tf_op jit(solution)/shard_map/ppermute | solution.py:23
  198.0 5.4 %collective-permute-start.11 = (bf16[2,8,16,128]{3,2,1,0:T(8,128)(2,1)S(1)}, bf16[2,8,16,128]{3,2,1,0:T(8,128)(2,1)S(1)}, u32[]{:S(2)}, u32[]{:S(2)}) collective-permute-start(bf16[2,8,16,128]{3,2,1,0:T(8,128)(2,1)S(1)} %get-tuple-element.27), channel_id=1, source_target_pairs={{0,1},{1,2},{2,3},{3,4},{4,5},{5,6},{6,7},{7,8},{8,9},{9,10},{10,1... | collective-permute-start | bytes 196616 | tf_op jit(solution)/shard_map/ppermute | solution.py:21
  215.4 3.9 %collective-permute-start.14 = (bf16[2,8,16,128]{3,2,1,0:T(8,128)(2,1)S(1)}, bf16[2,8,16,128]{3,2,1,0:T(8,128)(2,1)S(1)}, u32[]{:S(2)}, u32[]{:S(2)}) collective-permute-start(bf16[2,8,16,128]{3,2,1,0:T(8,128)(2,1)S(1)} %get-tuple-element.24), channel_id=1, source_target_pairs={{1,0},{2,1},{3,2},{4,3},{5,4},{6,5},{7,6},{8,7},{9,8},{10,9},{11,1... | collective-permute-start | bytes 196616 | tf_op jit(solution)/shard_map/ppermute | solution.py:23
  219.3 8.0 %collective-permute-start.15 = (bf16[2,8,16,128]{3,2,1,0:T(8,128)(2,1)S(1)}, bf16[2,8,16,128]{3,2,1,0:T(8,128)(2,1)S(1)}, u32[]{:S(2)}, u32[]{:S(2)}) collective-permute-start(bf16[2,8,16,128]{3,2,1,0:T(8,128)(2,1)S(1)} %get-tuple-element.23), channel_id=1, source_target_pairs={{0,1},{1,2},{2,3},{3,4},{4,5},{5,6},{6,7},{7,8},{8,9},{9,10},{10,1... | collective-permute-start | bytes 196616 | tf_op jit(solution)/shard_map/ppermute | solution.py:21
  (164 shorter events, 59.4 us)
Async XLA Ops:
  6.5 12.0 %copy-start.2 = (bf16[8,16,4,128]{3,2,1,0:T(4,128)(2,1)S(1)}, bf16[8,16,4,128]{3,2,1,0:T(4,128)(2,1)}, u32[]{:S(2)}) copy-start(bf16[8,16,4,128]{3,2,1,0:T(4,128)(2,1)} %param.7) | copy-start | bytes 393220
  6.5 77.6 %all-gather.2.cloned.1.call-start = ((), (), s32[]{:S(2)}) async-start(), calls=%async_computation.6 | async-start | bytes 5898240 | tf_op jit(solution)/shard_map/all_gather | solution.py:88
  7.4 16.7 %copy-start = (bf16[2,3456,128]{2,1,0:T(8,128)(2,1)S(1)}, bf16[2,3456,128]{2,1,0:T(8,128)(2,1)}, u32[]{:S(2)}) copy-start(bf16[2,3456,128]{2,1,0:T(8,128)(2,1)} %param.10) | copy-start | bytes 5308420
  18.6 6.3 %collective-permute-start = (bf16[8,2,16,128]{3,2,1,0:T(8,128)(2,1)S(1)}, bf16[8,2,16,128]{3,2,1,0:T(8,128)(2,1)S(1)}, u32[]{:S(2)}, u32[]{:S(2)}) collective-permute-start(bf16[8,2,16,128]{3,2,1,0:T(8,128)(2,1)S(1)} %get-tuple-element.43), channel_id=1, source_target_pairs={{0,32},{32,64},{64,96},{96,128},{128,160},{160,192},{192,224},{1,3... | collective-permute-start | bytes 196616 | tf_op jit(solution)/shard_map/ppermute | solution.py:21
  22.1 5.9 %collective-permute-start.1 = (bf16[8,2,16,128]{3,2,1,0:T(8,128)(2,1)S(1)}, bf16[8,2,16,128]{3,2,1,0:T(8,128)(2,1)S(1)}, u32[]{:S(2)}, u32[]{:S(2)}) collective-permute-start(bf16[8,2,16,128]{3,2,1,0:T(8,128)(2,1)S(1)} %get-tuple-element.44), channel_id=1, source_target_pairs={{32,0},{64,32},{96,64},{128,96},{160,128},{192,160},{224,192},{33,... | collective-permute-start | bytes 196616 | tf_op jit(solution)/shard_map/ppermute | solution.py:23
  24.2 13.0 %copy-start.5 = (s32[2,3]{1,0:T(2,128)S(1)}, s32[2,3]{1,0:T(2,128)}, u32[]{:S(2)}) copy-start(s32[2,3]{1,0:T(2,128)} %param.9) | copy-start | bytes 76
  28.0 11.6 %collective-permute-start.2 = (bf16[2,8,16,128]{3,2,1,0:T(8,128)(2,1)S(1)}, bf16[2,8,16,128]{3,2,1,0:T(8,128)(2,1)S(1)}, u32[]{:S(2)}, u32[]{:S(2)}) collective-permute-start(bf16[2,8,16,128]{3,2,1,0:T(8,128)(2,1)S(1)} %get-tuple-element.38), channel_id=1, source_target_pairs={{0,1},{1,2},{2,3},{3,4},{4,5},{5,6},{6,7},{7,8},{8,9},{9,10},{10,1... | collective-permute-start | bytes 196616 | tf_op jit(solution)/shard_map/ppermute | solution.py:21
  35.2 10.6 %collective-permute-start.3 = (bf16[2,8,16,128]{3,2,1,0:T(8,128)(2,1)S(1)}, bf16[2,8,16,128]{3,2,1,0:T(8,128)(2,1)S(1)}, u32[]{:S(2)}, u32[]{:S(2)}) collective-permute-start(bf16[2,8,16,128]{3,2,1,0:T(8,128)(2,1)S(1)} %get-tuple-element.37), channel_id=1, source_target_pairs={{1,0},{2,1},{3,2},{4,3},{5,4},{6,5},{7,6},{8,7},{9,8},{10,9},{11,1... | collective-permute-start | bytes 196616 | tf_op jit(solution)/shard_map/ppermute | solution.py:23
  49.3 5.4 %collective-permute-start.4 = (bf16[8,2,16,128]{3,2,1,0:T(8,128)(2,1)S(1)}, bf16[8,2,16,128]{3,2,1,0:T(8,128)(2,1)S(1)}, u32[]{:S(2)}, u32[]{:S(2)}) collective-permute-start(bf16[8,2,16,128]{3,2,1,0:T(8,128)(2,1)S(1)} %get-tuple-element.41), channel_id=1, source_target_pairs={{0,32},{32,64},{64,96},{96,128},{128,160},{160,192},{192,224},{1,3... | collective-permute-start | bytes 196616 | tf_op jit(solution)/shard_map/ppermute | solution.py:21
  51.2 6.4 %collective-permute-start.5 = (bf16[8,2,16,128]{3,2,1,0:T(8,128)(2,1)S(1)}, bf16[8,2,16,128]{3,2,1,0:T(8,128)(2,1)S(1)}, u32[]{:S(2)}, u32[]{:S(2)}) collective-permute-start(bf16[8,2,16,128]{3,2,1,0:T(8,128)(2,1)S(1)} %get-tuple-element.42), channel_id=1, source_target_pairs={{32,0},{64,32},{96,64},{128,96},{160,128},{192,160},{224,192},{33,... | collective-permute-start | bytes 196616 | tf_op jit(solution)/shard_map/ppermute | solution.py:23
  57.7 6.5 %collective-permute-start.6 = (bf16[2,8,16,128]{3,2,1,0:T(8,128)(2,1)S(1)}, bf16[2,8,16,128]{3,2,1,0:T(8,128)(2,1)S(1)}, u32[]{:S(2)}, u32[]{:S(2)}) collective-permute-start(bf16[2,8,16,128]{3,2,1,0:T(8,128)(2,1)S(1)} %get-tuple-element.34), channel_id=1, source_target_pairs={{0,1},{1,2},{2,3},{3,4},{4,5},{5,6},{6,7},{7,8},{8,9},{9,10},{10,1... | collective-permute-start | bytes 196616 | tf_op jit(solution)/shard_map/ppermute | solution.py:21
  60.3 10.6 %collective-permute-start.7 = (bf16[2,8,16,128]{3,2,1,0:T(8,128)(2,1)S(1)}, bf16[2,8,16,128]{3,2,1,0:T(8,128)(2,1)S(1)}, u32[]{:S(2)}, u32[]{:S(2)}) collective-permute-start(bf16[2,8,16,128]{3,2,1,0:T(8,128)(2,1)S(1)} %get-tuple-element.33), channel_id=1, source_target_pairs={{1,0},{2,1},{3,2},{4,3},{5,4},{6,5},{7,6},{8,7},{9,8},{10,9},{11,1... | collective-permute-start | bytes 196616 | tf_op jit(solution)/shard_map/ppermute | solution.py:23
  88.0 13.2 %all-to-all-start.1 = ((bf16[8,32,1024]{2,1,0:T(8,128)(2,1)}), bf16[8,32,1024]{2,1,0:T(8,128)(2,1)S(1)}, u32[]{:S(2)}, u32[]{:S(2)}) async-start(bf16[8,32,1024]{2,1,0:T(8,128)(2,1)} %broadcast_in_dim.9), calls=%async_computation.1 | async-start | bytes 1048576 | tf_op jit(solution)/shard_map/all_to_all | solution.py:32
  101.5 25.8 %copy-start.6 = (bf16[32,128]{1,0:T(8,128)(2,1)S(1)}, bf16[32,128]{1,0:T(8,128)(2,1)}, u32[]{:S(2)}) copy-start(bf16[32,128]{1,0:T(8,128)(2,1)} %param.13) | copy-start | bytes 24580
  131.9 22.8 %all-to-all-start.3 = ((bf16[32,32,256]{2,1,0:T(8,128)(2,1)}), bf16[32,32,256]{2,1,0:T(8,128)(2,1)}, u32[]{:S(2)}, u32[]{:S(2)}) async-start(bf16[32,32,256]{2,1,0:T(8,128)(2,1)} %pad_maximum_fusion), calls=%async_computation.3 | async-start | bytes 1048576 | tf_op jit(solution)/shard_map/all_to_all | solution.py:73
  177.7 14.6 %all-to-all-start.5 = ((bf16[8,1,8,16,128]{4,3,2,1,0:T(8,128)(2,1)}), bf16[8,1,8,16,128]{4,3,2,1,0:T(8,128)(2,1)S(1)}, u32[]{:S(2)}, u32[]{:S(2)}) async-start(bf16[8,1,8,16,128]{4,3,2,1,0:T(8,128)(2,1)} %constant_dynamic-update-slice_fusion.2), calls=%async_computation.5 | async-start | bytes 524288 | tf_op jit(solution)/shard_map/all_to_all | solution.py:235
  181.8 7.3 %collective-permute-start.8 = (f32[8,2,16,128]{3,2,1,0:T(8,128)S(1)}, f32[8,2,16,128]{3,2,1,0:T(8,128)}, u32[]{:S(2)}, u32[]{:S(2)}) collective-permute-start(f32[8,2,16,128]{3,2,1,0:T(8,128)S(1)} %get-tuple-element.29), channel_id=1, source_target_pairs={{0,32},{32,64},{64,96},{96,128},{128,160},{160,192},{192,224},{1,3... | collective-permute-start | bytes 393224 | tf_op jit(solution)/shard_map/ppermute | solution.py:21
  184.9 7.4 %collective-permute-start.9 = (f32[8,2,16,128]{3,2,1,0:T(8,128)S(1)}, f32[8,2,16,128]{3,2,1,0:T(8,128)}, u32[]{:S(2)}, u32[]{:S(2)}) collective-permute-start(f32[8,2,16,128]{3,2,1,0:T(8,128)S(1)} %get-tuple-element.30), channel_id=1, source_target_pairs={{32,0},{64,32},{96,64},{128,96},{160,128},{192,160},{224,192},{33,... | collective-permute-start | bytes 393224 | tf_op jit(solution)/shard_map/ppermute | solution.py:23
  193.4 10.1 %collective-permute-start.10 = (bf16[2,8,16,128]{3,2,1,0:T(8,128)(2,1)S(1)}, bf16[2,8,16,128]{3,2,1,0:T(8,128)(2,1)S(1)}, u32[]{:S(2)}, u32[]{:S(2)}) collective-permute-start(bf16[2,8,16,128]{3,2,1,0:T(8,128)(2,1)S(1)} %get-tuple-element.28), channel_id=1, source_target_pairs={{1,0},{2,1},{3,2},{4,3},{5,4},{6,5},{7,6},{8,7},{9,8},{10,9},{11,1... | collective-permute-start | bytes 196616 | tf_op jit(solution)/shard_map/ppermute | solution.py:23
  198.0 6.6 %collective-permute-start.11 = (bf16[2,8,16,128]{3,2,1,0:T(8,128)(2,1)S(1)}, bf16[2,8,16,128]{3,2,1,0:T(8,128)(2,1)S(1)}, u32[]{:S(2)}, u32[]{:S(2)}) collective-permute-start(bf16[2,8,16,128]{3,2,1,0:T(8,128)(2,1)S(1)} %get-tuple-element.27), channel_id=1, source_target_pairs={{0,1},{1,2},{2,3},{3,4},{4,5},{5,6},{6,7},{7,8},{8,9},{9,10},{10,1... | collective-permute-start | bytes 196616 | tf_op jit(solution)/shard_map/ppermute | solution.py:21
  207.1 6.6 %collective-permute-start.12 = (bf16[8,2,16,128]{3,2,1,0:T(8,128)(2,1)S(1)}, bf16[8,2,16,128]{3,2,1,0:T(8,128)(2,1)S(1)}, u32[]{:S(2)}, u32[]{:S(2)}) collective-permute-start(bf16[8,2,16,128]{3,2,1,0:T(8,128)(2,1)S(1)} %get-tuple-element.39), channel_id=1, source_target_pairs={{0,32},{32,64},{64,96},{96,128},{128,160},{160,192},{192,224},{1,3... | collective-permute-start | bytes 196616 | tf_op jit(solution)/shard_map/ppermute | solution.py:21
  209.5 5.9 %collective-permute-start.13 = (bf16[8,2,16,128]{3,2,1,0:T(8,128)(2,1)S(1)}, bf16[8,2,16,128]{3,2,1,0:T(8,128)(2,1)S(1)}, u32[]{:S(2)}, u32[]{:S(2)}) collective-permute-start(bf16[8,2,16,128]{3,2,1,0:T(8,128)(2,1)S(1)} %get-tuple-element.40), channel_id=1, source_target_pairs={{32,0},{64,32},{96,64},{128,96},{160,128},{192,160},{224,192},{33,... | collective-permute-start | bytes 196616 | tf_op jit(solution)/shard_map/ppermute | solution.py:23
  215.4 11.9 %collective-permute-start.14 = (bf16[2,8,16,128]{3,2,1,0:T(8,128)(2,1)S(1)}, bf16[2,8,16,128]{3,2,1,0:T(8,128)(2,1)S(1)}, u32[]{:S(2)}, u32[]{:S(2)}) collective-permute-start(bf16[2,8,16,128]{3,2,1,0:T(8,128)(2,1)S(1)} %get-tuple-element.24), channel_id=1, source_target_pairs={{1,0},{2,1},{3,2},{4,3},{5,4},{6,5},{7,6},{8,7},{9,8},{10,9},{11,1... | collective-permute-start | bytes 196616 | tf_op jit(solution)/shard_map/ppermute | solution.py:23
  219.3 9.3 %collective-permute-start.15 = (bf16[2,8,16,128]{3,2,1,0:T(8,128)(2,1)S(1)}, bf16[2,8,16,128]{3,2,1,0:T(8,128)(2,1)S(1)}, u32[]{:S(2)}, u32[]{:S(2)}) collective-permute-start(bf16[2,8,16,128]{3,2,1,0:T(8,128)(2,1)S(1)} %get-tuple-element.23), channel_id=1, source_target_pairs={{0,1},{1,2},{2,3},{3,4},{4,5},{5,6},{6,7},{7,8},{8,9},{9,10},{10,1... | collective-permute-start | bytes 196616 | tf_op jit(solution)/shard_map/ppermute | solution.py:21
  (4 other events, 11.9 us)
Sparse Core Ops, SparseCore 0:
  18.7 65.3 all-gather.1

commit v11 on v10

--- a/solution.py
+++ b/solution.py
@@ -157,6 +157,11 @@
         hidden = (
             hidden.astype(jnp.float32) + gate_mask * (conv_out * jax.nn.sigmoid(conv_out))
         ).astype(jnp.bfloat16)
+    sigma = jax.nn.sigmoid(conv_outs[-1])
+    slope = padded_2(
+        gate_mask * sigma * (1.0 + conv_outs[-1] * (1.0 - sigma)), (("zslab", 1),), DMAX
+    )
+    hidden, slope = lax.optimization_barrier((hidden, slope))
     slab_view = lax.all_to_all(hidden, "zslab", split_axis=0, concat_axis=1, tiled=True)
     x_local, z_total = (slab_view.shape[0], slab_view.shape[1])
     y_blocks, z_blocks = (y_cells // PY, z_total // PZ)
@@ -239,9 +244,6 @@
         conv_out = conv_outs[layer_num]
         sigma = jax.nn.sigmoid(conv_out)
         if layer_num == LAYERS - 1:
-            slope = padded_2(
-                gate_mask * sigma * (1.0 + conv_out * (1.0 - sigma)), (("zslab", 1),), DMAX
-            )
             slope_grad = (slope * wide_grad.astype(jnp.float32)).astype(jnp.bfloat16)
             padded = padded_2(slope_grad, (("blk", 0),), DMAX)
         else:

time: 242 us -> 240 us (level)
  blocking collectives: 56.5 us -> 52.6 us
  waiting for transfers between devices: 45.3 us -> 48.5 us
    all_to_all x1, waiting for transfers between devices: 0.01 us -> 3.97 us  [local(): lax.all_to_all(grid_grad, 'zslab', split_axis=0, concat_axis=1, tiled=True)]
    all_to_all x2, blocking collectives: 37.2 us -> 34.3 us  [copy_for_each(): lax.all_to_all(jnp.broadcast_to(shard[None], (peers, *shard.shape)), axis...]
    unnamed x36 -> x38, local copies, waits for them, and re-layouts: 6.42 us -> 6.8 us
  transfers between devices with their start and end apart: 20 -> 20, of which waited for: 12 -> 13; matrix products, arithmetic and copies ran while one was open for 6% -> 6% of each run, Pallas kernels for 0% -> 0%
where the time goes in v11:
time: 240 us; the launch traced here: 236 us
  starting transfers between devices  73.3 us (31%)
  blocking collectives  52.6 us (22%)
  waiting for transfers between devices  48.5 us (20%)
  local copies, waits for them, and re-layouts  19.2 us (8%)
  between operations  18.1 us (8%)
  matrix products  17.5 us (7%)
  other arithmetic  7.05 us (3%)
    all_to_all x2, blocking collectives, copy_for_each(): lax.all_to_all(jnp.broadcast_to(shard[None], (peers, *shard.shape)), axis...  34.3 us
    ppermute x8, starting transfers between devices, padded_2(): lax.ppermute(tail, axis, [(i, (i + 1) % count) for i in range(ends)])  31.9 us
    ppermute x8, starting transfers between devices, padded_2(): lax.ppermute(head, axis, [((i + 1) % count, i) for i in range(ends)])  24.6 us
    ppermute x8, waiting for transfers between devices, padded_2(): lax.ppermute(head, axis, [((i + 1) % count, i) for i in range(ends)])  23.9 us
    all_to_all x1, waiting for transfers between devices, sum_at_owner(): lax.all_to_all(cut_along(shard, dim, peers), axis, 0, 0, tiled=True)  14.4 us
    all_gather x1, blocking collectives, gather_weights(): lax.all_gather(rows, 'blk', axis=0, tiled=True, axis_index_groups=near)  9.96 us
    all_to_all x1, blocking collectives, local(): lax.all_to_all(hidden, 'zslab', split_axis=0, concat_axis=1, tiled=True)  8.34 us
    all_to_all x1, starting transfers between devices, sum_at_owner(): lax.all_to_all(cut_along(shard, dim, peers), axis, 0, 0, tiled=True)  8.22 us
  transfers between devices with their start and end apart: 20, of which 13 were waited for; matrix products, arithmetic and copies ran while one was open for 6% of the time, Pallas kernels for 0%

profile of v11, /device:TPU:103, one launch (start us, length us, event | category | flops | bytes accessed | tf_op | source)
XLA Modules:
  0.0 236.1 jit_solution(16266992251678625090)
XLA Ops:
  8.6 10.0 %all_gather.6 = bf16[320,1024]{1,0:T(8,128)(2,1)} all-gather(bf16[80,1024]{1,0:T(8,128)(2,1)S(1)} %maximum_maximum_fusion.3), channel_id=1, replica_groups={{0,1,2,3},{4,5,6,7},{8,9,10,11},{12,13,14,15},{16,17,18,19},{20,21,22,2..., dimensions={0}, use_global_device_ids=true | all-gather | bytes 819200 | tf_op jit(solution)/shard_map/all_gather | solution.py:87
  18.6 3.5 %collective-permute-start = (bf16[8,2,16,128]{3,2,1,0:T(8,128)(2,1)S(1)}, bf16[8,2,16,128]{3,2,1,0:T(8,128)(2,1)S(1)}, u32[]{:S(2)}, u32[]{:S(2)}) collective-permute-start(bf16[8,2,16,128]{3,2,1,0:T(8,128)(2,1)S(1)} %get-tuple-element.47), channel_id=1, source_target_pairs={{0,32},{32,64},{64,96},{96,128},{128,160},{160,192},{192,224},{1,3... | collective-permute-start | bytes 196616 | tf_op jit(solution)/shard_map/ppermute | solution.py:21
  24.9 3.1 %collective-permute-done.1 = bf16[8,2,16,128]{3,2,1,0:T(8,128)(2,1)S(1)} collective-permute-done((bf16[8,2,16,128]{3,2,1,0:T(8,128)(2,1)S(1)}, bf16[8,2,16,128]{3,2,1,0:T(8,128)(2,1)S(1)}, u32[]{:S(2)}, u32[]{:S(2)}) %collective-permute-start.1) | collective-permute-done | bytes 65568 | tf_op jit(solution)/shard_map/ppermute | solution.py:23
  28.0 7.2 %collective-permute-start.2 = (bf16[2,8,16,128]{3,2,1,0:T(8,128)(2,1)S(1)}, bf16[2,8,16,128]{3,2,1,0:T(8,128)(2,1)S(1)}, u32[]{:S(2)}, u32[]{:S(2)}) collective-permute-start(bf16[2,8,16,128]{3,2,1,0:T(8,128)(2,1)S(1)} %get-tuple-element.42), channel_id=1, source_target_pairs={{0,1},{1,2},{2,3},{3,4},{4,5},{5,6},{6,7},{7,8},{8,9},{9,10},{10,1... | collective-permute-start | bytes 196616 | tf_op jit(solution)/shard_map/ppermute | solution.py:21
  39.8 6.0 %collective-permute-done.3 = bf16[2,8,16,128]{3,2,1,0:T(8,128)(2,1)S(1)} collective-permute-done((bf16[2,8,16,128]{3,2,1,0:T(8,128)(2,1)S(1)}, bf16[2,8,16,128]{3,2,1,0:T(8,128)(2,1)S(1)}, u32[]{:S(2)}, u32[]{:S(2)}) %collective-permute-start.3) | collective-permute-done | bytes 65568 | tf_op jit(solution)/shard_map/ppermute | solution.py:23
  51.2 3.4 %collective-permute-start.5 = (bf16[8,2,16,128]{3,2,1,0:T(8,128)(2,1)S(1)}, bf16[8,2,16,128]{3,2,1,0:T(8,128)(2,1)S(1)}, u32[]{:S(2)}, u32[]{:S(2)}) collective-permute-start(bf16[8,2,16,128]{3,2,1,0:T(8,128)(2,1)S(1)} %get-tuple-element.46), channel_id=1, source_target_pairs={{32,0},{64,32},{96,64},{128,96},{160,128},{192,160},{224,192},{33,... | collective-permute-start | bytes 196616 | tf_op jit(solution)/shard_map/ppermute | solution.py:23
  64.1 6.8 %collective-permute-done.7 = bf16[2,8,16,128]{3,2,1,0:T(8,128)(2,1)S(1)} collective-permute-done((bf16[2,8,16,128]{3,2,1,0:T(8,128)(2,1)S(1)}, bf16[2,8,16,128]{3,2,1,0:T(8,128)(2,1)S(1)}, u32[]{:S(2)}, u32[]{:S(2)}) %collective-permute-start.7) | collective-permute-done | bytes 65568 | tf_op jit(solution)/shard_map/ppermute | solution.py:23
  73.1 3.0 %collective-permute-start.8 = (f32[8,2,16,128]{3,2,1,0:T(8,128)S(1)}, f32[8,2,16,128]{3,2,1,0:T(8,128)S(1)}, u32[]{:S(2)}, u32[]{:S(2)}) collective-permute-start(f32[8,2,16,128]{3,2,1,0:T(8,128)S(1)} %get-tuple-element.33), channel_id=1, source_target_pairs={{0,32},{32,64},{64,96},{96,128},{128,160},{160,192},{192,224},{1,3... | collective-permute-start | bytes 393224 | tf_op jit(solution)/shard_map/ppermute | solution.py:21
  79.2 3.9 %collective-permute-done.9 = f32[8,2,16,128]{3,2,1,0:T(8,128)S(1)} collective-permute-done((f32[8,2,16,128]{3,2,1,0:T(8,128)S(1)}, f32[8,2,16,128]{3,2,1,0:T(8,128)S(1)}, u32[]{:S(2)}, u32[]{:S(2)}) %collective-permute-start.9) | collective-permute-done | bytes 131104 | tf_op jit(solution)/shard_map/ppermute | solution.py:23
  83.9 8.3 %all_to_all.38 = bf16[8,4,16,128]{3,2,1,0:T(8,128)(2,1)S(1)} all-to-all(bf16[8,4,16,128]{3,2,1,0:T(8,128)(2,1)S(1)} %get-tuple-element.7), channel_id=1, replica_groups=mesh['zslab'=8,'blk'=32] {'zslab'}, dimensions={0} | all-to-all | bytes 262144 | tf_op jit(solution)/shard_map/all_to_all | solution.py:165
  92.5 3.0 %fusion.26 = bf16[32,1024]{1,0:T(8,128)(2,1)S(1)} fusion(bf16[32,80,1024]{2,1,0:T(8,128)(2,1)} %bitcast.297, bf16[32,32,64]{2,1,0:T(8,128)(2,1)S(1)} %reshape_reshape.9), kind=kOutput, calls=%fused_computation.31 | convolution fusion | flops 134250496 | bytes 4390912 | tf_op jit(solution)/shard_map/tbf,bfd->td/dot_general | solution.py:174
  96.4 4.4 %all-to-all-start.1 = ((bf16[8,32,1024]{2,1,0:T(8,128)(2,1)}), bf16[8,32,1024]{2,1,0:T(8,128)(2,1)S(1)}, u32[]{:S(2)}, u32[]{:S(2)}) async-start(bf16[8,32,1024]{2,1,0:T(8,128)(2,1)} %broadcast_in_dim.9), calls=%async_computation.1 | async-start | bytes 1048576 | tf_op jit(solution)/shard_map/all_to_all | solution.py:32
  107.9 22.6 %all_to_all.39 = bf16[32,32,256]{2,1,0:T(8,128)(2,1)S(1)} all-to-all(bf16[32,32,256]{2,1,0:T(8,128)(2,1)S(1)} %broadcast_in_dim.10), channel_id=1, replica_groups=mesh['zslab'=8,'blk'=32] {'blk'}, dimensions={0} | all-to-all | bytes 1048576 | tf_op jit(solution)/shard_map/all_to_all | solution.py:32
  135.6 8.2 %all-to-all-start.3 = ((bf16[32,32,256]{2,1,0:T(8,128)(2,1)}), bf16[32,32,256]{2,1,0:T(8,128)(2,1)}, u32[]{:S(2)}, u32[]{:S(2)}) async-start(bf16[32,32,256]{2,1,0:T(8,128)(2,1)} %pad_maximum_fusion.1), calls=%async_computation.3 | async-start | bytes 1048576 | tf_op jit(solution)/shard_map/all_to_all | solution.py:73
  143.9 14.4 %all-to-all-done.3 = bf16[32,32,256]{2,1,0:T(8,128)(2,1)} async-done(((bf16[32,32,256]{2,1,0:T(8,128)(2,1)}), bf16[32,32,256]{2,1,0:T(8,128)(2,1)}, u32[]{:S(2)}, u32[]{:S(2)}) %all-to-all-start.3) | async-done | bytes 524320 | tf_op jit(solution)/shard_map/all_to_all | solution.py:73
  159.9 11.7 %all_to_all.40 = bf16[8,32,1024]{2,1,0:T(8,128)(2,1)S(1)} all-to-all(bf16[8,32,1024]{2,1,0:T(8,128)(2,1)S(1)} %broadcast_in_dim.11), channel_id=1, replica_groups=mesh['zslab'=8,'blk'=32] {'zslab'}, dimensions={0} | all-to-all | bytes 1048576 | tf_op jit(solution)/shard_map/all_to_all | solution.py:32
  171.7 4.2 %fusion.4 = bf16[32,32,64]{2,0,1:T(8,128)(2,1)S(1)} fusion(bf16[32,80,1024]{2,1,0:T(8,128)(2,1)} %bitcast.299, bf16[32,1024]{1,0:T(8,128)(2,1)S(1)} %reduce_sum.58), kind=kOutput, calls=%fused_computation.4 | convolution fusion | flops 134283264 | bytes 4390912 | tf_op jit(solution)/shard_map/td,bfd->tbf/dot_general | solution.py:228
  181.1 4.1 %all-to-all-start.5 = ((bf16[8,1,8,16,128]{4,3,2,1,0:T(8,128)(2,1)}), bf16[8,1,8,16,128]{4,3,2,1,0:T(8,128)(2,1)S(1)}, u32[]{:S(2)}, u32[]{:S(2)}) async-start(bf16[8,1,8,16,128]{4,3,2,1,0:T(8,128)(2,1)} %constant_dynamic-update-slice_fusion.2), calls=%async_computation.5 | async-start | bytes 524288 | tf_op jit(solution)/shard_map/all_to_all | solution.py:240
  186.5 4.0 %all-to-all-done.5 = bf16[8,1,8,16,128]{4,3,2,1,0:T(8,128)(2,1)S(1)} async-done(((bf16[8,1,8,16,128]{4,3,2,1,0:T(8,128)(2,1)}), bf16[8,1,8,16,128]{4,3,2,1,0:T(8,128)(2,1)S(1)}, u32[]{:S(2)}, u32[]{:S(2)}) %all-to-all-start.5) | async-done | bytes 262176 | tf_op jit(solution)/shard_map/all_to_all | solution.py:240
  190.5 5.0 %collective-permute-start.10 = (bf16[2,8,16,128]{3,2,1,0:T(8,128)(2,1)S(1)}, bf16[2,8,16,128]{3,2,1,0:T(8,128)(2,1)S(1)}, u32[]{:S(2)}, u32[]{:S(2)}) collective-permute-start(bf16[2,8,16,128]{3,2,1,0:T(8,128)(2,1)S(1)} %get-tuple-element.32), channel_id=1, source_target_pairs={{1,0},{2,1},{3,2},{4,3},{5,4},{6,5},{7,6},{8,7},{9,8},{10,9},{11,1... | collective-permute-start | bytes 196616 | tf_op jit(solution)/shard_map/ppermute | solution.py:23
  195.6 4.8 %collective-permute-start.11 = (bf16[2,8,16,128]{3,2,1,0:T(8,128)(2,1)S(1)}, bf16[2,8,16,128]{3,2,1,0:T(8,128)(2,1)S(1)}, u32[]{:S(2)}, u32[]{:S(2)}) collective-permute-start(bf16[2,8,16,128]{3,2,1,0:T(8,128)(2,1)S(1)} %get-tuple-element.31), channel_id=1, source_target_pairs={{0,1},{1,2},{2,3},{3,4},{4,5},{5,6},{6,7},{7,8},{8,9},{9,10},{10,1... | collective-permute-start | bytes 196616 | tf_op jit(solution)/shard_map/ppermute | solution.py:21
  206.9 3.3 %collective-permute-start.13 = (bf16[8,2,16,128]{3,2,1,0:T(8,128)(2,1)S(1)}, bf16[8,2,16,128]{3,2,1,0:T(8,128)(2,1)S(1)}, u32[]{:S(2)}, u32[]{:S(2)}) collective-permute-start(bf16[8,2,16,128]{3,2,1,0:T(8,128)(2,1)S(1)} %get-tuple-element.44), channel_id=1, source_target_pairs={{32,0},{64,32},{96,64},{128,96},{160,128},{192,160},{224,192},{33,... | collective-permute-start | bytes 196616 | tf_op jit(solution)/shard_map/ppermute | solution.py:23
  212.9 4.8 %collective-permute-start.14 = (bf16[2,8,16,128]{3,2,1,0:T(8,128)(2,1)S(1)}, bf16[2,8,16,128]{3,2,1,0:T(8,128)(2,1)S(1)}, u32[]{:S(2)}, u32[]{:S(2)}) collective-permute-start(bf16[2,8,16,128]{3,2,1,0:T(8,128)(2,1)S(1)} %get-tuple-element.28), channel_id=1, source_target_pairs={{1,0},{2,1},{3,2},{4,3},{5,4},{6,5},{7,6},{8,7},{9,8},{10,9},{11,1... | collective-permute-start | bytes 196616 | tf_op jit(solution)/shard_map/ppermute | solution.py:23
  217.7 7.0 %collective-permute-start.15 = (bf16[2,8,16,128]{3,2,1,0:T(8,128)(2,1)S(1)}, bf16[2,8,16,128]{3,2,1,0:T(8,128)(2,1)S(1)}, u32[]{:S(2)}, u32[]{:S(2)}) collective-permute-start(bf16[2,8,16,128]{3,2,1,0:T(8,128)(2,1)S(1)} %get-tuple-element.27), channel_id=1, source_target_pairs={{0,1},{1,2},{2,3},{3,4},{4,5},{5,6},{6,7},{7,8},{8,9},{9,10},{10,1... | collective-permute-start | bytes 196616 | tf_op jit(solution)/shard_map/ppermute | solution.py:21
  (167 shorter events, 61.4 us)
Async XLA Ops:
  6.5 12.0 %copy-start.2 = (bf16[8,16,4,128]{3,2,1,0:T(4,128)(2,1)S(1)}, bf16[8,16,4,128]{3,2,1,0:T(4,128)(2,1)}, u32[]{:S(2)}) copy-start(bf16[8,16,4,128]{3,2,1,0:T(4,128)(2,1)} %param.7) | copy-start | bytes 393220
  6.5 85.9 %all-gather.2.cloned.1.call-start = ((), (), s32[]{:S(2)}) async-start(), calls=%async_computation.6 | async-start | bytes 5898240 | tf_op jit(solution)/shard_map/all_gather | solution.py:88
  7.4 16.7 %copy-start.1 = (bf16[2,3456,128]{2,1,0:T(8,128)(2,1)S(1)}, bf16[2,3456,128]{2,1,0:T(8,128)(2,1)}, u32[]{:S(2)}) copy-start(bf16[2,3456,128]{2,1,0:T(8,128)(2,1)} %param.10) | copy-start | bytes 5308420
  18.6 6.3 %collective-permute-start = (bf16[8,2,16,128]{3,2,1,0:T(8,128)(2,1)S(1)}, bf16[8,2,16,128]{3,2,1,0:T(8,128)(2,1)S(1)}, u32[]{:S(2)}, u32[]{:S(2)}) collective-permute-start(bf16[8,2,16,128]{3,2,1,0:T(8,128)(2,1)S(1)} %get-tuple-element.47), channel_id=1, source_target_pairs={{0,32},{32,64},{64,96},{96,128},{128,160},{160,192},{192,224},{1,3... | collective-permute-start | bytes 196616 | tf_op jit(solution)/shard_map/ppermute | solution.py:21
  22.1 5.9 %collective-permute-start.1 = (bf16[8,2,16,128]{3,2,1,0:T(8,128)(2,1)S(1)}, bf16[8,2,16,128]{3,2,1,0:T(8,128)(2,1)S(1)}, u32[]{:S(2)}, u32[]{:S(2)}) collective-permute-start(bf16[8,2,16,128]{3,2,1,0:T(8,128)(2,1)S(1)} %get-tuple-element.48), channel_id=1, source_target_pairs={{32,0},{64,32},{96,64},{128,96},{160,128},{192,160},{224,192},{33,... | collective-permute-start | bytes 196616 | tf_op jit(solution)/shard_map/ppermute | solution.py:23
  24.2 13.0 %copy-start.6 = (s32[2,3]{1,0:T(2,128)S(1)}, s32[2,3]{1,0:T(2,128)}, u32[]{:S(2)}) copy-start(s32[2,3]{1,0:T(2,128)} %param.9) | copy-start | bytes 76
  28.0 11.8 %collective-permute-start.2 = (bf16[2,8,16,128]{3,2,1,0:T(8,128)(2,1)S(1)}, bf16[2,8,16,128]{3,2,1,0:T(8,128)(2,1)S(1)}, u32[]{:S(2)}, u32[]{:S(2)}) collective-permute-start(bf16[2,8,16,128]{3,2,1,0:T(8,128)(2,1)S(1)} %get-tuple-element.42), channel_id=1, source_target_pairs={{0,1},{1,2},{2,3},{3,4},{4,5},{5,6},{6,7},{7,8},{8,9},{9,10},{10,1... | collective-permute-start | bytes 196616 | tf_op jit(solution)/shard_map/ppermute | solution.py:21
  35.2 10.6 %collective-permute-start.3 = (bf16[2,8,16,128]{3,2,1,0:T(8,128)(2,1)S(1)}, bf16[2,8,16,128]{3,2,1,0:T(8,128)(2,1)S(1)}, u32[]{:S(2)}, u32[]{:S(2)}) collective-permute-start(bf16[2,8,16,128]{3,2,1,0:T(8,128)(2,1)S(1)} %get-tuple-element.41), channel_id=1, source_target_pairs={{1,0},{2,1},{3,2},{4,3},{5,4},{6,5},{7,6},{8,7},{9,8},{10,9},{11,1... | collective-permute-start | bytes 196616 | tf_op jit(solution)/shard_map/ppermute | solution.py:23
  49.3 5.4 %collective-permute-start.4 = (bf16[8,2,16,128]{3,2,1,0:T(8,128)(2,1)S(1)}, bf16[8,2,16,128]{3,2,1,0:T(8,128)(2,1)S(1)}, u32[]{:S(2)}, u32[]{:S(2)}) collective-permute-start(bf16[8,2,16,128]{3,2,1,0:T(8,128)(2,1)S(1)} %get-tuple-element.45), channel_id=1, source_target_pairs={{0,32},{32,64},{64,96},{96,128},{128,160},{160,192},{192,224},{1,3... | collective-permute-start | bytes 196616 | tf_op jit(solution)/shard_map/ppermute | solution.py:21
  51.2 6.4 %collective-permute-start.5 = (bf16[8,2,16,128]{3,2,1,0:T(8,128)(2,1)S(1)}, bf16[8,2,16,128]{3,2,1,0:T(8,128)(2,1)S(1)}, u32[]{:S(2)}, u32[]{:S(2)}) collective-permute-start(bf16[8,2,16,128]{3,2,1,0:T(8,128)(2,1)S(1)} %get-tuple-element.46), channel_id=1, source_target_pairs={{32,0},{64,32},{96,64},{128,96},{160,128},{192,160},{224,192},{33,... | collective-permute-start | bytes 196616 | tf_op jit(solution)/shard_map/ppermute | solution.py:23
  57.7 6.4 %collective-permute-start.6 = (bf16[2,8,16,128]{3,2,1,0:T(8,128)(2,1)S(1)}, bf16[2,8,16,128]{3,2,1,0:T(8,128)(2,1)S(1)}, u32[]{:S(2)}, u32[]{:S(2)}) collective-permute-start(bf16[2,8,16,128]{3,2,1,0:T(8,128)(2,1)S(1)} %get-tuple-element.38), channel_id=1, source_target_pairs={{0,1},{1,2},{2,3},{3,4},{4,5},{5,6},{6,7},{7,8},{8,9},{9,10},{10,1... | collective-permute-start | bytes 196616 | tf_op jit(solution)/shard_map/ppermute | solution.py:21
  60.2 10.6 %collective-permute-start.7 = (bf16[2,8,16,128]{3,2,1,0:T(8,128)(2,1)S(1)}, bf16[2,8,16,128]{3,2,1,0:T(8,128)(2,1)S(1)}, u32[]{:S(2)}, u32[]{:S(2)}) collective-permute-start(bf16[2,8,16,128]{3,2,1,0:T(8,128)(2,1)S(1)} %get-tuple-element.37), channel_id=1, source_target_pairs={{1,0},{2,1},{3,2},{4,3},{5,4},{6,5},{7,6},{8,7},{9,8},{10,9},{11,1... | collective-permute-start | bytes 196616 | tf_op jit(solution)/shard_map/ppermute | solution.py:23
  73.1 6.1 %collective-permute-start.8 = (f32[8,2,16,128]{3,2,1,0:T(8,128)S(1)}, f32[8,2,16,128]{3,2,1,0:T(8,128)S(1)}, u32[]{:S(2)}, u32[]{:S(2)}) collective-permute-start(f32[8,2,16,128]{3,2,1,0:T(8,128)S(1)} %get-tuple-element.33), channel_id=1, source_target_pairs={{0,32},{32,64},{64,96},{96,128},{128,160},{160,192},{192,224},{1,3... | collective-permute-start | bytes 393224 | tf_op jit(solution)/shard_map/ppermute | solution.py:21
  76.0 7.0 %collective-permute-start.9 = (f32[8,2,16,128]{3,2,1,0:T(8,128)S(1)}, f32[8,2,16,128]{3,2,1,0:T(8,128)S(1)}, u32[]{:S(2)}, u32[]{:S(2)}) collective-permute-start(f32[8,2,16,128]{3,2,1,0:T(8,128)S(1)} %get-tuple-element.34), channel_id=1, source_target_pairs={{32,0},{64,32},{96,64},{128,96},{160,128},{192,160},{224,192},{33,... | collective-permute-start | bytes 393224 | tf_op jit(solution)/shard_map/ppermute | solution.py:23
  96.4 11.1 %all-to-all-start.1 = ((bf16[8,32,1024]{2,1,0:T(8,128)(2,1)}), bf16[8,32,1024]{2,1,0:T(8,128)(2,1)S(1)}, u32[]{:S(2)}, u32[]{:S(2)}) async-start(bf16[8,32,1024]{2,1,0:T(8,128)(2,1)} %broadcast_in_dim.9), calls=%async_computation.1 | async-start | bytes 1048576 | tf_op jit(solution)/shard_map/all_to_all | solution.py:32
  107.8 23.2 %copy-start.7 = (bf16[32,128]{1,0:T(8,128)(2,1)S(1)}, bf16[32,128]{1,0:T(8,128)(2,1)}, u32[]{:S(2)}) copy-start(bf16[32,128]{1,0:T(8,128)(2,1)} %param.13) | copy-start | bytes 24580
  135.6 22.8 %all-to-all-start.3 = ((bf16[32,32,256]{2,1,0:T(8,128)(2,1)}), bf16[32,32,256]{2,1,0:T(8,128)(2,1)}, u32[]{:S(2)}, u32[]{:S(2)}) async-start(bf16[32,32,256]{2,1,0:T(8,128)(2,1)} %pad_maximum_fusion.1), calls=%async_computation.3 | async-start | bytes 1048576 | tf_op jit(solution)/shard_map/all_to_all | solution.py:73
  181.1 9.4 %all-to-all-start.5 = ((bf16[8,1,8,16,128]{4,3,2,1,0:T(8,128)(2,1)}), bf16[8,1,8,16,128]{4,3,2,1,0:T(8,128)(2,1)S(1)}, u32[]{:S(2)}, u32[]{:S(2)}) async-start(bf16[8,1,8,16,128]{4,3,2,1,0:T(8,128)(2,1)} %constant_dynamic-update-slice_fusion.2), calls=%async_computation.5 | async-start | bytes 524288 | tf_op jit(solution)/shard_map/all_to_all | solution.py:240
  190.5 10.0 %collective-permute-start.10 = (bf16[2,8,16,128]{3,2,1,0:T(8,128)(2,1)S(1)}, bf16[2,8,16,128]{3,2,1,0:T(8,128)(2,1)S(1)}, u32[]{:S(2)}, u32[]{:S(2)}) collective-permute-start(bf16[2,8,16,128]{3,2,1,0:T(8,128)(2,1)S(1)} %get-tuple-element.32), channel_id=1, source_target_pairs={{1,0},{2,1},{3,2},{4,3},{5,4},{6,5},{7,6},{8,7},{9,8},{10,9},{11,1... | collective-permute-start | bytes 196616 | tf_op jit(solution)/shard_map/ppermute | solution.py:23
  195.6 6.1 %collective-permute-start.11 = (bf16[2,8,16,128]{3,2,1,0:T(8,128)(2,1)S(1)}, bf16[2,8,16,128]{3,2,1,0:T(8,128)(2,1)S(1)}, u32[]{:S(2)}, u32[]{:S(2)}) collective-permute-start(bf16[2,8,16,128]{3,2,1,0:T(8,128)(2,1)S(1)} %get-tuple-element.31), channel_id=1, source_target_pairs={{0,1},{1,2},{2,3},{3,4},{4,5},{5,6},{6,7},{7,8},{8,9},{9,10},{10,1... | collective-permute-start | bytes 196616 | tf_op jit(solution)/shard_map/ppermute | solution.py:21
  205.0 6.6 %collective-permute-start.12 = (bf16[8,2,16,128]{3,2,1,0:T(8,128)(2,1)S(1)}, bf16[8,2,16,128]{3,2,1,0:T(8,128)(2,1)S(1)}, u32[]{:S(2)}, u32[]{:S(2)}) collective-permute-start(bf16[8,2,16,128]{3,2,1,0:T(8,128)(2,1)S(1)} %get-tuple-element.43), channel_id=1, source_target_pairs={{0,32},{32,64},{64,96},{96,128},{128,160},{160,192},{192,224},{1,3... | collective-permute-start | bytes 196616 | tf_op jit(solution)/shard_map/ppermute | solution.py:21
  206.9 5.9 %collective-permute-start.13 = (bf16[8,2,16,128]{3,2,1,0:T(8,128)(2,1)S(1)}, bf16[8,2,16,128]{3,2,1,0:T(8,128)(2,1)S(1)}, u32[]{:S(2)}, u32[]{:S(2)}) collective-permute-start(bf16[8,2,16,128]{3,2,1,0:T(8,128)(2,1)S(1)} %get-tuple-element.44), channel_id=1, source_target_pairs={{32,0},{64,32},{96,64},{128,96},{160,128},{192,160},{224,192},{33,... | collective-permute-start | bytes 196616 | tf_op jit(solution)/shard_map/ppermute | solution.py:23
  212.9 11.9 %collective-permute-start.14 = (bf16[2,8,16,128]{3,2,1,0:T(8,128)(2,1)S(1)}, bf16[2,8,16,128]{3,2,1,0:T(8,128)(2,1)S(1)}, u32[]{:S(2)}, u32[]{:S(2)}) collective-permute-start(bf16[2,8,16,128]{3,2,1,0:T(8,128)(2,1)S(1)} %get-tuple-element.28), channel_id=1, source_target_pairs={{1,0},{2,1},{3,2},{4,3},{5,4},{6,5},{7,6},{8,7},{9,8},{10,9},{11,1... | collective-permute-start | bytes 196616 | tf_op jit(solution)/shard_map/ppermute | solution.py:23
  217.7 8.3 %collective-permute-start.15 = (bf16[2,8,16,128]{3,2,1,0:T(8,128)(2,1)S(1)}, bf16[2,8,16,128]{3,2,1,0:T(8,128)(2,1)S(1)}, u32[]{:S(2)}, u32[]{:S(2)}) collective-permute-start(bf16[2,8,16,128]{3,2,1,0:T(8,128)(2,1)S(1)} %get-tuple-element.27), channel_id=1, source_target_pairs={{0,1},{1,2},{2,3},{3,4},{4,5},{5,6},{6,7},{7,8},{8,9},{9,10},{10,1... | collective-permute-start | bytes 196616 | tf_op jit(solution)/shard_map/ppermute | solution.py:21
  (5 other events, 12.9 us)
Sparse Core Ops, SparseCore 0:
  18.7 65.3 all-gather.1

commit v12 on v7

--- a/solution.py
+++ b/solution.py
@@ -173,21 +173,24 @@
     projected = jnp.einsum(
         "td,sde->ste", tokens, qkv_rows, preferred_element_type=jnp.float32
     ).astype(jnp.bfloat16)
-    key_rows, value_rows = jnp.split(
-        joined_along(copy_for_each(jnp.concatenate([projected[1], projected[2]], axis=1), "blk"), 0),
-        2,
-        axis=1,
-    )
     tok_rows = tokens.shape[0]
     head_cols = projected.shape[2]
     heads_here = head_cols // HD
     inv_root = HD ** (-0.5)
-    queries = projected[0].reshape(tok_rows, heads_here, HD)
-    key_all = key_rows.reshape(-1, heads_here, HD)
-    value_all = value_rows.reshape(-1, heads_here, HD)
+    everything = joined_along(
+        copy_for_each(
+            jnp.concatenate([projected[0], projected[1], projected[2], out_grad], axis=1), "blk"
+        ),
+        0,
+    )
+    query_all, key_all, value_all, grad_all = [
+        part.reshape(-1, heads_here, HD) for part in jnp.split(everything, 4, axis=1)
+    ]
+    first = lax.axis_index("blk") * tok_rows
     grad_out = out_grad.reshape(tok_rows, heads_here, HD)
+    values_here = projected[2].reshape(tok_rows, heads_here, HD)
     scores = (
-        jnp.einsum("qhd,khd->hqk", queries, key_all, preferred_element_type=jnp.float32) * inv_root
+        jnp.einsum("qhd,khd->hqk", query_all, key_all, preferred_element_type=jnp.float32) * inv_root
     )
     top_score = jnp.max(scores, axis=2, keepdims=True)
     expo = jnp.exp(scores - top_score)
@@ -195,26 +198,22 @@
     probs = expo / total
     probs_b = probs.astype(jnp.bfloat16)
     attended = jnp.einsum("hqk,khd->qhd", probs_b, value_all, preferred_element_type=jnp.float32)
-    row_delta = jnp.sum(grad_out.astype(jnp.float32) * attended, axis=2).T[:, :, None]
-    score_grad = jnp.einsum("qhd,khd->hqk", grad_out, value_all, preferred_element_type=jnp.float32)
-    dscore = (probs * (score_grad - row_delta) * inv_root).astype(jnp.bfloat16)
-    grad_query = jnp.einsum("hqk,khd->qhd", dscore, key_all, preferred_element_type=jnp.float32)
+    row_delta = jnp.sum(grad_all.astype(jnp.float32) * attended, axis=2).T[:, :, None]
+    probs_rows = lax.dynamic_slice_in_dim(probs, first, tok_rows, axis=1)
+    delta_rows = lax.dynamic_slice_in_dim(row_delta, first, tok_rows, axis=1)
+    grad_rows = jnp.einsum("qhd,khd->hqk", grad_out, value_all, preferred_element_type=jnp.float32)
+    dscore_rows = (probs_rows * (grad_rows - delta_rows) * inv_root).astype(jnp.bfloat16)
+    grad_query = jnp.einsum("hqk,khd->qhd", dscore_rows, key_all, preferred_element_type=jnp.float32)
     grad_query = grad_query.astype(jnp.bfloat16).reshape(tok_rows, head_cols)
-    key_term = jnp.einsum("hqk,qhd->khd", dscore, queries, preferred_element_type=jnp.float32)
-    value_term = jnp.einsum("hqk,qhd->khd", probs_b, grad_out, preferred_element_type=jnp.float32)
-    key_value_grad = sum_at_owner(
-        jnp.concatenate(
-            [
-                key_term.reshape(tok_rows * lax.axis_size("blk"), head_cols),
-                value_term.reshape(tok_rows * lax.axis_size("blk"), head_cols),
-            ],
-            axis=1,
-        ).astype(jnp.bfloat16),
-        "blk",
-        0,
-    ).astype(jnp.bfloat16)
-    grad_key = key_value_grad[:, :head_cols]
-    grad_value = key_value_grad[:, head_cols:]
+    probs_cols = lax.dynamic_slice_in_dim(probs, first, tok_rows, axis=2)
+    grad_cols = jnp.einsum("qhd,khd->hqk", grad_all, values_here, preferred_element_type=jnp.float32)
+    dscore_cols = (probs_cols * (grad_cols - row_delta) * inv_root).astype(jnp.bfloat16)
+    grad_key = jnp.einsum("hqk,qhd->khd", dscore_cols, query_all, preferred_element_type=jnp.float32)
+    grad_key = grad_key.astype(jnp.bfloat16).reshape(tok_rows, head_cols)
+    grad_value = jnp.einsum(
+        "hqk,qhd->khd", probs_cols.astype(jnp.bfloat16), grad_all, preferred_element_type=jnp.float32
+    )
+    grad_value = grad_value.astype(jnp.bfloat16).reshape(tok_rows, head_cols)
     stacked_grads = jnp.stack([grad_query, grad_key, grad_value])
     partial_grad = jnp.einsum(
         "ste,sde->td", stacked_grads, qkv_rows, preferred_element_type=jnp.float32

time: 239 us -> 240 us (level); the launches traced: 235 us -> 238 us
  blocking collectives: 64.7 us -> 41.5 us
  waiting for transfers between devices: 43.7 us -> 53.5 us
  matrix products: 17.4 us -> 24.7 us
  starting transfers between devices: 70.5 us -> 77.8 us
    all_to_all x1 -> x2, waiting for transfers between devices: 4.05 us -> 29.6 us  [copy_for_each(): lax.all_to_all(jnp.broadcast_to(shard[None], (peers, *shard.shape)), axis...]
    all_to_all x2 -> x1, blocking collectives: 37.2 us -> 12.4 us  [copy_for_each(): lax.all_to_all(jnp.broadcast_to(shard[None], (peers, *shard.shape)), axis...]
    all_to_all x1 -> x0, waiting for transfers between devices: 14.4 us -> none  [sum_at_owner(): lax.all_to_all(cut_along(shard, dim, peers), axis, 0, 0, tiled=True)]
    all_to_all x1 -> x2, starting transfers between devices: 5.19 us -> 16.1 us  [copy_for_each(): lax.all_to_all(jnp.broadcast_to(shard[None], (peers, *shard.shape)), axis...]
    ppermute x8, starting transfers between devices: 32.6 us -> 43.2 us  [padded_2(): lax.ppermute(tail, axis, [(i, (i + 1) % count) for i in range(ends)])]
    all_to_all x1 -> x0, starting transfers between devices: 8.22 us -> none  [sum_at_owner(): lax.all_to_all(cut_along(shard, dim, peers), axis, 0, 0, tiled=True)]
    ppermute x8, waiting for transfers between devices: 22 us -> 14.5 us  [padded_2(): lax.ppermute(head, axis, [((i + 1) % count, i) for i in range(ends)])]
    ppermute x8, starting transfers between devices: 24.5 us -> 18.5 us  [padded_2(): lax.ppermute(head, axis, [((i + 1) % count, i) for i in range(ends)])]
  transfers between devices with their start and end apart: 19 -> 19, of which waited for: 12 -> 10; matrix products, arithmetic and copies ran while one was open for 6% -> 6% of each run, Pallas kernels for 0% -> 0%
where the time goes in v12:
time: 240 us; the launch traced here: 238 us
  starting transfers between devices  77.8 us (32%)
  waiting for transfers between devices  53.5 us (22%)
  blocking collectives  41.5 us (17%)
  matrix products  24.7 us (10%)
  between operations  18.2 us (8%)
  local copies, waits for them, and re-layouts  15.4 us (6%)
  other arithmetic  6.87 us (3%)
    ppermute x8, starting transfers between devices, padded_2(): lax.ppermute(tail, axis, [(i, (i + 1) % count) for i in range(ends)])  43.2 us
    all_to_all x2, waiting for transfers between devices, copy_for_each(): lax.all_to_all(jnp.broadcast_to(shard[None], (peers, *shard.shape)), axis...  29.6 us
    ppermute x8, starting transfers between devices, padded_2(): lax.ppermute(head, axis, [((i + 1) % count, i) for i in range(ends)])  18.5 us
    all_to_all x2, starting transfers between devices, copy_for_each(): lax.all_to_all(jnp.broadcast_to(shard[None], (peers, *shard.shape)), axis...  16.1 us
    ppermute x8, waiting for transfers between devices, padded_2(): lax.ppermute(head, axis, [((i + 1) % count, i) for i in range(ends)])  14.5 us
    all_to_all x1, blocking collectives, copy_for_each(): lax.all_to_all(jnp.broadcast_to(shard[None], (peers, *shard.shape)), axis...  12.4 us
    all_to_all x1, blocking collectives, local(): lax.all_to_all(hidden, 'zslab', split_axis=0, concat_axis=1, tiled=True)  11.2 us
    all_gather x1, blocking collectives, gather_weights(): lax.all_gather(rows, 'blk', axis=0, tiled=True, axis_index_groups=near)  9.96 us
  transfers between devices with their start and end apart: 19, of which 10 were waited for; matrix products, arithmetic and copies ran while one was open for 6% of the time, Pallas kernels for 0%

profile of v12, /device:TPU:103, one launch (start us, length us, event | category | flops | bytes accessed | tf_op | source)
XLA Modules:
  0.0 238.1 jit_solution(13184209613224299985)
XLA Ops:
  8.6 10.0 %all_gather.6 = bf16[320,1024]{1,0:T(8,128)(2,1)} all-gather(bf16[80,1024]{1,0:T(8,128)(2,1)S(1)} %maximum_maximum_fusion.4), channel_id=1, replica_groups={{0,1,2,3},{4,5,6,7},{8,9,10,11},{12,13,14,15},{16,17,18,19},{20,21,22,2..., dimensions={0}, use_global_device_ids=true | all-gather | bytes 819200 | tf_op jit(solution)/shard_map/all_gather | solution.py:87
  21.1 3.7 %collective-permute-start = (bf16[8,2,16,128]{3,2,1,0:T(8,128)(2,1)S(1)}, bf16[8,2,16,128]{3,2,1,0:T(8,128)(2,1)S(1)}, u32[]{:S(2)}, u32[]{:S(2)}) collective-permute-start(bf16[8,2,16,128]{3,2,1,0:T(8,128)(2,1)S(1)} %get-tuple-element.41), channel_id=1, source_target_pairs={{0,32},{32,64},{64,96},{96,128},{128,160},{160,192},{192,224},{1,3... | collective-permute-start | bytes 196616 | tf_op jit(solution)/shard_map/ppermute | solution.py:21
  26.1 3.5 %collective-permute-start.3 = (bf16[2,8,16,128]{3,2,1,0:T(8,128)(2,1)S(1)}, bf16[2,8,16,128]{3,2,1,0:T(8,128)(2,1)S(1)}, u32[]{:S(2)}, u32[]{:S(2)}) collective-permute-start(bf16[2,8,16,128]{3,2,1,0:T(8,128)(2,1)S(1)} %get-tuple-element.33), channel_id=1, source_target_pairs={{1,0},{2,1},{3,2},{4,3},{5,4},{6,5},{7,6},{8,7},{9,8},{10,9},{11,1... | collective-permute-start | bytes 196616 | tf_op jit(solution)/shard_map/ppermute | solution.py:23
  29.6 5.7 %collective-permute-start.2 = (bf16[2,8,16,128]{3,2,1,0:T(8,128)(2,1)S(1)}, bf16[2,8,16,128]{3,2,1,0:T(8,128)(2,1)S(1)}, u32[]{:S(2)}, u32[]{:S(2)}) collective-permute-start(bf16[2,8,16,128]{3,2,1,0:T(8,128)(2,1)S(1)} %get-tuple-element.34), channel_id=1, source_target_pairs={{0,1},{1,2},{2,3},{3,4},{4,5},{5,6},{6,7},{7,8},{8,9},{9,10},{10,1... | collective-permute-start | bytes 196616 | tf_op jit(solution)/shard_map/ppermute | solution.py:21
  43.4 4.6 %collective-permute-start.4 = (bf16[8,2,16,128]{3,2,1,0:T(8,128)(2,1)S(1)}, bf16[8,2,16,128]{3,2,1,0:T(8,128)(2,1)S(1)}, u32[]{:S(2)}, u32[]{:S(2)}) collective-permute-start(bf16[8,2,16,128]{3,2,1,0:T(8,128)(2,1)S(1)} %get-tuple-element.39), channel_id=1, source_target_pairs={{0,32},{32,64},{64,96},{96,128},{128,160},{160,192},{192,224},{1,3... | collective-permute-start | bytes 196616 | tf_op jit(solution)/shard_map/ppermute | solution.py:21
  51.5 9.2 %collective-permute-start.6 = (bf16[2,8,16,128]{3,2,1,0:T(8,128)(2,1)S(1)}, bf16[2,8,16,128]{3,2,1,0:T(8,128)(2,1)S(1)}, u32[]{:S(2)}, u32[]{:S(2)}) collective-permute-start(bf16[2,8,16,128]{3,2,1,0:T(8,128)(2,1)S(1)} %get-tuple-element.30), channel_id=1, source_target_pairs={{0,1},{1,2},{2,3},{3,4},{4,5},{5,6},{6,7},{7,8},{8,9},{9,10},{10,1... | collective-permute-start | bytes 196616 | tf_op jit(solution)/shard_map/ppermute | solution.py:21
  66.1 11.2 %all_to_all.33 = bf16[8,4,16,128]{3,2,1,0:T(8,128)(2,1)S(1)} all-to-all(bf16[8,4,16,128]{3,2,1,0:T(8,128)(2,1)S(1)} %get-tuple-element.54), channel_id=1, replica_groups=mesh['zslab'=8,'blk'=32] {'zslab'}, dimensions={0} | all-to-all | bytes 262144 | tf_op jit(solution)/shard_map/all_to_all | solution.py:160
  77.5 6.6 %all-gather.2.cloned.1.call-done = bf16[2560,1024]{1,0:T(8,128)(2,1)} async-done(((bf16[320,1024]{1,0:T(8,128)(2,1)}), bf16[2560,1024]{1,0:T(8,128)(2,1)}) %all-gather.2.cloned.1.call-update) | async-done | bytes 5242896 | tf_op jit(solution)/shard_map/all_gather | solution.py:88
  84.1 3.0 %fusion.42 = bf16[32,1024]{1,0:T(8,128)(2,1)S(1)} fusion(bf16[32,80,1024]{2,1,0:T(8,128)(2,1)} %bitcast.258, bf16[32,32,64]{2,1,0:T(8,128)(2,1)S(1)} %reshape_reshape.9), kind=kOutput, calls=%fused_computation.41 | convolution fusion | flops 134250496 | bytes 4390912 | tf_op jit(solution)/shard_map/tbf,bfd->td/dot_general | solution.py:169
  88.0 5.2 %all-to-all-start.1 = ((bf16[8,32,1024]{2,1,0:T(8,128)(2,1)}), bf16[8,32,1024]{2,1,0:T(8,128)(2,1)S(1)}, u32[]{:S(2)}, u32[]{:S(2)}) async-start(bf16[8,32,1024]{2,1,0:T(8,128)(2,1)} %broadcast_in_dim.9), calls=%async_computation.1 | async-start | bytes 1048576 | tf_op jit(solution)/shard_map/all_to_all | solution.py:32
  97.2 4.0 %all-to-all-done.1 = bf16[8,32,1024]{2,1,0:T(8,128)(2,1)S(1)} async-done(((bf16[8,32,1024]{2,1,0:T(8,128)(2,1)}), bf16[8,32,1024]{2,1,0:T(8,128)(2,1)S(1)}, u32[]{:S(2)}, u32[]{:S(2)}) %all-to-all-start.1) | async-done | bytes 524320 | tf_op jit(solution)/shard_map/all_to_all | solution.py:32
  102.7 11.0 %all-to-all-start.2 = ((bf16[32,32,512]{2,1,0:T(8,128)(2,1)}), bf16[32,32,512]{2,1,0:T(8,128)(2,1)}, u32[]{:S(2)}, u32[]{:S(2)}) async-start(bf16[32,32,512]{2,1,0:T(8,128)(2,1)} %broadcast_in_dim.10), calls=%async_computation.2 | async-start | bytes 2097152 | tf_op jit(solution)/shard_map/all_to_all | solution.py:32
  113.6 25.6 %all-to-all-done.2 = bf16[32,32,512]{2,1,0:T(8,128)(2,1)} async-done(((bf16[32,32,512]{2,1,0:T(8,128)(2,1)}), bf16[32,32,512]{2,1,0:T(8,128)(2,1)}, u32[]{:S(2)}, u32[]{:S(2)}) %all-to-all-start.2) | async-done | bytes 1048608 | tf_op jit(solution)/shard_map/all_to_all | solution.py:32
  147.4 3.1 %fusion.20 = f32[1024]{0:T(1024)S(1)} fusion(f32[1024,1024]{1,0:T(8,128)} %fusion.4, bf16[1024,128]{0,1:T(8,128)(2,1)S(1)} %copy.122, bf16[1024,512]{1,0:T(8,128)(2,1)} %bitcast.40), kind=kOutput, calls=%fused_computation.17 | convolution fusion | flops 269876224 | bytes 4722688 | tf_op jit(solution)/shard_map/hqk,khd->qhd/dot_general | solution.py:200
  154.2 12.4 %all_to_all.34 = bf16[8,32,1024]{2,1,0:T(8,128)(2,1)S(1)} all-to-all(bf16[8,32,1024]{2,1,0:T(8,128)(2,1)S(1)} %broadcast_in_dim.11), channel_id=1, replica_groups=mesh['zslab'=8,'blk'=32] {'zslab'}, dimensions={0} | all-to-all | bytes 1048576 | tf_op jit(solution)/shard_map/all_to_all | solution.py:32
  166.7 4.2 %fusion.17 = bf16[32,32,64]{2,0,1:T(8,128)(2,1)S(1)} fusion(bf16[32,80,1024]{2,1,0:T(8,128)(2,1)} %bitcast.260, bf16[32,1024]{1,0:T(8,128)(2,1)S(1)} %reduce_sum.45), kind=kOutput, calls=%fused_computation.16 | convolution fusion | flops 134283264 | bytes 4390912 | tf_op jit(solution)/shard_map/td,bfd->tbf/dot_general | solution.py:222
  171.3 7.9 %all_to_all.35 = bf16[1,32,16,128]{3,2,0,1:T(8,128)(2,1)S(1)} all-to-all(bf16[1,32,16,128]{3,2,0,1:T(8,128)(2,1)S(1)} %bitcast.246), channel_id=1, replica_groups=mesh['zslab'=8,'blk'=32] {'zslab'}, dimensions={1} | all-to-all | bytes 262144 | tf_op jit(solution)/shard_map/all_to_all | solution.py:229
  179.4 2.9 %collective-permute-start.9 = (bf16[8,2,16,128]{3,2,1,0:T(8,128)(2,1)S(1)}, bf16[8,2,16,128]{3,2,1,0:T(8,128)(2,1)S(1)}, u32[]{:S(2)}, u32[]{:S(2)}) collective-permute-start(bf16[8,2,16,128]{3,2,1,0:T(8,128)(2,1)S(1)} %get-tuple-element.38), channel_id=1, source_target_pairs={{32,0},{64,32},{96,64},{128,96},{160,128},{192,160},{224,192},{33,... | collective-permute-start | bytes 196616 | tf_op jit(solution)/shard_map/ppermute | solution.py:23
  182.3 3.3 %collective-permute-start.8 = (bf16[8,2,16,128]{3,2,1,0:T(8,128)(2,1)S(1)}, bf16[8,2,16,128]{3,2,1,0:T(8,128)(2,1)S(1)}, u32[]{:S(2)}, u32[]{:S(2)}) collective-permute-start(bf16[8,2,16,128]{3,2,1,0:T(8,128)(2,1)S(1)} %get-tuple-element.37), channel_id=1, source_target_pairs={{0,32},{32,64},{64,96},{96,128},{128,160},{160,192},{192,224},{1,3... | collective-permute-start | bytes 196616 | tf_op jit(solution)/shard_map/ppermute | solution.py:21
  187.3 9.2 %collective-permute-start.11 = (bf16[2,8,16,128]{3,2,1,0:T(8,128)(2,1)S(1)}, bf16[2,8,16,128]{3,2,1,0:T(8,128)(2,1)S(1)}, u32[]{:S(2)}, u32[]{:S(2)}) collective-permute-start(bf16[2,8,16,128]{3,2,1,0:T(8,128)(2,1)S(1)} %get-tuple-element.25), channel_id=1, source_target_pairs={{0,1},{1,2},{2,3},{3,4},{4,5},{5,6},{6,7},{7,8},{8,9},{9,10},{10,1... | collective-permute-start | bytes 196616 | tf_op jit(solution)/shard_map/ppermute | solution.py:21
  198.6 7.2 %collective-permute-done.10 = bf16[2,8,16,128]{3,2,1,0:T(8,128)(2,1)S(1)} collective-permute-done((bf16[2,8,16,128]{3,2,1,0:T(8,128)(2,1)S(1)}, bf16[2,8,16,128]{3,2,1,0:T(8,128)(2,1)S(1)}, u32[]{:S(2)}, u32[]{:S(2)}) %collective-permute-start.10) | collective-permute-done | bytes 65568 | tf_op jit(solution)/shard_map/ppermute | solution.py:23
  210.3 4.3 %collective-permute-start.12 = (bf16[8,2,16,128]{3,2,1,0:T(8,128)(2,1)S(1)}, bf16[8,2,16,128]{3,2,1,0:T(8,128)(2,1)S(1)}, u32[]{:S(2)}, u32[]{:S(2)}) collective-permute-start(bf16[8,2,16,128]{3,2,1,0:T(8,128)(2,1)S(1)} %get-tuple-element.35), channel_id=1, source_target_pairs={{0,32},{32,64},{64,96},{96,128},{128,160},{160,192},{192,224},{1,3... | collective-permute-start | bytes 196616 | tf_op jit(solution)/shard_map/ppermute | solution.py:21
  216.0 3.2 %collective-permute-start.15 = (bf16[2,8,16,128]{3,2,1,0:T(8,128)(2,1)S(1)}, bf16[2,8,16,128]{3,2,1,0:T(8,128)(2,1)S(1)}, u32[]{:S(2)}, u32[]{:S(2)}) collective-permute-start(bf16[2,8,16,128]{3,2,1,0:T(8,128)(2,1)S(1)} %get-tuple-element.21), channel_id=1, source_target_pairs={{0,1},{1,2},{2,3},{3,4},{4,5},{5,6},{6,7},{7,8},{8,9},{9,10},{10,1... | collective-permute-start | bytes 196616 | tf_op jit(solution)/shard_map/ppermute | solution.py:21
  221.2 7.2 %collective-permute-done.14 = bf16[2,8,16,128]{3,2,1,0:T(8,128)(2,1)S(1)} collective-permute-done((bf16[2,8,16,128]{3,2,1,0:T(8,128)(2,1)S(1)}, bf16[2,8,16,128]{3,2,1,0:T(8,128)(2,1)S(1)}, u32[]{:S(2)}, u32[]{:S(2)}) %collective-permute-start.14) | collective-permute-done | bytes 65568 | tf_op jit(solution)/shard_map/ppermute | solution.py:23
  (155 shorter events, 51.6 us)
Async XLA Ops:
  6.5 12.0 %copy-start.1 = (bf16[8,16,4,128]{3,2,1,0:T(4,128)(2,1)S(1)}, bf16[8,16,4,128]{3,2,1,0:T(4,128)(2,1)}, u32[]{:S(2)}) copy-start(bf16[8,16,4,128]{3,2,1,0:T(4,128)(2,1)} %param.7) | copy-start | bytes 393220
  6.5 77.6 %all-gather.2.cloned.1.call-start = ((), (), s32[]{:S(2)}) async-start(), calls=%async_computation.5 | async-start | bytes 5898240 | tf_op jit(solution)/shard_map/all_gather | solution.py:88
  7.4 17.5 %copy-start = (bf16[2,3456,128]{2,1,0:T(8,128)(2,1)S(1)}, bf16[2,3456,128]{2,1,0:T(8,128)(2,1)}, u32[]{:S(2)}) copy-start(bf16[2,3456,128]{2,1,0:T(8,128)(2,1)} %param.10) | copy-start | bytes 5308420
  18.6 7.1 %collective-permute-start.1 = (bf16[8,2,16,128]{3,2,1,0:T(8,128)(2,1)S(1)}, bf16[8,2,16,128]{3,2,1,0:T(8,128)(2,1)S(1)}, u32[]{:S(2)}, u32[]{:S(2)}) collective-permute-start(bf16[8,2,16,128]{3,2,1,0:T(8,128)(2,1)S(1)} %get-tuple-element.42), channel_id=1, source_target_pairs={{32,0},{64,32},{96,64},{128,96},{160,128},{192,160},{224,192},{33,... | collective-permute-start | bytes 196616 | tf_op jit(solution)/shard_map/ppermute | solution.py:23
  21.1 5.0 %collective-permute-start = (bf16[8,2,16,128]{3,2,1,0:T(8,128)(2,1)S(1)}, bf16[8,2,16,128]{3,2,1,0:T(8,128)(2,1)S(1)}, u32[]{:S(2)}, u32[]{:S(2)}) collective-permute-start(bf16[8,2,16,128]{3,2,1,0:T(8,128)(2,1)S(1)} %get-tuple-element.41), channel_id=1, source_target_pairs={{0,32},{32,64},{64,96},{96,128},{128,160},{160,192},{192,224},{1,3... | collective-permute-start | bytes 196616 | tf_op jit(solution)/shard_map/ppermute | solution.py:21
  24.9 10.4 %copy-start.5 = (s32[2,3]{1,0:T(2,128)S(1)}, s32[2,3]{1,0:T(2,128)}, u32[]{:S(2)}) copy-start(s32[2,3]{1,0:T(2,128)} %param.9) | copy-start | bytes 76
  26.1 11.8 %collective-permute-start.3 = (bf16[2,8,16,128]{3,2,1,0:T(8,128)(2,1)S(1)}, bf16[2,8,16,128]{3,2,1,0:T(8,128)(2,1)S(1)}, u32[]{:S(2)}, u32[]{:S(2)}) collective-permute-start(bf16[2,8,16,128]{3,2,1,0:T(8,128)(2,1)S(1)} %get-tuple-element.33), channel_id=1, source_target_pairs={{1,0},{2,1},{3,2},{4,3},{5,4},{6,5},{7,6},{8,7},{9,8},{10,9},{11,1... | collective-permute-start | bytes 196616 | tf_op jit(solution)/shard_map/ppermute | solution.py:23
  29.6 8.4 %collective-permute-start.2 = (bf16[2,8,16,128]{3,2,1,0:T(8,128)(2,1)S(1)}, bf16[2,8,16,128]{3,2,1,0:T(8,128)(2,1)S(1)}, u32[]{:S(2)}, u32[]{:S(2)}) collective-permute-start(bf16[2,8,16,128]{3,2,1,0:T(8,128)(2,1)S(1)} %get-tuple-element.34), channel_id=1, source_target_pairs={{0,1},{1,2},{2,3},{3,4},{4,5},{5,6},{6,7},{7,8},{8,9},{9,10},{10,1... | collective-permute-start | bytes 196616 | tf_op jit(solution)/shard_map/ppermute | solution.py:21
  41.5 6.6 %collective-permute-start.5 = (bf16[8,2,16,128]{3,2,1,0:T(8,128)(2,1)S(1)}, bf16[8,2,16,128]{3,2,1,0:T(8,128)(2,1)S(1)}, u32[]{:S(2)}, u32[]{:S(2)}) collective-permute-start(bf16[8,2,16,128]{3,2,1,0:T(8,128)(2,1)S(1)} %get-tuple-element.40), channel_id=1, source_target_pairs={{32,0},{64,32},{96,64},{128,96},{160,128},{192,160},{224,192},{33,... | collective-permute-start | bytes 196616 | tf_op jit(solution)/shard_map/ppermute | solution.py:23
  43.4 6.1 %collective-permute-start.4 = (bf16[8,2,16,128]{3,2,1,0:T(8,128)(2,1)S(1)}, bf16[8,2,16,128]{3,2,1,0:T(8,128)(2,1)S(1)}, u32[]{:S(2)}, u32[]{:S(2)}) collective-permute-start(bf16[8,2,16,128]{3,2,1,0:T(8,128)(2,1)S(1)} %get-tuple-element.39), channel_id=1, source_target_pairs={{0,32},{32,64},{64,96},{96,128},{128,160},{160,192},{192,224},{1,3... | collective-permute-start | bytes 196616 | tf_op jit(solution)/shard_map/ppermute | solution.py:21
  49.5 13.2 %collective-permute-start.7 = (bf16[2,8,16,128]{3,2,1,0:T(8,128)(2,1)S(1)}, bf16[2,8,16,128]{3,2,1,0:T(8,128)(2,1)S(1)}, u32[]{:S(2)}, u32[]{:S(2)}) collective-permute-start(bf16[2,8,16,128]{3,2,1,0:T(8,128)(2,1)S(1)} %get-tuple-element.29), channel_id=1, source_target_pairs={{1,0},{2,1},{3,2},{4,3},{5,4},{6,5},{7,6},{8,7},{9,8},{10,9},{11,1... | collective-permute-start | bytes 196616 | tf_op jit(solution)/shard_map/ppermute | solution.py:23
  51.5 11.8 %collective-permute-start.6 = (bf16[2,8,16,128]{3,2,1,0:T(8,128)(2,1)S(1)}, bf16[2,8,16,128]{3,2,1,0:T(8,128)(2,1)S(1)}, u32[]{:S(2)}, u32[]{:S(2)}) collective-permute-start(bf16[2,8,16,128]{3,2,1,0:T(8,128)(2,1)S(1)} %get-tuple-element.30), channel_id=1, source_target_pairs={{0,1},{1,2},{2,3},{3,4},{4,5},{5,6},{6,7},{7,8},{8,9},{9,10},{10,1... | collective-permute-start | bytes 196616 | tf_op jit(solution)/shard_map/ppermute | solution.py:21
  88.0 13.2 %all-to-all-start.1 = ((bf16[8,32,1024]{2,1,0:T(8,128)(2,1)}), bf16[8,32,1024]{2,1,0:T(8,128)(2,1)S(1)}, u32[]{:S(2)}, u32[]{:S(2)}) async-start(bf16[8,32,1024]{2,1,0:T(8,128)(2,1)} %broadcast_in_dim.9), calls=%async_computation.1 | async-start | bytes 1048576 | tf_op jit(solution)/shard_map/all_to_all | solution.py:32
  95.9 5.6 %copy-start.6 = (bf16[32,128]{1,0:T(8,128)(2,1)S(1)}, bf16[32,128]{1,0:T(8,128)(2,1)}, u32[]{:S(2)}) copy-start(bf16[32,128]{1,0:T(8,128)(2,1)} %param.13) | copy-start | bytes 24580
  102.7 36.6 %all-to-all-start.2 = ((bf16[32,32,512]{2,1,0:T(8,128)(2,1)}), bf16[32,32,512]{2,1,0:T(8,128)(2,1)}, u32[]{:S(2)}, u32[]{:S(2)}) async-start(bf16[32,32,512]{2,1,0:T(8,128)(2,1)} %broadcast_in_dim.10), calls=%async_computation.2 | async-start | bytes 2097152 | tf_op jit(solution)/shard_map/all_to_all | solution.py:32
  171.0 8.2 %copy-start.3 = (f32[8,4,16,128]{3,2,1,0:T(8,128)S(1)}, f32[8,4,16,128]{3,2,1,0:T(8,128)}, u32[]{:S(2)}) copy-start(f32[8,4,16,128]{3,2,1,0:T(8,128)} %get-tuple-element.55) | copy-start | bytes 786436
  179.4 7.5 %collective-permute-start.9 = (bf16[8,2,16,128]{3,2,1,0:T(8,128)(2,1)S(1)}, bf16[8,2,16,128]{3,2,1,0:T(8,128)(2,1)S(1)}, u32[]{:S(2)}, u32[]{:S(2)}) collective-permute-start(bf16[8,2,16,128]{3,2,1,0:T(8,128)(2,1)S(1)} %get-tuple-element.38), channel_id=1, source_target_pairs={{32,0},{64,32},{96,64},{128,96},{160,128},{192,160},{224,192},{33,... | collective-permute-start | bytes 196616 | tf_op jit(solution)/shard_map/ppermute | solution.py:23
  182.3 5.0 %collective-permute-start.8 = (bf16[8,2,16,128]{3,2,1,0:T(8,128)(2,1)S(1)}, bf16[8,2,16,128]{3,2,1,0:T(8,128)(2,1)S(1)}, u32[]{:S(2)}, u32[]{:S(2)}) collective-permute-start(bf16[8,2,16,128]{3,2,1,0:T(8,128)(2,1)S(1)} %get-tuple-element.37), channel_id=1, source_target_pairs={{0,32},{32,64},{64,96},{96,128},{128,160},{160,192},{192,224},{1,3... | collective-permute-start | bytes 196616 | tf_op jit(solution)/shard_map/ppermute | solution.py:21
  187.3 11.2 %collective-permute-start.11 = (bf16[2,8,16,128]{3,2,1,0:T(8,128)(2,1)S(1)}, bf16[2,8,16,128]{3,2,1,0:T(8,128)(2,1)S(1)}, u32[]{:S(2)}, u32[]{:S(2)}) collective-permute-start(bf16[2,8,16,128]{3,2,1,0:T(8,128)(2,1)S(1)} %get-tuple-element.25), channel_id=1, source_target_pairs={{0,1},{1,2},{2,3},{3,4},{4,5},{5,6},{6,7},{7,8},{8,9},{9,10},{10,1... | collective-permute-start | bytes 196616 | tf_op jit(solution)/shard_map/ppermute | solution.py:21
  196.6 9.2 %collective-permute-start.10 = (bf16[2,8,16,128]{3,2,1,0:T(8,128)(2,1)S(1)}, bf16[2,8,16,128]{3,2,1,0:T(8,128)(2,1)S(1)}, u32[]{:S(2)}, u32[]{:S(2)}) collective-permute-start(bf16[2,8,16,128]{3,2,1,0:T(8,128)(2,1)S(1)} %get-tuple-element.26), channel_id=1, source_target_pairs={{1,0},{2,1},{3,2},{4,3},{5,4},{6,5},{7,6},{8,7},{9,8},{10,9},{11,1... | collective-permute-start | bytes 196616 | tf_op jit(solution)/shard_map/ppermute | solution.py:23
  208.4 7.5 %collective-permute-start.13 = (bf16[8,2,16,128]{3,2,1,0:T(8,128)(2,1)S(1)}, bf16[8,2,16,128]{3,2,1,0:T(8,128)(2,1)S(1)}, u32[]{:S(2)}, u32[]{:S(2)}) collective-permute-start(bf16[8,2,16,128]{3,2,1,0:T(8,128)(2,1)S(1)} %get-tuple-element.36), channel_id=1, source_target_pairs={{32,0},{64,32},{96,64},{128,96},{160,128},{192,160},{224,192},{33,... | collective-permute-start | bytes 196616 | tf_op jit(solution)/shard_map/ppermute | solution.py:23
  210.3 5.6 %collective-permute-start.12 = (bf16[8,2,16,128]{3,2,1,0:T(8,128)(2,1)S(1)}, bf16[8,2,16,128]{3,2,1,0:T(8,128)(2,1)S(1)}, u32[]{:S(2)}, u32[]{:S(2)}) collective-permute-start(bf16[8,2,16,128]{3,2,1,0:T(8,128)(2,1)S(1)} %get-tuple-element.35), channel_id=1, source_target_pairs={{0,32},{32,64},{64,96},{96,128},{128,160},{160,192},{192,224},{1,3... | collective-permute-start | bytes 196616 | tf_op jit(solution)/shard_map/ppermute | solution.py:21
  216.0 5.3 %collective-permute-start.15 = (bf16[2,8,16,128]{3,2,1,0:T(8,128)(2,1)S(1)}, bf16[2,8,16,128]{3,2,1,0:T(8,128)(2,1)S(1)}, u32[]{:S(2)}, u32[]{:S(2)}) collective-permute-start(bf16[2,8,16,128]{3,2,1,0:T(8,128)(2,1)S(1)} %get-tuple-element.21), channel_id=1, source_target_pairs={{0,1},{1,2},{2,3},{3,4},{4,5},{5,6},{6,7},{7,8},{8,9},{9,10},{10,1... | collective-permute-start | bytes 196616 | tf_op jit(solution)/shard_map/ppermute | solution.py:21
  219.2 9.2 %collective-permute-start.14 = (bf16[2,8,16,128]{3,2,1,0:T(8,128)(2,1)S(1)}, bf16[2,8,16,128]{3,2,1,0:T(8,128)(2,1)S(1)}, u32[]{:S(2)}, u32[]{:S(2)}) collective-permute-start(bf16[2,8,16,128]{3,2,1,0:T(8,128)(2,1)S(1)} %get-tuple-element.22), channel_id=1, source_target_pairs={{1,0},{2,1},{3,2},{4,3},{5,4},{6,5},{7,6},{8,7},{9,8},{10,9},{11,1... | collective-permute-start | bytes 196616 | tf_op jit(solution)/shard_map/ppermute | solution.py:23
  (3 other events, 2.6 us)
Sparse Core Ops, SparseCore 0:
  18.7 65.3 all-gather.1

commit v13 on v12

--- a/solution.py
+++ b/solution.py
@@ -74,7 +74,7 @@
     return jnp.sum(pieces.astype(jnp.float32), axis=0)
 
 
-def gather_weights(embed_weight, qkv_weight):
+def gather_weights(embed_weight, qkv_weight, after):
     _, feat, width = embed_weight.shape
     qkv_flat = qkv_weight.reshape(-1, width)
     extra = -qkv_flat.shape[0] % 16
@@ -85,14 +85,24 @@
     near = [list(range(start, start + 4)) for start in range(0, peers, 4)]
     far = [list(range(start, peers, 4)) for start in range(4)]
     gathered = lax.all_gather(rows, "blk", axis=0, tiled=True, axis_index_groups=near)
-    gathered = lax.all_gather(gathered, "blk", axis=0, tiled=True, axis_index_groups=far)
+    half = gathered.shape[0] // 2
+    odd = (lax.axis_index("blk") & 1) != 0
+    mine = jnp.where(odd, gathered[half:], gathered[:half])
+    own = lax.all_gather(mine, "blk", axis=0, tiled=True, axis_index_groups=far)
+    own, after = lax.optimization_barrier((own, after))
+    other = lax.ppermute(own, "blk", [(i, i ^ 1) for i in range(peers)])
+    own = own.reshape(len(far[0]), half, width)
+    other = other.reshape(len(far[0]), half, width)
+    gathered = jnp.concatenate(
+        [jnp.where(odd, other, own), jnp.where(odd, own, other)], axis=1
+    )
     gathered = gathered.reshape(peers, rows.shape[0], width)
     embed_rows = gathered[:, :feat, :]
     qkv_rows = gathered[:, feat : feat + qkv_flat.shape[0], :].reshape(peers, *qkv_weight.shape)
     qkv_rows = jnp.moveaxis(qkv_rows, 0, 1).reshape(
         qkv_weight.shape[0], peers * qkv_weight.shape[1], qkv_weight.shape[2]
     )
-    return embed_rows, qkv_rows
+    return embed_rows, qkv_rows, after
 
 
 def with_rim(volume):
@@ -158,13 +168,13 @@
             hidden.astype(jnp.float32) + gate_mask * (conv_out * jax.nn.sigmoid(conv_out))
         ).astype(jnp.bfloat16)
     slab_view = lax.all_to_all(hidden, "zslab", split_axis=0, concat_axis=1, tiled=True)
+    embed_rows, qkv_rows, slab_view = gather_weights(embed_weight, qkv_weight, slab_view)
     x_local, z_total = (slab_view.shape[0], slab_view.shape[1])
     y_blocks, z_blocks = (y_cells // PY, z_total // PZ)
     patches = slab_view.reshape(x_local, z_blocks, PZ, y_blocks, PY, channels).transpose(
         3, 1, 0, 4, 2, 5
     )
     patches = patches.reshape(y_blocks * z_blocks, x_local, PY * PZ * channels)
-    embed_rows, qkv_rows = gather_weights(embed_weight, qkv_weight)
     patches = patches.reshape(patches.shape[0], embed_rows.shape[0], embed_rows.shape[1])
     partial_value = jnp.einsum(
         "tbf,bfd->td", patches, embed_rows, preferred_element_type=jnp.float32

time: 240 us -> 242 us (level)
  other arithmetic: 6.87 us -> 11 us
  local copies, waits for them, and re-layouts: 15.4 us -> 19.1 us
    all_gather x1, waiting for transfers between devices: 6.61 us -> 0.01 us  [gather_weights(): own = lax.all_gather(mine, 'blk', axis=0, tiled=True, axis_index_groups=far)]
    ppermute x0 -> x1, waiting for transfers between devices: none -> 5 us  [gather_weights(): other = lax.ppermute(own, 'blk', [(i, i ^ 1) for i in range(peers)])]
    select_n x0 -> x2, other arithmetic: none -> 3.63 us  [the longest x1 2.87 us: gather_weights(): jnp.where(odd, other, own)]
    unnamed x31 -> x29, local copies, waits for them, and re-layouts: 3.25 us -> 5.6 us
  transfers between devices with their start and end apart: 19 -> 20, of which waited for: 10 -> 9; matrix products, arithmetic and copies ran while one was open for 6% -> 7% of each run, Pallas kernels for 0% -> 0%
where the time goes in v13:
time: 242 us; the launch traced here: 240 us
  starting transfers between devices  76.9 us (32%)
  waiting for transfers between devices  52.5 us (22%)
  blocking collectives  39.5 us (16%)
  matrix products  22.6 us (9%)
  local copies, waits for them, and re-layouts  19.1 us (8%)
  between operations  18.3 us (8%)
  other arithmetic  11 us (5%)
    ppermute x8, starting transfers between devices, padded_2(): lax.ppermute(tail, axis, [(i, (i + 1) % count) for i in range(ends)])  42.6 us
    all_to_all x2, waiting for transfers between devices, copy_for_each(): lax.all_to_all(jnp.broadcast_to(shard[None], (peers, *shard.shape)), axis...  30.9 us
    all_to_all x2, starting transfers between devices, copy_for_each(): lax.all_to_all(jnp.broadcast_to(shard[None], (peers, *shard.shape)), axis...  17.3 us
    ppermute x8, starting transfers between devices, padded_2(): lax.ppermute(head, axis, [((i + 1) % count, i) for i in range(ends)])  17 us
    ppermute x8, waiting for transfers between devices, padded_2(): lax.ppermute(head, axis, [((i + 1) % count, i) for i in range(ends)])  14.5 us
    all_to_all x1, blocking collectives, copy_for_each(): lax.all_to_all(jnp.broadcast_to(shard[None], (peers, *shard.shape)), axis...  11.7 us
    all_to_all x1, blocking collectives, local(): lax.all_to_all(hidden, 'zslab', split_axis=0, concat_axis=1, tiled=True)  10.1 us
    all_gather x1, blocking collectives, gather_weights(): lax.all_gather(rows, 'blk', axis=0, tiled=True, axis_index_groups=near)  9.51 us
  transfers between devices with their start and end apart: 20, of which 9 were waited for; matrix products, arithmetic and copies ran while one was open for 7% of the time, Pallas kernels for 0%

profile of v13, /device:TPU:103, one launch (start us, length us, event | category | flops | bytes accessed | tf_op | source)
XLA Modules:
  0.0 239.8 jit_solution(10394661806101977245)
XLA Ops:
  9.9 3.7 %collective-permute-start = (bf16[8,2,16,128]{3,2,1,0:T(8,128)(2,1)S(1)}, bf16[8,2,16,128]{3,2,1,0:T(8,128)(2,1)S(1)}, u32[]{:S(2)}, u32[]{:S(2)}) collective-permute-start(bf16[8,2,16,128]{3,2,1,0:T(8,128)(2,1)S(1)} %get-tuple-element.47), channel_id=1, source_target_pairs={{0,32},{32,64},{64,96},{96,128},{128,160},{160,192},{192,224},{1,3... | collective-permute-start | bytes 196616 | tf_op jit(solution)/shard_map/ppermute | solution.py:21
  15.6 9.5 %all_gather.6 = bf16[320,1024]{1,0:T(8,128)(2,1)S(1)} all-gather(bf16[80,1024]{1,0:T(8,128)(2,1)S(1)} %maximum_maximum_fusion.4), channel_id=1, replica_groups={{0,1,2,3},{4,5,6,7},{8,9,10,11},{12,13,14,15},{16,17,18,19},{20,21,22,2..., dimensions={0}, use_global_device_ids=true | all-gather | bytes 819200 | tf_op jit(solution)/shard_map/all_gather | solution.py:87
  30.2 7.1 %collective-permute-start.2 = (bf16[2,8,16,128]{3,2,1,0:T(8,128)(2,1)S(1)}, bf16[2,8,16,128]{3,2,1,0:T(8,128)(2,1)S(1)}, u32[]{:S(2)}, u32[]{:S(2)}) collective-permute-start(bf16[2,8,16,128]{3,2,1,0:T(8,128)(2,1)S(1)} %get-tuple-element.40), channel_id=1, source_target_pairs={{0,1},{1,2},{2,3},{3,4},{4,5},{5,6},{6,7},{7,8},{8,9},{9,10},{10,1... | collective-permute-start | bytes 196616 | tf_op jit(solution)/shard_map/ppermute | solution.py:21
  45.4 4.3 %collective-permute-start.4 = (bf16[8,2,16,128]{3,2,1,0:T(8,128)(2,1)S(1)}, bf16[8,2,16,128]{3,2,1,0:T(8,128)(2,1)S(1)}, u32[]{:S(2)}, u32[]{:S(2)}) collective-permute-start(bf16[8,2,16,128]{3,2,1,0:T(8,128)(2,1)S(1)} %get-tuple-element.45), channel_id=1, source_target_pairs={{0,32},{32,64},{64,96},{96,128},{128,160},{160,192},{192,224},{1,3... | collective-permute-start | bytes 196616 | tf_op jit(solution)/shard_map/ppermute | solution.py:21
  53.0 7.8 %collective-permute-start.6 = (bf16[2,8,16,128]{3,2,1,0:T(8,128)(2,1)S(1)}, bf16[2,8,16,128]{3,2,1,0:T(8,128)(2,1)S(1)}, u32[]{:S(2)}, u32[]{:S(2)}) collective-permute-start(bf16[2,8,16,128]{3,2,1,0:T(8,128)(2,1)S(1)} %get-tuple-element.36), channel_id=1, source_target_pairs={{0,1},{1,2},{2,3},{3,4},{4,5},{5,6},{6,7},{7,8},{8,9},{9,10},{10,1... | collective-permute-start | bytes 196616 | tf_op jit(solution)/shard_map/ppermute | solution.py:21
  66.1 10.1 %all_to_all.36 = bf16[8,4,16,128]{3,2,1,0:T(8,128)(2,1)S(1)} all-to-all(bf16[8,4,16,128]{3,2,1,0:T(8,128)(2,1)S(1)} %get-tuple-element.60), channel_id=1, replica_groups=mesh['zslab'=8,'blk'=32] {'zslab'}, dimensions={0} | all-to-all | bytes 262144 | tf_op jit(solution)/shard_map/all_to_all | solution.py:170
  76.4 5.0 %collective-permute-done.8 = bf16[1280,1024]{1,0:T(8,128)(2,1)} collective-permute-done((bf16[1280,1024]{1,0:T(8,128)(2,1)}, bf16[1280,1024]{1,0:T(8,128)(2,1)}, u32[]{:S(2)}, u32[]{:S(2)}) %collective-permute-start.8) | collective-permute-done | bytes 2621472 | tf_op jit(solution)/shard_map/ppermute | solution.py:93
  81.4 2.9 %broadcast_select_fusion.1 = (bf16[1280,1024]{1,0:T(8,128)(2,1)S(1)}, bf16[1280,1024]{1,0:T(8,128)(2,1)S(1)}) fusion(bf16[1280,1024]{1,0:T(8,128)(2,1)} %collective-permute-done.8, bf16[1280,1024]{1,0:T(8,128)(2,1)} %all-gather.2.cloned.1.call-done, pred[]{:T(512)S(6)} %ne.3), kind=kLoop, calls=%fused_computation.10 | loop fusion | flops 2621440 | bytes 10485761 | tf_op jit(solution)/shard_map/jit(_where)/select_n | solution.py:97
  88.1 4.4 %all-to-all-start.1 = ((bf16[8,32,1024]{2,1,0:T(8,128)(2,1)}), bf16[8,32,1024]{2,1,0:T(8,128)(2,1)S(1)}, u32[]{:S(2)}, u32[]{:S(2)}) async-start(bf16[8,32,1024]{2,1,0:T(8,128)(2,1)} %broadcast_in_dim.9), calls=%async_computation.1 | async-start | bytes 1048576 | tf_op jit(solution)/shard_map/all_to_all | solution.py:32
  96.4 5.3 %all-to-all-done.1 = bf16[8,32,1024]{2,1,0:T(8,128)(2,1)S(1)} async-done(((bf16[8,32,1024]{2,1,0:T(8,128)(2,1)}), bf16[8,32,1024]{2,1,0:T(8,128)(2,1)S(1)}, u32[]{:S(2)}, u32[]{:S(2)}) %all-to-all-start.1) | async-done | bytes 524320 | tf_op jit(solution)/shard_map/all_to_all | solution.py:32
  103.2 12.9 %all-to-all-start.2 = ((bf16[32,32,512]{2,1,0:T(8,128)(2,1)}), bf16[32,32,512]{2,1,0:T(8,128)(2,1)}, u32[]{:S(2)}, u32[]{:S(2)}) async-start(bf16[32,32,512]{2,1,0:T(8,128)(2,1)} %broadcast_in_dim.10), calls=%async_computation.2 | async-start | bytes 2097152 | tf_op jit(solution)/shard_map/all_to_all | solution.py:32
  116.1 25.6 %all-to-all-done.2 = bf16[32,32,512]{2,1,0:T(8,128)(2,1)} async-done(((bf16[32,32,512]{2,1,0:T(8,128)(2,1)}), bf16[32,32,512]{2,1,0:T(8,128)(2,1)}, u32[]{:S(2)}, u32[]{:S(2)}) %all-to-all-start.2) | async-done | bytes 1048608 | tf_op jit(solution)/shard_map/all_to_all | solution.py:32
  145.4 2.8 %fusion.4 = f32[1024,1024]{1,0:T(8,128)} fusion(f32[1024,1024]{1,0:T(8,128)S(1)} %get-tuple-element.63, f32[1024]{0:T(1024)S(1)} %fusion.5, f32[1024]{0:T(1024)S(1)} %get-tuple-element.62), kind=kLoop, calls=%fused_computation.7 | loop fusion | flops 3145728 | bytes 8396800 | tf_op jit(solution)/shard_map/div | solution.py:208
  149.9 3.1 %fusion.20 = f32[1024]{0:T(1024)S(1)} fusion(f32[1024,1024]{1,0:T(8,128)} %fusion.4, bf16[1024,128]{0,1:T(8,128)(2,1)S(1)} %copy.121, bf16[1024,512]{1,0:T(8,128)(2,1)} %bitcast.43), kind=kOutput, calls=%fused_computation.20 | convolution fusion | flops 269876224 | bytes 4722688 | tf_op jit(solution)/shard_map/hqk,khd->qhd/dot_general | solution.py:210
  156.7 11.7 %all_to_all.37 = bf16[8,32,1024]{2,1,0:T(8,128)(2,1)S(1)} all-to-all(bf16[8,32,1024]{2,1,0:T(8,128)(2,1)S(1)} %broadcast_in_dim.11), channel_id=1, replica_groups=mesh['zslab'=8,'blk'=32] {'zslab'}, dimensions={0} | all-to-all | bytes 1048576 | tf_op jit(solution)/shard_map/all_to_all | solution.py:32
  168.5 4.2 %fusion.17 = bf16[32,32,64]{2,0,1:T(8,128)(2,1)S(1)} fusion(bf16[32,80,1024]{2,1,0:T(8,128)(2,1)} %bitcast.228, bf16[32,1024]{1,0:T(8,128)(2,1)S(1)} %reduce_sum.45), kind=kOutput, calls=%fused_computation.19 | convolution fusion | flops 134283264 | bytes 4390912 | tf_op jit(solution)/shard_map/td,bfd->tbf/dot_general | solution.py:232
  173.0 8.1 %all_to_all.38 = bf16[1,32,16,128]{3,2,0,1:T(8,128)(2,1)S(1)} all-to-all(bf16[1,32,16,128]{3,2,0,1:T(8,128)(2,1)S(1)} %bitcast.252), channel_id=1, replica_groups=mesh['zslab'=8,'blk'=32] {'zslab'}, dimensions={1} | all-to-all | bytes 262144 | tf_op jit(solution)/shard_map/all_to_all | solution.py:239
  181.3 2.9 %collective-permute-start.10 = (bf16[8,2,16,128]{3,2,1,0:T(8,128)(2,1)S(1)}, bf16[8,2,16,128]{3,2,1,0:T(8,128)(2,1)S(1)}, u32[]{:S(2)}, u32[]{:S(2)}) collective-permute-start(bf16[8,2,16,128]{3,2,1,0:T(8,128)(2,1)S(1)} %get-tuple-element.44), channel_id=1, source_target_pairs={{32,0},{64,32},{96,64},{128,96},{160,128},{192,160},{224,192},{33,... | collective-permute-start | bytes 196616 | tf_op jit(solution)/shard_map/ppermute | solution.py:23
  184.2 3.3 %collective-permute-start.9 = (bf16[8,2,16,128]{3,2,1,0:T(8,128)(2,1)S(1)}, bf16[8,2,16,128]{3,2,1,0:T(8,128)(2,1)S(1)}, u32[]{:S(2)}, u32[]{:S(2)}) collective-permute-start(bf16[8,2,16,128]{3,2,1,0:T(8,128)(2,1)S(1)} %get-tuple-element.43), channel_id=1, source_target_pairs={{0,32},{32,64},{64,96},{96,128},{128,160},{160,192},{192,224},{1,3... | collective-permute-start | bytes 196616 | tf_op jit(solution)/shard_map/ppermute | solution.py:21
  189.3 9.0 %collective-permute-start.12 = (bf16[2,8,16,128]{3,2,1,0:T(8,128)(2,1)S(1)}, bf16[2,8,16,128]{3,2,1,0:T(8,128)(2,1)S(1)}, u32[]{:S(2)}, u32[]{:S(2)}) collective-permute-start(bf16[2,8,16,128]{3,2,1,0:T(8,128)(2,1)S(1)} %get-tuple-element.31), channel_id=1, source_target_pairs={{0,1},{1,2},{2,3},{3,4},{4,5},{5,6},{6,7},{7,8},{8,9},{9,10},{10,1... | collective-permute-start | bytes 196616 | tf_op jit(solution)/shard_map/ppermute | solution.py:21
  200.3 7.2 %collective-permute-done.11 = bf16[2,8,16,128]{3,2,1,0:T(8,128)(2,1)S(1)} collective-permute-done((bf16[2,8,16,128]{3,2,1,0:T(8,128)(2,1)S(1)}, bf16[2,8,16,128]{3,2,1,0:T(8,128)(2,1)S(1)}, u32[]{:S(2)}, u32[]{:S(2)}) %collective-permute-start.11) | collective-permute-done | bytes 65568 | tf_op jit(solution)/shard_map/ppermute | solution.py:23
  212.0 4.3 %collective-permute-start.13 = (bf16[8,2,16,128]{3,2,1,0:T(8,128)(2,1)S(1)}, bf16[8,2,16,128]{3,2,1,0:T(8,128)(2,1)S(1)}, u32[]{:S(2)}, u32[]{:S(2)}) collective-permute-start(bf16[8,2,16,128]{3,2,1,0:T(8,128)(2,1)S(1)} %get-tuple-element.41), channel_id=1, source_target_pairs={{0,32},{32,64},{64,96},{96,128},{128,160},{160,192},{192,224},{1,3... | collective-permute-start | bytes 196616 | tf_op jit(solution)/shard_map/ppermute | solution.py:21
  217.7 3.2 %collective-permute-start.16 = (bf16[2,8,16,128]{3,2,1,0:T(8,128)(2,1)S(1)}, bf16[2,8,16,128]{3,2,1,0:T(8,128)(2,1)S(1)}, u32[]{:S(2)}, u32[]{:S(2)}) collective-permute-start(bf16[2,8,16,128]{3,2,1,0:T(8,128)(2,1)S(1)} %get-tuple-element.27), channel_id=1, source_target_pairs={{0,1},{1,2},{2,3},{3,4},{4,5},{5,6},{6,7},{7,8},{8,9},{9,10},{10,1... | collective-permute-start | bytes 196616 | tf_op jit(solution)/shard_map/ppermute | solution.py:21
  222.9 7.2 %collective-permute-done.15 = bf16[2,8,16,128]{3,2,1,0:T(8,128)(2,1)S(1)} collective-permute-done((bf16[2,8,16,128]{3,2,1,0:T(8,128)(2,1)S(1)}, bf16[2,8,16,128]{3,2,1,0:T(8,128)(2,1)S(1)}, u32[]{:S(2)}, u32[]{:S(2)}) %collective-permute-start.15) | collective-permute-done | bytes 65568 | tf_op jit(solution)/shard_map/ppermute | solution.py:23
  (158 shorter events, 56.0 us)
Async XLA Ops:
  6.5 69.7 %all-gather.2.cloned.1.call-start = ((), (), s32[]{:S(2)}) async-start(), calls=%async_computation.5 | async-start | bytes 2949120 | tf_op jit(solution)/shard_map/all_gather | solution.py:91
  7.5 20.6 %collective-permute-start.1 = (bf16[8,2,16,128]{3,2,1,0:T(8,128)(2,1)S(1)}, bf16[8,2,16,128]{3,2,1,0:T(8,128)(2,1)S(1)}, u32[]{:S(2)}, u32[]{:S(2)}) collective-permute-start(bf16[8,2,16,128]{3,2,1,0:T(8,128)(2,1)S(1)} %get-tuple-element.48), channel_id=1, source_target_pairs={{32,0},{64,32},{96,64},{128,96},{160,128},{192,160},{224,192},{33,... | collective-permute-start | bytes 196616 | tf_op jit(solution)/shard_map/ppermute | solution.py:23
  9.9 18.2 %collective-permute-start = (bf16[8,2,16,128]{3,2,1,0:T(8,128)(2,1)S(1)}, bf16[8,2,16,128]{3,2,1,0:T(8,128)(2,1)S(1)}, u32[]{:S(2)}, u32[]{:S(2)}) collective-permute-start(bf16[8,2,16,128]{3,2,1,0:T(8,128)(2,1)S(1)} %get-tuple-element.47), channel_id=1, source_target_pairs={{0,32},{32,64},{64,96},{96,128},{128,160},{160,192},{192,224},{1,3... | collective-permute-start | bytes 196616 | tf_op jit(solution)/shard_map/ppermute | solution.py:21
  27.4 9.9 %copy-start.4 = (s32[2,3]{1,0:T(2,128)S(1)}, s32[2,3]{1,0:T(2,128)}, u32[]{:S(2)}) copy-start(s32[2,3]{1,0:T(2,128)} %param.9) | copy-start | bytes 76
  28.2 11.8 %collective-permute-start.3 = (bf16[2,8,16,128]{3,2,1,0:T(8,128)(2,1)S(1)}, bf16[2,8,16,128]{3,2,1,0:T(8,128)(2,1)S(1)}, u32[]{:S(2)}, u32[]{:S(2)}) collective-permute-start(bf16[2,8,16,128]{3,2,1,0:T(8,128)(2,1)S(1)} %get-tuple-element.39), channel_id=1, source_target_pairs={{1,0},{2,1},{3,2},{4,3},{5,4},{6,5},{7,6},{8,7},{9,8},{10,9},{11,1... | collective-permute-start | bytes 196616 | tf_op jit(solution)/shard_map/ppermute | solution.py:23
  30.2 9.8 %collective-permute-start.2 = (bf16[2,8,16,128]{3,2,1,0:T(8,128)(2,1)S(1)}, bf16[2,8,16,128]{3,2,1,0:T(8,128)(2,1)S(1)}, u32[]{:S(2)}, u32[]{:S(2)}) collective-permute-start(bf16[2,8,16,128]{3,2,1,0:T(8,128)(2,1)S(1)} %get-tuple-element.40), channel_id=1, source_target_pairs={{0,1},{1,2},{2,3},{3,4},{4,5},{5,6},{6,7},{7,8},{8,9},{9,10},{10,1... | collective-permute-start | bytes 196616 | tf_op jit(solution)/shard_map/ppermute | solution.py:21
  43.5 6.3 %collective-permute-start.5 = (bf16[8,2,16,128]{3,2,1,0:T(8,128)(2,1)S(1)}, bf16[8,2,16,128]{3,2,1,0:T(8,128)(2,1)S(1)}, u32[]{:S(2)}, u32[]{:S(2)}) collective-permute-start(bf16[8,2,16,128]{3,2,1,0:T(8,128)(2,1)S(1)} %get-tuple-element.46), channel_id=1, source_target_pairs={{32,0},{64,32},{96,64},{128,96},{160,128},{192,160},{224,192},{33,... | collective-permute-start | bytes 196616 | tf_op jit(solution)/shard_map/ppermute | solution.py:23
  45.4 5.6 %collective-permute-start.4 = (bf16[8,2,16,128]{3,2,1,0:T(8,128)(2,1)S(1)}, bf16[8,2,16,128]{3,2,1,0:T(8,128)(2,1)S(1)}, u32[]{:S(2)}, u32[]{:S(2)}) collective-permute-start(bf16[8,2,16,128]{3,2,1,0:T(8,128)(2,1)S(1)} %get-tuple-element.45), channel_id=1, source_target_pairs={{0,32},{32,64},{64,96},{96,128},{128,160},{160,192},{192,224},{1,3... | collective-permute-start | bytes 196616 | tf_op jit(solution)/shard_map/ppermute | solution.py:21
  51.1 11.7 %collective-permute-start.7 = (bf16[2,8,16,128]{3,2,1,0:T(8,128)(2,1)S(1)}, bf16[2,8,16,128]{3,2,1,0:T(8,128)(2,1)S(1)}, u32[]{:S(2)}, u32[]{:S(2)}) collective-permute-start(bf16[2,8,16,128]{3,2,1,0:T(8,128)(2,1)S(1)} %get-tuple-element.35), channel_id=1, source_target_pairs={{1,0},{2,1},{3,2},{4,3},{5,4},{6,5},{7,6},{8,7},{9,8},{10,9},{11,1... | collective-permute-start | bytes 196616 | tf_op jit(solution)/shard_map/ppermute | solution.py:23
  53.0 10.2 %collective-permute-start.6 = (bf16[2,8,16,128]{3,2,1,0:T(8,128)(2,1)S(1)}, bf16[2,8,16,128]{3,2,1,0:T(8,128)(2,1)S(1)}, u32[]{:S(2)}, u32[]{:S(2)}) collective-permute-start(bf16[2,8,16,128]{3,2,1,0:T(8,128)(2,1)S(1)} %get-tuple-element.36), channel_id=1, source_target_pairs={{0,1},{1,2},{2,3},{3,4},{4,5},{5,6},{6,7},{7,8},{8,9},{9,10},{10,1... | collective-permute-start | bytes 196616 | tf_op jit(solution)/shard_map/ppermute | solution.py:21
  76.2 5.3 %collective-permute-start.8 = (bf16[1280,1024]{1,0:T(8,128)(2,1)}, bf16[1280,1024]{1,0:T(8,128)(2,1)}, u32[]{:S(2)}, u32[]{:S(2)}) collective-permute-start(bf16[1280,1024]{1,0:T(8,128)(2,1)} %all-gather.2.cloned.1.call-done), channel_id=1, source_target_pairs={{0,1},{1,0},{2,3},{3,2},{4,5},{5,4},{6,7},{7,6},{8,9},{9,8},{10,11... | collective-permute-start | bytes 7864328 | tf_op jit(solution)/shard_map/ppermute | solution.py:93
  84.9 2.3 copy-start
  88.1 13.6 %all-to-all-start.1 = ((bf16[8,32,1024]{2,1,0:T(8,128)(2,1)}), bf16[8,32,1024]{2,1,0:T(8,128)(2,1)S(1)}, u32[]{:S(2)}, u32[]{:S(2)}) async-start(bf16[8,32,1024]{2,1,0:T(8,128)(2,1)} %broadcast_in_dim.9), calls=%async_computation.1 | async-start | bytes 1048576 | tf_op jit(solution)/shard_map/all_to_all | solution.py:32
  95.2 6.8 %copy-start.5 = (bf16[32,128]{1,0:T(8,128)(2,1)S(1)}, bf16[32,128]{1,0:T(8,128)(2,1)}, u32[]{:S(2)}) copy-start(bf16[32,128]{1,0:T(8,128)(2,1)} %param.13) | copy-start | bytes 24580
  103.2 38.5 %all-to-all-start.2 = ((bf16[32,32,512]{2,1,0:T(8,128)(2,1)}), bf16[32,32,512]{2,1,0:T(8,128)(2,1)}, u32[]{:S(2)}, u32[]{:S(2)}) async-start(bf16[32,32,512]{2,1,0:T(8,128)(2,1)} %broadcast_in_dim.10), calls=%async_computation.2 | async-start | bytes 2097152 | tf_op jit(solution)/shard_map/all_to_all | solution.py:32
  172.7 8.4 %copy-start.2 = (f32[8,4,16,128]{3,2,1,0:T(8,128)S(1)}, f32[8,4,16,128]{3,2,1,0:T(8,128)}, u32[]{:S(2)}) copy-start(f32[8,4,16,128]{3,2,1,0:T(8,128)} %get-tuple-element.61) | copy-start | bytes 786436
  181.3 7.5 %collective-permute-start.10 = (bf16[8,2,16,128]{3,2,1,0:T(8,128)(2,1)S(1)}, bf16[8,2,16,128]{3,2,1,0:T(8,128)(2,1)S(1)}, u32[]{:S(2)}, u32[]{:S(2)}) collective-permute-start(bf16[8,2,16,128]{3,2,1,0:T(8,128)(2,1)S(1)} %get-tuple-element.44), channel_id=1, source_target_pairs={{32,0},{64,32},{96,64},{128,96},{160,128},{192,160},{224,192},{33,... | collective-permute-start | bytes 196616 | tf_op jit(solution)/shard_map/ppermute | solution.py:23
  184.2 5.0 %collective-permute-start.9 = (bf16[8,2,16,128]{3,2,1,0:T(8,128)(2,1)S(1)}, bf16[8,2,16,128]{3,2,1,0:T(8,128)(2,1)S(1)}, u32[]{:S(2)}, u32[]{:S(2)}) collective-permute-start(bf16[8,2,16,128]{3,2,1,0:T(8,128)(2,1)S(1)} %get-tuple-element.43), channel_id=1, source_target_pairs={{0,32},{32,64},{64,96},{96,128},{128,160},{160,192},{192,224},{1,3... | collective-permute-start | bytes 196616 | tf_op jit(solution)/shard_map/ppermute | solution.py:21
  189.3 11.0 %collective-permute-start.12 = (bf16[2,8,16,128]{3,2,1,0:T(8,128)(2,1)S(1)}, bf16[2,8,16,128]{3,2,1,0:T(8,128)(2,1)S(1)}, u32[]{:S(2)}, u32[]{:S(2)}) collective-permute-start(bf16[2,8,16,128]{3,2,1,0:T(8,128)(2,1)S(1)} %get-tuple-element.31), channel_id=1, source_target_pairs={{0,1},{1,2},{2,3},{3,4},{4,5},{5,6},{6,7},{7,8},{8,9},{9,10},{10,1... | collective-permute-start | bytes 196616 | tf_op jit(solution)/shard_map/ppermute | solution.py:21
  198.2 9.2 %collective-permute-start.11 = (bf16[2,8,16,128]{3,2,1,0:T(8,128)(2,1)S(1)}, bf16[2,8,16,128]{3,2,1,0:T(8,128)(2,1)S(1)}, u32[]{:S(2)}, u32[]{:S(2)}) collective-permute-start(bf16[2,8,16,128]{3,2,1,0:T(8,128)(2,1)S(1)} %get-tuple-element.32), channel_id=1, source_target_pairs={{1,0},{2,1},{3,2},{4,3},{5,4},{6,5},{7,6},{8,7},{9,8},{10,9},{11,1... | collective-permute-start | bytes 196616 | tf_op jit(solution)/shard_map/ppermute | solution.py:23
  210.1 7.5 %collective-permute-start.14 = (bf16[8,2,16,128]{3,2,1,0:T(8,128)(2,1)S(1)}, bf16[8,2,16,128]{3,2,1,0:T(8,128)(2,1)S(1)}, u32[]{:S(2)}, u32[]{:S(2)}) collective-permute-start(bf16[8,2,16,128]{3,2,1,0:T(8,128)(2,1)S(1)} %get-tuple-element.42), channel_id=1, source_target_pairs={{32,0},{64,32},{96,64},{128,96},{160,128},{192,160},{224,192},{33,... | collective-permute-start | bytes 196616 | tf_op jit(solution)/shard_map/ppermute | solution.py:23
  212.0 5.6 %collective-permute-start.13 = (bf16[8,2,16,128]{3,2,1,0:T(8,128)(2,1)S(1)}, bf16[8,2,16,128]{3,2,1,0:T(8,128)(2,1)S(1)}, u32[]{:S(2)}, u32[]{:S(2)}) collective-permute-start(bf16[8,2,16,128]{3,2,1,0:T(8,128)(2,1)S(1)} %get-tuple-element.41), channel_id=1, source_target_pairs={{0,32},{32,64},{64,96},{96,128},{128,160},{160,192},{192,224},{1,3... | collective-permute-start | bytes 196616 | tf_op jit(solution)/shard_map/ppermute | solution.py:21
  217.7 5.3 %collective-permute-start.16 = (bf16[2,8,16,128]{3,2,1,0:T(8,128)(2,1)S(1)}, bf16[2,8,16,128]{3,2,1,0:T(8,128)(2,1)S(1)}, u32[]{:S(2)}, u32[]{:S(2)}) collective-permute-start(bf16[2,8,16,128]{3,2,1,0:T(8,128)(2,1)S(1)} %get-tuple-element.27), channel_id=1, source_target_pairs={{0,1},{1,2},{2,3},{3,4},{4,5},{5,6},{6,7},{7,8},{8,9},{9,10},{10,1... | collective-permute-start | bytes 196616 | tf_op jit(solution)/shard_map/ppermute | solution.py:21
  220.9 9.2 %collective-permute-start.15 = (bf16[2,8,16,128]{3,2,1,0:T(8,128)(2,1)S(1)}, bf16[2,8,16,128]{3,2,1,0:T(8,128)(2,1)S(1)}, u32[]{:S(2)}, u32[]{:S(2)}) collective-permute-start(bf16[2,8,16,128]{3,2,1,0:T(8,128)(2,1)S(1)} %get-tuple-element.28), channel_id=1, source_target_pairs={{1,0},{2,1},{3,2},{4,3},{5,4},{6,5},{7,6},{8,7},{9,8},{10,9},{11,1... | collective-permute-start | bytes 196616 | tf_op jit(solution)/shard_map/ppermute | solution.py:23
  (3 other events, 2.6 us)
Sparse Core Ops, SparseCore 0:
  26.0 39.6 all-gather.1

commit v14 on v8

--- a/solution.py
+++ b/solution.py
@@ -74,7 +74,7 @@
     return jnp.sum(pieces.astype(jnp.float32), axis=0)
 
 
-def gather_weights(embed_weight, qkv_weight):
+def gather_weights(embed_weight, qkv_weight, after):
     _, feat, width = embed_weight.shape
     qkv_flat = qkv_weight.reshape(-1, width)
     extra = -qkv_flat.shape[0] % 16
@@ -89,6 +89,7 @@
     odd = (lax.axis_index("blk") & 1) != 0
     mine = jnp.where(odd, gathered[half:], gathered[:half])
     own = lax.all_gather(mine, "blk", axis=0, tiled=True, axis_index_groups=far)
+    own, after = lax.optimization_barrier((own, after))
     other = lax.ppermute(own, "blk", [(i, i ^ 1) for i in range(peers)])
     own = own.reshape(len(far[0]), half, width)
     other = other.reshape(len(far[0]), half, width)
@@ -101,7 +102,7 @@
     qkv_rows = jnp.moveaxis(qkv_rows, 0, 1).reshape(
         qkv_weight.shape[0], peers * qkv_weight.shape[1], qkv_weight.shape[2]
     )
-    return embed_rows, qkv_rows
+    return embed_rows, qkv_rows, after
 
 
 def with_rim(volume):
@@ -167,13 +168,13 @@
             hidden.astype(jnp.float32) + gate_mask * (conv_out * jax.nn.sigmoid(conv_out))
         ).astype(jnp.bfloat16)
     slab_view = lax.all_to_all(hidden, "zslab", split_axis=0, concat_axis=1, tiled=True)
+    embed_rows, qkv_rows, slab_view = gather_weights(embed_weight, qkv_weight, slab_view)
     x_local, z_total = (slab_view.shape[0], slab_view.shape[1])
     y_blocks, z_blocks = (y_cells // PY, z_total // PZ)
     patches = slab_view.reshape(x_local, z_blocks, PZ, y_blocks, PY, channels).transpose(
         3, 1, 0, 4, 2, 5
     )
     patches = patches.reshape(y_blocks * z_blocks, x_local, PY * PZ * channels)
-    embed_rows, qkv_rows = gather_weights(embed_weight, qkv_weight)
     patches = patches.reshape(patches.shape[0], embed_rows.shape[0], embed_rows.shape[1])
     partial_value = jnp.einsum(
         "tbf,bfd->td", patches, embed_rows, preferred_element_type=jnp.float32

time: 242 us -> 244 us (level)
  waiting for transfers between devices: 35.4 us -> 41.5 us
  starting transfers between devices: 75.8 us -> 71.8 us
  blocking collectives: 64.1 us -> 66.6 us
    ppermute x1, waiting for transfers between devices: 0.01 us -> 5 us  [gather_weights(): other = lax.ppermute(own, 'blk', [(i, i ^ 1) for i in range(peers)])]
    ppermute x1, starting transfers between devices: 3.82 us -> 0.01 us  [gather_weights(): other = lax.ppermute(own, 'blk', [(i, i ^ 1) for i in range(peers)])]
    unnamed x35 -> x27, local copies, waits for them, and re-layouts: 5.62 us -> 4.5 us
  transfers between devices with their start and end apart: 20 -> 20, of which waited for: 8 -> 9; matrix products, arithmetic and copies ran while one was open for 8% -> 7% of each run, Pallas kernels for 0% -> 0%
where the time goes in v14:
time: 244 us; the launch traced here: 241 us
  starting transfers between devices  71.8 us (29%)
  blocking collectives  66.6 us (27%)
  waiting for transfers between devices  41.5 us (17%)
  between operations  18.1 us (7%)
  local copies, waits for them, and re-layouts  17.7 us (7%)
  matrix products  15.2 us (6%)
  other arithmetic  10.5 us (4%)
    ppermute x8, starting transfers between devices, padded_2(): lax.ppermute(tail, axis, [(i, (i + 1) % count) for i in range(ends)])  42.1 us
    all_to_all x2, blocking collectives, copy_for_each(): lax.all_to_all(jnp.broadcast_to(shard[None], (peers, *shard.shape)), axis...  39 us
    ppermute x8, starting transfers between devices, padded_2(): lax.ppermute(head, axis, [((i + 1) % count, i) for i in range(ends)])  17.1 us
    ppermute x8, waiting for transfers between devices, padded_2(): lax.ppermute(head, axis, [((i + 1) % count, i) for i in range(ends)])  14.5 us
    all_to_all x1, waiting for transfers between devices, sum_at_owner(): lax.all_to_all(cut_along(shard, dim, peers), axis, 0, 0, tiled=True)  14.4 us
    all_to_all x1, blocking collectives, local(): lax.all_to_all(hidden, 'zslab', split_axis=0, concat_axis=1, tiled=True)  10 us
    all_gather x1, blocking collectives, gather_weights(): lax.all_gather(rows, 'blk', axis=0, tiled=True, axis_index_groups=near)  9.51 us
    all_to_all x1, starting transfers between devices, sum_at_owner(): lax.all_to_all(cut_along(shard, dim, peers), axis, 0, 0, tiled=True)  8.21 us
  transfers between devices with their start and end apart: 20, of which 9 were waited for; matrix products, arithmetic and copies ran while one was open for 7% of the time, Pallas kernels for 0%

profile of v14, /device:TPU:103, one launch (start us, length us, event | category | flops | bytes accessed | tf_op | source)
XLA Modules:
  0.0 241.4 jit_solution(11489893751170330333)
XLA Ops:
  7.5 2.5 %collective-permute-start.1 = (bf16[8,2,16,128]{3,2,1,0:T(8,128)(2,1)S(1)}, bf16[8,2,16,128]{3,2,1,0:T(8,128)(2,1)S(1)}, u32[]{:S(2)}, u32[]{:S(2)}) collective-permute-start(bf16[8,2,16,128]{3,2,1,0:T(8,128)(2,1)S(1)} %get-tuple-element.48), channel_id=1, source_target_pairs={{32,0},{64,32},{96,64},{128,96},{160,128},{192,160},{224,192},{33,... | collective-permute-start | bytes 196616 | tf_op jit(solution)/shard_map/ppermute | solution.py:23
  9.9 3.7 %collective-permute-start = (bf16[8,2,16,128]{3,2,1,0:T(8,128)(2,1)S(1)}, bf16[8,2,16,128]{3,2,1,0:T(8,128)(2,1)S(1)}, u32[]{:S(2)}, u32[]{:S(2)}) collective-permute-start(bf16[8,2,16,128]{3,2,1,0:T(8,128)(2,1)S(1)} %get-tuple-element.47), channel_id=1, source_target_pairs={{0,32},{32,64},{64,96},{96,128},{128,160},{160,192},{192,224},{1,3... | collective-permute-start | bytes 196616 | tf_op jit(solution)/shard_map/ppermute | solution.py:21
  15.6 9.5 %all_gather.6 = bf16[320,1024]{1,0:T(8,128)(2,1)S(1)} all-gather(bf16[80,1024]{1,0:T(8,128)(2,1)S(1)} %maximum_maximum_fusion.4), channel_id=1, replica_groups={{0,1,2,3},{4,5,6,7},{8,9,10,11},{12,13,14,15},{16,17,18,19},{20,21,22,2..., dimensions={0}, use_global_device_ids=true | all-gather | bytes 819200 | tf_op jit(solution)/shard_map/all_gather | solution.py:87
  30.2 7.1 %collective-permute-start.2 = (bf16[2,8,16,128]{3,2,1,0:T(8,128)(2,1)S(1)}, bf16[2,8,16,128]{3,2,1,0:T(8,128)(2,1)S(1)}, u32[]{:S(2)}, u32[]{:S(2)}) collective-permute-start(bf16[2,8,16,128]{3,2,1,0:T(8,128)(2,1)S(1)} %get-tuple-element.40), channel_id=1, source_target_pairs={{0,1},{1,2},{2,3},{3,4},{4,5},{5,6},{6,7},{7,8},{8,9},{9,10},{10,1... | collective-permute-start | bytes 196616 | tf_op jit(solution)/shard_map/ppermute | solution.py:21
  45.3 4.3 %collective-permute-start.4 = (bf16[8,2,16,128]{3,2,1,0:T(8,128)(2,1)S(1)}, bf16[8,2,16,128]{3,2,1,0:T(8,128)(2,1)S(1)}, u32[]{:S(2)}, u32[]{:S(2)}) collective-permute-start(bf16[8,2,16,128]{3,2,1,0:T(8,128)(2,1)S(1)} %get-tuple-element.45), channel_id=1, source_target_pairs={{0,32},{32,64},{64,96},{96,128},{128,160},{160,192},{192,224},{1,3... | collective-permute-start | bytes 196616 | tf_op jit(solution)/shard_map/ppermute | solution.py:21
  53.1 7.7 %collective-permute-start.6 = (bf16[2,8,16,128]{3,2,1,0:T(8,128)(2,1)S(1)}, bf16[2,8,16,128]{3,2,1,0:T(8,128)(2,1)S(1)}, u32[]{:S(2)}, u32[]{:S(2)}) collective-permute-start(bf16[2,8,16,128]{3,2,1,0:T(8,128)(2,1)S(1)} %get-tuple-element.36), channel_id=1, source_target_pairs={{0,1},{1,2},{2,3},{3,4},{4,5},{5,6},{6,7},{7,8},{8,9},{9,10},{10,1... | collective-permute-start | bytes 196616 | tf_op jit(solution)/shard_map/ppermute | solution.py:21
  66.1 10.0 %all_to_all.41 = bf16[8,4,16,128]{3,2,1,0:T(8,128)(2,1)S(1)} all-to-all(bf16[8,4,16,128]{3,2,1,0:T(8,128)(2,1)S(1)} %get-tuple-element.61), channel_id=1, replica_groups=mesh['zslab'=8,'blk'=32] {'zslab'}, dimensions={0} | all-to-all | bytes 262144 | tf_op jit(solution)/shard_map/all_to_all | solution.py:170
  76.4 5.0 %collective-permute-done.8 = bf16[1280,1024]{1,0:T(8,128)(2,1)} collective-permute-done((bf16[1280,1024]{1,0:T(8,128)(2,1)}, bf16[1280,1024]{1,0:T(8,128)(2,1)}, u32[]{:S(2)}, u32[]{:S(2)}) %collective-permute-start.8) | collective-permute-done | bytes 2621472 | tf_op jit(solution)/shard_map/ppermute | solution.py:93
  81.4 2.9 %broadcast_select_fusion.1 = (bf16[1280,1024]{1,0:T(8,128)(2,1)S(1)}, bf16[1280,1024]{1,0:T(8,128)(2,1)S(1)}) fusion(bf16[1280,1024]{1,0:T(8,128)(2,1)} %collective-permute-done.8, bf16[1280,1024]{1,0:T(8,128)(2,1)} %all-gather.2.cloned.1.call-done, pred[]{:T(512)S(6)} %ne.3), kind=kLoop, calls=%fused_computation.6 | loop fusion | flops 2621440 | bytes 10485761 | tf_op jit(solution)/shard_map/jit(_where)/select_n | solution.py:97
  88.0 4.4 %all-to-all-start.1 = ((bf16[8,32,1024]{2,1,0:T(8,128)(2,1)}), bf16[8,32,1024]{2,1,0:T(8,128)(2,1)S(1)}, u32[]{:S(2)}, u32[]{:S(2)}) async-start(bf16[8,32,1024]{2,1,0:T(8,128)(2,1)} %broadcast_in_dim.9), calls=%async_computation.1 | async-start | bytes 1048576 | tf_op jit(solution)/shard_map/all_to_all | solution.py:32
  96.4 5.3 %all-to-all-done.1 = bf16[8,32,1024]{2,1,0:T(8,128)(2,1)S(1)} async-done(((bf16[8,32,1024]{2,1,0:T(8,128)(2,1)}), bf16[8,32,1024]{2,1,0:T(8,128)(2,1)S(1)}, u32[]{:S(2)}, u32[]{:S(2)}) %all-to-all-start.1) | async-done | bytes 524320 | tf_op jit(solution)/shard_map/all_to_all | solution.py:32
  102.1 27.3 %all_to_all.42 = bf16[32,32,256]{2,1,0:T(8,128)(2,1)S(1)} all-to-all(bf16[32,32,256]{2,1,0:T(8,128)(2,1)S(1)} %broadcast_in_dim.10), channel_id=1, replica_groups=mesh['zslab'=8,'blk'=32] {'blk'}, dimensions={0} | all-to-all | bytes 1048576 | tf_op jit(solution)/shard_map/all_to_all | solution.py:32
  134.4 8.2 %all-to-all-start.3 = ((bf16[32,32,256]{2,1,0:T(8,128)(2,1)}), bf16[32,32,256]{2,1,0:T(8,128)(2,1)}, u32[]{:S(2)}, u32[]{:S(2)}) async-start(bf16[32,32,256]{2,1,0:T(8,128)(2,1)} %pad_maximum_fusion.1), calls=%async_computation.3 | async-start | bytes 1048576 | tf_op jit(solution)/shard_map/all_to_all | solution.py:73
  142.8 14.4 %all-to-all-done.3 = bf16[32,32,256]{2,1,0:T(8,128)(2,1)} async-done(((bf16[32,32,256]{2,1,0:T(8,128)(2,1)}), bf16[32,32,256]{2,1,0:T(8,128)(2,1)}, u32[]{:S(2)}, u32[]{:S(2)}) %all-to-all-start.3) | async-done | bytes 524320 | tf_op jit(solution)/shard_map/all_to_all | solution.py:73
  158.8 11.7 %all_to_all.43 = bf16[8,32,1024]{2,1,0:T(8,128)(2,1)S(1)} all-to-all(bf16[8,32,1024]{2,1,0:T(8,128)(2,1)S(1)} %broadcast_in_dim.11), channel_id=1, replica_groups=mesh['zslab'=8,'blk'=32] {'zslab'}, dimensions={0} | all-to-all | bytes 1048576 | tf_op jit(solution)/shard_map/all_to_all | solution.py:32
  170.6 4.2 %fusion.4 = bf16[32,32,64]{2,0,1:T(8,128)(2,1)S(1)} fusion(bf16[32,80,1024]{2,1,0:T(8,128)(2,1)} %bitcast.225, bf16[32,1024]{1,0:T(8,128)(2,1)S(1)} %reduce_sum.58), kind=kOutput, calls=%fused_computation.7 | convolution fusion | flops 134283264 | bytes 4390912 | tf_op jit(solution)/shard_map/td,bfd->tbf/dot_general | solution.py:233
  175.1 8.1 %all_to_all.44 = bf16[1,32,16,128]{3,2,0,1:T(8,128)(2,1)S(1)} all-to-all(bf16[1,32,16,128]{3,2,0,1:T(8,128)(2,1)S(1)} %bitcast.254), channel_id=1, replica_groups=mesh['zslab'=8,'blk'=32] {'zslab'}, dimensions={1} | all-to-all | bytes 262144 | tf_op jit(solution)/shard_map/all_to_all | solution.py:240
  183.4 2.9 %collective-permute-start.10 = (bf16[8,2,16,128]{3,2,1,0:T(8,128)(2,1)S(1)}, bf16[8,2,16,128]{3,2,1,0:T(8,128)(2,1)S(1)}, u32[]{:S(2)}, u32[]{:S(2)}) collective-permute-start(bf16[8,2,16,128]{3,2,1,0:T(8,128)(2,1)S(1)} %get-tuple-element.44), channel_id=1, source_target_pairs={{32,0},{64,32},{96,64},{128,96},{160,128},{192,160},{224,192},{33,... | collective-permute-start | bytes 196616 | tf_op jit(solution)/shard_map/ppermute | solution.py:23
  186.3 3.3 %collective-permute-start.9 = (bf16[8,2,16,128]{3,2,1,0:T(8,128)(2,1)S(1)}, bf16[8,2,16,128]{3,2,1,0:T(8,128)(2,1)S(1)}, u32[]{:S(2)}, u32[]{:S(2)}) collective-permute-start(bf16[8,2,16,128]{3,2,1,0:T(8,128)(2,1)S(1)} %get-tuple-element.43), channel_id=1, source_target_pairs={{0,32},{32,64},{64,96},{96,128},{128,160},{160,192},{192,224},{1,3... | collective-permute-start | bytes 196616 | tf_op jit(solution)/shard_map/ppermute | solution.py:21
  191.3 8.8 %collective-permute-start.12 = (bf16[2,8,16,128]{3,2,1,0:T(8,128)(2,1)S(1)}, bf16[2,8,16,128]{3,2,1,0:T(8,128)(2,1)S(1)}, u32[]{:S(2)}, u32[]{:S(2)}) collective-permute-start(bf16[2,8,16,128]{3,2,1,0:T(8,128)(2,1)S(1)} %get-tuple-element.31), channel_id=1, source_target_pairs={{0,1},{1,2},{2,3},{3,4},{4,5},{5,6},{6,7},{7,8},{8,9},{9,10},{10,1... | collective-permute-start | bytes 196616 | tf_op jit(solution)/shard_map/ppermute | solution.py:21
  202.2 7.2 %collective-permute-done.11 = bf16[2,8,16,128]{3,2,1,0:T(8,128)(2,1)S(1)} collective-permute-done((bf16[2,8,16,128]{3,2,1,0:T(8,128)(2,1)S(1)}, bf16[2,8,16,128]{3,2,1,0:T(8,128)(2,1)S(1)}, u32[]{:S(2)}, u32[]{:S(2)}) %collective-permute-start.11) | collective-permute-done | bytes 65568 | tf_op jit(solution)/shard_map/ppermute | solution.py:23
  213.9 4.3 %collective-permute-start.13 = (bf16[8,2,16,128]{3,2,1,0:T(8,128)(2,1)S(1)}, bf16[8,2,16,128]{3,2,1,0:T(8,128)(2,1)S(1)}, u32[]{:S(2)}, u32[]{:S(2)}) collective-permute-start(bf16[8,2,16,128]{3,2,1,0:T(8,128)(2,1)S(1)} %get-tuple-element.41), channel_id=1, source_target_pairs={{0,32},{32,64},{64,96},{96,128},{128,160},{160,192},{192,224},{1,3... | collective-permute-start | bytes 196616 | tf_op jit(solution)/shard_map/ppermute | solution.py:21
  219.6 3.0 %collective-permute-start.16 = (bf16[2,8,16,128]{3,2,1,0:T(8,128)(2,1)S(1)}, bf16[2,8,16,128]{3,2,1,0:T(8,128)(2,1)S(1)}, u32[]{:S(2)}, u32[]{:S(2)}) collective-permute-start(bf16[2,8,16,128]{3,2,1,0:T(8,128)(2,1)S(1)} %get-tuple-element.27), channel_id=1, source_target_pairs={{0,1},{1,2},{2,3},{3,4},{4,5},{5,6},{6,7},{7,8},{8,9},{9,10},{10,1... | collective-permute-start | bytes 196616 | tf_op jit(solution)/shard_map/ppermute | solution.py:21
  224.5 7.2 %collective-permute-done.15 = bf16[2,8,16,128]{3,2,1,0:T(8,128)(2,1)S(1)} collective-permute-done((bf16[2,8,16,128]{3,2,1,0:T(8,128)(2,1)S(1)}, bf16[2,8,16,128]{3,2,1,0:T(8,128)(2,1)S(1)}, u32[]{:S(2)}, u32[]{:S(2)}) %collective-permute-start.15) | collective-permute-done | bytes 65568 | tf_op jit(solution)/shard_map/ppermute | solution.py:23
  (160 shorter events, 50.5 us)
Async XLA Ops:
  6.5 69.6 %all-gather.2.cloned.1.call-start = ((), (), s32[]{:S(2)}) async-start(), calls=%async_computation.6 | async-start | bytes 2949120 | tf_op jit(solution)/shard_map/all_gather | solution.py:91
  7.5 20.7 %collective-permute-start.1 = (bf16[8,2,16,128]{3,2,1,0:T(8,128)(2,1)S(1)}, bf16[8,2,16,128]{3,2,1,0:T(8,128)(2,1)S(1)}, u32[]{:S(2)}, u32[]{:S(2)}) collective-permute-start(bf16[8,2,16,128]{3,2,1,0:T(8,128)(2,1)S(1)} %get-tuple-element.48), channel_id=1, source_target_pairs={{32,0},{64,32},{96,64},{128,96},{160,128},{192,160},{224,192},{33,... | collective-permute-start | bytes 196616 | tf_op jit(solution)/shard_map/ppermute | solution.py:23
  9.9 18.2 %collective-permute-start = (bf16[8,2,16,128]{3,2,1,0:T(8,128)(2,1)S(1)}, bf16[8,2,16,128]{3,2,1,0:T(8,128)(2,1)S(1)}, u32[]{:S(2)}, u32[]{:S(2)}) collective-permute-start(bf16[8,2,16,128]{3,2,1,0:T(8,128)(2,1)S(1)} %get-tuple-element.47), channel_id=1, source_target_pairs={{0,32},{32,64},{64,96},{96,128},{128,160},{160,192},{192,224},{1,3... | collective-permute-start | bytes 196616 | tf_op jit(solution)/shard_map/ppermute | solution.py:21
  27.4 9.9 %copy-start.4 = (s32[2,3]{1,0:T(2,128)S(1)}, s32[2,3]{1,0:T(2,128)}, u32[]{:S(2)}) copy-start(s32[2,3]{1,0:T(2,128)} %param.9) | copy-start | bytes 76
  28.2 11.7 %collective-permute-start.3 = (bf16[2,8,16,128]{3,2,1,0:T(8,128)(2,1)S(1)}, bf16[2,8,16,128]{3,2,1,0:T(8,128)(2,1)S(1)}, u32[]{:S(2)}, u32[]{:S(2)}) collective-permute-start(bf16[2,8,16,128]{3,2,1,0:T(8,128)(2,1)S(1)} %get-tuple-element.39), channel_id=1, source_target_pairs={{1,0},{2,1},{3,2},{4,3},{5,4},{6,5},{7,6},{8,7},{9,8},{10,9},{11,1... | collective-permute-start | bytes 196616 | tf_op jit(solution)/shard_map/ppermute | solution.py:23
  30.2 9.7 %collective-permute-start.2 = (bf16[2,8,16,128]{3,2,1,0:T(8,128)(2,1)S(1)}, bf16[2,8,16,128]{3,2,1,0:T(8,128)(2,1)S(1)}, u32[]{:S(2)}, u32[]{:S(2)}) collective-permute-start(bf16[2,8,16,128]{3,2,1,0:T(8,128)(2,1)S(1)} %get-tuple-element.40), channel_id=1, source_target_pairs={{0,1},{1,2},{2,3},{3,4},{4,5},{5,6},{6,7},{7,8},{8,9},{9,10},{10,1... | collective-permute-start | bytes 196616 | tf_op jit(solution)/shard_map/ppermute | solution.py:21
  43.4 6.3 %collective-permute-start.5 = (bf16[8,2,16,128]{3,2,1,0:T(8,128)(2,1)S(1)}, bf16[8,2,16,128]{3,2,1,0:T(8,128)(2,1)S(1)}, u32[]{:S(2)}, u32[]{:S(2)}) collective-permute-start(bf16[8,2,16,128]{3,2,1,0:T(8,128)(2,1)S(1)} %get-tuple-element.46), channel_id=1, source_target_pairs={{32,0},{64,32},{96,64},{128,96},{160,128},{192,160},{224,192},{33,... | collective-permute-start | bytes 196616 | tf_op jit(solution)/shard_map/ppermute | solution.py:23
  45.3 5.8 %collective-permute-start.4 = (bf16[8,2,16,128]{3,2,1,0:T(8,128)(2,1)S(1)}, bf16[8,2,16,128]{3,2,1,0:T(8,128)(2,1)S(1)}, u32[]{:S(2)}, u32[]{:S(2)}) collective-permute-start(bf16[8,2,16,128]{3,2,1,0:T(8,128)(2,1)S(1)} %get-tuple-element.45), channel_id=1, source_target_pairs={{0,32},{32,64},{64,96},{96,128},{128,160},{160,192},{192,224},{1,3... | collective-permute-start | bytes 196616 | tf_op jit(solution)/shard_map/ppermute | solution.py:21
  51.1 11.7 %collective-permute-start.7 = (bf16[2,8,16,128]{3,2,1,0:T(8,128)(2,1)S(1)}, bf16[2,8,16,128]{3,2,1,0:T(8,128)(2,1)S(1)}, u32[]{:S(2)}, u32[]{:S(2)}) collective-permute-start(bf16[2,8,16,128]{3,2,1,0:T(8,128)(2,1)S(1)} %get-tuple-element.35), channel_id=1, source_target_pairs={{1,0},{2,1},{3,2},{4,3},{5,4},{6,5},{7,6},{8,7},{9,8},{10,9},{11,1... | collective-permute-start | bytes 196616 | tf_op jit(solution)/shard_map/ppermute | solution.py:23
  53.1 10.2 %collective-permute-start.6 = (bf16[2,8,16,128]{3,2,1,0:T(8,128)(2,1)S(1)}, bf16[2,8,16,128]{3,2,1,0:T(8,128)(2,1)S(1)}, u32[]{:S(2)}, u32[]{:S(2)}) collective-permute-start(bf16[2,8,16,128]{3,2,1,0:T(8,128)(2,1)S(1)} %get-tuple-element.36), channel_id=1, source_target_pairs={{0,1},{1,2},{2,3},{3,4},{4,5},{5,6},{6,7},{7,8},{8,9},{9,10},{10,1... | collective-permute-start | bytes 196616 | tf_op jit(solution)/shard_map/ppermute | solution.py:21
  76.1 5.3 %collective-permute-start.8 = (bf16[1280,1024]{1,0:T(8,128)(2,1)}, bf16[1280,1024]{1,0:T(8,128)(2,1)}, u32[]{:S(2)}, u32[]{:S(2)}) collective-permute-start(bf16[1280,1024]{1,0:T(8,128)(2,1)} %all-gather.2.cloned.1.call-done), channel_id=1, source_target_pairs={{0,1},{1,0},{2,3},{3,2},{4,5},{5,4},{6,7},{7,6},{8,9},{9,8},{10,11... | collective-permute-start | bytes 7864328 | tf_op jit(solution)/shard_map/ppermute | solution.py:93
  84.9 2.3 copy-start
  88.0 13.6 %all-to-all-start.1 = ((bf16[8,32,1024]{2,1,0:T(8,128)(2,1)}), bf16[8,32,1024]{2,1,0:T(8,128)(2,1)S(1)}, u32[]{:S(2)}, u32[]{:S(2)}) async-start(bf16[8,32,1024]{2,1,0:T(8,128)(2,1)} %broadcast_in_dim.9), calls=%async_computation.1 | async-start | bytes 1048576 | tf_op jit(solution)/shard_map/all_to_all | solution.py:32
  102.0 27.9 %copy-start.5 = (bf16[32,128]{1,0:T(8,128)(2,1)S(1)}, bf16[32,128]{1,0:T(8,128)(2,1)}, u32[]{:S(2)}) copy-start(bf16[32,128]{1,0:T(8,128)(2,1)} %param.13) | copy-start | bytes 24580
  134.4 22.8 %all-to-all-start.3 = ((bf16[32,32,256]{2,1,0:T(8,128)(2,1)}), bf16[32,32,256]{2,1,0:T(8,128)(2,1)}, u32[]{:S(2)}, u32[]{:S(2)}) async-start(bf16[32,32,256]{2,1,0:T(8,128)(2,1)} %pad_maximum_fusion.1), calls=%async_computation.3 | async-start | bytes 1048576 | tf_op jit(solution)/shard_map/all_to_all | solution.py:73
  174.8 8.4 %copy-start.2 = (f32[8,4,16,128]{3,2,1,0:T(8,128)S(1)}, f32[8,4,16,128]{3,2,1,0:T(8,128)}, u32[]{:S(2)}) copy-start(f32[8,4,16,128]{3,2,1,0:T(8,128)} %get-tuple-element.62) | copy-start | bytes 786436
  183.4 7.5 %collective-permute-start.10 = (bf16[8,2,16,128]{3,2,1,0:T(8,128)(2,1)S(1)}, bf16[8,2,16,128]{3,2,1,0:T(8,128)(2,1)S(1)}, u32[]{:S(2)}, u32[]{:S(2)}) collective-permute-start(bf16[8,2,16,128]{3,2,1,0:T(8,128)(2,1)S(1)} %get-tuple-element.44), channel_id=1, source_target_pairs={{32,0},{64,32},{96,64},{128,96},{160,128},{192,160},{224,192},{33,... | collective-permute-start | bytes 196616 | tf_op jit(solution)/shard_map/ppermute | solution.py:23
  186.3 5.0 %collective-permute-start.9 = (bf16[8,2,16,128]{3,2,1,0:T(8,128)(2,1)S(1)}, bf16[8,2,16,128]{3,2,1,0:T(8,128)(2,1)S(1)}, u32[]{:S(2)}, u32[]{:S(2)}) collective-permute-start(bf16[8,2,16,128]{3,2,1,0:T(8,128)(2,1)S(1)} %get-tuple-element.43), channel_id=1, source_target_pairs={{0,32},{32,64},{64,96},{96,128},{128,160},{160,192},{192,224},{1,3... | collective-permute-start | bytes 196616 | tf_op jit(solution)/shard_map/ppermute | solution.py:21
  191.3 10.8 %collective-permute-start.12 = (bf16[2,8,16,128]{3,2,1,0:T(8,128)(2,1)S(1)}, bf16[2,8,16,128]{3,2,1,0:T(8,128)(2,1)S(1)}, u32[]{:S(2)}, u32[]{:S(2)}) collective-permute-start(bf16[2,8,16,128]{3,2,1,0:T(8,128)(2,1)S(1)} %get-tuple-element.31), channel_id=1, source_target_pairs={{0,1},{1,2},{2,3},{3,4},{4,5},{5,6},{6,7},{7,8},{8,9},{9,10},{10,1... | collective-permute-start | bytes 196616 | tf_op jit(solution)/shard_map/ppermute | solution.py:21
  200.2 9.2 %collective-permute-start.11 = (bf16[2,8,16,128]{3,2,1,0:T(8,128)(2,1)S(1)}, bf16[2,8,16,128]{3,2,1,0:T(8,128)(2,1)S(1)}, u32[]{:S(2)}, u32[]{:S(2)}) collective-permute-start(bf16[2,8,16,128]{3,2,1,0:T(8,128)(2,1)S(1)} %get-tuple-element.32), channel_id=1, source_target_pairs={{1,0},{2,1},{3,2},{4,3},{5,4},{6,5},{7,6},{8,7},{9,8},{10,9},{11,1... | collective-permute-start | bytes 196616 | tf_op jit(solution)/shard_map/ppermute | solution.py:23
  212.0 7.5 %collective-permute-start.14 = (bf16[8,2,16,128]{3,2,1,0:T(8,128)(2,1)S(1)}, bf16[8,2,16,128]{3,2,1,0:T(8,128)(2,1)S(1)}, u32[]{:S(2)}, u32[]{:S(2)}) collective-permute-start(bf16[8,2,16,128]{3,2,1,0:T(8,128)(2,1)S(1)} %get-tuple-element.42), channel_id=1, source_target_pairs={{32,0},{64,32},{96,64},{128,96},{160,128},{192,160},{224,192},{33,... | collective-permute-start | bytes 196616 | tf_op jit(solution)/shard_map/ppermute | solution.py:23
  213.9 5.6 %collective-permute-start.13 = (bf16[8,2,16,128]{3,2,1,0:T(8,128)(2,1)S(1)}, bf16[8,2,16,128]{3,2,1,0:T(8,128)(2,1)S(1)}, u32[]{:S(2)}, u32[]{:S(2)}) collective-permute-start(bf16[8,2,16,128]{3,2,1,0:T(8,128)(2,1)S(1)} %get-tuple-element.41), channel_id=1, source_target_pairs={{0,32},{32,64},{64,96},{96,128},{128,160},{160,192},{192,224},{1,3... | collective-permute-start | bytes 196616 | tf_op jit(solution)/shard_map/ppermute | solution.py:21
  219.6 5.0 %collective-permute-start.16 = (bf16[2,8,16,128]{3,2,1,0:T(8,128)(2,1)S(1)}, bf16[2,8,16,128]{3,2,1,0:T(8,128)(2,1)S(1)}, u32[]{:S(2)}, u32[]{:S(2)}) collective-permute-start(bf16[2,8,16,128]{3,2,1,0:T(8,128)(2,1)S(1)} %get-tuple-element.27), channel_id=1, source_target_pairs={{0,1},{1,2},{2,3},{3,4},{4,5},{5,6},{6,7},{7,8},{8,9},{9,10},{10,1... | collective-permute-start | bytes 196616 | tf_op jit(solution)/shard_map/ppermute | solution.py:21
  222.5 9.2 %collective-permute-start.15 = (bf16[2,8,16,128]{3,2,1,0:T(8,128)(2,1)S(1)}, bf16[2,8,16,128]{3,2,1,0:T(8,128)(2,1)S(1)}, u32[]{:S(2)}, u32[]{:S(2)}) collective-permute-start(bf16[2,8,16,128]{3,2,1,0:T(8,128)(2,1)S(1)} %get-tuple-element.28), channel_id=1, source_target_pairs={{1,0},{2,1},{3,2},{4,3},{5,4},{6,5},{7,6},{8,7},{9,8},{10,9},{11,1... | collective-permute-start | bytes 196616 | tf_op jit(solution)/shard_map/ppermute | solution.py:23
  (3 other events, 2.6 us)
Sparse Core Ops, SparseCore 0:
  26.0 39.6 all-gather.1

commit v15 on v9

--- a/solution.py
+++ b/solution.py
@@ -84,16 +84,13 @@
 
 def gather_weights(embed_weight, qkv_weight):
     _, feat, width = embed_weight.shape
+    peers = lax.axis_size("blk")
+    embed_rows = gathered_in_stages(embed_weight[0], "blk").reshape(peers, feat, width)
     qkv_flat = qkv_weight.reshape(-1, width)
     extra = -qkv_flat.shape[0] % 16
-    rows = jnp.concatenate(
-        [embed_weight[0], qkv_flat, jnp.zeros((extra, width), qkv_flat.dtype)], axis=0
-    )
-    peers = lax.axis_size("blk")
-    gathered = gathered_in_stages(rows, "blk")
-    gathered = gathered.reshape(peers, rows.shape[0], width)
-    embed_rows = gathered[:, :feat, :]
-    qkv_rows = gathered[:, feat : feat + qkv_flat.shape[0], :].reshape(peers, *qkv_weight.shape)
+    rows = jnp.concatenate([qkv_flat, jnp.zeros((extra, width), qkv_flat.dtype)], axis=0)
+    gathered = gathered_in_stages(rows, "blk").reshape(peers, rows.shape[0], width)
+    qkv_rows = gathered[:, : qkv_flat.shape[0], :].reshape(peers, *qkv_weight.shape)
     qkv_rows = jnp.moveaxis(qkv_rows, 0, 1).reshape(
         qkv_weight.shape[0], peers * qkv_weight.shape[1], qkv_weight.shape[2]
     )
@@ -179,7 +176,9 @@
         "td,sde->ste", tokens, qkv_rows, preferred_element_type=jnp.float32
     ).astype(jnp.bfloat16)
     key_rows, value_rows = jnp.split(
-        gathered_in_stages(jnp.concatenate([projected[1], projected[2]], axis=1), "blk"), 2, axis=1
+        joined_along(copy_for_each(jnp.concatenate([projected[1], projected[2]], axis=1), "blk"), 0),
+        2,
+        axis=1,
     )
     tok_rows = tokens.shape[0]
     head_cols = projected.shape[2]

time: 248 us -> 251 us (1.012)
  blocking collectives: 67.8 us -> 73.7 us
  starting transfers between devices: 77 us -> 71.6 us
  waiting for transfers between devices: 43.7 us -> 47.8 us
    all_to_all x1 -> x2, blocking collectives: 11.9 us -> 40.4 us  [copy_for_each(): lax.all_to_all(jnp.broadcast_to(shard[None], (peers, *shard.shape)), axis...]
    all_gather x1 -> x0, blocking collectives: 19.7 us -> none  [gathered_in_stages(): return lax.all_gather(rows, axis, axis=0, tiled=True, axis_index_groups=far)]
    all_gather x1 -> x2, waiting for transfers between devices: 0.75 us -> 13.3 us  [gathered_in_stages(): return lax.all_gather(rows, axis, axis=0, tiled=True, axis_index_groups=far)]
    all_to_all x1, starting transfers between devices: 14.7 us -> 8.22 us  [sum_at_owner(): lax.all_to_all(cut_along(shard, dim, peers), axis, 0, 0, tiled=True)]
    ppermute x8, waiting for transfers between devices: 22 us -> 17.6 us  [padded_2(): lax.ppermute(head, axis, [((i + 1) % count, i) for i in range(ends)])]
    all_to_all x1, waiting for transfers between devices: 4.05 us -> 0.01 us  [copy_for_each(): lax.all_to_all(jnp.broadcast_to(shard[None], (peers, *shard.shape)), axis...]
    all_gather x2, blocking collectives: 18.7 us -> 15.8 us  [gathered_in_stages(): lax.all_gather(rows, axis, axis=0, tiled=True, axis_index_groups=near)]
  transfers between devices with their start and end apart: 19 -> 20, of which waited for: 12 -> 9; matrix products, arithmetic and copies ran while one was open for 6% -> 7% of each run, Pallas kernels for 0% -> 0%
where the time goes in v15:
time: 251 us; the launch traced here: 247 us
  blocking collectives  73.7 us (29%)
  starting transfers between devices  71.6 us (29%)
  waiting for transfers between devices  47.8 us (19%)
  between operations  18.2 us (7%)
  matrix products  17.5 us (7%)
  local copies, waits for them, and re-layouts  11.7 us (5%)
  other arithmetic  6.32 us (3%)
    all_to_all x2, blocking collectives, copy_for_each(): lax.all_to_all(jnp.broadcast_to(shard[None], (peers, *shard.shape)), axis...  40.4 us
    ppermute x8, starting transfers between devices, padded_2(): lax.ppermute(tail, axis, [(i, (i + 1) % count) for i in range(ends)])  33.2 us
    ppermute x8, starting transfers between devices, padded_2(): lax.ppermute(head, axis, [((i + 1) % count, i) for i in range(ends)])  25.2 us
    ppermute x8, waiting for transfers between devices, padded_2(): lax.ppermute(head, axis, [((i + 1) % count, i) for i in range(ends)])  17.6 us
    all_gather x2, blocking collectives, gathered_in_stages(): lax.all_gather(rows, axis, axis=0, tiled=True, axis_index_groups=near)  15.8 us
    all_to_all x1, waiting for transfers between devices, sum_at_owner(): lax.all_to_all(cut_along(shard, dim, peers), axis, 0, 0, tiled=True)  14.4 us
    all_gather x2, waiting for transfers between devices, gathered_in_stages(): return lax.all_gather(rows, axis, axis=0, tiled=True, axis_index_groups=far)  13.3 us
    all_to_all x1, blocking collectives, local(): lax.all_to_all(hidden, 'zslab', split_axis=0, concat_axis=1, tiled=True)  9.41 us
  transfers between devices with their start and end apart: 20, of which 9 were waited for; matrix products, arithmetic and copies ran while one was open for 7% of the time, Pallas kernels for 0%

profile of v15, /device:TPU:103, one launch (start us, length us, event | category | flops | bytes accessed | tf_op | source)
XLA Modules:
  0.0 246.8 jit_solution(15349338211288598946)
XLA Ops:
  6.5 9.6 %all-gather = bf16[1,256,1024]{2,1,0:T(8,128)(2,1)} all-gather(bf16[1,64,1024]{2,1,0:T(8,128)(2,1)} %param.11), channel_id=2, replica_groups={{0,1,2,3},{4,5,6,7},{8,9,10,11},{12,13,14,15},{16,17,18,19},{20,21,22,2..., dimensions={1}, use_global_device_ids=true | all-gather | bytes 655360 | tf_op jit(solution)/shard_map/all_gather | solution.py:81
  16.2 3.5 %collective-permute-start = (bf16[8,2,16,128]{3,2,1,0:T(8,128)(2,1)S(1)}, bf16[8,2,16,128]{3,2,1,0:T(8,128)(2,1)S(1)}, u32[]{:S(2)}, u32[]{:S(2)}) collective-permute-start(bf16[8,2,16,128]{3,2,1,0:T(8,128)(2,1)S(1)} %get-tuple-element.41), channel_id=1, source_target_pairs={{0,32},{32,64},{64,96},{96,128},{128,160},{160,192},{192,224},{1,3... | collective-permute-start | bytes 196616 | tf_op jit(solution)/shard_map/ppermute | solution.py:21
  25.6 8.1 %collective-permute-start.2 = (bf16[2,8,16,128]{3,2,1,0:T(8,128)(2,1)S(1)}, bf16[2,8,16,128]{3,2,1,0:T(8,128)(2,1)S(1)}, u32[]{:S(2)}, u32[]{:S(2)}) collective-permute-start(bf16[2,8,16,128]{3,2,1,0:T(8,128)(2,1)S(1)} %get-tuple-element.34), channel_id=1, source_target_pairs={{0,1},{1,2},{2,3},{3,4},{4,5},{5,6},{6,7},{7,8},{8,9},{9,10},{10,1... | collective-permute-start | bytes 196616 | tf_op jit(solution)/shard_map/ppermute | solution.py:21
  38.3 6.0 %collective-permute-done.3 = bf16[2,8,16,128]{3,2,1,0:T(8,128)(2,1)S(1)} collective-permute-done((bf16[2,8,16,128]{3,2,1,0:T(8,128)(2,1)S(1)}, bf16[2,8,16,128]{3,2,1,0:T(8,128)(2,1)S(1)}, u32[]{:S(2)}, u32[]{:S(2)}) %collective-permute-start.3) | collective-permute-done | bytes 65568 | tf_op jit(solution)/shard_map/ppermute | solution.py:23
  49.1 3.4 %collective-permute-start.5 = (bf16[8,2,16,128]{3,2,1,0:T(8,128)(2,1)S(1)}, bf16[8,2,16,128]{3,2,1,0:T(8,128)(2,1)S(1)}, u32[]{:S(2)}, u32[]{:S(2)}) collective-permute-start(bf16[8,2,16,128]{3,2,1,0:T(8,128)(2,1)S(1)} %get-tuple-element.40), channel_id=1, source_target_pairs={{32,0},{64,32},{96,64},{128,96},{160,128},{192,160},{224,192},{33,... | collective-permute-start | bytes 196616 | tf_op jit(solution)/shard_map/ppermute | solution.py:23
  52.6 6.2 %all_gather.12 = bf16[64,1024]{1,0:T(8,128)(2,1)} all-gather(bf16[16,1024]{1,0:T(8,128)(2,1)S(1)} %concatenate.155), channel_id=1, replica_groups={{0,1,2,3},{4,5,6,7},{8,9,10,11},{12,13,14,15},{16,17,18,19},{20,21,22,2..., dimensions={0}, use_global_device_ids=true | all-gather | bytes 163840 | tf_op jit(solution)/shard_map/all_gather | solution.py:81
  58.9 3.5 %collective-permute-start.6 = (bf16[2,8,16,128]{3,2,1,0:T(8,128)(2,1)S(1)}, bf16[2,8,16,128]{3,2,1,0:T(8,128)(2,1)S(1)}, u32[]{:S(2)}, u32[]{:S(2)}) collective-permute-start(bf16[2,8,16,128]{3,2,1,0:T(8,128)(2,1)S(1)} %get-tuple-element.30), channel_id=1, source_target_pairs={{0,1},{1,2},{2,3},{3,4},{4,5},{5,6},{6,7},{7,8},{8,9},{9,10},{10,1... | collective-permute-start | bytes 196616 | tf_op jit(solution)/shard_map/ppermute | solution.py:21
  66.3 6.6 %collective-permute-done.7 = bf16[2,8,16,128]{3,2,1,0:T(8,128)(2,1)S(1)} collective-permute-done((bf16[2,8,16,128]{3,2,1,0:T(8,128)(2,1)S(1)}, bf16[2,8,16,128]{3,2,1,0:T(8,128)(2,1)S(1)}, u32[]{:S(2)}, u32[]{:S(2)}) %collective-permute-start.7) | collective-permute-done | bytes 65568 | tf_op jit(solution)/shard_map/ppermute | solution.py:23
  75.8 9.4 %all_to_all.38 = bf16[8,4,16,128]{3,2,1,0:T(8,128)(2,1)S(1)} all-to-all(bf16[8,4,16,128]{3,2,1,0:T(8,128)(2,1)S(1)} %get-tuple-element.55), channel_id=1, replica_groups=mesh['zslab'=8,'blk'=32] {'zslab'}, dimensions={0} | all-to-all | bytes 262144 | tf_op jit(solution)/shard_map/all_to_all | solution.py:162
  85.5 3.0 %fusion.16 = bf16[32,1024]{1,0:T(8,128)(2,1)S(1)} fusion(bf16[32,64,1024]{2,1,0:T(8,128)(2,1)} %bitcast.218, bf16[32,32,64]{2,1,0:T(8,128)(2,1)S(1)} %reshape_reshape.9), kind=kOutput, calls=%fused_computation.27 | convolution fusion | flops 134250496 | bytes 4390912 | tf_op jit(solution)/shard_map/tbf,bfd->td/dot_general | solution.py:171
  89.4 5.0 %all-to-all-start.1 = ((bf16[8,32,1024]{2,1,0:T(8,128)(2,1)}), bf16[8,32,1024]{2,1,0:T(8,128)(2,1)}, u32[]{:S(2)}, u32[]{:S(2)}) async-start(bf16[8,32,1024]{2,1,0:T(8,128)(2,1)} %broadcast_in_dim.6), calls=%async_computation.1 | async-start | bytes 1048576 | tf_op jit(solution)/shard_map/all_to_all | solution.py:32
  94.4 13.3 %all-gather.5.cloned.1.call-done = bf16[512,1024]{1,0:T(8,128)(2,1)} async-done(((bf16[64,1024]{1,0:T(8,128)(2,1)}), bf16[512,1024]{1,0:T(8,128)(2,1)}) %all-gather.5.cloned.1.call-update) | async-done | bytes 1048592 | tf_op jit(solution)/shard_map/all_gather | solution.py:82
  111.0 26.9 %all_to_all.39 = bf16[32,32,256]{2,1,0:T(8,128)(2,1)S(1)} all-to-all(bf16[32,32,256]{2,1,0:T(8,128)(2,1)S(1)} %broadcast_in_dim.7), channel_id=1, replica_groups=mesh['zslab'=8,'blk'=32] {'blk'}, dimensions={0} | all-to-all | bytes 1048576 | tf_op jit(solution)/shard_map/all_to_all | solution.py:32
  143.0 8.2 %all-to-all-start.3 = ((bf16[32,32,256]{2,1,0:T(8,128)(2,1)}), bf16[32,32,256]{2,1,0:T(8,128)(2,1)}, u32[]{:S(2)}, u32[]{:S(2)}) async-start(bf16[32,32,256]{2,1,0:T(8,128)(2,1)} %pad_maximum_fusion), calls=%async_computation.3 | async-start | bytes 1048576 | tf_op jit(solution)/shard_map/all_to_all | solution.py:73
  151.4 14.4 %all-to-all-done.3 = bf16[32,32,256]{2,1,0:T(8,128)(2,1)} async-done(((bf16[32,32,256]{2,1,0:T(8,128)(2,1)}), bf16[32,32,256]{2,1,0:T(8,128)(2,1)}, u32[]{:S(2)}, u32[]{:S(2)}) %all-to-all-start.3) | async-done | bytes 524320 | tf_op jit(solution)/shard_map/all_to_all | solution.py:73
  167.3 13.5 %all_to_all.40 = bf16[8,32,1024]{2,1,0:T(8,128)(2,1)S(1)} all-to-all(bf16[8,32,1024]{2,1,0:T(8,128)(2,1)S(1)} %broadcast_in_dim.8), channel_id=1, replica_groups=mesh['zslab'=8,'blk'=32] {'zslab'}, dimensions={0} | all-to-all | bytes 1048576 | tf_op jit(solution)/shard_map/all_to_all | solution.py:32
  180.9 4.2 %convolution_convert_fusion = bf16[32,32,64]{2,0,1:T(8,128)(2,1)S(1)} fusion(bf16[32,64,1024]{2,1,0:T(8,128)(2,1)} %bitcast.219, bf16[32,1024]{1,0:T(8,128)(2,1)S(1)} %reduce_sum.58), kind=kOutput, calls=%fused_computation | convolution fusion | flops 134283264 | bytes 4390912 | tf_op jit(solution)/shard_map/td,bfd->tbf/dot_general | solution.py:225
  185.4 8.1 %all_to_all.41 = bf16[1,32,16,128]{3,2,0,1:T(8,128)(2,1)S(1)} all-to-all(bf16[1,32,16,128]{3,2,0,1:T(8,128)(2,1)S(1)} %bitcast.254), channel_id=1, replica_groups=mesh['zslab'=8,'blk'=32] {'zslab'}, dimensions={1} | all-to-all | bytes 262144 | tf_op jit(solution)/shard_map/all_to_all | solution.py:232
  193.7 2.7 %collective-permute-start.8 = (bf16[8,2,16,128]{3,2,1,0:T(8,128)(2,1)S(1)}, bf16[8,2,16,128]{3,2,1,0:T(8,128)(2,1)S(1)}, u32[]{:S(2)}, u32[]{:S(2)}) collective-permute-start(bf16[8,2,16,128]{3,2,1,0:T(8,128)(2,1)S(1)} %get-tuple-element.37), channel_id=1, source_target_pairs={{0,32},{32,64},{64,96},{96,128},{128,160},{160,192},{192,224},{1,3... | collective-permute-start | bytes 196616 | tf_op jit(solution)/shard_map/ppermute | solution.py:21
  202.5 5.8 %collective-permute-start.10 = (bf16[2,8,16,128]{3,2,1,0:T(8,128)(2,1)S(1)}, bf16[2,8,16,128]{3,2,1,0:T(8,128)(2,1)S(1)}, u32[]{:S(2)}, u32[]{:S(2)}) collective-permute-start(bf16[2,8,16,128]{3,2,1,0:T(8,128)(2,1)S(1)} %get-tuple-element.26), channel_id=1, source_target_pairs={{1,0},{2,1},{3,2},{4,3},{5,4},{6,5},{7,6},{8,7},{9,8},{10,9},{11,1... | collective-permute-start | bytes 196616 | tf_op jit(solution)/shard_map/ppermute | solution.py:23
  208.3 4.7 %collective-permute-start.11 = (bf16[2,8,16,128]{3,2,1,0:T(8,128)(2,1)S(1)}, bf16[2,8,16,128]{3,2,1,0:T(8,128)(2,1)S(1)}, u32[]{:S(2)}, u32[]{:S(2)}) collective-permute-start(bf16[2,8,16,128]{3,2,1,0:T(8,128)(2,1)S(1)} %get-tuple-element.25), channel_id=1, source_target_pairs={{0,1},{1,2},{2,3},{3,4},{4,5},{5,6},{6,7},{7,8},{8,9},{9,10},{10,1... | collective-permute-start | bytes 196616 | tf_op jit(solution)/shard_map/ppermute | solution.py:21
  218.9 3.4 %collective-permute-start.13 = (bf16[8,2,16,128]{3,2,1,0:T(8,128)(2,1)S(1)}, bf16[8,2,16,128]{3,2,1,0:T(8,128)(2,1)S(1)}, u32[]{:S(2)}, u32[]{:S(2)}) collective-permute-start(bf16[8,2,16,128]{3,2,1,0:T(8,128)(2,1)S(1)} %get-tuple-element.36), channel_id=1, source_target_pairs={{32,0},{64,32},{96,64},{128,96},{160,128},{192,160},{224,192},{33,... | collective-permute-start | bytes 196616 | tf_op jit(solution)/shard_map/ppermute | solution.py:23
  224.8 4.1 %collective-permute-start.14 = (bf16[2,8,16,128]{3,2,1,0:T(8,128)(2,1)S(1)}, bf16[2,8,16,128]{3,2,1,0:T(8,128)(2,1)S(1)}, u32[]{:S(2)}, u32[]{:S(2)}) collective-permute-start(bf16[2,8,16,128]{3,2,1,0:T(8,128)(2,1)S(1)} %get-tuple-element.22), channel_id=1, source_target_pairs={{1,0},{2,1},{3,2},{4,3},{5,4},{6,5},{7,6},{8,7},{9,8},{10,9},{11,1... | collective-permute-start | bytes 196616 | tf_op jit(solution)/shard_map/ppermute | solution.py:23
  229.0 6.8 %collective-permute-start.15 = (bf16[2,8,16,128]{3,2,1,0:T(8,128)(2,1)S(1)}, bf16[2,8,16,128]{3,2,1,0:T(8,128)(2,1)S(1)}, u32[]{:S(2)}, u32[]{:S(2)}) collective-permute-start(bf16[2,8,16,128]{3,2,1,0:T(8,128)(2,1)S(1)} %get-tuple-element.21), channel_id=1, source_target_pairs={{0,1},{1,2},{2,3},{3,4},{4,5},{5,6},{6,7},{7,8},{8,9},{9,10},{10,1... | collective-permute-start | bytes 196616 | tf_op jit(solution)/shard_map/ppermute | solution.py:21
  (156 shorter events, 48.0 us)
Async XLA Ops:
  6.5 9.7 %copy-start = (bf16[8,16,4,128]{3,2,1,0:T(4,128)(2,1)S(1)}, bf16[8,16,4,128]{3,2,1,0:T(4,128)(2,1)}, u32[]{:S(2)}) copy-start(bf16[8,16,4,128]{3,2,1,0:T(4,128)(2,1)} %param.7) | copy-start | bytes 393220
  6.5 78.9 %all-gather.7.cloned.1.call-start = ((), (), s32[]{:S(2)}) async-start(), calls=%async_computation.7 | async-start | bytes 4718592 | tf_op jit(solution)/shard_map/all_gather | solution.py:82
  16.1 91.6 %all-gather.5.cloned.1.call-start = ((), (), s32[]{:S(2)}) async-start(), calls=%async_computation.6 | async-start | bytes 1179648 | tf_op jit(solution)/shard_map/all_gather | solution.py:82
  16.2 7.7 %collective-permute-start = (bf16[8,2,16,128]{3,2,1,0:T(8,128)(2,1)S(1)}, bf16[8,2,16,128]{3,2,1,0:T(8,128)(2,1)S(1)}, u32[]{:S(2)}, u32[]{:S(2)}) collective-permute-start(bf16[8,2,16,128]{3,2,1,0:T(8,128)(2,1)S(1)} %get-tuple-element.41), channel_id=1, source_target_pairs={{0,32},{32,64},{64,96},{96,128},{128,160},{160,192},{192,224},{1,3... | collective-permute-start | bytes 196616 | tf_op jit(solution)/shard_map/ppermute | solution.py:21
  19.7 5.9 %collective-permute-start.1 = (bf16[8,2,16,128]{3,2,1,0:T(8,128)(2,1)S(1)}, bf16[8,2,16,128]{3,2,1,0:T(8,128)(2,1)S(1)}, u32[]{:S(2)}, u32[]{:S(2)}) collective-permute-start(bf16[8,2,16,128]{3,2,1,0:T(8,128)(2,1)S(1)} %get-tuple-element.42), channel_id=1, source_target_pairs={{32,0},{64,32},{96,64},{128,96},{160,128},{192,160},{224,192},{33,... | collective-permute-start | bytes 196616 | tf_op jit(solution)/shard_map/ppermute | solution.py:23
  23.2 12.5 %copy-start.4 = (s32[2,3]{1,0:T(2,128)S(1)}, s32[2,3]{1,0:T(2,128)}, u32[]{:S(2)}) copy-start(s32[2,3]{1,0:T(2,128)} %param.9) | copy-start | bytes 76
  25.6 12.6 %collective-permute-start.2 = (bf16[2,8,16,128]{3,2,1,0:T(8,128)(2,1)S(1)}, bf16[2,8,16,128]{3,2,1,0:T(8,128)(2,1)S(1)}, u32[]{:S(2)}, u32[]{:S(2)}) collective-permute-start(bf16[2,8,16,128]{3,2,1,0:T(8,128)(2,1)S(1)} %get-tuple-element.34), channel_id=1, source_target_pairs={{0,1},{1,2},{2,3},{3,4},{4,5},{5,6},{6,7},{7,8},{8,9},{9,10},{10,1... | collective-permute-start | bytes 196616 | tf_op jit(solution)/shard_map/ppermute | solution.py:21
  33.8 10.6 %collective-permute-start.3 = (bf16[2,8,16,128]{3,2,1,0:T(8,128)(2,1)S(1)}, bf16[2,8,16,128]{3,2,1,0:T(8,128)(2,1)S(1)}, u32[]{:S(2)}, u32[]{:S(2)}) collective-permute-start(bf16[2,8,16,128]{3,2,1,0:T(8,128)(2,1)S(1)} %get-tuple-element.33), channel_id=1, source_target_pairs={{1,0},{2,1},{3,2},{4,3},{5,4},{6,5},{7,6},{8,7},{9,8},{10,9},{11,1... | collective-permute-start | bytes 196616 | tf_op jit(solution)/shard_map/ppermute | solution.py:23
  47.2 11.6 %collective-permute-start.4 = (bf16[8,2,16,128]{3,2,1,0:T(8,128)(2,1)S(1)}, bf16[8,2,16,128]{3,2,1,0:T(8,128)(2,1)S(1)}, u32[]{:S(2)}, u32[]{:S(2)}) collective-permute-start(bf16[8,2,16,128]{3,2,1,0:T(8,128)(2,1)S(1)} %get-tuple-element.39), channel_id=1, source_target_pairs={{0,32},{32,64},{64,96},{96,128},{128,160},{160,192},{192,224},{1,3... | collective-permute-start | bytes 196616 | tf_op jit(solution)/shard_map/ppermute | solution.py:21
  49.1 9.7 %collective-permute-start.5 = (bf16[8,2,16,128]{3,2,1,0:T(8,128)(2,1)S(1)}, bf16[8,2,16,128]{3,2,1,0:T(8,128)(2,1)S(1)}, u32[]{:S(2)}, u32[]{:S(2)}) collective-permute-start(bf16[8,2,16,128]{3,2,1,0:T(8,128)(2,1)S(1)} %get-tuple-element.40), channel_id=1, source_target_pairs={{32,0},{64,32},{96,64},{128,96},{160,128},{192,160},{224,192},{33,... | collective-permute-start | bytes 196616 | tf_op jit(solution)/shard_map/ppermute | solution.py:23
  58.9 7.4 %collective-permute-start.6 = (bf16[2,8,16,128]{3,2,1,0:T(8,128)(2,1)S(1)}, bf16[2,8,16,128]{3,2,1,0:T(8,128)(2,1)S(1)}, u32[]{:S(2)}, u32[]{:S(2)}) collective-permute-start(bf16[2,8,16,128]{3,2,1,0:T(8,128)(2,1)S(1)} %get-tuple-element.30), channel_id=1, source_target_pairs={{0,1},{1,2},{2,3},{3,4},{4,5},{5,6},{6,7},{7,8},{8,9},{9,10},{10,1... | collective-permute-start | bytes 196616 | tf_op jit(solution)/shard_map/ppermute | solution.py:21
  62.3 10.6 %collective-permute-start.7 = (bf16[2,8,16,128]{3,2,1,0:T(8,128)(2,1)S(1)}, bf16[2,8,16,128]{3,2,1,0:T(8,128)(2,1)S(1)}, u32[]{:S(2)}, u32[]{:S(2)}) collective-permute-start(bf16[2,8,16,128]{3,2,1,0:T(8,128)(2,1)S(1)} %get-tuple-element.29), channel_id=1, source_target_pairs={{1,0},{2,1},{3,2},{4,3},{5,4},{6,5},{7,6},{8,7},{9,8},{10,9},{11,1... | collective-permute-start | bytes 196616 | tf_op jit(solution)/shard_map/ppermute | solution.py:23
  89.4 20.1 %all-to-all-start.1 = ((bf16[8,32,1024]{2,1,0:T(8,128)(2,1)}), bf16[8,32,1024]{2,1,0:T(8,128)(2,1)}, u32[]{:S(2)}, u32[]{:S(2)}) async-start(bf16[8,32,1024]{2,1,0:T(8,128)(2,1)} %broadcast_in_dim.6), calls=%async_computation.1 | async-start | bytes 1048576 | tf_op jit(solution)/shard_map/all_to_all | solution.py:32
  110.9 27.5 %copy-start.5 = (bf16[32,128]{1,0:T(8,128)(2,1)S(1)}, bf16[32,128]{1,0:T(8,128)(2,1)}, u32[]{:S(2)}) copy-start(bf16[32,128]{1,0:T(8,128)(2,1)} %param.13) | copy-start | bytes 24580
  143.0 22.8 %all-to-all-start.3 = ((bf16[32,32,256]{2,1,0:T(8,128)(2,1)}), bf16[32,32,256]{2,1,0:T(8,128)(2,1)}, u32[]{:S(2)}, u32[]{:S(2)}) async-start(bf16[32,32,256]{2,1,0:T(8,128)(2,1)} %pad_maximum_fusion), calls=%async_computation.3 | async-start | bytes 1048576 | tf_op jit(solution)/shard_map/all_to_all | solution.py:73
  185.1 8.4 %copy-start.1 = (f32[8,4,16,128]{3,2,1,0:T(8,128)S(1)}, f32[8,4,16,128]{3,2,1,0:T(8,128)}, u32[]{:S(2)}) copy-start(f32[8,4,16,128]{3,2,1,0:T(8,128)} %get-tuple-element.56) | copy-start | bytes 786436
  193.7 6.8 %collective-permute-start.8 = (bf16[8,2,16,128]{3,2,1,0:T(8,128)(2,1)S(1)}, bf16[8,2,16,128]{3,2,1,0:T(8,128)(2,1)S(1)}, u32[]{:S(2)}, u32[]{:S(2)}) collective-permute-start(bf16[8,2,16,128]{3,2,1,0:T(8,128)(2,1)S(1)} %get-tuple-element.37), channel_id=1, source_target_pairs={{0,32},{32,64},{64,96},{96,128},{128,160},{160,192},{192,224},{1,3... | collective-permute-start | bytes 196616 | tf_op jit(solution)/shard_map/ppermute | solution.py:21
  196.4 6.0 %collective-permute-start.9 = (bf16[8,2,16,128]{3,2,1,0:T(8,128)(2,1)S(1)}, bf16[8,2,16,128]{3,2,1,0:T(8,128)(2,1)S(1)}, u32[]{:S(2)}, u32[]{:S(2)}) collective-permute-start(bf16[8,2,16,128]{3,2,1,0:T(8,128)(2,1)S(1)} %get-tuple-element.38), channel_id=1, source_target_pairs={{32,0},{64,32},{96,64},{128,96},{160,128},{192,160},{224,192},{33,... | collective-permute-start | bytes 196616 | tf_op jit(solution)/shard_map/ppermute | solution.py:23
  202.5 10.6 %collective-permute-start.10 = (bf16[2,8,16,128]{3,2,1,0:T(8,128)(2,1)S(1)}, bf16[2,8,16,128]{3,2,1,0:T(8,128)(2,1)S(1)}, u32[]{:S(2)}, u32[]{:S(2)}) collective-permute-start(bf16[2,8,16,128]{3,2,1,0:T(8,128)(2,1)S(1)} %get-tuple-element.26), channel_id=1, source_target_pairs={{1,0},{2,1},{3,2},{4,3},{5,4},{6,5},{7,6},{8,7},{9,8},{10,9},{11,1... | collective-permute-start | bytes 196616 | tf_op jit(solution)/shard_map/ppermute | solution.py:23
  208.3 6.0 %collective-permute-start.11 = (bf16[2,8,16,128]{3,2,1,0:T(8,128)(2,1)S(1)}, bf16[2,8,16,128]{3,2,1,0:T(8,128)(2,1)S(1)}, u32[]{:S(2)}, u32[]{:S(2)}) collective-permute-start(bf16[2,8,16,128]{3,2,1,0:T(8,128)(2,1)S(1)} %get-tuple-element.25), channel_id=1, source_target_pairs={{0,1},{1,2},{2,3},{3,4},{4,5},{5,6},{6,7},{7,8},{8,9},{9,10},{10,1... | collective-permute-start | bytes 196616 | tf_op jit(solution)/shard_map/ppermute | solution.py:21
  217.0 6.6 %collective-permute-start.12 = (bf16[8,2,16,128]{3,2,1,0:T(8,128)(2,1)S(1)}, bf16[8,2,16,128]{3,2,1,0:T(8,128)(2,1)S(1)}, u32[]{:S(2)}, u32[]{:S(2)}) collective-permute-start(bf16[8,2,16,128]{3,2,1,0:T(8,128)(2,1)S(1)} %get-tuple-element.35), channel_id=1, source_target_pairs={{0,32},{32,64},{64,96},{96,128},{128,160},{160,192},{192,224},{1,3... | collective-permute-start | bytes 196616 | tf_op jit(solution)/shard_map/ppermute | solution.py:21
  218.9 5.9 %collective-permute-start.13 = (bf16[8,2,16,128]{3,2,1,0:T(8,128)(2,1)S(1)}, bf16[8,2,16,128]{3,2,1,0:T(8,128)(2,1)S(1)}, u32[]{:S(2)}, u32[]{:S(2)}) collective-permute-start(bf16[8,2,16,128]{3,2,1,0:T(8,128)(2,1)S(1)} %get-tuple-element.36), channel_id=1, source_target_pairs={{32,0},{64,32},{96,64},{128,96},{160,128},{192,160},{224,192},{33,... | collective-permute-start | bytes 196616 | tf_op jit(solution)/shard_map/ppermute | solution.py:23
  224.8 11.1 %collective-permute-start.14 = (bf16[2,8,16,128]{3,2,1,0:T(8,128)(2,1)S(1)}, bf16[2,8,16,128]{3,2,1,0:T(8,128)(2,1)S(1)}, u32[]{:S(2)}, u32[]{:S(2)}) collective-permute-start(bf16[2,8,16,128]{3,2,1,0:T(8,128)(2,1)S(1)} %get-tuple-element.22), channel_id=1, source_target_pairs={{1,0},{2,1},{3,2},{4,3},{5,4},{6,5},{7,6},{8,7},{9,8},{10,9},{11,1... | collective-permute-start | bytes 196616 | tf_op jit(solution)/shard_map/ppermute | solution.py:23
  229.0 8.1 %collective-permute-start.15 = (bf16[2,8,16,128]{3,2,1,0:T(8,128)(2,1)S(1)}, bf16[2,8,16,128]{3,2,1,0:T(8,128)(2,1)S(1)}, u32[]{:S(2)}, u32[]{:S(2)}) collective-permute-start(bf16[2,8,16,128]{3,2,1,0:T(8,128)(2,1)S(1)} %get-tuple-element.21), channel_id=1, source_target_pairs={{0,1},{1,2},{2,3},{3,4},{4,5},{5,6},{6,7},{7,8},{8,9},{9,10},{10,1... | collective-permute-start | bytes 196616 | tf_op jit(solution)/shard_map/ppermute | solution.py:21
  (3 other events, 8.2 us)
Sparse Core Ops, SparseCore 0:
  16.3 55.6 all-gather.6
  73.7 33.9 all-gather.4

commit v16 on v7

--- a/solution.py
+++ b/solution.py
@@ -72,6 +72,16 @@
     peers = lax.axis_size(axis)
     pieces = lax.all_to_all(cut_along(shard, dim, peers), axis, 0, 0, tiled=True)
     return jnp.sum(pieces.astype(jnp.float32), axis=0)
+
+
+def gathered_near_then_far(rows, axis):
+    peers = lax.axis_size(axis)
+    near = [list(range(start, start + 4)) for start in range(0, peers, 4)]
+    far = [list(range(start, peers, 4)) for start in range(4)]
+    rows = lax.all_gather(rows, axis, axis=0, tiled=True, axis_index_groups=near)
+    copies = jnp.broadcast_to(rows[None], (len(far[0]), *rows.shape))
+    copies = lax.all_to_all(copies, axis, 0, 0, tiled=True, axis_index_groups=far)
+    return copies.reshape(-1, *rows.shape[1:])
 
 
 def gather_weights(embed_weight, qkv_weight):
@@ -174,9 +184,7 @@
         "td,sde->ste", tokens, qkv_rows, preferred_element_type=jnp.float32
     ).astype(jnp.bfloat16)
     key_rows, value_rows = jnp.split(
-        joined_along(copy_for_each(jnp.concatenate([projected[1], projected[2]], axis=1), "blk"), 0),
-        2,
-        axis=1,
+        gathered_near_then_far(jnp.concatenate([projected[1], projected[2]], axis=1), "blk"), 2, axis=1
     )
     tok_rows = tokens.shape[0]
     head_cols = projected.shape[2]

time: 239 us -> 243 us (1.017)
  blocking collectives: 64.7 us -> 67.5 us
    all_to_all x2 -> x1, blocking collectives: 37.2 us -> 11.7 us  [copy_for_each(): lax.all_to_all(jnp.broadcast_to(shard[None], (peers, *shard.shape)), axis...]
    all_to_all x0 -> x1, blocking collectives: none -> 19.5 us  [gathered_near_then_far(): lax.all_to_all(copies, axis, 0, 0, tiled=True, axis_index_groups=far)]
    all_gather x0 -> x1, blocking collectives: none -> 8.75 us  [gathered_near_then_far(): lax.all_gather(rows, axis, axis=0, tiled=True, axis_index_groups=near)]
where the time goes in v16:
time: 243 us; the launch traced here: 239 us
  starting transfers between devices  71.7 us (30%)
  blocking collectives  67.5 us (28%)
  waiting for transfers between devices  43.7 us (18%)
  between operations  18.1 us (7%)
  matrix products  17.4 us (7%)
  local copies, waits for them, and re-layouts  13.9 us (6%)
  other arithmetic  6.38 us (3%)
    ppermute x8, starting transfers between devices, padded_2(): lax.ppermute(tail, axis, [(i, (i + 1) % count) for i in range(ends)])  31.6 us
    ppermute x8, starting transfers between devices, padded_2(): lax.ppermute(head, axis, [((i + 1) % count, i) for i in range(ends)])  24.9 us
    ppermute x8, waiting for transfers between devices, padded_2(): lax.ppermute(head, axis, [((i + 1) % count, i) for i in range(ends)])  22.1 us
    all_to_all x1, blocking collectives, gathered_near_then_far(): lax.all_to_all(copies, axis, 0, 0, tiled=True, axis_index_groups=far)  19.5 us
    all_to_all x1, waiting for transfers between devices, sum_at_owner(): lax.all_to_all(cut_along(shard, dim, peers), axis, 0, 0, tiled=True)  14.5 us
    all_to_all x1, blocking collectives, copy_for_each(): lax.all_to_all(jnp.broadcast_to(shard[None], (peers, *shard.shape)), axis...  11.7 us
    all_gather x1, blocking collectives, gather_weights(): lax.all_gather(rows, 'blk', axis=0, tiled=True, axis_index_groups=near)  9.96 us
    all_to_all x1, starting transfers between devices, sum_at_owner(): lax.all_to_all(cut_along(shard, dim, peers), axis, 0, 0, tiled=True)  9.93 us
  transfers between devices with their start and end apart: 19, of which 12 were waited for; matrix products, arithmetic and copies ran while one was open for 6% of the time, Pallas kernels for 0%

profile of v16, /device:TPU:103, one launch (start us, length us, event | category | flops | bytes accessed | tf_op | source)
XLA Modules:
  0.0 238.7 jit_solution(7334508468554081791)
XLA Ops:
  8.6 10.0 %all_gather.9 = bf16[320,1024]{1,0:T(8,128)(2,1)} all-gather(bf16[80,1024]{1,0:T(8,128)(2,1)S(1)} %maximum_maximum_fusion.4), channel_id=1, replica_groups={{0,1,2,3},{4,5,6,7},{8,9,10,11},{12,13,14,15},{16,17,18,19},{20,21,22,2..., dimensions={0}, use_global_device_ids=true | all-gather | bytes 819200 | tf_op jit(solution)/shard_map/all_gather | solution.py:97
  18.6 3.5 %collective-permute-start = (bf16[8,2,16,128]{3,2,1,0:T(8,128)(2,1)S(1)}, bf16[8,2,16,128]{3,2,1,0:T(8,128)(2,1)S(1)}, u32[]{:S(2)}, u32[]{:S(2)}) collective-permute-start(bf16[8,2,16,128]{3,2,1,0:T(8,128)(2,1)S(1)} %get-tuple-element.41), channel_id=1, source_target_pairs={{0,32},{32,64},{64,96},{96,128},{128,160},{160,192},{192,224},{1,3... | collective-permute-start | bytes 196616 | tf_op jit(solution)/shard_map/ppermute | solution.py:21
  24.9 3.1 %collective-permute-done.1 = bf16[8,2,16,128]{3,2,1,0:T(8,128)(2,1)S(1)} collective-permute-done((bf16[8,2,16,128]{3,2,1,0:T(8,128)(2,1)S(1)}, bf16[8,2,16,128]{3,2,1,0:T(8,128)(2,1)S(1)}, u32[]{:S(2)}, u32[]{:S(2)}) %collective-permute-start.1) | collective-permute-done | bytes 65568 | tf_op jit(solution)/shard_map/ppermute | solution.py:23
  28.0 7.2 %collective-permute-start.2 = (bf16[2,8,16,128]{3,2,1,0:T(8,128)(2,1)S(1)}, bf16[2,8,16,128]{3,2,1,0:T(8,128)(2,1)S(1)}, u32[]{:S(2)}, u32[]{:S(2)}) collective-permute-start(bf16[2,8,16,128]{3,2,1,0:T(8,128)(2,1)S(1)} %get-tuple-element.34), channel_id=1, source_target_pairs={{0,1},{1,2},{2,3},{3,4},{4,5},{5,6},{6,7},{7,8},{8,9},{9,10},{10,1... | collective-permute-start | bytes 196616 | tf_op jit(solution)/shard_map/ppermute | solution.py:21
  39.7 6.1 %collective-permute-done.3 = bf16[2,8,16,128]{3,2,1,0:T(8,128)(2,1)S(1)} collective-permute-done((bf16[2,8,16,128]{3,2,1,0:T(8,128)(2,1)S(1)}, bf16[2,8,16,128]{3,2,1,0:T(8,128)(2,1)S(1)}, u32[]{:S(2)}, u32[]{:S(2)}) %collective-permute-start.3) | collective-permute-done | bytes 65568 | tf_op jit(solution)/shard_map/ppermute | solution.py:23
  51.2 3.4 %collective-permute-start.5 = (bf16[8,2,16,128]{3,2,1,0:T(8,128)(2,1)S(1)}, bf16[8,2,16,128]{3,2,1,0:T(8,128)(2,1)S(1)}, u32[]{:S(2)}, u32[]{:S(2)}) collective-permute-start(bf16[8,2,16,128]{3,2,1,0:T(8,128)(2,1)S(1)} %get-tuple-element.40), channel_id=1, source_target_pairs={{32,0},{64,32},{96,64},{128,96},{160,128},{192,160},{224,192},{33,... | collective-permute-start | bytes 196616 | tf_op jit(solution)/shard_map/ppermute | solution.py:23
  54.7 2.9 %collective-permute-done.5 = bf16[8,2,16,128]{3,2,1,0:T(8,128)(2,1)S(1)} collective-permute-done((bf16[8,2,16,128]{3,2,1,0:T(8,128)(2,1)S(1)}, bf16[8,2,16,128]{3,2,1,0:T(8,128)(2,1)S(1)}, u32[]{:S(2)}, u32[]{:S(2)}) %collective-permute-start.5) | collective-permute-done | bytes 65568 | tf_op jit(solution)/shard_map/ppermute | solution.py:23
  64.2 6.6 %collective-permute-done.7 = bf16[2,8,16,128]{3,2,1,0:T(8,128)(2,1)S(1)} collective-permute-done((bf16[2,8,16,128]{3,2,1,0:T(8,128)(2,1)S(1)}, bf16[2,8,16,128]{3,2,1,0:T(8,128)(2,1)S(1)}, u32[]{:S(2)}, u32[]{:S(2)}) %collective-permute-start.7) | collective-permute-done | bytes 65568 | tf_op jit(solution)/shard_map/ppermute | solution.py:23
  73.7 9.4 %all_to_all.38 = bf16[8,4,16,128]{3,2,1,0:T(8,128)(2,1)S(1)} all-to-all(bf16[8,4,16,128]{3,2,1,0:T(8,128)(2,1)S(1)} %get-tuple-element.55), channel_id=1, replica_groups=mesh['zslab'=8,'blk'=32] {'zslab'}, dimensions={0} | all-to-all | bytes 262144 | tf_op jit(solution)/shard_map/all_to_all | solution.py:170
  84.1 3.0 %fusion.26 = bf16[32,1024]{1,0:T(8,128)(2,1)S(1)} fusion(bf16[32,80,1024]{2,1,0:T(8,128)(2,1)} %bitcast.261, bf16[32,32,64]{2,1,0:T(8,128)(2,1)S(1)} %reshape_reshape.9), kind=kOutput, calls=%fused_computation.31 | convolution fusion | flops 134250496 | bytes 4390912 | tf_op jit(solution)/shard_map/tbf,bfd->td/dot_general | solution.py:179
  88.0 5.2 %all-to-all-start.1 = ((bf16[8,32,1024]{2,1,0:T(8,128)(2,1)}), bf16[8,32,1024]{2,1,0:T(8,128)(2,1)S(1)}, u32[]{:S(2)}, u32[]{:S(2)}) async-start(bf16[8,32,1024]{2,1,0:T(8,128)(2,1)} %broadcast_in_dim.9), calls=%async_computation.1 | async-start | bytes 1048576 | tf_op jit(solution)/shard_map/all_to_all | solution.py:32
  97.1 4.0 %all-to-all-done.1 = bf16[8,32,1024]{2,1,0:T(8,128)(2,1)S(1)} async-done(((bf16[8,32,1024]{2,1,0:T(8,128)(2,1)}), bf16[8,32,1024]{2,1,0:T(8,128)(2,1)S(1)}, u32[]{:S(2)}, u32[]{:S(2)}) %all-to-all-start.1) | async-done | bytes 524320 | tf_op jit(solution)/shard_map/all_to_all | solution.py:32
  101.5 8.7 %all_gather.11 = bf16[128,256]{1,0:T(8,128)(2,1)S(1)} all-gather(bf16[32,256]{1,0:T(8,128)(2,1)S(1)} %pad_maximum_fusion.25), channel_id=1, replica_groups={{0,1,2,3},{4,5,6,7},{8,9,10,11},{12,13,14,15},{16,17,18,19},{20,21,22,2..., dimensions={0}, use_global_device_ids=true | all-gather | bytes 81920 | tf_op jit(solution)/shard_map/all_gather | solution.py:81
  110.3 19.5 %all_to_all.39 = bf16[8,128,256]{2,1,0:T(8,128)(2,1)S(1)} all-to-all(bf16[8,128,256]{2,1,0:T(8,128)(2,1)S(1)} %broadcast_in_dim.10), channel_id=1, replica_groups={{0,4,8,12,16,20,24,28},{1,5,9,13,17,21,25,29},{2,6,10,14,18,22,26,30},{..., dimensions={0} | all-to-all | bytes 1048576 | tf_op jit(solution)/shard_map/all_to_all | solution.py:83
  134.9 9.9 %all-to-all-start.3 = ((bf16[32,32,256]{2,1,0:T(8,128)(2,1)}), bf16[32,32,256]{2,1,0:T(8,128)(2,1)}, u32[]{:S(2)}, u32[]{:S(2)}) async-start(bf16[32,32,256]{2,1,0:T(8,128)(2,1)} %pad_maximum_fusion), calls=%async_computation.3 | async-start | bytes 1048576 | tf_op jit(solution)/shard_map/all_to_all | solution.py:73
  145.0 14.5 %all-to-all-done.3 = bf16[32,32,256]{2,1,0:T(8,128)(2,1)} async-done(((bf16[32,32,256]{2,1,0:T(8,128)(2,1)}), bf16[32,32,256]{2,1,0:T(8,128)(2,1)}, u32[]{:S(2)}, u32[]{:S(2)}) %all-to-all-start.3) | async-done | bytes 524320 | tf_op jit(solution)/shard_map/all_to_all | solution.py:73
  161.0 11.7 %all_to_all.40 = bf16[8,32,1024]{2,1,0:T(8,128)(2,1)S(1)} all-to-all(bf16[8,32,1024]{2,1,0:T(8,128)(2,1)S(1)} %broadcast_in_dim.11), channel_id=1, replica_groups=mesh['zslab'=8,'blk'=32] {'zslab'}, dimensions={0} | all-to-all | bytes 1048576 | tf_op jit(solution)/shard_map/all_to_all | solution.py:32
  172.8 4.2 %fusion.4 = bf16[32,32,64]{2,0,1:T(8,128)(2,1)S(1)} fusion(bf16[32,80,1024]{2,1,0:T(8,128)(2,1)} %bitcast.263, bf16[32,1024]{1,0:T(8,128)(2,1)S(1)} %reduce_sum.58), kind=kOutput, calls=%fused_computation.4 | convolution fusion | flops 134283264 | bytes 4390912 | tf_op jit(solution)/shard_map/td,bfd->tbf/dot_general | solution.py:231
  177.4 8.1 %all_to_all.41 = bf16[1,32,16,128]{3,2,0,1:T(8,128)(2,1)S(1)} all-to-all(bf16[1,32,16,128]{3,2,0,1:T(8,128)(2,1)S(1)} %bitcast.248), channel_id=1, replica_groups=mesh['zslab'=8,'blk'=32] {'zslab'}, dimensions={1} | all-to-all | bytes 262144 | tf_op jit(solution)/shard_map/all_to_all | solution.py:238
  194.4 5.8 %collective-permute-start.10 = (bf16[2,8,16,128]{3,2,1,0:T(8,128)(2,1)S(1)}, bf16[2,8,16,128]{3,2,1,0:T(8,128)(2,1)S(1)}, u32[]{:S(2)}, u32[]{:S(2)}) collective-permute-start(bf16[2,8,16,128]{3,2,1,0:T(8,128)(2,1)S(1)} %get-tuple-element.26), channel_id=1, source_target_pairs={{1,0},{2,1},{3,2},{4,3},{5,4},{6,5},{7,6},{8,7},{9,8},{10,9},{11,1... | collective-permute-start | bytes 196616 | tf_op jit(solution)/shard_map/ppermute | solution.py:23
  200.2 4.9 %collective-permute-start.11 = (bf16[2,8,16,128]{3,2,1,0:T(8,128)(2,1)S(1)}, bf16[2,8,16,128]{3,2,1,0:T(8,128)(2,1)S(1)}, u32[]{:S(2)}, u32[]{:S(2)}) collective-permute-start(bf16[2,8,16,128]{3,2,1,0:T(8,128)(2,1)S(1)} %get-tuple-element.25), channel_id=1, source_target_pairs={{0,1},{1,2},{2,3},{3,4},{4,5},{5,6},{6,7},{7,8},{8,9},{9,10},{10,1... | collective-permute-start | bytes 196616 | tf_op jit(solution)/shard_map/ppermute | solution.py:21
  210.9 3.4 %collective-permute-start.13 = (bf16[8,2,16,128]{3,2,1,0:T(8,128)(2,1)S(1)}, bf16[8,2,16,128]{3,2,1,0:T(8,128)(2,1)S(1)}, u32[]{:S(2)}, u32[]{:S(2)}) collective-permute-start(bf16[8,2,16,128]{3,2,1,0:T(8,128)(2,1)S(1)} %get-tuple-element.36), channel_id=1, source_target_pairs={{32,0},{64,32},{96,64},{128,96},{160,128},{192,160},{224,192},{33,... | collective-permute-start | bytes 196616 | tf_op jit(solution)/shard_map/ppermute | solution.py:23
  216.8 4.1 %collective-permute-start.14 = (bf16[2,8,16,128]{3,2,1,0:T(8,128)(2,1)S(1)}, bf16[2,8,16,128]{3,2,1,0:T(8,128)(2,1)S(1)}, u32[]{:S(2)}, u32[]{:S(2)}) collective-permute-start(bf16[2,8,16,128]{3,2,1,0:T(8,128)(2,1)S(1)} %get-tuple-element.22), channel_id=1, source_target_pairs={{1,0},{2,1},{3,2},{4,3},{5,4},{6,5},{7,6},{8,7},{9,8},{10,9},{11,1... | collective-permute-start | bytes 196616 | tf_op jit(solution)/shard_map/ppermute | solution.py:23
  220.9 6.9 %collective-permute-start.15 = (bf16[2,8,16,128]{3,2,1,0:T(8,128)(2,1)S(1)}, bf16[2,8,16,128]{3,2,1,0:T(8,128)(2,1)S(1)}, u32[]{:S(2)}, u32[]{:S(2)}) collective-permute-start(bf16[2,8,16,128]{3,2,1,0:T(8,128)(2,1)S(1)} %get-tuple-element.21), channel_id=1, source_target_pairs={{0,1},{1,2},{2,3},{3,4},{4,5},{5,6},{6,7},{7,8},{8,9},{9,10},{10,1... | collective-permute-start | bytes 196616 | tf_op jit(solution)/shard_map/ppermute | solution.py:21
  (158 shorter events, 54.4 us)
Async XLA Ops:
  6.5 12.0 %copy-start.1 = (bf16[8,16,4,128]{3,2,1,0:T(4,128)(2,1)S(1)}, bf16[8,16,4,128]{3,2,1,0:T(4,128)(2,1)}, u32[]{:S(2)}) copy-start(bf16[8,16,4,128]{3,2,1,0:T(4,128)(2,1)} %param.7) | copy-start | bytes 393220
  6.5 77.6 %all-gather.2.cloned.1.call-start = ((), (), s32[]{:S(2)}) async-start(), calls=%async_computation.6 | async-start | bytes 5898240 | tf_op jit(solution)/shard_map/all_gather | solution.py:98
  7.4 16.7 %copy-start = (bf16[2,3456,128]{2,1,0:T(8,128)(2,1)S(1)}, bf16[2,3456,128]{2,1,0:T(8,128)(2,1)}, u32[]{:S(2)}) copy-start(bf16[2,3456,128]{2,1,0:T(8,128)(2,1)} %param.10) | copy-start | bytes 5308420
  18.6 6.3 %collective-permute-start = (bf16[8,2,16,128]{3,2,1,0:T(8,128)(2,1)S(1)}, bf16[8,2,16,128]{3,2,1,0:T(8,128)(2,1)S(1)}, u32[]{:S(2)}, u32[]{:S(2)}) collective-permute-start(bf16[8,2,16,128]{3,2,1,0:T(8,128)(2,1)S(1)} %get-tuple-element.41), channel_id=1, source_target_pairs={{0,32},{32,64},{64,96},{96,128},{128,160},{160,192},{192,224},{1,3... | collective-permute-start | bytes 196616 | tf_op jit(solution)/shard_map/ppermute | solution.py:21
  22.1 5.9 %collective-permute-start.1 = (bf16[8,2,16,128]{3,2,1,0:T(8,128)(2,1)S(1)}, bf16[8,2,16,128]{3,2,1,0:T(8,128)(2,1)S(1)}, u32[]{:S(2)}, u32[]{:S(2)}) collective-permute-start(bf16[8,2,16,128]{3,2,1,0:T(8,128)(2,1)S(1)} %get-tuple-element.42), channel_id=1, source_target_pairs={{32,0},{64,32},{96,64},{128,96},{160,128},{192,160},{224,192},{33,... | collective-permute-start | bytes 196616 | tf_op jit(solution)/shard_map/ppermute | solution.py:23
  24.2 13.0 %copy-start.5 = (s32[2,3]{1,0:T(2,128)S(1)}, s32[2,3]{1,0:T(2,128)}, u32[]{:S(2)}) copy-start(s32[2,3]{1,0:T(2,128)} %param.9) | copy-start | bytes 76
  28.0 11.7 %collective-permute-start.2 = (bf16[2,8,16,128]{3,2,1,0:T(8,128)(2,1)S(1)}, bf16[2,8,16,128]{3,2,1,0:T(8,128)(2,1)S(1)}, u32[]{:S(2)}, u32[]{:S(2)}) collective-permute-start(bf16[2,8,16,128]{3,2,1,0:T(8,128)(2,1)S(1)} %get-tuple-element.34), channel_id=1, source_target_pairs={{0,1},{1,2},{2,3},{3,4},{4,5},{5,6},{6,7},{7,8},{8,9},{9,10},{10,1... | collective-permute-start | bytes 196616 | tf_op jit(solution)/shard_map/ppermute | solution.py:21
  35.2 10.6 %collective-permute-start.3 = (bf16[2,8,16,128]{3,2,1,0:T(8,128)(2,1)S(1)}, bf16[2,8,16,128]{3,2,1,0:T(8,128)(2,1)S(1)}, u32[]{:S(2)}, u32[]{:S(2)}) collective-permute-start(bf16[2,8,16,128]{3,2,1,0:T(8,128)(2,1)S(1)} %get-tuple-element.33), channel_id=1, source_target_pairs={{1,0},{2,1},{3,2},{4,3},{5,4},{6,5},{7,6},{8,7},{9,8},{10,9},{11,1... | collective-permute-start | bytes 196616 | tf_op jit(solution)/shard_map/ppermute | solution.py:23
  49.3 5.4 %collective-permute-start.4 = (bf16[8,2,16,128]{3,2,1,0:T(8,128)(2,1)S(1)}, bf16[8,2,16,128]{3,2,1,0:T(8,128)(2,1)S(1)}, u32[]{:S(2)}, u32[]{:S(2)}) collective-permute-start(bf16[8,2,16,128]{3,2,1,0:T(8,128)(2,1)S(1)} %get-tuple-element.39), channel_id=1, source_target_pairs={{0,32},{32,64},{64,96},{96,128},{128,160},{160,192},{192,224},{1,3... | collective-permute-start | bytes 196616 | tf_op jit(solution)/shard_map/ppermute | solution.py:21
  51.2 6.4 %collective-permute-start.5 = (bf16[8,2,16,128]{3,2,1,0:T(8,128)(2,1)S(1)}, bf16[8,2,16,128]{3,2,1,0:T(8,128)(2,1)S(1)}, u32[]{:S(2)}, u32[]{:S(2)}) collective-permute-start(bf16[8,2,16,128]{3,2,1,0:T(8,128)(2,1)S(1)} %get-tuple-element.40), channel_id=1, source_target_pairs={{32,0},{64,32},{96,64},{128,96},{160,128},{192,160},{224,192},{33,... | collective-permute-start | bytes 196616 | tf_op jit(solution)/shard_map/ppermute | solution.py:23
  57.7 6.5 %collective-permute-start.6 = (bf16[2,8,16,128]{3,2,1,0:T(8,128)(2,1)S(1)}, bf16[2,8,16,128]{3,2,1,0:T(8,128)(2,1)S(1)}, u32[]{:S(2)}, u32[]{:S(2)}) collective-permute-start(bf16[2,8,16,128]{3,2,1,0:T(8,128)(2,1)S(1)} %get-tuple-element.30), channel_id=1, source_target_pairs={{0,1},{1,2},{2,3},{3,4},{4,5},{5,6},{6,7},{7,8},{8,9},{9,10},{10,1... | collective-permute-start | bytes 196616 | tf_op jit(solution)/shard_map/ppermute | solution.py:21
  60.3 10.6 %collective-permute-start.7 = (bf16[2,8,16,128]{3,2,1,0:T(8,128)(2,1)S(1)}, bf16[2,8,16,128]{3,2,1,0:T(8,128)(2,1)S(1)}, u32[]{:S(2)}, u32[]{:S(2)}) collective-permute-start(bf16[2,8,16,128]{3,2,1,0:T(8,128)(2,1)S(1)} %get-tuple-element.29), channel_id=1, source_target_pairs={{1,0},{2,1},{3,2},{4,3},{5,4},{6,5},{7,6},{8,7},{9,8},{10,9},{11,1... | collective-permute-start | bytes 196616 | tf_op jit(solution)/shard_map/ppermute | solution.py:23
  88.0 13.2 %all-to-all-start.1 = ((bf16[8,32,1024]{2,1,0:T(8,128)(2,1)}), bf16[8,32,1024]{2,1,0:T(8,128)(2,1)S(1)}, u32[]{:S(2)}, u32[]{:S(2)}) async-start(bf16[8,32,1024]{2,1,0:T(8,128)(2,1)} %broadcast_in_dim.9), calls=%async_computation.1 | async-start | bytes 1048576 | tf_op jit(solution)/shard_map/all_to_all | solution.py:32
  101.5 28.8 %copy-start.6 = (bf16[32,128]{1,0:T(8,128)(2,1)S(1)}, bf16[32,128]{1,0:T(8,128)(2,1)}, u32[]{:S(2)}) copy-start(bf16[32,128]{1,0:T(8,128)(2,1)} %param.13) | copy-start | bytes 24580
  134.9 24.6 %all-to-all-start.3 = ((bf16[32,32,256]{2,1,0:T(8,128)(2,1)}), bf16[32,32,256]{2,1,0:T(8,128)(2,1)}, u32[]{:S(2)}, u32[]{:S(2)}) async-start(bf16[32,32,256]{2,1,0:T(8,128)(2,1)} %pad_maximum_fusion), calls=%async_computation.3 | async-start | bytes 1048576 | tf_op jit(solution)/shard_map/all_to_all | solution.py:73
  177.1 8.4 %copy-start.3 = (f32[8,4,16,128]{3,2,1,0:T(8,128)S(1)}, f32[8,4,16,128]{3,2,1,0:T(8,128)}, u32[]{:S(2)}) copy-start(f32[8,4,16,128]{3,2,1,0:T(8,128)} %get-tuple-element.56) | copy-start | bytes 786436
  185.7 6.6 %collective-permute-start.8 = (bf16[8,2,16,128]{3,2,1,0:T(8,128)(2,1)S(1)}, bf16[8,2,16,128]{3,2,1,0:T(8,128)(2,1)S(1)}, u32[]{:S(2)}, u32[]{:S(2)}) collective-permute-start(bf16[8,2,16,128]{3,2,1,0:T(8,128)(2,1)S(1)} %get-tuple-element.37), channel_id=1, source_target_pairs={{0,32},{32,64},{64,96},{96,128},{128,160},{160,192},{192,224},{1,3... | collective-permute-start | bytes 196616 | tf_op jit(solution)/shard_map/ppermute | solution.py:21
  188.4 6.0 %collective-permute-start.9 = (bf16[8,2,16,128]{3,2,1,0:T(8,128)(2,1)S(1)}, bf16[8,2,16,128]{3,2,1,0:T(8,128)(2,1)S(1)}, u32[]{:S(2)}, u32[]{:S(2)}) collective-permute-start(bf16[8,2,16,128]{3,2,1,0:T(8,128)(2,1)S(1)} %get-tuple-element.38), channel_id=1, source_target_pairs={{32,0},{64,32},{96,64},{128,96},{160,128},{192,160},{224,192},{33,... | collective-permute-start | bytes 196616 | tf_op jit(solution)/shard_map/ppermute | solution.py:23
  194.4 10.9 %collective-permute-start.10 = (bf16[2,8,16,128]{3,2,1,0:T(8,128)(2,1)S(1)}, bf16[2,8,16,128]{3,2,1,0:T(8,128)(2,1)S(1)}, u32[]{:S(2)}, u32[]{:S(2)}) collective-permute-start(bf16[2,8,16,128]{3,2,1,0:T(8,128)(2,1)S(1)} %get-tuple-element.26), channel_id=1, source_target_pairs={{1,0},{2,1},{3,2},{4,3},{5,4},{6,5},{7,6},{8,7},{9,8},{10,9},{11,1... | collective-permute-start | bytes 196616 | tf_op jit(solution)/shard_map/ppermute | solution.py:23
  200.2 6.1 %collective-permute-start.11 = (bf16[2,8,16,128]{3,2,1,0:T(8,128)(2,1)S(1)}, bf16[2,8,16,128]{3,2,1,0:T(8,128)(2,1)S(1)}, u32[]{:S(2)}, u32[]{:S(2)}) collective-permute-start(bf16[2,8,16,128]{3,2,1,0:T(8,128)(2,1)S(1)} %get-tuple-element.25), channel_id=1, source_target_pairs={{0,1},{1,2},{2,3},{3,4},{4,5},{5,6},{6,7},{7,8},{8,9},{9,10},{10,1... | collective-permute-start | bytes 196616 | tf_op jit(solution)/shard_map/ppermute | solution.py:21
  208.9 6.6 %collective-permute-start.12 = (bf16[8,2,16,128]{3,2,1,0:T(8,128)(2,1)S(1)}, bf16[8,2,16,128]{3,2,1,0:T(8,128)(2,1)S(1)}, u32[]{:S(2)}, u32[]{:S(2)}) collective-permute-start(bf16[8,2,16,128]{3,2,1,0:T(8,128)(2,1)S(1)} %get-tuple-element.35), channel_id=1, source_target_pairs={{0,32},{32,64},{64,96},{96,128},{128,160},{160,192},{192,224},{1,3... | collective-permute-start | bytes 196616 | tf_op jit(solution)/shard_map/ppermute | solution.py:21
  210.9 5.9 %collective-permute-start.13 = (bf16[8,2,16,128]{3,2,1,0:T(8,128)(2,1)S(1)}, bf16[8,2,16,128]{3,2,1,0:T(8,128)(2,1)S(1)}, u32[]{:S(2)}, u32[]{:S(2)}) collective-permute-start(bf16[8,2,16,128]{3,2,1,0:T(8,128)(2,1)S(1)} %get-tuple-element.36), channel_id=1, source_target_pairs={{32,0},{64,32},{96,64},{128,96},{160,128},{192,160},{224,192},{33,... | collective-permute-start | bytes 196616 | tf_op jit(solution)/shard_map/ppermute | solution.py:23
  216.8 11.1 %collective-permute-start.14 = (bf16[2,8,16,128]{3,2,1,0:T(8,128)(2,1)S(1)}, bf16[2,8,16,128]{3,2,1,0:T(8,128)(2,1)S(1)}, u32[]{:S(2)}, u32[]{:S(2)}) collective-permute-start(bf16[2,8,16,128]{3,2,1,0:T(8,128)(2,1)S(1)} %get-tuple-element.22), channel_id=1, source_target_pairs={{1,0},{2,1},{3,2},{4,3},{5,4},{6,5},{7,6},{8,7},{9,8},{10,9},{11,1... | collective-permute-start | bytes 196616 | tf_op jit(solution)/shard_map/ppermute | solution.py:23
  220.9 8.2 %collective-permute-start.15 = (bf16[2,8,16,128]{3,2,1,0:T(8,128)(2,1)S(1)}, bf16[2,8,16,128]{3,2,1,0:T(8,128)(2,1)S(1)}, u32[]{:S(2)}, u32[]{:S(2)}) collective-permute-start(bf16[2,8,16,128]{3,2,1,0:T(8,128)(2,1)S(1)} %get-tuple-element.21), channel_id=1, source_target_pairs={{0,1},{1,2},{2,3},{3,4},{4,5},{5,6},{6,7},{7,8},{8,9},{9,10},{10,1... | collective-permute-start | bytes 196616 | tf_op jit(solution)/shard_map/ppermute | solution.py:21
  (3 other events, 2.6 us)
Sparse Core Ops, SparseCore 0:
  18.7 65.3 all-gather.1

commit v17 on v7

--- a/solution.py
+++ b/solution.py
@@ -82,8 +82,8 @@
         [embed_weight[0], qkv_flat, jnp.zeros((extra, width), qkv_flat.dtype)], axis=0
     )
     peers = lax.axis_size("blk")
-    near = [list(range(start, start + 4)) for start in range(0, peers, 4)]
-    far = [list(range(start, peers, 4)) for start in range(4)]
+    near = [list(range(start, start + 8)) for start in range(0, peers, 8)]
+    far = [list(range(start, peers, 8)) for start in range(8)]
     gathered = lax.all_gather(rows, "blk", axis=0, tiled=True, axis_index_groups=near)
     gathered = lax.all_gather(gathered, "blk", axis=0, tiled=True, axis_index_groups=far)
     gathered = gathered.reshape(peers, rows.shape[0], width)

time: 239 us -> 296 us (1.24)
  waiting for transfers between devices: 43.7 us -> 106 us
  blocking collectives: 64.7 us -> 53.4 us
  starting transfers between devices: 70.5 us -> 73.9 us
    all_gather x1, waiting for transfers between devices: 0.75 us -> 43.1 us  [gather_weights(): lax.all_gather(gathered, 'blk', axis=0, tiled=True, axis_index_groups=far)]
    all_gather x0 -> x1, waiting for transfers between devices: none -> 22.1 us  [gather_weights(): lax.all_gather(rows, 'blk', axis=0, tiled=True, axis_index_groups=near)]
    all_gather x1 -> x0, blocking collectives: 9.96 us -> none  [gather_weights(): lax.all_gather(rows, 'blk', axis=0, tiled=True, axis_index_groups=near)]
  transfers between devices with their start and end apart: 19 -> 20, of which waited for: 12 -> 12; matrix products, arithmetic and copies ran while one was open for 6% -> 5% of each run, Pallas kernels for 0% -> 0%
where the time goes in v17:
time: 296 us; the launch traced here: 292 us
  waiting for transfers between devices  106 us (36%)
  starting transfers between devices  73.9 us (25%)
  blocking collectives  53.4 us (18%)
  between operations  18 us (6%)
  matrix products  17.4 us (6%)
  local copies, waits for them, and re-layouts  16.3 us (6%)
  other arithmetic  6.92 us (2%)
    all_gather x1, waiting for transfers between devices, gather_weights(): lax.all_gather(gathered, 'blk', axis=0, tiled=True, axis_index_groups=far)  43.1 us
    all_to_all x2, blocking collectives, copy_for_each(): lax.all_to_all(jnp.broadcast_to(shard[None], (peers, *shard.shape)), axis...  35.4 us
    ppermute x8, starting transfers between devices, padded_2(): lax.ppermute(tail, axis, [(i, (i + 1) % count) for i in range(ends)])  34.6 us
    ppermute x8, starting transfers between devices, padded_2(): lax.ppermute(head, axis, [((i + 1) % count, i) for i in range(ends)])  23 us
    all_gather x1, waiting for transfers between devices, gather_weights(): lax.all_gather(rows, 'blk', axis=0, tiled=True, axis_index_groups=near)  22.1 us
    ppermute x8, waiting for transfers between devices, padded_2(): lax.ppermute(head, axis, [((i + 1) % count, i) for i in range(ends)])  19.8 us
    all_to_all x1, waiting for transfers between devices, sum_at_owner(): lax.all_to_all(cut_along(shard, dim, peers), axis, 0, 0, tiled=True)  14.4 us
    all_to_all x1, blocking collectives, local(): lax.all_to_all(hidden, 'zslab', split_axis=0, concat_axis=1, tiled=True)  9.82 us
  transfers between devices with their start and end apart: 20, of which 12 were waited for; matrix products, arithmetic and copies ran while one was open for 5% of the time, Pallas kernels for 0%

profile of v17, /device:TPU:103, one launch (start us, length us, event | category | flops | bytes accessed | tf_op | source)
XLA Modules:
  0.0 292.1 jit_solution(11628235922256349898)
XLA Ops:
  10.1 3.5 %collective-permute-start = (bf16[8,2,16,128]{3,2,1,0:T(8,128)(2,1)S(1)}, bf16[8,2,16,128]{3,2,1,0:T(8,128)(2,1)S(1)}, u32[]{:S(2)}, u32[]{:S(2)}) collective-permute-start(bf16[8,2,16,128]{3,2,1,0:T(8,128)(2,1)S(1)} %get-tuple-element.41), channel_id=1, source_target_pairs={{0,32},{32,64},{64,96},{96,128},{128,160},{160,192},{192,224},{1,3... | collective-permute-start | bytes 196616 | tf_op jit(solution)/shard_map/ppermute | solution.py:21
  15.5 22.1 %all-gather.3.cloned.1.call-done = bf16[640,1024]{1,0:T(8,128)(2,1)} async-done(((bf16[80,1024]{1,0:T(8,128)(2,1)}), bf16[640,1024]{1,0:T(8,128)(2,1)}) %all-gather.3.cloned.1.call-update) | async-done | bytes 1310736 | tf_op jit(solution)/shard_map/all_gather | solution.py:87
  39.9 6.1 %collective-permute-start.2 = (bf16[2,8,16,128]{3,2,1,0:T(8,128)(2,1)S(1)}, bf16[2,8,16,128]{3,2,1,0:T(8,128)(2,1)S(1)}, u32[]{:S(2)}, u32[]{:S(2)}) collective-permute-start(bf16[2,8,16,128]{3,2,1,0:T(8,128)(2,1)S(1)} %get-tuple-element.34), channel_id=1, source_target_pairs={{0,1},{1,2},{2,3},{3,4},{4,5},{5,6},{6,7},{7,8},{8,9},{9,10},{10,1... | collective-permute-start | bytes 196616 | tf_op jit(solution)/shard_map/ppermute | solution.py:21
  50.5 4.7 %collective-permute-done.3 = bf16[2,8,16,128]{3,2,1,0:T(8,128)(2,1)S(1)} collective-permute-done((bf16[2,8,16,128]{3,2,1,0:T(8,128)(2,1)S(1)}, bf16[2,8,16,128]{3,2,1,0:T(8,128)(2,1)S(1)}, u32[]{:S(2)}, u32[]{:S(2)}) %collective-permute-start.3) | collective-permute-done | bytes 65568 | tf_op jit(solution)/shard_map/ppermute | solution.py:23
  58.7 3.4 %collective-permute-start.4 = (bf16[8,2,16,128]{3,2,1,0:T(8,128)(2,1)S(1)}, bf16[8,2,16,128]{3,2,1,0:T(8,128)(2,1)S(1)}, u32[]{:S(2)}, u32[]{:S(2)}) collective-permute-start(bf16[8,2,16,128]{3,2,1,0:T(8,128)(2,1)S(1)} %get-tuple-element.39), channel_id=1, source_target_pairs={{0,32},{32,64},{64,96},{96,128},{128,160},{160,192},{192,224},{1,3... | collective-permute-start | bytes 196616 | tf_op jit(solution)/shard_map/ppermute | solution.py:21
  64.1 4.3 %collective-permute-done.5 = bf16[8,2,16,128]{3,2,1,0:T(8,128)(2,1)S(1)} collective-permute-done((bf16[8,2,16,128]{3,2,1,0:T(8,128)(2,1)S(1)}, bf16[8,2,16,128]{3,2,1,0:T(8,128)(2,1)S(1)}, u32[]{:S(2)}, u32[]{:S(2)}) %collective-permute-start.5) | collective-permute-done | bytes 65568 | tf_op jit(solution)/shard_map/ppermute | solution.py:23
  68.5 4.2 %collective-permute-start.6 = (bf16[2,8,16,128]{3,2,1,0:T(8,128)(2,1)S(1)}, bf16[2,8,16,128]{3,2,1,0:T(8,128)(2,1)S(1)}, u32[]{:S(2)}, u32[]{:S(2)}) collective-permute-start(bf16[2,8,16,128]{3,2,1,0:T(8,128)(2,1)S(1)} %get-tuple-element.30), channel_id=1, source_target_pairs={{0,1},{1,2},{2,3},{3,4},{4,5},{5,6},{6,7},{7,8},{8,9},{9,10},{10,1... | collective-permute-start | bytes 196616 | tf_op jit(solution)/shard_map/ppermute | solution.py:21
  76.6 7.5 %collective-permute-done.7 = bf16[2,8,16,128]{3,2,1,0:T(8,128)(2,1)S(1)} collective-permute-done((bf16[2,8,16,128]{3,2,1,0:T(8,128)(2,1)S(1)}, bf16[2,8,16,128]{3,2,1,0:T(8,128)(2,1)S(1)}, u32[]{:S(2)}, u32[]{:S(2)}) %collective-permute-start.7) | collective-permute-done | bytes 65568 | tf_op jit(solution)/shard_map/ppermute | solution.py:23
  87.0 9.8 %all_to_all.38 = bf16[8,4,16,128]{3,2,1,0:T(8,128)(2,1)S(1)} all-to-all(bf16[8,4,16,128]{3,2,1,0:T(8,128)(2,1)S(1)} %get-tuple-element.55), channel_id=1, replica_groups=mesh['zslab'=8,'blk'=32] {'zslab'}, dimensions={0} | all-to-all | bytes 262144 | tf_op jit(solution)/shard_map/all_to_all | solution.py:160
  97.0 43.1 %all-gather.5.cloned.1.call-done = bf16[2560,1024]{1,0:T(8,128)(2,1)} async-done(((bf16[640,1024]{1,0:T(8,128)(2,1)}), bf16[2560,1024]{1,0:T(8,128)(2,1)}) %all-gather.5.cloned.1.call-update) | async-done | bytes 5242896 | tf_op jit(solution)/shard_map/all_gather | solution.py:88
  140.1 3.0 %fusion.26 = bf16[32,1024]{1,0:T(8,128)(2,1)S(1)} fusion(bf16[32,80,1024]{2,1,0:T(8,128)(2,1)} %bitcast.261, bf16[32,32,64]{2,1,0:T(8,128)(2,1)S(1)} %reshape_reshape.9), kind=kOutput, calls=%fused_computation.31 | convolution fusion | flops 134250496 | bytes 4390912 | tf_op jit(solution)/shard_map/tbf,bfd->td/dot_general | solution.py:169
  144.0 8.1 %all-to-all-start.1 = ((bf16[8,32,1024]{2,1,0:T(8,128)(2,1)}), bf16[8,32,1024]{2,1,0:T(8,128)(2,1)S(1)}, u32[]{:S(2)}, u32[]{:S(2)}) async-start(bf16[8,32,1024]{2,1,0:T(8,128)(2,1)} %broadcast_in_dim.9), calls=%async_computation.1 | async-start | bytes 1048576 | tf_op jit(solution)/shard_map/all_to_all | solution.py:32
  156.0 4.3 %all-to-all-done.1 = bf16[8,32,1024]{2,1,0:T(8,128)(2,1)S(1)} async-done(((bf16[8,32,1024]{2,1,0:T(8,128)(2,1)}), bf16[8,32,1024]{2,1,0:T(8,128)(2,1)S(1)}, u32[]{:S(2)}, u32[]{:S(2)}) %all-to-all-start.1) | async-done | bytes 524320 | tf_op jit(solution)/shard_map/all_to_all | solution.py:32
  160.8 23.5 %all_to_all.39 = bf16[32,32,256]{2,1,0:T(8,128)(2,1)S(1)} all-to-all(bf16[32,32,256]{2,1,0:T(8,128)(2,1)S(1)} %broadcast_in_dim.10), channel_id=1, replica_groups=mesh['zslab'=8,'blk'=32] {'blk'}, dimensions={0} | all-to-all | bytes 1048576 | tf_op jit(solution)/shard_map/all_to_all | solution.py:32
  189.4 8.2 %all-to-all-start.3 = ((bf16[32,32,256]{2,1,0:T(8,128)(2,1)}), bf16[32,32,256]{2,1,0:T(8,128)(2,1)}, u32[]{:S(2)}, u32[]{:S(2)}) async-start(bf16[32,32,256]{2,1,0:T(8,128)(2,1)} %pad_maximum_fusion), calls=%async_computation.3 | async-start | bytes 1048576 | tf_op jit(solution)/shard_map/all_to_all | solution.py:73
  197.8 14.4 %all-to-all-done.3 = bf16[32,32,256]{2,1,0:T(8,128)(2,1)} async-done(((bf16[32,32,256]{2,1,0:T(8,128)(2,1)}), bf16[32,32,256]{2,1,0:T(8,128)(2,1)}, u32[]{:S(2)}, u32[]{:S(2)}) %all-to-all-start.3) | async-done | bytes 524320 | tf_op jit(solution)/shard_map/all_to_all | solution.py:73
  213.7 11.9 %all_to_all.40 = bf16[8,32,1024]{2,1,0:T(8,128)(2,1)S(1)} all-to-all(bf16[8,32,1024]{2,1,0:T(8,128)(2,1)S(1)} %broadcast_in_dim.11), channel_id=1, replica_groups=mesh['zslab'=8,'blk'=32] {'zslab'}, dimensions={0} | all-to-all | bytes 1048576 | tf_op jit(solution)/shard_map/all_to_all | solution.py:32
  225.7 4.2 %fusion.4 = bf16[32,32,64]{2,0,1:T(8,128)(2,1)S(1)} fusion(bf16[32,80,1024]{2,1,0:T(8,128)(2,1)} %bitcast.263, bf16[32,1024]{1,0:T(8,128)(2,1)S(1)} %reduce_sum.58), kind=kOutput, calls=%fused_computation.4 | convolution fusion | flops 134283264 | bytes 4390912 | tf_op jit(solution)/shard_map/td,bfd->tbf/dot_general | solution.py:223
  230.3 8.1 %all_to_all.41 = bf16[1,32,16,128]{3,2,0,1:T(8,128)(2,1)S(1)} all-to-all(bf16[1,32,16,128]{3,2,0,1:T(8,128)(2,1)S(1)} %bitcast.248), channel_id=1, replica_groups=mesh['zslab'=8,'blk'=32] {'zslab'}, dimensions={1} | all-to-all | bytes 262144 | tf_op jit(solution)/shard_map/all_to_all | solution.py:230
  247.3 5.8 %collective-permute-start.10 = (bf16[2,8,16,128]{3,2,1,0:T(8,128)(2,1)S(1)}, bf16[2,8,16,128]{3,2,1,0:T(8,128)(2,1)S(1)}, u32[]{:S(2)}, u32[]{:S(2)}) collective-permute-start(bf16[2,8,16,128]{3,2,1,0:T(8,128)(2,1)S(1)} %get-tuple-element.26), channel_id=1, source_target_pairs={{1,0},{2,1},{3,2},{4,3},{5,4},{6,5},{7,6},{8,7},{9,8},{10,9},{11,1... | collective-permute-start | bytes 196616 | tf_op jit(solution)/shard_map/ppermute | solution.py:23
  253.1 5.4 %collective-permute-start.11 = (bf16[2,8,16,128]{3,2,1,0:T(8,128)(2,1)S(1)}, bf16[2,8,16,128]{3,2,1,0:T(8,128)(2,1)S(1)}, u32[]{:S(2)}, u32[]{:S(2)}) collective-permute-start(bf16[2,8,16,128]{3,2,1,0:T(8,128)(2,1)S(1)} %get-tuple-element.25), channel_id=1, source_target_pairs={{0,1},{1,2},{2,3},{3,4},{4,5},{5,6},{6,7},{7,8},{8,9},{9,10},{10,1... | collective-permute-start | bytes 196616 | tf_op jit(solution)/shard_map/ppermute | solution.py:21
  264.2 3.4 %collective-permute-start.13 = (bf16[8,2,16,128]{3,2,1,0:T(8,128)(2,1)S(1)}, bf16[8,2,16,128]{3,2,1,0:T(8,128)(2,1)S(1)}, u32[]{:S(2)}, u32[]{:S(2)}) collective-permute-start(bf16[8,2,16,128]{3,2,1,0:T(8,128)(2,1)S(1)} %get-tuple-element.36), channel_id=1, source_target_pairs={{32,0},{64,32},{96,64},{128,96},{160,128},{192,160},{224,192},{33,... | collective-permute-start | bytes 196616 | tf_op jit(solution)/shard_map/ppermute | solution.py:23
  270.2 3.6 %collective-permute-start.14 = (bf16[2,8,16,128]{3,2,1,0:T(8,128)(2,1)S(1)}, bf16[2,8,16,128]{3,2,1,0:T(8,128)(2,1)S(1)}, u32[]{:S(2)}, u32[]{:S(2)}) collective-permute-start(bf16[2,8,16,128]{3,2,1,0:T(8,128)(2,1)S(1)} %get-tuple-element.22), channel_id=1, source_target_pairs={{1,0},{2,1},{3,2},{4,3},{5,4},{6,5},{7,6},{8,7},{9,8},{10,9},{11,1... | collective-permute-start | bytes 196616 | tf_op jit(solution)/shard_map/ppermute | solution.py:23
  273.8 7.4 %collective-permute-start.15 = (bf16[2,8,16,128]{3,2,1,0:T(8,128)(2,1)S(1)}, bf16[2,8,16,128]{3,2,1,0:T(8,128)(2,1)S(1)}, u32[]{:S(2)}, u32[]{:S(2)}) collective-permute-start(bf16[2,8,16,128]{3,2,1,0:T(8,128)(2,1)S(1)} %get-tuple-element.21), channel_id=1, source_target_pairs={{0,1},{1,2},{2,3},{3,4},{4,5},{5,6},{6,7},{7,8},{8,9},{9,10},{10,1... | collective-permute-start | bytes 196616 | tf_op jit(solution)/shard_map/ppermute | solution.py:21
  (155 shorter events, 53.9 us)
Async XLA Ops:
  6.5 31.0 %all-gather.3.cloned.1.call-start = ((), (), s32[]{:S(2)}) async-start(), calls=%async_computation.6 | async-start | bytes 1474560 | tf_op jit(solution)/shard_map/all_gather | solution.py:87
  9.1 131.1 %all-gather.5.cloned.1.call-start = ((), (), s32[]{:S(2)}) async-start(), calls=%async_computation.7 | async-start | bytes 6553600 | tf_op jit(solution)/shard_map/all_gather | solution.py:88
  10.1 29.8 %collective-permute-start = (bf16[8,2,16,128]{3,2,1,0:T(8,128)(2,1)S(1)}, bf16[8,2,16,128]{3,2,1,0:T(8,128)(2,1)S(1)}, u32[]{:S(2)}, u32[]{:S(2)}) collective-permute-start(bf16[8,2,16,128]{3,2,1,0:T(8,128)(2,1)S(1)} %get-tuple-element.41), channel_id=1, source_target_pairs={{0,32},{32,64},{64,96},{96,128},{128,160},{160,192},{192,224},{1,3... | collective-permute-start | bytes 196616 | tf_op jit(solution)/shard_map/ppermute | solution.py:21
  13.6 26.3 %collective-permute-start.1 = (bf16[8,2,16,128]{3,2,1,0:T(8,128)(2,1)S(1)}, bf16[8,2,16,128]{3,2,1,0:T(8,128)(2,1)S(1)}, u32[]{:S(2)}, u32[]{:S(2)}) collective-permute-start(bf16[8,2,16,128]{3,2,1,0:T(8,128)(2,1)S(1)} %get-tuple-element.42), channel_id=1, source_target_pairs={{32,0},{64,32},{96,64},{128,96},{160,128},{192,160},{224,192},{33,... | collective-permute-start | bytes 196616 | tf_op jit(solution)/shard_map/ppermute | solution.py:23
  39.2 8.8 %copy-start.3 = (s32[2,3]{1,0:T(2,128)S(1)}, s32[2,3]{1,0:T(2,128)}, u32[]{:S(2)}) copy-start(s32[2,3]{1,0:T(2,128)} %param.9) | copy-start | bytes 76
  39.9 10.5 %collective-permute-start.2 = (bf16[2,8,16,128]{3,2,1,0:T(8,128)(2,1)S(1)}, bf16[2,8,16,128]{3,2,1,0:T(8,128)(2,1)S(1)}, u32[]{:S(2)}, u32[]{:S(2)}) collective-permute-start(bf16[2,8,16,128]{3,2,1,0:T(8,128)(2,1)S(1)} %get-tuple-element.34), channel_id=1, source_target_pairs={{0,1},{1,2},{2,3},{3,4},{4,5},{5,6},{6,7},{7,8},{8,9},{9,10},{10,1... | collective-permute-start | bytes 196616 | tf_op jit(solution)/shard_map/ppermute | solution.py:21
  46.0 9.2 %collective-permute-start.3 = (bf16[2,8,16,128]{3,2,1,0:T(8,128)(2,1)S(1)}, bf16[2,8,16,128]{3,2,1,0:T(8,128)(2,1)S(1)}, u32[]{:S(2)}, u32[]{:S(2)}) collective-permute-start(bf16[2,8,16,128]{3,2,1,0:T(8,128)(2,1)S(1)} %get-tuple-element.33), channel_id=1, source_target_pairs={{1,0},{2,1},{3,2},{4,3},{5,4},{6,5},{7,6},{8,7},{9,8},{10,9},{11,1... | collective-permute-start | bytes 196616 | tf_op jit(solution)/shard_map/ppermute | solution.py:23
  58.7 5.4 %collective-permute-start.4 = (bf16[8,2,16,128]{3,2,1,0:T(8,128)(2,1)S(1)}, bf16[8,2,16,128]{3,2,1,0:T(8,128)(2,1)S(1)}, u32[]{:S(2)}, u32[]{:S(2)}) collective-permute-start(bf16[8,2,16,128]{3,2,1,0:T(8,128)(2,1)S(1)} %get-tuple-element.39), channel_id=1, source_target_pairs={{0,32},{32,64},{64,96},{96,128},{128,160},{160,192},{192,224},{1,3... | collective-permute-start | bytes 196616 | tf_op jit(solution)/shard_map/ppermute | solution.py:21
  62.1 6.3 %collective-permute-start.5 = (bf16[8,2,16,128]{3,2,1,0:T(8,128)(2,1)S(1)}, bf16[8,2,16,128]{3,2,1,0:T(8,128)(2,1)S(1)}, u32[]{:S(2)}, u32[]{:S(2)}) collective-permute-start(bf16[8,2,16,128]{3,2,1,0:T(8,128)(2,1)S(1)} %get-tuple-element.40), channel_id=1, source_target_pairs={{32,0},{64,32},{96,64},{128,96},{160,128},{192,160},{224,192},{33,... | collective-permute-start | bytes 196616 | tf_op jit(solution)/shard_map/ppermute | solution.py:23
  68.5 8.1 %collective-permute-start.6 = (bf16[2,8,16,128]{3,2,1,0:T(8,128)(2,1)S(1)}, bf16[2,8,16,128]{3,2,1,0:T(8,128)(2,1)S(1)}, u32[]{:S(2)}, u32[]{:S(2)}) collective-permute-start(bf16[2,8,16,128]{3,2,1,0:T(8,128)(2,1)S(1)} %get-tuple-element.30), channel_id=1, source_target_pairs={{0,1},{1,2},{2,3},{3,4},{4,5},{5,6},{6,7},{7,8},{8,9},{9,10},{10,1... | collective-permute-start | bytes 196616 | tf_op jit(solution)/shard_map/ppermute | solution.py:21
  72.7 11.5 %collective-permute-start.7 = (bf16[2,8,16,128]{3,2,1,0:T(8,128)(2,1)S(1)}, bf16[2,8,16,128]{3,2,1,0:T(8,128)(2,1)S(1)}, u32[]{:S(2)}, u32[]{:S(2)}) collective-permute-start(bf16[2,8,16,128]{3,2,1,0:T(8,128)(2,1)S(1)} %get-tuple-element.29), channel_id=1, source_target_pairs={{1,0},{2,1},{3,2},{4,3},{5,4},{6,5},{7,6},{8,7},{9,8},{10,9},{11,1... | collective-permute-start | bytes 196616 | tf_op jit(solution)/shard_map/ppermute | solution.py:23
  144.0 16.3 %all-to-all-start.1 = ((bf16[8,32,1024]{2,1,0:T(8,128)(2,1)}), bf16[8,32,1024]{2,1,0:T(8,128)(2,1)S(1)}, u32[]{:S(2)}, u32[]{:S(2)}) async-start(bf16[8,32,1024]{2,1,0:T(8,128)(2,1)} %broadcast_in_dim.9), calls=%async_computation.1 | async-start | bytes 1048576 | tf_op jit(solution)/shard_map/all_to_all | solution.py:32
  160.7 24.1 %copy-start.4 = (bf16[32,128]{1,0:T(8,128)(2,1)S(1)}, bf16[32,128]{1,0:T(8,128)(2,1)}, u32[]{:S(2)}) copy-start(bf16[32,128]{1,0:T(8,128)(2,1)} %param.13) | copy-start | bytes 24580
  189.4 22.8 %all-to-all-start.3 = ((bf16[32,32,256]{2,1,0:T(8,128)(2,1)}), bf16[32,32,256]{2,1,0:T(8,128)(2,1)}, u32[]{:S(2)}, u32[]{:S(2)}) async-start(bf16[32,32,256]{2,1,0:T(8,128)(2,1)} %pad_maximum_fusion), calls=%async_computation.3 | async-start | bytes 1048576 | tf_op jit(solution)/shard_map/all_to_all | solution.py:73
  230.0 8.4 %copy-start.1 = (f32[8,4,16,128]{3,2,1,0:T(8,128)S(1)}, f32[8,4,16,128]{3,2,1,0:T(8,128)}, u32[]{:S(2)}) copy-start(f32[8,4,16,128]{3,2,1,0:T(8,128)} %get-tuple-element.56) | copy-start | bytes 786436
  238.6 6.6 %collective-permute-start.8 = (bf16[8,2,16,128]{3,2,1,0:T(8,128)(2,1)S(1)}, bf16[8,2,16,128]{3,2,1,0:T(8,128)(2,1)S(1)}, u32[]{:S(2)}, u32[]{:S(2)}) collective-permute-start(bf16[8,2,16,128]{3,2,1,0:T(8,128)(2,1)S(1)} %get-tuple-element.37), channel_id=1, source_target_pairs={{0,32},{32,64},{64,96},{96,128},{128,160},{160,192},{192,224},{1,3... | collective-permute-start | bytes 196616 | tf_op jit(solution)/shard_map/ppermute | solution.py:21
  241.3 5.9 %collective-permute-start.9 = (bf16[8,2,16,128]{3,2,1,0:T(8,128)(2,1)S(1)}, bf16[8,2,16,128]{3,2,1,0:T(8,128)(2,1)S(1)}, u32[]{:S(2)}, u32[]{:S(2)}) collective-permute-start(bf16[8,2,16,128]{3,2,1,0:T(8,128)(2,1)S(1)} %get-tuple-element.38), channel_id=1, source_target_pairs={{32,0},{64,32},{96,64},{128,96},{160,128},{192,160},{224,192},{33,... | collective-permute-start | bytes 196616 | tf_op jit(solution)/shard_map/ppermute | solution.py:23
  247.3 11.4 %collective-permute-start.10 = (bf16[2,8,16,128]{3,2,1,0:T(8,128)(2,1)S(1)}, bf16[2,8,16,128]{3,2,1,0:T(8,128)(2,1)S(1)}, u32[]{:S(2)}, u32[]{:S(2)}) collective-permute-start(bf16[2,8,16,128]{3,2,1,0:T(8,128)(2,1)S(1)} %get-tuple-element.26), channel_id=1, source_target_pairs={{1,0},{2,1},{3,2},{4,3},{5,4},{6,5},{7,6},{8,7},{9,8},{10,9},{11,1... | collective-permute-start | bytes 196616 | tf_op jit(solution)/shard_map/ppermute | solution.py:23
  253.1 6.6 %collective-permute-start.11 = (bf16[2,8,16,128]{3,2,1,0:T(8,128)(2,1)S(1)}, bf16[2,8,16,128]{3,2,1,0:T(8,128)(2,1)S(1)}, u32[]{:S(2)}, u32[]{:S(2)}) collective-permute-start(bf16[2,8,16,128]{3,2,1,0:T(8,128)(2,1)S(1)} %get-tuple-element.25), channel_id=1, source_target_pairs={{0,1},{1,2},{2,3},{3,4},{4,5},{5,6},{6,7},{7,8},{8,9},{9,10},{10,1... | collective-permute-start | bytes 196616 | tf_op jit(solution)/shard_map/ppermute | solution.py:21
  260.8 1.0 copy-start.5
  262.3 6.6 %collective-permute-start.12 = (bf16[8,2,16,128]{3,2,1,0:T(8,128)(2,1)S(1)}, bf16[8,2,16,128]{3,2,1,0:T(8,128)(2,1)S(1)}, u32[]{:S(2)}, u32[]{:S(2)}) collective-permute-start(bf16[8,2,16,128]{3,2,1,0:T(8,128)(2,1)S(1)} %get-tuple-element.35), channel_id=1, source_target_pairs={{0,32},{32,64},{64,96},{96,128},{128,160},{160,192},{192,224},{1,3... | collective-permute-start | bytes 196616 | tf_op jit(solution)/shard_map/ppermute | solution.py:21
  264.2 5.9 %collective-permute-start.13 = (bf16[8,2,16,128]{3,2,1,0:T(8,128)(2,1)S(1)}, bf16[8,2,16,128]{3,2,1,0:T(8,128)(2,1)S(1)}, u32[]{:S(2)}, u32[]{:S(2)}) collective-permute-start(bf16[8,2,16,128]{3,2,1,0:T(8,128)(2,1)S(1)} %get-tuple-element.36), channel_id=1, source_target_pairs={{32,0},{64,32},{96,64},{128,96},{160,128},{192,160},{224,192},{33,... | collective-permute-start | bytes 196616 | tf_op jit(solution)/shard_map/ppermute | solution.py:23
  270.2 11.1 %collective-permute-start.14 = (bf16[2,8,16,128]{3,2,1,0:T(8,128)(2,1)S(1)}, bf16[2,8,16,128]{3,2,1,0:T(8,128)(2,1)S(1)}, u32[]{:S(2)}, u32[]{:S(2)}) collective-permute-start(bf16[2,8,16,128]{3,2,1,0:T(8,128)(2,1)S(1)} %get-tuple-element.22), channel_id=1, source_target_pairs={{1,0},{2,1},{3,2},{4,3},{5,4},{6,5},{7,6},{8,7},{9,8},{10,9},{11,1... | collective-permute-start | bytes 196616 | tf_op jit(solution)/shard_map/ppermute | solution.py:23
  273.8 8.7 %collective-permute-start.15 = (bf16[2,8,16,128]{3,2,1,0:T(8,128)(2,1)S(1)}, bf16[2,8,16,128]{3,2,1,0:T(8,128)(2,1)S(1)}, u32[]{:S(2)}, u32[]{:S(2)}) collective-permute-start(bf16[2,8,16,128]{3,2,1,0:T(8,128)(2,1)S(1)} %get-tuple-element.21), channel_id=1, source_target_pairs={{0,1},{1,2},{2,3},{3,4},{4,5},{5,6},{6,7},{7,8},{8,9},{9,10},{10,1... | collective-permute-start | bytes 196616 | tf_op jit(solution)/shard_map/ppermute | solution.py:21
  (2 other events, 1.6 us)
Sparse Core Ops, SparseCore 0:
  9.2 28.2 all-gather.2
  39.4 100.7 all-gather.4

commit v18 on v11

--- a/solution.py
+++ b/solution.py
@@ -158,9 +158,9 @@
             hidden.astype(jnp.float32) + gate_mask * (conv_out * jax.nn.sigmoid(conv_out))
         ).astype(jnp.bfloat16)
     sigma = jax.nn.sigmoid(conv_outs[-1])
-    slope = padded_2(
-        gate_mask * sigma * (1.0 + conv_outs[-1] * (1.0 - sigma)), (("zslab", 1),), DMAX
-    )
+    slope = gate_mask * sigma * (1.0 + conv_outs[-1] * (1.0 - sigma))
+    rim = padded_2(slope.astype(jnp.bfloat16), (("zslab", 1),), DMAX).astype(jnp.float32)
+    slope = jnp.concatenate([rim[:, :DMAX], slope, rim[:, -DMAX:]], axis=1)
     hidden, slope = lax.optimization_barrier((hidden, slope))
     slab_view = lax.all_to_all(hidden, "zslab", split_axis=0, concat_axis=1, tiled=True)
     x_local, z_total = (slab_view.shape[0], slab_view.shape[1])

time: 240 us -> 243 us (1.012)
  waiting for transfers between devices: 48.5 us -> 45.4 us
    ppermute x8, waiting for transfers between devices: 23.9 us -> 19.9 us  [padded_2(): lax.ppermute(head, axis, [((i + 1) % count, i) for i in range(ends)])]
    ppermute x8, starting transfers between devices: 31.9 us -> 34.5 us  [padded_2(): lax.ppermute(tail, axis, [(i, (i + 1) % count) for i in range(ends)])]
    unnamed x38 -> x34, local copies, waits for them, and re-layouts: 6.8 us -> 7.76 us
  transfers between devices with their start and end apart: 20 -> 20, of which waited for: 13 -> 11; matrix products, arithmetic and copies ran while one was open for 6% -> 7% of each run, Pallas kernels for 0% -> 0%
where the time goes in v18:
time: 243 us; the launch traced here: 239 us
  starting transfers between devices  74.9 us (31%)
  blocking collectives  55 us (23%)
  waiting for transfers between devices  45.4 us (19%)
  local copies, waits for them, and re-layouts  21.6 us (9%)
  between operations  18.2 us (7%)
  matrix products  17.5 us (7%)
  other arithmetic  6.97 us (3%)
    all_to_all x2, blocking collectives, copy_for_each(): lax.all_to_all(jnp.broadcast_to(shard[None], (peers, *shard.shape)), axis...  35.7 us
    ppermute x8, starting transfers between devices, padded_2(): lax.ppermute(tail, axis, [(i, (i + 1) % count) for i in range(ends)])  34.5 us
    ppermute x8, starting transfers between devices, padded_2(): lax.ppermute(head, axis, [((i + 1) % count, i) for i in range(ends)])  23.5 us
    ppermute x8, waiting for transfers between devices, padded_2(): lax.ppermute(head, axis, [((i + 1) % count, i) for i in range(ends)])  19.9 us
    all_to_all x1, waiting for transfers between devices, sum_at_owner(): lax.all_to_all(cut_along(shard, dim, peers), axis, 0, 0, tiled=True)  14.4 us
    all_gather x1, blocking collectives, gather_weights(): lax.all_gather(rows, 'blk', axis=0, tiled=True, axis_index_groups=near)  9.96 us
    all_to_all x1, blocking collectives, local(): lax.all_to_all(hidden, 'zslab', split_axis=0, concat_axis=1, tiled=True)  9.33 us
    all_to_all x1, starting transfers between devices, sum_at_owner(): lax.all_to_all(cut_along(shard, dim, peers), axis, 0, 0, tiled=True)  8.22 us
  transfers between devices with their start and end apart: 20, of which 11 were waited for; matrix products, arithmetic and copies ran while one was open for 7% of the time, Pallas kernels for 0%

profile of v18, /device:TPU:103, one launch (start us, length us, event | category | flops | bytes accessed | tf_op | source)
XLA Modules:
  0.0 239.5 jit_solution(4377014524932720210)
XLA Ops:
  7.5 3.5 %collective-permute-start = (bf16[8,2,16,128]{3,2,1,0:T(8,128)(2,1)S(1)}, bf16[8,2,16,128]{3,2,1,0:T(8,128)(2,1)S(1)}, u32[]{:S(2)}, u32[]{:S(2)}) collective-permute-start(bf16[8,2,16,128]{3,2,1,0:T(8,128)(2,1)S(1)} %get-tuple-element.50), channel_id=1, source_target_pairs={{0,32},{32,64},{64,96},{96,128},{128,160},{160,192},{192,224},{1,3... | collective-permute-start | bytes 196616 | tf_op jit(solution)/shard_map/ppermute | solution.py:21
  14.8 10.0 %all_gather.6 = bf16[320,1024]{1,0:T(8,128)(2,1)} all-gather(bf16[80,1024]{1,0:T(8,128)(2,1)S(1)} %maximum_maximum_fusion.3), channel_id=1, replica_groups={{0,1,2,3},{4,5,6,7},{8,9,10,11},{12,13,14,15},{16,17,18,19},{20,21,22,2..., dimensions={0}, use_global_device_ids=true | all-gather | bytes 819200 | tf_op jit(solution)/shard_map/all_gather | solution.py:87
  27.1 5.6 %collective-permute-start.2 = (bf16[2,8,16,128]{3,2,1,0:T(8,128)(2,1)S(1)}, bf16[2,8,16,128]{3,2,1,0:T(8,128)(2,1)S(1)}, u32[]{:S(2)}, u32[]{:S(2)}) collective-permute-start(bf16[2,8,16,128]{3,2,1,0:T(8,128)(2,1)S(1)} %get-tuple-element.43), channel_id=1, source_target_pairs={{0,1},{1,2},{2,3},{3,4},{4,5},{5,6},{6,7},{7,8},{8,9},{9,10},{10,1... | collective-permute-start | bytes 196616 | tf_op jit(solution)/shard_map/ppermute | solution.py:21
  37.3 4.6 %collective-permute-done.3 = bf16[2,8,16,128]{3,2,1,0:T(8,128)(2,1)S(1)} collective-permute-done((bf16[2,8,16,128]{3,2,1,0:T(8,128)(2,1)S(1)}, bf16[2,8,16,128]{3,2,1,0:T(8,128)(2,1)S(1)}, u32[]{:S(2)}, u32[]{:S(2)}) %collective-permute-start.3) | collective-permute-done | bytes 65568 | tf_op jit(solution)/shard_map/ppermute | solution.py:23
  45.4 5.4 %collective-permute-start.4 = (bf16[8,2,16,128]{3,2,1,0:T(8,128)(2,1)S(1)}, bf16[8,2,16,128]{3,2,1,0:T(8,128)(2,1)S(1)}, u32[]{:S(2)}, u32[]{:S(2)}) collective-permute-start(bf16[8,2,16,128]{3,2,1,0:T(8,128)(2,1)S(1)} %get-tuple-element.48), channel_id=1, source_target_pairs={{0,32},{32,64},{64,96},{96,128},{128,160},{160,192},{192,224},{1,3... | collective-permute-start | bytes 196616 | tf_op jit(solution)/shard_map/ppermute | solution.py:21
  52.7 4.4 %collective-permute-done.5 = bf16[8,2,16,128]{3,2,1,0:T(8,128)(2,1)S(1)} collective-permute-done((bf16[8,2,16,128]{3,2,1,0:T(8,128)(2,1)S(1)}, bf16[8,2,16,128]{3,2,1,0:T(8,128)(2,1)S(1)}, u32[]{:S(2)}, u32[]{:S(2)}) %collective-permute-start.5) | collective-permute-done | bytes 65568 | tf_op jit(solution)/shard_map/ppermute | solution.py:23
  57.1 3.4 %collective-permute-start.6 = (bf16[2,8,16,128]{3,2,1,0:T(8,128)(2,1)S(1)}, bf16[2,8,16,128]{3,2,1,0:T(8,128)(2,1)S(1)}, u32[]{:S(2)}, u32[]{:S(2)}) collective-permute-start(bf16[2,8,16,128]{3,2,1,0:T(8,128)(2,1)S(1)} %get-tuple-element.39), channel_id=1, source_target_pairs={{0,1},{1,2},{2,3},{3,4},{4,5},{5,6},{6,7},{7,8},{8,9},{9,10},{10,1... | collective-permute-start | bytes 196616 | tf_op jit(solution)/shard_map/ppermute | solution.py:21
  64.5 6.6 %collective-permute-done.7 = bf16[2,8,16,128]{3,2,1,0:T(8,128)(2,1)S(1)} collective-permute-done((bf16[2,8,16,128]{3,2,1,0:T(8,128)(2,1)S(1)}, bf16[2,8,16,128]{3,2,1,0:T(8,128)(2,1)S(1)}, u32[]{:S(2)}, u32[]{:S(2)}) %collective-permute-start.7) | collective-permute-done | bytes 65568 | tf_op jit(solution)/shard_map/ppermute | solution.py:23
  75.2 3.4 %collective-permute-start.9 = (bf16[8,2,16,128]{3,2,1,0:T(8,128)(2,1)S(1)}, bf16[8,2,16,128]{3,2,1,0:T(8,128)(2,1)S(1)}, u32[]{:S(2)}, u32[]{:S(2)}) collective-permute-start(bf16[8,2,16,128]{3,2,1,0:T(8,128)(2,1)S(1)} %get-tuple-element.47), channel_id=1, source_target_pairs={{32,0},{64,32},{96,64},{128,96},{160,128},{192,160},{224,192},{33,... | collective-permute-start | bytes 196616 | tf_op jit(solution)/shard_map/ppermute | solution.py:23
  82.6 9.3 %all_to_all.38 = bf16[8,4,16,128]{3,2,1,0:T(8,128)(2,1)S(1)} all-to-all(bf16[8,4,16,128]{3,2,1,0:T(8,128)(2,1)S(1)} %get-tuple-element.7), channel_id=1, replica_groups=mesh['zslab'=8,'blk'=32] {'zslab'}, dimensions={0} | all-to-all | bytes 262144 | tf_op jit(solution)/shard_map/all_to_all | solution.py:165
  96.1 4.4 %all-to-all-start.1 = ((bf16[8,32,1024]{2,1,0:T(8,128)(2,1)}), bf16[8,32,1024]{2,1,0:T(8,128)(2,1)S(1)}, u32[]{:S(2)}, u32[]{:S(2)}) async-start(bf16[8,32,1024]{2,1,0:T(8,128)(2,1)} %broadcast_in_dim.9), calls=%async_computation.1 | async-start | bytes 1048576 | tf_op jit(solution)/shard_map/all_to_all | solution.py:32
  104.4 4.5 %all-to-all-done.1 = bf16[8,32,1024]{2,1,0:T(8,128)(2,1)S(1)} async-done(((bf16[8,32,1024]{2,1,0:T(8,128)(2,1)}), bf16[8,32,1024]{2,1,0:T(8,128)(2,1)S(1)}, u32[]{:S(2)}, u32[]{:S(2)}) %all-to-all-start.1) | async-done | bytes 524320 | tf_op jit(solution)/shard_map/all_to_all | solution.py:32
  109.3 23.8 %all_to_all.39 = bf16[32,32,256]{2,1,0:T(8,128)(2,1)S(1)} all-to-all(bf16[32,32,256]{2,1,0:T(8,128)(2,1)S(1)} %broadcast_in_dim.10), channel_id=1, replica_groups=mesh['zslab'=8,'blk'=32] {'blk'}, dimensions={0} | all-to-all | bytes 1048576 | tf_op jit(solution)/shard_map/all_to_all | solution.py:32
  138.2 8.2 %all-to-all-start.3 = ((bf16[32,32,256]{2,1,0:T(8,128)(2,1)}), bf16[32,32,256]{2,1,0:T(8,128)(2,1)}, u32[]{:S(2)}, u32[]{:S(2)}) async-start(bf16[32,32,256]{2,1,0:T(8,128)(2,1)} %pad_maximum_fusion.1), calls=%async_computation.3 | async-start | bytes 1048576 | tf_op jit(solution)/shard_map/all_to_all | solution.py:73
  146.6 14.4 %all-to-all-done.3 = bf16[32,32,256]{2,1,0:T(8,128)(2,1)} async-done(((bf16[32,32,256]{2,1,0:T(8,128)(2,1)}), bf16[32,32,256]{2,1,0:T(8,128)(2,1)}, u32[]{:S(2)}, u32[]{:S(2)}) %all-to-all-start.3) | async-done | bytes 524320 | tf_op jit(solution)/shard_map/all_to_all | solution.py:73
  162.6 11.9 %all_to_all.40 = bf16[8,32,1024]{2,1,0:T(8,128)(2,1)S(1)} all-to-all(bf16[8,32,1024]{2,1,0:T(8,128)(2,1)S(1)} %broadcast_in_dim.11), channel_id=1, replica_groups=mesh['zslab'=8,'blk'=32] {'zslab'}, dimensions={0} | all-to-all | bytes 1048576 | tf_op jit(solution)/shard_map/all_to_all | solution.py:32
  174.6 4.2 %fusion.4 = bf16[32,32,64]{2,0,1:T(8,128)(2,1)S(1)} fusion(bf16[32,80,1024]{2,1,0:T(8,128)(2,1)} %bitcast.299, bf16[32,1024]{1,0:T(8,128)(2,1)S(1)} %reduce_sum.58), kind=kOutput, calls=%fused_computation.4 | convolution fusion | flops 134283264 | bytes 4390912 | tf_op jit(solution)/shard_map/td,bfd->tbf/dot_general | solution.py:228
  184.0 4.2 %all-to-all-start.5 = ((bf16[8,1,8,16,128]{4,3,2,1,0:T(8,128)(2,1)}), bf16[8,1,8,16,128]{4,3,2,1,0:T(8,128)(2,1)S(1)}, u32[]{:S(2)}, u32[]{:S(2)}) async-start(bf16[8,1,8,16,128]{4,3,2,1,0:T(8,128)(2,1)} %constant_dynamic-update-slice_fusion.2), calls=%async_computation.5 | async-start | bytes 524288 | tf_op jit(solution)/shard_map/all_to_all | solution.py:240
  189.6 4.0 %all-to-all-done.5 = bf16[8,1,8,16,128]{4,3,2,1,0:T(8,128)(2,1)S(1)} async-done(((bf16[8,1,8,16,128]{4,3,2,1,0:T(8,128)(2,1)}), bf16[8,1,8,16,128]{4,3,2,1,0:T(8,128)(2,1)S(1)}, u32[]{:S(2)}, u32[]{:S(2)}) %all-to-all-start.5) | async-done | bytes 262176 | tf_op jit(solution)/shard_map/all_to_all | solution.py:240
  193.6 4.9 %collective-permute-start.10 = (bf16[2,8,16,128]{3,2,1,0:T(8,128)(2,1)S(1)}, bf16[2,8,16,128]{3,2,1,0:T(8,128)(2,1)S(1)}, u32[]{:S(2)}, u32[]{:S(2)}) collective-permute-start(bf16[2,8,16,128]{3,2,1,0:T(8,128)(2,1)S(1)} %get-tuple-element.33), channel_id=1, source_target_pairs={{1,0},{2,1},{3,2},{4,3},{5,4},{6,5},{7,6},{8,7},{9,8},{10,9},{11,1... | collective-permute-start | bytes 196616 | tf_op jit(solution)/shard_map/ppermute | solution.py:23
  198.5 5.2 %collective-permute-start.11 = (bf16[2,8,16,128]{3,2,1,0:T(8,128)(2,1)S(1)}, bf16[2,8,16,128]{3,2,1,0:T(8,128)(2,1)S(1)}, u32[]{:S(2)}, u32[]{:S(2)}) collective-permute-start(bf16[2,8,16,128]{3,2,1,0:T(8,128)(2,1)S(1)} %get-tuple-element.32), channel_id=1, source_target_pairs={{0,1},{1,2},{2,3},{3,4},{4,5},{5,6},{6,7},{7,8},{8,9},{9,10},{10,1... | collective-permute-start | bytes 196616 | tf_op jit(solution)/shard_map/ppermute | solution.py:21
  210.3 3.3 %collective-permute-start.13 = (bf16[8,2,16,128]{3,2,1,0:T(8,128)(2,1)S(1)}, bf16[8,2,16,128]{3,2,1,0:T(8,128)(2,1)S(1)}, u32[]{:S(2)}, u32[]{:S(2)}) collective-permute-start(bf16[8,2,16,128]{3,2,1,0:T(8,128)(2,1)S(1)} %get-tuple-element.45), channel_id=1, source_target_pairs={{32,0},{64,32},{96,64},{128,96},{160,128},{192,160},{224,192},{33,... | collective-permute-start | bytes 196616 | tf_op jit(solution)/shard_map/ppermute | solution.py:23
  216.2 4.4 %collective-permute-start.14 = (bf16[2,8,16,128]{3,2,1,0:T(8,128)(2,1)S(1)}, bf16[2,8,16,128]{3,2,1,0:T(8,128)(2,1)S(1)}, u32[]{:S(2)}, u32[]{:S(2)}) collective-permute-start(bf16[2,8,16,128]{3,2,1,0:T(8,128)(2,1)S(1)} %get-tuple-element.29), channel_id=1, source_target_pairs={{1,0},{2,1},{3,2},{4,3},{5,4},{6,5},{7,6},{8,7},{9,8},{10,9},{11,1... | collective-permute-start | bytes 196616 | tf_op jit(solution)/shard_map/ppermute | solution.py:23
  220.6 7.5 %collective-permute-start.15 = (bf16[2,8,16,128]{3,2,1,0:T(8,128)(2,1)S(1)}, bf16[2,8,16,128]{3,2,1,0:T(8,128)(2,1)S(1)}, u32[]{:S(2)}, u32[]{:S(2)}) collective-permute-start(bf16[2,8,16,128]{3,2,1,0:T(8,128)(2,1)S(1)} %get-tuple-element.28), channel_id=1, source_target_pairs={{0,1},{1,2},{2,3},{3,4},{4,5},{5,6},{6,7},{7,8},{8,9},{9,10},{10,1... | collective-permute-start | bytes 196616 | tf_op jit(solution)/shard_map/ppermute | solution.py:21
  (164 shorter events, 60.3 us)
Async XLA Ops:
  6.5 85.6 %all-gather.2.cloned.1.call-start = ((), (), s32[]{:S(2)}) async-start(), calls=%async_computation.6 | async-start | bytes 5898240 | tf_op jit(solution)/shard_map/all_gather | solution.py:88
  7.5 19.5 %collective-permute-start = (bf16[8,2,16,128]{3,2,1,0:T(8,128)(2,1)S(1)}, bf16[8,2,16,128]{3,2,1,0:T(8,128)(2,1)S(1)}, u32[]{:S(2)}, u32[]{:S(2)}) collective-permute-start(bf16[8,2,16,128]{3,2,1,0:T(8,128)(2,1)S(1)} %get-tuple-element.50), channel_id=1, source_target_pairs={{0,32},{32,64},{64,96},{96,128},{128,160},{160,192},{192,224},{1,3... | collective-permute-start | bytes 196616 | tf_op jit(solution)/shard_map/ppermute | solution.py:21
  11.0 16.1 %collective-permute-start.1 = (bf16[8,2,16,128]{3,2,1,0:T(8,128)(2,1)S(1)}, bf16[8,2,16,128]{3,2,1,0:T(8,128)(2,1)S(1)}, u32[]{:S(2)}, u32[]{:S(2)}) collective-permute-start(bf16[8,2,16,128]{3,2,1,0:T(8,128)(2,1)S(1)} %get-tuple-element.51), channel_id=1, source_target_pairs={{32,0},{64,32},{96,64},{128,96},{160,128},{192,160},{224,192},{33,... | collective-permute-start | bytes 196616 | tf_op jit(solution)/shard_map/ppermute | solution.py:23
  26.3 8.3 %copy-start.4 = (s32[2,3]{1,0:T(2,128)S(1)}, s32[2,3]{1,0:T(2,128)}, u32[]{:S(2)}) copy-start(s32[2,3]{1,0:T(2,128)} %param.9) | copy-start | bytes 76
  27.1 10.2 %collective-permute-start.2 = (bf16[2,8,16,128]{3,2,1,0:T(8,128)(2,1)S(1)}, bf16[2,8,16,128]{3,2,1,0:T(8,128)(2,1)S(1)}, u32[]{:S(2)}, u32[]{:S(2)}) collective-permute-start(bf16[2,8,16,128]{3,2,1,0:T(8,128)(2,1)S(1)} %get-tuple-element.43), channel_id=1, source_target_pairs={{0,1},{1,2},{2,3},{3,4},{4,5},{5,6},{6,7},{7,8},{8,9},{9,10},{10,1... | collective-permute-start | bytes 196616 | tf_op jit(solution)/shard_map/ppermute | solution.py:21
  32.7 9.2 %collective-permute-start.3 = (bf16[2,8,16,128]{3,2,1,0:T(8,128)(2,1)S(1)}, bf16[2,8,16,128]{3,2,1,0:T(8,128)(2,1)S(1)}, u32[]{:S(2)}, u32[]{:S(2)}) collective-permute-start(bf16[2,8,16,128]{3,2,1,0:T(8,128)(2,1)S(1)} %get-tuple-element.42), channel_id=1, source_target_pairs={{1,0},{2,1},{3,2},{4,3},{5,4},{6,5},{7,6},{8,7},{9,8},{10,9},{11,1... | collective-permute-start | bytes 196616 | tf_op jit(solution)/shard_map/ppermute | solution.py:23
  45.4 7.3 %collective-permute-start.4 = (bf16[8,2,16,128]{3,2,1,0:T(8,128)(2,1)S(1)}, bf16[8,2,16,128]{3,2,1,0:T(8,128)(2,1)S(1)}, u32[]{:S(2)}, u32[]{:S(2)}) collective-permute-start(bf16[8,2,16,128]{3,2,1,0:T(8,128)(2,1)S(1)} %get-tuple-element.48), channel_id=1, source_target_pairs={{0,32},{32,64},{64,96},{96,128},{128,160},{160,192},{192,224},{1,3... | collective-permute-start | bytes 196616 | tf_op jit(solution)/shard_map/ppermute | solution.py:21
  50.8 6.3 %collective-permute-start.5 = (bf16[8,2,16,128]{3,2,1,0:T(8,128)(2,1)S(1)}, bf16[8,2,16,128]{3,2,1,0:T(8,128)(2,1)S(1)}, u32[]{:S(2)}, u32[]{:S(2)}) collective-permute-start(bf16[8,2,16,128]{3,2,1,0:T(8,128)(2,1)S(1)} %get-tuple-element.49), channel_id=1, source_target_pairs={{32,0},{64,32},{96,64},{128,96},{160,128},{192,160},{224,192},{33,... | collective-permute-start | bytes 196616 | tf_op jit(solution)/shard_map/ppermute | solution.py:23
  57.1 7.3 %collective-permute-start.6 = (bf16[2,8,16,128]{3,2,1,0:T(8,128)(2,1)S(1)}, bf16[2,8,16,128]{3,2,1,0:T(8,128)(2,1)S(1)}, u32[]{:S(2)}, u32[]{:S(2)}) collective-permute-start(bf16[2,8,16,128]{3,2,1,0:T(8,128)(2,1)S(1)} %get-tuple-element.39), channel_id=1, source_target_pairs={{0,1},{1,2},{2,3},{3,4},{4,5},{5,6},{6,7},{7,8},{8,9},{9,10},{10,1... | collective-permute-start | bytes 196616 | tf_op jit(solution)/shard_map/ppermute | solution.py:21
  60.5 10.6 %collective-permute-start.7 = (bf16[2,8,16,128]{3,2,1,0:T(8,128)(2,1)S(1)}, bf16[2,8,16,128]{3,2,1,0:T(8,128)(2,1)S(1)}, u32[]{:S(2)}, u32[]{:S(2)}) collective-permute-start(bf16[2,8,16,128]{3,2,1,0:T(8,128)(2,1)S(1)} %get-tuple-element.38), channel_id=1, source_target_pairs={{1,0},{2,1},{3,2},{4,3},{5,4},{6,5},{7,6},{8,7},{9,8},{10,9},{11,1... | collective-permute-start | bytes 196616 | tf_op jit(solution)/shard_map/ppermute | solution.py:23
  73.3 5.4 %collective-permute-start.8 = (bf16[8,2,16,128]{3,2,1,0:T(8,128)(2,1)S(1)}, bf16[8,2,16,128]{3,2,1,0:T(8,128)(2,1)S(1)}, u32[]{:S(2)}, u32[]{:S(2)}) collective-permute-start(bf16[8,2,16,128]{3,2,1,0:T(8,128)(2,1)S(1)} %get-tuple-element.46), channel_id=1, source_target_pairs={{0,32},{32,64},{64,96},{96,128},{128,160},{160,192},{192,224},{1,3... | collective-permute-start | bytes 196616 | tf_op jit(solution)/shard_map/ppermute | solution.py:21
  75.2 6.4 %collective-permute-start.9 = (bf16[8,2,16,128]{3,2,1,0:T(8,128)(2,1)S(1)}, bf16[8,2,16,128]{3,2,1,0:T(8,128)(2,1)S(1)}, u32[]{:S(2)}, u32[]{:S(2)}) collective-permute-start(bf16[8,2,16,128]{3,2,1,0:T(8,128)(2,1)S(1)} %get-tuple-element.47), channel_id=1, source_target_pairs={{32,0},{64,32},{96,64},{128,96},{160,128},{192,160},{224,192},{33,... | collective-permute-start | bytes 196616 | tf_op jit(solution)/shard_map/ppermute | solution.py:23
  96.1 12.9 %all-to-all-start.1 = ((bf16[8,32,1024]{2,1,0:T(8,128)(2,1)}), bf16[8,32,1024]{2,1,0:T(8,128)(2,1)S(1)}, u32[]{:S(2)}, u32[]{:S(2)}) async-start(bf16[8,32,1024]{2,1,0:T(8,128)(2,1)} %broadcast_in_dim.9), calls=%async_computation.1 | async-start | bytes 1048576 | tf_op jit(solution)/shard_map/all_to_all | solution.py:32
  109.2 24.4 %copy-start.5 = (bf16[32,128]{1,0:T(8,128)(2,1)S(1)}, bf16[32,128]{1,0:T(8,128)(2,1)}, u32[]{:S(2)}) copy-start(bf16[32,128]{1,0:T(8,128)(2,1)} %param.13) | copy-start | bytes 24580
  138.2 22.8 %all-to-all-start.3 = ((bf16[32,32,256]{2,1,0:T(8,128)(2,1)}), bf16[32,32,256]{2,1,0:T(8,128)(2,1)}, u32[]{:S(2)}, u32[]{:S(2)}) async-start(bf16[32,32,256]{2,1,0:T(8,128)(2,1)} %pad_maximum_fusion.1), calls=%async_computation.3 | async-start | bytes 1048576 | tf_op jit(solution)/shard_map/all_to_all | solution.py:73
  184.0 9.5 %copy-start = (f32[8,8,16,128]{3,2,1,0:T(8,128)S(1)}, f32[8,8,16,128]{3,2,1,0:T(8,128)}, u32[]{:S(2)}) copy-start(f32[8,8,16,128]{3,2,1,0:T(8,128)} %pad_maximum_fusion) | copy-start | bytes 1572868
  184.0 9.5 %all-to-all-start.5 = ((bf16[8,1,8,16,128]{4,3,2,1,0:T(8,128)(2,1)}), bf16[8,1,8,16,128]{4,3,2,1,0:T(8,128)(2,1)S(1)}, u32[]{:S(2)}, u32[]{:S(2)}) async-start(bf16[8,1,8,16,128]{4,3,2,1,0:T(8,128)(2,1)} %constant_dynamic-update-slice_fusion.2), calls=%async_computation.5 | async-start | bytes 524288 | tf_op jit(solution)/shard_map/all_to_all | solution.py:240
  193.6 10.2 %collective-permute-start.10 = (bf16[2,8,16,128]{3,2,1,0:T(8,128)(2,1)S(1)}, bf16[2,8,16,128]{3,2,1,0:T(8,128)(2,1)S(1)}, u32[]{:S(2)}, u32[]{:S(2)}) collective-permute-start(bf16[2,8,16,128]{3,2,1,0:T(8,128)(2,1)S(1)} %get-tuple-element.33), channel_id=1, source_target_pairs={{1,0},{2,1},{3,2},{4,3},{5,4},{6,5},{7,6},{8,7},{9,8},{10,9},{11,1... | collective-permute-start | bytes 196616 | tf_op jit(solution)/shard_map/ppermute | solution.py:23
  198.5 6.6 %collective-permute-start.11 = (bf16[2,8,16,128]{3,2,1,0:T(8,128)(2,1)S(1)}, bf16[2,8,16,128]{3,2,1,0:T(8,128)(2,1)S(1)}, u32[]{:S(2)}, u32[]{:S(2)}) collective-permute-start(bf16[2,8,16,128]{3,2,1,0:T(8,128)(2,1)S(1)} %get-tuple-element.32), channel_id=1, source_target_pairs={{0,1},{1,2},{2,3},{3,4},{4,5},{5,6},{6,7},{7,8},{8,9},{9,10},{10,1... | collective-permute-start | bytes 196616 | tf_op jit(solution)/shard_map/ppermute | solution.py:21
  206.1 1.0 copy-start.6
  208.3 6.6 %collective-permute-start.12 = (bf16[8,2,16,128]{3,2,1,0:T(8,128)(2,1)S(1)}, bf16[8,2,16,128]{3,2,1,0:T(8,128)(2,1)S(1)}, u32[]{:S(2)}, u32[]{:S(2)}) collective-permute-start(bf16[8,2,16,128]{3,2,1,0:T(8,128)(2,1)S(1)} %get-tuple-element.44), channel_id=1, source_target_pairs={{0,32},{32,64},{64,96},{96,128},{128,160},{160,192},{192,224},{1,3... | collective-permute-start | bytes 196616 | tf_op jit(solution)/shard_map/ppermute | solution.py:21
  210.3 5.9 %collective-permute-start.13 = (bf16[8,2,16,128]{3,2,1,0:T(8,128)(2,1)S(1)}, bf16[8,2,16,128]{3,2,1,0:T(8,128)(2,1)S(1)}, u32[]{:S(2)}, u32[]{:S(2)}) collective-permute-start(bf16[8,2,16,128]{3,2,1,0:T(8,128)(2,1)S(1)} %get-tuple-element.45), channel_id=1, source_target_pairs={{32,0},{64,32},{96,64},{128,96},{160,128},{192,160},{224,192},{33,... | collective-permute-start | bytes 196616 | tf_op jit(solution)/shard_map/ppermute | solution.py:23
  216.2 11.9 %collective-permute-start.14 = (bf16[2,8,16,128]{3,2,1,0:T(8,128)(2,1)S(1)}, bf16[2,8,16,128]{3,2,1,0:T(8,128)(2,1)S(1)}, u32[]{:S(2)}, u32[]{:S(2)}) collective-permute-start(bf16[2,8,16,128]{3,2,1,0:T(8,128)(2,1)S(1)} %get-tuple-element.29), channel_id=1, source_target_pairs={{1,0},{2,1},{3,2},{4,3},{5,4},{6,5},{7,6},{8,7},{9,8},{10,9},{11,1... | collective-permute-start | bytes 196616 | tf_op jit(solution)/shard_map/ppermute | solution.py:23
  220.6 8.8 %collective-permute-start.15 = (bf16[2,8,16,128]{3,2,1,0:T(8,128)(2,1)S(1)}, bf16[2,8,16,128]{3,2,1,0:T(8,128)(2,1)S(1)}, u32[]{:S(2)}, u32[]{:S(2)}) collective-permute-start(bf16[2,8,16,128]{3,2,1,0:T(8,128)(2,1)S(1)} %get-tuple-element.28), channel_id=1, source_target_pairs={{0,1},{1,2},{2,3},{3,4},{4,5},{5,6},{6,7},{7,8},{8,9},{9,10},{10,1... | collective-permute-start | bytes 196616 | tf_op jit(solution)/shard_map/ppermute | solution.py:21
  (3 other events, 2.6 us)
Sparse Core Ops, SparseCore 0:
  24.9 66.1 all-gather.1

commit v19 on v7

--- a/solution.py
+++ b/solution.py
@@ -77,7 +77,7 @@
 def gather_weights(embed_weight, qkv_weight):
     _, feat, width = embed_weight.shape
     qkv_flat = qkv_weight.reshape(-1, width)
-    extra = -qkv_flat.shape[0] % 16
+    extra = -qkv_flat.shape[0] % 4
     rows = jnp.concatenate(
         [embed_weight[0], qkv_flat, jnp.zeros((extra, width), qkv_flat.dtype)], axis=0
     )

time: 239 us -> 247 us (1.033); the launches traced: 235 us -> 246 us
  local copies, waits for them, and re-layouts: 13.9 us -> 22 us
  waiting for transfers between devices: 43.7 us -> 46.7 us
    reshape x0 -> x1, local copies, waits for them, and re-layouts: none -> 7.27 us  [gather_weights(): gathered = gathered.reshape(peers, rows.shape[0], width)]
    ppermute x8, starting transfers between devices: 32.6 us -> 37.3 us  [padded_2(): lax.ppermute(tail, axis, [(i, (i + 1) % count) for i in range(ends)])]
    ppermute x8, starting transfers between devices: 24.5 us -> 20.3 us  [padded_2(): lax.ppermute(head, axis, [((i + 1) % count, i) for i in range(ends)])]
    all_gather x1, waiting for transfers between devices: 0.75 us -> 3.43 us  [gather_weights(): lax.all_gather(gathered, 'blk', axis=0, tiled=True, axis_index_groups=far)]
  transfers between devices with their start and end apart: 19 -> 19, of which waited for: 12 -> 11; matrix products, arithmetic and copies ran while one was open for 6% -> 5% of each run, Pallas kernels for 0% -> 0%
where the time goes in v19:
time: 247 us; the launch traced here: 246 us
  starting transfers between devices  71 us (29%)
  blocking collectives  64.3 us (26%)
  waiting for transfers between devices  46.7 us (19%)
  local copies, waits for them, and re-layouts  22 us (9%)
  between operations  18.3 us (7%)
  matrix products  17.4 us (7%)
  other arithmetic  6.19 us (3%)
    ppermute x8, starting transfers between devices, padded_2(): lax.ppermute(tail, axis, [(i, (i + 1) % count) for i in range(ends)])  37.3 us
    all_to_all x2, blocking collectives, copy_for_each(): lax.all_to_all(jnp.broadcast_to(shard[None], (peers, *shard.shape)), axis...  37.2 us
    ppermute x8, waiting for transfers between devices, padded_2(): lax.ppermute(head, axis, [((i + 1) % count, i) for i in range(ends)])  23.8 us
    ppermute x8, starting transfers between devices, padded_2(): lax.ppermute(head, axis, [((i + 1) % count, i) for i in range(ends)])  20.3 us
    all_to_all x1, waiting for transfers between devices, sum_at_owner(): lax.all_to_all(cut_along(shard, dim, peers), axis, 0, 0, tiled=True)  14.4 us
    all_gather x1, blocking collectives, gather_weights(): lax.all_gather(rows, 'blk', axis=0, tiled=True, axis_index_groups=near)  9.64 us
    all_to_all x1, blocking collectives, local(): lax.all_to_all(hidden, 'zslab', split_axis=0, concat_axis=1, tiled=True)  9.34 us
    all_to_all x1, starting transfers between devices, sum_at_owner(): lax.all_to_all(cut_along(shard, dim, peers), axis, 0, 0, tiled=True)  8.22 us
  transfers between devices with their start and end apart: 19, of which 11 were waited for; matrix products, arithmetic and copies ran while one was open for 5% of the time, Pallas kernels for 0%

profile of v19, /device:TPU:103, one launch (start us, length us, event | category | flops | bytes accessed | tf_op | source)
XLA Modules:
  0.0 245.9 jit_solution(5792938057822958116)
XLA Ops:
  8.2 9.6 %all-gather = bf16[4,76,1024]{2,1,0:T(8,128)(2,1)S(1)} all-gather(bf16[1,76,1024]{2,1,0:T(8,128)(2,1)S(1)} %maximum_bitcast_fusion), channel_id=1, replica_groups={{0,1,2,3},{4,5,6,7},{8,9,10,11},{12,13,14,15},{16,17,18,19},{20,21,22,2..., dimensions={0}, use_global_device_ids=true | all-gather | bytes 778240 | tf_op jit(solution)/shard_map/all_gather | solution.py:87
  18.9 3.5 %collective-permute-start = (bf16[8,2,16,128]{3,2,1,0:T(8,128)(2,1)S(1)}, bf16[8,2,16,128]{3,2,1,0:T(8,128)(2,1)S(1)}, u32[]{:S(2)}, u32[]{:S(2)}) collective-permute-start(bf16[8,2,16,128]{3,2,1,0:T(8,128)(2,1)S(1)} %get-tuple-element.41), channel_id=1, source_target_pairs={{0,32},{32,64},{64,96},{96,128},{128,160},{160,192},{192,224},{1,3... | collective-permute-start | bytes 196616 | tf_op jit(solution)/shard_map/ppermute | solution.py:21
  25.2 3.1 %collective-permute-done.1 = bf16[8,2,16,128]{3,2,1,0:T(8,128)(2,1)S(1)} collective-permute-done((bf16[8,2,16,128]{3,2,1,0:T(8,128)(2,1)S(1)}, bf16[8,2,16,128]{3,2,1,0:T(8,128)(2,1)S(1)}, u32[]{:S(2)}, u32[]{:S(2)}) %collective-permute-start.1) | collective-permute-done | bytes 65568 | tf_op jit(solution)/shard_map/ppermute | solution.py:23
  28.4 3.5 %collective-permute-start.3 = (bf16[2,8,16,128]{3,2,1,0:T(8,128)(2,1)S(1)}, bf16[2,8,16,128]{3,2,1,0:T(8,128)(2,1)S(1)}, u32[]{:S(2)}, u32[]{:S(2)}) collective-permute-start(bf16[2,8,16,128]{3,2,1,0:T(8,128)(2,1)S(1)} %get-tuple-element.33), channel_id=1, source_target_pairs={{1,0},{2,1},{3,2},{4,3},{5,4},{6,5},{7,6},{8,7},{9,8},{10,9},{11,1... | collective-permute-start | bytes 196616 | tf_op jit(solution)/shard_map/ppermute | solution.py:23
  31.9 5.7 %collective-permute-start.2 = (bf16[2,8,16,128]{3,2,1,0:T(8,128)(2,1)S(1)}, bf16[2,8,16,128]{3,2,1,0:T(8,128)(2,1)S(1)}, u32[]{:S(2)}, u32[]{:S(2)}) collective-permute-start(bf16[2,8,16,128]{3,2,1,0:T(8,128)(2,1)S(1)} %get-tuple-element.34), channel_id=1, source_target_pairs={{0,1},{1,2},{2,3},{3,4},{4,5},{5,6},{6,7},{7,8},{8,9},{9,10},{10,1... | collective-permute-start | bytes 196616 | tf_op jit(solution)/shard_map/ppermute | solution.py:21
  45.7 3.2 %collective-permute-start.5 = (bf16[8,2,16,128]{3,2,1,0:T(8,128)(2,1)S(1)}, bf16[8,2,16,128]{3,2,1,0:T(8,128)(2,1)S(1)}, u32[]{:S(2)}, u32[]{:S(2)}) collective-permute-start(bf16[8,2,16,128]{3,2,1,0:T(8,128)(2,1)S(1)} %get-tuple-element.40), channel_id=1, source_target_pairs={{32,0},{64,32},{96,64},{128,96},{160,128},{192,160},{224,192},{33,... | collective-permute-start | bytes 196616 | tf_op jit(solution)/shard_map/ppermute | solution.py:23
  49.4 3.1 %collective-permute-done.5 = bf16[8,2,16,128]{3,2,1,0:T(8,128)(2,1)S(1)} collective-permute-done((bf16[8,2,16,128]{3,2,1,0:T(8,128)(2,1)S(1)}, bf16[8,2,16,128]{3,2,1,0:T(8,128)(2,1)S(1)}, u32[]{:S(2)}, u32[]{:S(2)}) %collective-permute-start.5) | collective-permute-done | bytes 65568 | tf_op jit(solution)/shard_map/ppermute | solution.py:23
  54.4 9.1 %collective-permute-start.6 = (bf16[2,8,16,128]{3,2,1,0:T(8,128)(2,1)S(1)}, bf16[2,8,16,128]{3,2,1,0:T(8,128)(2,1)S(1)}, u32[]{:S(2)}, u32[]{:S(2)}) collective-permute-start(bf16[2,8,16,128]{3,2,1,0:T(8,128)(2,1)S(1)} %get-tuple-element.30), channel_id=1, source_target_pairs={{0,1},{1,2},{2,3},{3,4},{4,5},{5,6},{6,7},{7,8},{8,9},{9,10},{10,1... | collective-permute-start | bytes 196616 | tf_op jit(solution)/shard_map/ppermute | solution.py:21
  69.0 9.3 %all_to_all.38 = bf16[8,4,16,128]{3,2,1,0:T(8,128)(2,1)S(1)} all-to-all(bf16[8,4,16,128]{3,2,1,0:T(8,128)(2,1)S(1)} %get-tuple-element.55), channel_id=1, replica_groups=mesh['zslab'=8,'blk'=32] {'zslab'}, dimensions={0} | all-to-all | bytes 262144 | tf_op jit(solution)/shard_map/all_to_all | solution.py:160
  78.6 3.4 %all-gather.3.cloned.1.call-done = bf16[2432,1024]{1,0:T(8,128)(2,1)} async-done(((bf16[304,1024]{1,0:T(8,128)(2,1)}), bf16[2432,1024]{1,0:T(8,128)(2,1)}) %all-gather.3.cloned.1.call-update) | async-done | bytes 4980752 | tf_op jit(solution)/shard_map/all_gather | solution.py:88
  82.0 7.3 %reshape.173 = bf16[32,76,1024]{2,1,0:T(8,128)(2,1)} reshape(bf16[2432,1024]{1,0:T(8,128)(2,1)} %all-gather.3.cloned.1.call-done) | data formatting | bytes 9961472 | tf_op jit(solution)/shard_map/reshape | solution.py:89
  89.3 3.0 %fusion.26 = bf16[32,1024]{1,0:T(8,128)(2,1)S(1)} fusion(bf16[32,76,1024]{2,1,0:T(8,128)(2,1)} %reshape.173, bf16[32,32,64]{2,1,0:T(8,128)(2,1)S(1)} %reshape_reshape.9), kind=kOutput, calls=%fused_computation.31 | convolution fusion | flops 134250496 | bytes 4390912 | tf_op jit(solution)/shard_map/tbf,bfd->td/dot_general | solution.py:169
  93.2 5.2 %all-to-all-start.1 = ((bf16[8,32,1024]{2,1,0:T(8,128)(2,1)}), bf16[8,32,1024]{2,1,0:T(8,128)(2,1)S(1)}, u32[]{:S(2)}, u32[]{:S(2)}) async-start(bf16[8,32,1024]{2,1,0:T(8,128)(2,1)} %broadcast_in_dim.6), calls=%async_computation.1 | async-start | bytes 1048576 | tf_op jit(solution)/shard_map/all_to_all | solution.py:32
  102.2 4.1 %all-to-all-done.1 = bf16[8,32,1024]{2,1,0:T(8,128)(2,1)S(1)} async-done(((bf16[8,32,1024]{2,1,0:T(8,128)(2,1)}), bf16[8,32,1024]{2,1,0:T(8,128)(2,1)S(1)}, u32[]{:S(2)}, u32[]{:S(2)}) %all-to-all-start.1) | async-done | bytes 524320 | tf_op jit(solution)/shard_map/all_to_all | solution.py:32
  106.7 25.2 %all_to_all.39 = bf16[32,32,256]{2,1,0:T(8,128)(2,1)S(1)} all-to-all(bf16[32,32,256]{2,1,0:T(8,128)(2,1)S(1)} %broadcast_in_dim.7), channel_id=1, replica_groups=mesh['zslab'=8,'blk'=32] {'blk'}, dimensions={0} | all-to-all | bytes 1048576 | tf_op jit(solution)/shard_map/all_to_all | solution.py:32
  137.1 8.2 %all-to-all-start.3 = ((bf16[32,32,256]{2,1,0:T(8,128)(2,1)}), bf16[32,32,256]{2,1,0:T(8,128)(2,1)}, u32[]{:S(2)}, u32[]{:S(2)}) async-start(bf16[32,32,256]{2,1,0:T(8,128)(2,1)} %pad_maximum_fusion), calls=%async_computation.3 | async-start | bytes 1048576 | tf_op jit(solution)/shard_map/all_to_all | solution.py:73
  145.5 14.4 %all-to-all-done.3 = bf16[32,32,256]{2,1,0:T(8,128)(2,1)} async-done(((bf16[32,32,256]{2,1,0:T(8,128)(2,1)}), bf16[32,32,256]{2,1,0:T(8,128)(2,1)}, u32[]{:S(2)}, u32[]{:S(2)}) %all-to-all-start.3) | async-done | bytes 524320 | tf_op jit(solution)/shard_map/all_to_all | solution.py:73
  161.4 11.9 %all_to_all.40 = bf16[8,32,1024]{2,1,0:T(8,128)(2,1)S(1)} all-to-all(bf16[8,32,1024]{2,1,0:T(8,128)(2,1)S(1)} %broadcast_in_dim.8), channel_id=1, replica_groups=mesh['zslab'=8,'blk'=32] {'zslab'}, dimensions={0} | all-to-all | bytes 1048576 | tf_op jit(solution)/shard_map/all_to_all | solution.py:32
  173.4 4.2 %fusion.4 = bf16[32,32,64]{2,0,1:T(8,128)(2,1)S(1)} fusion(bf16[32,76,1024]{2,1,0:T(8,128)(2,1)} %reshape.173, bf16[32,1024]{1,0:T(8,128)(2,1)S(1)} %reduce_sum.58), kind=kOutput, calls=%fused_computation.4 | convolution fusion | flops 134283264 | bytes 4390912 | tf_op jit(solution)/shard_map/td,bfd->tbf/dot_general | solution.py:223
  178.0 8.1 %all_to_all.41 = bf16[1,32,16,128]{3,2,0,1:T(8,128)(2,1)S(1)} all-to-all(bf16[1,32,16,128]{3,2,0,1:T(8,128)(2,1)S(1)} %bitcast.249), channel_id=1, replica_groups=mesh['zslab'=8,'blk'=32] {'zslab'}, dimensions={1} | all-to-all | bytes 262144 | tf_op jit(solution)/shard_map/all_to_all | solution.py:230
  195.0 9.3 %collective-permute-start.11 = (bf16[2,8,16,128]{3,2,1,0:T(8,128)(2,1)S(1)}, bf16[2,8,16,128]{3,2,1,0:T(8,128)(2,1)S(1)}, u32[]{:S(2)}, u32[]{:S(2)}) collective-permute-start(bf16[2,8,16,128]{3,2,1,0:T(8,128)(2,1)S(1)} %get-tuple-element.25), channel_id=1, source_target_pairs={{0,1},{1,2},{2,3},{3,4},{4,5},{5,6},{6,7},{7,8},{8,9},{9,10},{10,1... | collective-permute-start | bytes 196616 | tf_op jit(solution)/shard_map/ppermute | solution.py:21
  206.3 7.2 %collective-permute-done.10 = bf16[2,8,16,128]{3,2,1,0:T(8,128)(2,1)S(1)} collective-permute-done((bf16[2,8,16,128]{3,2,1,0:T(8,128)(2,1)S(1)}, bf16[2,8,16,128]{3,2,1,0:T(8,128)(2,1)S(1)}, u32[]{:S(2)}, u32[]{:S(2)}) %collective-permute-start.10) | collective-permute-done | bytes 65568 | tf_op jit(solution)/shard_map/ppermute | solution.py:23
  218.1 3.4 %collective-permute-start.13 = (bf16[8,2,16,128]{3,2,1,0:T(8,128)(2,1)S(1)}, bf16[8,2,16,128]{3,2,1,0:T(8,128)(2,1)S(1)}, u32[]{:S(2)}, u32[]{:S(2)}) collective-permute-start(bf16[8,2,16,128]{3,2,1,0:T(8,128)(2,1)S(1)} %get-tuple-element.36), channel_id=1, source_target_pairs={{32,0},{64,32},{96,64},{128,96},{160,128},{192,160},{224,192},{33,... | collective-permute-start | bytes 196616 | tf_op jit(solution)/shard_map/ppermute | solution.py:23
  229.1 7.2 %collective-permute-done.14 = bf16[2,8,16,128]{3,2,1,0:T(8,128)(2,1)S(1)} collective-permute-done((bf16[2,8,16,128]{3,2,1,0:T(8,128)(2,1)S(1)}, bf16[2,8,16,128]{3,2,1,0:T(8,128)(2,1)S(1)}, u32[]{:S(2)}, u32[]{:S(2)}) %collective-permute-start.14) | collective-permute-done | bytes 65568 | tf_op jit(solution)/shard_map/ppermute | solution.py:23
  (158 shorter events, 55.2 us)
Async XLA Ops:
  6.5 75.4 %all-gather.3.cloned.1.call-start = ((), (), s32[]{:S(2)}) async-start(), calls=%async_computation.6 | async-start | bytes 5603328 | tf_op jit(solution)/shard_map/all_gather | solution.py:88
  8.2 10.7 %copy-start.1 = (bf16[8,16,4,128]{3,2,1,0:T(4,128)(2,1)S(1)}, bf16[8,16,4,128]{3,2,1,0:T(4,128)(2,1)}, u32[]{:S(2)}) copy-start(bf16[8,16,4,128]{3,2,1,0:T(4,128)(2,1)} %param.7) | copy-start | bytes 393220
  17.9 6.5 %copy-start = (bf16[2,3456,128]{2,1,0:T(8,128)(2,1)S(1)}, bf16[2,3456,128]{2,1,0:T(8,128)(2,1)}, u32[]{:S(2)}) copy-start(bf16[2,3456,128]{2,1,0:T(8,128)(2,1)} %param.10) | copy-start | bytes 5308420
  18.9 6.3 %collective-permute-start = (bf16[8,2,16,128]{3,2,1,0:T(8,128)(2,1)S(1)}, bf16[8,2,16,128]{3,2,1,0:T(8,128)(2,1)S(1)}, u32[]{:S(2)}, u32[]{:S(2)}) collective-permute-start(bf16[8,2,16,128]{3,2,1,0:T(8,128)(2,1)S(1)} %get-tuple-element.41), channel_id=1, source_target_pairs={{0,32},{32,64},{64,96},{96,128},{128,160},{160,192},{192,224},{1,3... | collective-permute-start | bytes 196616 | tf_op jit(solution)/shard_map/ppermute | solution.py:21
  22.4 5.9 %collective-permute-start.1 = (bf16[8,2,16,128]{3,2,1,0:T(8,128)(2,1)S(1)}, bf16[8,2,16,128]{3,2,1,0:T(8,128)(2,1)S(1)}, u32[]{:S(2)}, u32[]{:S(2)}) collective-permute-start(bf16[8,2,16,128]{3,2,1,0:T(8,128)(2,1)S(1)} %get-tuple-element.42), channel_id=1, source_target_pairs={{32,0},{64,32},{96,64},{128,96},{160,128},{192,160},{224,192},{33,... | collective-permute-start | bytes 196616 | tf_op jit(solution)/shard_map/ppermute | solution.py:23
  24.5 13.0 %copy-start.5 = (s32[2,3]{1,0:T(2,128)S(1)}, s32[2,3]{1,0:T(2,128)}, u32[]{:S(2)}) copy-start(s32[2,3]{1,0:T(2,128)} %param.9) | copy-start | bytes 76
  28.4 11.8 %collective-permute-start.3 = (bf16[2,8,16,128]{3,2,1,0:T(8,128)(2,1)S(1)}, bf16[2,8,16,128]{3,2,1,0:T(8,128)(2,1)S(1)}, u32[]{:S(2)}, u32[]{:S(2)}) collective-permute-start(bf16[2,8,16,128]{3,2,1,0:T(8,128)(2,1)S(1)} %get-tuple-element.33), channel_id=1, source_target_pairs={{1,0},{2,1},{3,2},{4,3},{5,4},{6,5},{7,6},{8,7},{9,8},{10,9},{11,1... | collective-permute-start | bytes 196616 | tf_op jit(solution)/shard_map/ppermute | solution.py:23
  31.9 8.3 %collective-permute-start.2 = (bf16[2,8,16,128]{3,2,1,0:T(8,128)(2,1)S(1)}, bf16[2,8,16,128]{3,2,1,0:T(8,128)(2,1)S(1)}, u32[]{:S(2)}, u32[]{:S(2)}) collective-permute-start(bf16[2,8,16,128]{3,2,1,0:T(8,128)(2,1)S(1)} %get-tuple-element.34), channel_id=1, source_target_pairs={{0,1},{1,2},{2,3},{3,4},{4,5},{5,6},{6,7},{7,8},{8,9},{9,10},{10,1... | collective-permute-start | bytes 196616 | tf_op jit(solution)/shard_map/ppermute | solution.py:21
  43.7 5.7 %collective-permute-start.4 = (bf16[8,2,16,128]{3,2,1,0:T(8,128)(2,1)S(1)}, bf16[8,2,16,128]{3,2,1,0:T(8,128)(2,1)S(1)}, u32[]{:S(2)}, u32[]{:S(2)}) collective-permute-start(bf16[8,2,16,128]{3,2,1,0:T(8,128)(2,1)S(1)} %get-tuple-element.39), channel_id=1, source_target_pairs={{0,32},{32,64},{64,96},{96,128},{128,160},{160,192},{192,224},{1,3... | collective-permute-start | bytes 196616 | tf_op jit(solution)/shard_map/ppermute | solution.py:21
  45.7 6.7 %collective-permute-start.5 = (bf16[8,2,16,128]{3,2,1,0:T(8,128)(2,1)S(1)}, bf16[8,2,16,128]{3,2,1,0:T(8,128)(2,1)S(1)}, u32[]{:S(2)}, u32[]{:S(2)}) collective-permute-start(bf16[8,2,16,128]{3,2,1,0:T(8,128)(2,1)S(1)} %get-tuple-element.40), channel_id=1, source_target_pairs={{32,0},{64,32},{96,64},{128,96},{160,128},{192,160},{224,192},{33,... | collective-permute-start | bytes 196616 | tf_op jit(solution)/shard_map/ppermute | solution.py:23
  52.5 13.1 %collective-permute-start.7 = (bf16[2,8,16,128]{3,2,1,0:T(8,128)(2,1)S(1)}, bf16[2,8,16,128]{3,2,1,0:T(8,128)(2,1)S(1)}, u32[]{:S(2)}, u32[]{:S(2)}) collective-permute-start(bf16[2,8,16,128]{3,2,1,0:T(8,128)(2,1)S(1)} %get-tuple-element.29), channel_id=1, source_target_pairs={{1,0},{2,1},{3,2},{4,3},{5,4},{6,5},{7,6},{8,7},{9,8},{10,9},{11,1... | collective-permute-start | bytes 196616 | tf_op jit(solution)/shard_map/ppermute | solution.py:23
  54.4 11.7 %collective-permute-start.6 = (bf16[2,8,16,128]{3,2,1,0:T(8,128)(2,1)S(1)}, bf16[2,8,16,128]{3,2,1,0:T(8,128)(2,1)S(1)}, u32[]{:S(2)}, u32[]{:S(2)}) collective-permute-start(bf16[2,8,16,128]{3,2,1,0:T(8,128)(2,1)S(1)} %get-tuple-element.30), channel_id=1, source_target_pairs={{0,1},{1,2},{2,3},{3,4},{4,5},{5,6},{6,7},{7,8},{8,9},{9,10},{10,1... | collective-permute-start | bytes 196616 | tf_op jit(solution)/shard_map/ppermute | solution.py:21
  93.2 13.2 %all-to-all-start.1 = ((bf16[8,32,1024]{2,1,0:T(8,128)(2,1)}), bf16[8,32,1024]{2,1,0:T(8,128)(2,1)S(1)}, u32[]{:S(2)}, u32[]{:S(2)}) async-start(bf16[8,32,1024]{2,1,0:T(8,128)(2,1)} %broadcast_in_dim.6), calls=%async_computation.1 | async-start | bytes 1048576 | tf_op jit(solution)/shard_map/all_to_all | solution.py:32
  106.7 25.8 %copy-start.6 = (bf16[32,128]{1,0:T(8,128)(2,1)S(1)}, bf16[32,128]{1,0:T(8,128)(2,1)}, u32[]{:S(2)}) copy-start(bf16[32,128]{1,0:T(8,128)(2,1)} %param.13) | copy-start | bytes 24580
  137.1 22.8 %all-to-all-start.3 = ((bf16[32,32,256]{2,1,0:T(8,128)(2,1)}), bf16[32,32,256]{2,1,0:T(8,128)(2,1)}, u32[]{:S(2)}, u32[]{:S(2)}) async-start(bf16[32,32,256]{2,1,0:T(8,128)(2,1)} %pad_maximum_fusion), calls=%async_computation.3 | async-start | bytes 1048576 | tf_op jit(solution)/shard_map/all_to_all | solution.py:73
  177.7 8.4 %copy-start.3 = (f32[8,4,16,128]{3,2,1,0:T(8,128)S(1)}, f32[8,4,16,128]{3,2,1,0:T(8,128)}, u32[]{:S(2)}) copy-start(f32[8,4,16,128]{3,2,1,0:T(8,128)} %get-tuple-element.56) | copy-start | bytes 786436
  186.3 6.6 %collective-permute-start.8 = (bf16[8,2,16,128]{3,2,1,0:T(8,128)(2,1)S(1)}, bf16[8,2,16,128]{3,2,1,0:T(8,128)(2,1)S(1)}, u32[]{:S(2)}, u32[]{:S(2)}) collective-permute-start(bf16[8,2,16,128]{3,2,1,0:T(8,128)(2,1)S(1)} %get-tuple-element.37), channel_id=1, source_target_pairs={{0,32},{32,64},{64,96},{96,128},{128,160},{160,192},{192,224},{1,3... | collective-permute-start | bytes 196616 | tf_op jit(solution)/shard_map/ppermute | solution.py:21
  189.0 5.9 %collective-permute-start.9 = (bf16[8,2,16,128]{3,2,1,0:T(8,128)(2,1)S(1)}, bf16[8,2,16,128]{3,2,1,0:T(8,128)(2,1)S(1)}, u32[]{:S(2)}, u32[]{:S(2)}) collective-permute-start(bf16[8,2,16,128]{3,2,1,0:T(8,128)(2,1)S(1)} %get-tuple-element.38), channel_id=1, source_target_pairs={{32,0},{64,32},{96,64},{128,96},{160,128},{192,160},{224,192},{33,... | collective-permute-start | bytes 196616 | tf_op jit(solution)/shard_map/ppermute | solution.py:23
  195.0 11.4 %collective-permute-start.11 = (bf16[2,8,16,128]{3,2,1,0:T(8,128)(2,1)S(1)}, bf16[2,8,16,128]{3,2,1,0:T(8,128)(2,1)S(1)}, u32[]{:S(2)}, u32[]{:S(2)}) collective-permute-start(bf16[2,8,16,128]{3,2,1,0:T(8,128)(2,1)S(1)} %get-tuple-element.25), channel_id=1, source_target_pairs={{0,1},{1,2},{2,3},{3,4},{4,5},{5,6},{6,7},{7,8},{8,9},{9,10},{10,1... | collective-permute-start | bytes 196616 | tf_op jit(solution)/shard_map/ppermute | solution.py:21
  204.3 9.2 %collective-permute-start.10 = (bf16[2,8,16,128]{3,2,1,0:T(8,128)(2,1)S(1)}, bf16[2,8,16,128]{3,2,1,0:T(8,128)(2,1)S(1)}, u32[]{:S(2)}, u32[]{:S(2)}) collective-permute-start(bf16[2,8,16,128]{3,2,1,0:T(8,128)(2,1)S(1)} %get-tuple-element.26), channel_id=1, source_target_pairs={{1,0},{2,1},{3,2},{4,3},{5,4},{6,5},{7,6},{8,7},{9,8},{10,9},{11,1... | collective-permute-start | bytes 196616 | tf_op jit(solution)/shard_map/ppermute | solution.py:23
  216.1 6.6 %collective-permute-start.12 = (bf16[8,2,16,128]{3,2,1,0:T(8,128)(2,1)S(1)}, bf16[8,2,16,128]{3,2,1,0:T(8,128)(2,1)S(1)}, u32[]{:S(2)}, u32[]{:S(2)}) collective-permute-start(bf16[8,2,16,128]{3,2,1,0:T(8,128)(2,1)S(1)} %get-tuple-element.35), channel_id=1, source_target_pairs={{0,32},{32,64},{64,96},{96,128},{128,160},{160,192},{192,224},{1,3... | collective-permute-start | bytes 196616 | tf_op jit(solution)/shard_map/ppermute | solution.py:21
  218.1 5.9 %collective-permute-start.13 = (bf16[8,2,16,128]{3,2,1,0:T(8,128)(2,1)S(1)}, bf16[8,2,16,128]{3,2,1,0:T(8,128)(2,1)S(1)}, u32[]{:S(2)}, u32[]{:S(2)}) collective-permute-start(bf16[8,2,16,128]{3,2,1,0:T(8,128)(2,1)S(1)} %get-tuple-element.36), channel_id=1, source_target_pairs={{32,0},{64,32},{96,64},{128,96},{160,128},{192,160},{224,192},{33,... | collective-permute-start | bytes 196616 | tf_op jit(solution)/shard_map/ppermute | solution.py:23
  224.0 5.1 %collective-permute-start.15 = (bf16[2,8,16,128]{3,2,1,0:T(8,128)(2,1)S(1)}, bf16[2,8,16,128]{3,2,1,0:T(8,128)(2,1)S(1)}, u32[]{:S(2)}, u32[]{:S(2)}) collective-permute-start(bf16[2,8,16,128]{3,2,1,0:T(8,128)(2,1)S(1)} %get-tuple-element.21), channel_id=1, source_target_pairs={{0,1},{1,2},{2,3},{3,4},{4,5},{5,6},{6,7},{7,8},{8,9},{9,10},{10,1... | collective-permute-start | bytes 196616 | tf_op jit(solution)/shard_map/ppermute | solution.py:21
  227.0 9.2 %collective-permute-start.14 = (bf16[2,8,16,128]{3,2,1,0:T(8,128)(2,1)S(1)}, bf16[2,8,16,128]{3,2,1,0:T(8,128)(2,1)S(1)}, u32[]{:S(2)}, u32[]{:S(2)}) collective-permute-start(bf16[2,8,16,128]{3,2,1,0:T(8,128)(2,1)S(1)} %get-tuple-element.22), channel_id=1, source_target_pairs={{1,0},{2,1},{3,2},{4,3},{5,4},{6,5},{7,6},{8,7},{9,8},{10,9},{11,1... | collective-permute-start | bytes 196616 | tf_op jit(solution)/shard_map/ppermute | solution.py:23
  (4 other events, 3.8 us)
Sparse Core Ops, SparseCore 0:
  19.0 62.9 all-gather.2
